TPU v7x, 32 devices: a whole 2x2x4 slice. The times are simulated.
32 devices in a mesh: groups: 2 (over y), ctx: 4 (over z), head: 4 (over x, core).
Axes of the slice: x: 2, y: 2, z: 4, core: 2. Of those that a mesh axis runs over, the one named last changes fastest.
Arguments:
- queries: bfloat16 [1024, 8192], P(('groups', 'ctx'), 'head'), parts along dimension 0, may hold values from -6 to 6
- key_states: bfloat16 [1024, 1024], P(('groups', 'ctx'), 'head'), parts along dimension 0, may hold values from -8.5 to 8.5
- value_states: bfloat16 [1024, 1024], P(('groups', 'ctx'), 'head'), parts along dimension 0, may hold values from -6 to 6
- out_grad: bfloat16 [1024, 8192], P(('groups', 'ctx'), 'head'), parts along dimension 0, may hold values from -6 to 6
- mask_flags: int32 [8, 4], P('groups'), parts along dimension 0, may hold values from 0 to 1, as said below
- shard_blocks: int32 [8], P('groups'), parts along dimension 0, may hold values from 0 to 3, each once
- key_proj: bfloat16 [8192, 1024], P(None, 'head'), may hold values from -0.1875 to 0.1875
- value_proj: bfloat16 [8192, 1024], P(None, 'head'), may hold values from -0.1875 to 0.1875
Outputs:
- query_grad: bfloat16 [1024, 8192], P(('groups', 'ctx'), 'head'), parts along dimension 0
- key_grad: bfloat16 [1024, 1024], P(('groups', 'ctx'), 'head'), parts along dimension 0
- value_grad: bfloat16 [1024, 1024], P(('groups', 'ctx'), 'head'), parts along dimension 0
- input_grad_t: bfloat16 [8192, 1024], P('head', ('groups', 'ctx')), parts along dimension 1
There are 2 independent parts, one for each index of `groups`. A program takes and returns all parts, laid end to end along the dimension named above; an argument that names none is the same for every part. Nothing has to cross between parts.
Inputs may be any that keep to these rules, and one draw needn't show every extreme that they name: mask_flags[b, b] = 1 for every block b. `shard_blocks`: a permutation of the block numbers.
All inputs are finite; a program needn't handle non-finite values.
Results may differ from a plain program's by a relative error of at most 0.039.
Values may be sent and summed in bfloat16 or wider, within the bound.
No kernel may reach another device: no remote copies, remote signals or barrier semaphores. Data moves between devices by JAX's collectives and lax.ppermute only.
A program may use at most 64 MiB of HBM per device.

v0:
```python
import math

import jax
import jax.numpy as jnp
from jax import lax
from jax.sharding import PartitionSpec as P

HD = 128
BLK = 128


masked_score = -1e30


def from_behind(value, axis, steps):
    count = lax.axis_size(axis)
    pairs = [(source, (source + steps) % count) for source in range(count)]
    return lax.ppermute(value, axis, pairs)


def select_rows(lookup, picked):
    onehot = (picked[:, None] == lax.iota(jnp.int32, lookup.shape[0])[None, :]).astype(jnp.int32)
    return jnp.sum(onehot[:, :, None] * lookup[None, :, :], axis=1)


def select_cols(lookup, picked):
    onehot = (picked[:, None] == lax.iota(jnp.int32, lookup.shape[1])[None, :]).astype(jnp.int32)
    return jnp.sum(lookup[:, None, :] * onehot[None, :, :], axis=2)


def local(
    queries, key_states, value_states, out_grad, mask_flags, shard_blocks, key_proj, value_proj
):
    rows_here = queries.shape[0]
    kv_cols = key_states.shape[1]
    kv_heads = kv_cols // HD
    group_size = queries.shape[1] // kv_cols
    inv_root = HD ** (-0.5)
    cycle_size = lax.axis_size("ctx")
    position = lax.axis_index("ctx")
    query_heads = queries.reshape(rows_here, kv_heads, group_size, HD)
    grad_heads = out_grad.reshape(rows_here, kv_heads, group_size, HD)
    own_blocks = lax.dynamic_slice_in_dim(
        shard_blocks, position * (rows_here // BLK), rows_here // BLK
    )
    own_flags = select_rows(mask_flags, own_blocks)

    def pair_mask(first_row, row_count):
        their_blocks = lax.dynamic_slice_in_dim(shard_blocks, first_row // BLK, row_count // BLK)
        pair_flags = select_cols(own_flags, their_blocks) > 0
        allowed = jnp.repeat(jnp.repeat(pair_flags, BLK, axis=0), BLK, axis=1)
        return (allowed, jnp.any(pair_flags))

    def score_block(key_block, allowed):
        key_heads = key_block.reshape(-1, kv_heads, HD)
        scores = (
            jnp.einsum("qkgd,tkd->kgqt", query_heads, key_heads, preferred_element_type=jnp.float32)
            * inv_root
        )
        return (jnp.where(allowed[None, None], scores, masked_score), key_heads)

    def forward_part(running, key_block, value_block, first_row):
        allowed, active = pair_mask(first_row, key_block.shape[0])

        def update(current):
            row_max, row_sum, weighted = current
            scores, key_heads = score_block(key_block, allowed)
            new_max = jnp.maximum(row_max, jnp.max(scores, axis=-1))
            rescale = jnp.exp(row_max - new_max)
            probs = jnp.exp(scores - new_max[..., None])
            value_heads = value_block.reshape(-1, kv_heads, HD)
            row_sum = row_sum * rescale + jnp.sum(probs, axis=-1)
            weighted = weighted * rescale[..., None] + jnp.einsum(
                "kgqt,tkd->kgqd",
                probs.astype(jnp.bfloat16),
                value_heads,
                preferred_element_type=jnp.float32,
            )
            return (new_max, row_sum, weighted)

        def unchanged(current):
            return current

        return lax.cond(active, update, unchanged, running)

    def backward_part(key_block, value_block, first_row, log_total, row_delta):
        row_count = key_block.shape[0]
        allowed, active = pair_mask(first_row, row_count)

        def compute(ignored):
            scores, key_heads = score_block(key_block, allowed)
            probs = jnp.exp(scores - log_total[..., None])
            value_heads = value_block.reshape(row_count, kv_heads, HD)
            dprobs = jnp.einsum(
                "qkgd,tkd->kgqt", grad_heads, value_heads, preferred_element_type=jnp.float32
            )
            dscores = (probs * (dprobs - row_delta[..., None])).astype(jnp.bfloat16)
            probs_low = probs.astype(jnp.bfloat16)
            query_term = (
                jnp.einsum("kgqt,tkd->qkgd", dscores, key_heads, preferred_element_type=jnp.float32)
                * inv_root
            )
            key_term = (
                jnp.einsum(
                    "kgqt,qkgd->tkd", dscores, query_heads, preferred_element_type=jnp.float32
                )
                * inv_root
            )
            value_term = jnp.einsum(
                "kgqt,qkgd->tkd", probs_low, grad_heads, preferred_element_type=jnp.float32
            )
            return (
                query_term,
                key_term.reshape(row_count, kv_cols),
                value_term.reshape(row_count, kv_cols),
            )

        def nothing(ignored):
            return (
                jnp.zeros((rows_here, kv_heads, group_size, HD), jnp.float32),
                jnp.zeros((row_count, kv_cols), jnp.float32),
                jnp.zeros((row_count, kv_cols), jnp.float32),
            )

        return lax.cond(active, compute, nothing, 0)

    def backward_piece(query_acc, key_rows, value_rows, first_row, log_total, row_delta):
        row_count = key_rows.shape[0]
        step_rows = math.gcd(row_count, 512)
        key_out = jnp.zeros((row_count, kv_cols), jnp.float32)
        value_out = jnp.zeros((row_count, kv_cols), jnp.float32)

        def backward_visit(turn_index, current):
            query_now, key_now, value_now = current
            offset = turn_index * step_rows
            query_term, key_term, value_term = backward_part(
                key_rows, value_rows, first_row + offset, log_total, row_delta
            )
            key_now = key_term
            value_now = value_term
            return (query_now + query_term, key_now, value_now)

        return lax.fori_loop(
            0, row_count // step_rows, backward_visit, (query_acc, key_out, value_out)
        )

    start_stats = (
        jnp.full((kv_heads, group_size, rows_here), masked_score, jnp.float32),
        jnp.zeros((kv_heads, group_size, rows_here), jnp.float32),
        jnp.zeros((kv_heads, group_size, rows_here, HD), jnp.float32),
    )
    query_start = jnp.zeros((rows_here, kv_heads, group_size, HD), jnp.float32)
    key_rows = lax.all_gather(key_states, "ctx", axis=0, tiled=True)
    value_rows = lax.all_gather(value_states, "ctx", axis=0, tiled=True)
    row_count = key_rows.shape[0]
    step_rows = math.gcd(row_count, 512)

    def forward_visit(turn_index, current):
        offset = turn_index * step_rows
        return forward_part(
            current,
            lax.dynamic_slice_in_dim(key_rows, offset, step_rows),
            lax.dynamic_slice_in_dim(value_rows, offset, step_rows),
            offset,
        )

    forward_stats = lax.fori_loop(0, row_count // step_rows, forward_visit, start_stats)
    row_max, row_sum, weighted = forward_stats
    finish_log_total = row_max + jnp.log(row_sum)
    attended = (weighted / row_sum[..., None]).astype(jnp.bfloat16)
    finish_row_delta = jnp.einsum(
        "kgqd,qkgd->kgq", attended, grad_heads, preferred_element_type=jnp.float32
    )
    log_total = finish_log_total
    row_delta = finish_row_delta

    def cycle_turn(turn_index, current):
        query_acc, key_block, value_block, key_acc, value_acc = current
        anchor = (position - turn_index) % cycle_size
        query_acc, key_term, value_term = backward_piece(
            query_acc, key_block, value_block, anchor * rows_here, log_total, row_delta
        )
        key_acc = key_acc + key_term
        value_acc = value_acc + value_term
        key_block, value_block = from_behind((key_block, value_block), "ctx", 1)
        key_acc, value_acc = from_behind((key_acc, value_acc), "ctx", 1)
        return (query_acc, key_block, value_block, key_acc, value_acc)

    zero_grads = jnp.zeros((rows_here, kv_cols), jnp.float32)
    query_acc, spent_keys, spent_values, key_acc, value_acc = lax.fori_loop(
        0, cycle_size, cycle_turn, (query_start, key_states, value_states, zero_grads, zero_grads)
    )
    query_grad = query_acc.reshape(rows_here, -1).astype(jnp.bfloat16)
    key_grad = key_acc.astype(jnp.bfloat16)
    value_grad = value_acc.astype(jnp.bfloat16)
    contraction = (((1,), (1,)), ((), ()))
    input_grad_t = lax.psum_scatter(
        lax.dot_general(key_proj, key_grad, contraction, preferred_element_type=jnp.float32)
        + lax.dot_general(value_proj, value_grad, contraction, preferred_element_type=jnp.float32),
        "head",
        scatter_dimension=0,
        tiled=True,
    ).astype(jnp.bfloat16)
    return (query_grad, key_grad, value_grad, input_grad_t)


def solution(mesh):
    return jax.shard_map(
        local,
        mesh=mesh,
        in_specs=(
            P(("groups", "ctx"), "head"),
            P(("groups", "ctx"), "head"),
            P(("groups", "ctx"), "head"),
            P(("groups", "ctx"), "head"),
            P("groups", None),
            P("groups"),
            P(None, "head"),
            P(None, "head"),
        ),
        out_specs=(
            P(("groups", "ctx"), "head"),
            P(("groups", "ctx"), "head"),
            P(("groups", "ctx"), "head"),
            P("head", ("groups", "ctx")),
        ),
        check_vma=False,
    )
```

profile of v0, /device:TPU:0, one launch (start us, length us, event | category | flops | bytes accessed | tf_op | source)
XLA Modules:
  0.0 206.5 jit_solution(3584630542921938377)
XLA Ops:
  15.6 15.8 %all_gather.6 = bf16[512,256]{1,0:T(8,128)(2,1)S(1)} all-gather(bf16[128,256]{1,0:T(8,128)(2,1)} %copy.125), channel_id=1, replica_groups=mesh['groups'=2,'ctx'=4,'head'=4] {'ctx'}, dimensions={0}, use_global_device_ids=true | all-gather | bytes 327680 | tf_op jit(solution)/shard_map/all_gather | solution.py:153
  31.4 14.8 %all_gather.7 = bf16[512,256]{1,0:T(8,128)(2,1)S(1)} all-gather(bf16[128,256]{1,0:T(8,128)(2,1)} %copy.126), channel_id=1, replica_groups=mesh['groups'=2,'ctx'=4,'head'=4] {'ctx'}, dimensions={0}, use_global_device_ids=true | all-gather | bytes 327680 | tf_op jit(solution)/shard_map/all_gather | solution.py:154
  47.7 7.7 %conditional.2 = ((f32[2,8,128]{2,1,0:T(8,128)S(1)}, f32[2,8,128]{2,1,0:T(8,128)S(1)}, f32[2,8,128,128]{3,2,1,0:T(8,128)S(1)})) conditional(s32[]{:T(128)} %convert_element_type.64, (f32[2,8,128]{2,1,0:T(8,128)S(1)}, f32[2,8,128]{2,1,0:T(8,128)S(1)}, f32[2,8,128,128]{3,2,1,0:T(8,128)S(1)}) %tuple.61, (s32[4]{0:T(128)S(1)}, ...), branch_computations={%region_3.4_spmd, %region_4.7_spmd} | conditional | flops 548933632 | bytes 33687636 | solution.py:84
  48.7 1.9 copy-done.1
  51.6 3.8 %fusion.9 = f32[2,8,128,128]{3,2,1,0:T(8,128)S(1)} fusion(f32[2,512,128,8]{2,1,3,0:T(8,128)} %copy-done.1, f32[2,8,128]{2,1,0:T(8,128)S(1)} %max.2, pred[512]{0:T(512)(128)(4,1)S(1)} %broadcast_bitcast_fusion, f32[2,8,128,128]{3,2,1,0:T(8,128)S(1)} %get-tuple-element.448, f32[2,8,128]{2,1,0:T(8,128)S(1)} %get-tuple-element.591, ...), kind=kOutput, calls=%fused_computation.11 | convolution fusion | flops 273154048 | bytes 6570496 | tf_op jit(solution)/shard_map/while/body/eval_jaxpr/cond/branch_1_fun/kgqt,tkd->kgqd/dot_general | solution.py:73
  58.2 79.8 %while.56 = (s32[]{:T(128)}, f32[128,2,8,128]{3,0,2,1:T(8,128)}, bf16[128,256]{1,0:T(8,128)(2,1)}, bf16[128,256]{1,0:T(8,128)(2,1)}, f32[128,256]{0,1:T(8,128)S(...) while((s32[]{:T(128)}, f32[128,2,8,128]{3,0,2,1:T(8,128)}, ...), condition=%wide.region_11.12_spmd.clone, body=%wide.region_7.11_spmd.clone.sunk | while | flops 338264096 | bytes 14893891 | solution.py:190
  63.8 2.0 fusion.47
  66.5 3.3 %conditional.5 = (f32[128,2,8,128]{3,0,2,1:T(8,128)S(1)}, f32[128,256]{0,1:T(8,128)S(1)}, f32[128,256]{0,1:T(8,128)S(1)}) conditional(s32[]{:T(128)} %convert_element_type.84, () %tuple.92, (pred[]{:T(512)}, bf16[128,256]{1,0:T(8,128)(2,1)}, bf16[128,2,8,128]{0,3,2,1:T(8,128)(2,1)S(1)}, f32[2,8,128]{2,1,0:T(8,128)S(1)}, bf16[128,256]{1,0:T(8,128)(2,1)}, ...), branch_computations={%region_9.9_spmd, %region_10.10_spmd} | conditional | flops 337674240 | bytes 8601625 | solution.py:125
  69.9 3.1 %collective-permute-start.2 = (f32[128,256]{0,1:T(8,128)S(1)}, f32[128,256]{0,1:T(8,128)S(1)}, u32[]{:S(2)}, u32[]{:S(2)}) collective-permute-start(f32[128,256]{0,1:T(8,128)S(1)} %add.149), channel_id=1, source_target_pairs={{0,4},{4,8},{8,12},{12,0},{1,5},{5,9},{9,13},{13,1},{2,6},{6,10},{... | collective-permute-start | bytes 393224 | tf_op jit(solution)/shard_map/while/body/eval_jaxpr/ppermute | solution.py:18
  76.7 4.9 %collective-permute-done.3 = f32[128,256]{0,1:T(8,128)S(1)} collective-permute-done((f32[128,256]{0,1:T(8,128)S(1)}, f32[128,256]{0,1:T(8,128)S(1)}, u32[]{:S(2)}, u32[]{:S(2)}) %collective-permute-start.3) | collective-permute-done | bytes 131104 | tf_op jit(solution)/shard_map/while/body/eval_jaxpr/ppermute | solution.py:18
  86.5 2.0 fusion.47
  89.1 3.4 %conditional.5 = (f32[128,2,8,128]{3,0,2,1:T(8,128)S(1)}, f32[128,256]{0,1:T(8,128)S(1)}, f32[128,256]{0,1:T(8,128)S(1)}) conditional(s32[]{:T(128)} %convert_element_type.84, () %tuple.92, (pred[]{:T(512)}, bf16[128,256]{1,0:T(8,128)(2,1)}, bf16[128,2,8,128]{0,3,2,1:T(8,128)(2,1)S(1)}, f32[2,8,128]{2,1,0:T(8,128)S(1)}, bf16[128,256]{1,0:T(8,128)(2,1)}, ...), branch_computations={%region_9.9_spmd, %region_10.10_spmd} | conditional | flops 337674240 | bytes 8601625 | solution.py:125
  95.3 2.3 %select_add_fusion.2 = f32[128,2,8,128]{3,0,2,1:T(8,128)} fusion(f32[128,2,8,128]{3,0,2,1:T(8,128)S(1)} %get-tuple-element.676, f32[128,2,8,128]{3,0,2,1:T(8,128)} %get-tuple-element.713, pred[]{:T(512)S(6)} %compare.16), kind=kLoop, calls=%fused_computation.39.clone.1 | loop fusion | flops 524288 | bytes 3145729 | tf_op jit(solution)/shard_map/while/body/eval_jaxpr/while/body/eval_jaxpr/add | solution.py:141
  97.6 1.8 collective-permute-done.2
  99.4 2.8 %collective-permute-done.3 = f32[128,256]{0,1:T(8,128)S(1)} collective-permute-done((f32[128,256]{0,1:T(8,128)S(1)}, f32[128,256]{0,1:T(8,128)S(1)}, u32[]{:S(2)}, u32[]{:S(2)}) %collective-permute-start.3) | collective-permute-done | bytes 131104 | tf_op jit(solution)/shard_map/while/body/eval_jaxpr/ppermute | solution.py:18
  107.0 2.0 fusion.47
  112.1 3.7 %collective-permute-start.3 = (f32[128,256]{0,1:T(8,128)S(1)}, f32[128,256]{0,1:T(8,128)S(1)}, u32[]{:S(2)}, u32[]{:S(2)}) collective-permute-start(f32[128,256]{0,1:T(8,128)S(1)} %add.150), channel_id=1, source_target_pairs={{0,4},{4,8},{8,12},{12,0},{1,5},{5,9},{9,13},{13,1},{2,6},{6,10},{... | collective-permute-start | bytes 393224 | tf_op jit(solution)/shard_map/while/body/eval_jaxpr/ppermute | solution.py:18
  115.8 2.3 %select_add_fusion.2 = f32[128,2,8,128]{3,0,2,1:T(8,128)} fusion(f32[128,2,8,128]{3,0,2,1:T(8,128)S(1)} %get-tuple-element.676, f32[128,2,8,128]{3,0,2,1:T(8,128)} %get-tuple-element.713, pred[]{:T(512)S(6)} %compare.16), kind=kLoop, calls=%fused_computation.39.clone.1 | loop fusion | flops 524288 | bytes 3145729 | tf_op jit(solution)/shard_map/while/body/eval_jaxpr/while/body/eval_jaxpr/add | solution.py:141
  126.0 2.0 fusion.47
  130.5 2.3 %collective-permute-start.3 = (f32[128,256]{0,1:T(8,128)S(1)}, f32[128,256]{0,1:T(8,128)S(1)}, u32[]{:S(2)}, u32[]{:S(2)}) collective-permute-start(f32[128,256]{0,1:T(8,128)S(1)} %add.150), channel_id=1, source_target_pairs={{0,4},{4,8},{8,12},{12,0},{1,5},{5,9},{9,13},{13,1},{2,6},{6,10},{... | collective-permute-start | bytes 393224 | tf_op jit(solution)/shard_map/while/body/eval_jaxpr/ppermute | solution.py:18
  132.9 2.3 %select_add_fusion.2 = f32[128,2,8,128]{3,0,2,1:T(8,128)} fusion(f32[128,2,8,128]{3,0,2,1:T(8,128)S(1)} %get-tuple-element.676, f32[128,2,8,128]{3,0,2,1:T(8,128)} %get-tuple-element.713, pred[]{:T(512)S(6)} %compare.16), kind=kLoop, calls=%fused_computation.39.clone.1 | loop fusion | flops 524288 | bytes 3145729 | tf_op jit(solution)/shard_map/while/body/eval_jaxpr/while/body/eval_jaxpr/add | solution.py:141
  139.2 3.8 %fusion.34 = f32[128,8192]{1,0:T(8,128)S(1)} fusion(bf16[128,256]{1,0:T(8,128)(2,1)S(1)} %copy.45, bf16[8192,256]{1,0:T(8,128)(2,1)} %param.20), kind=kOutput, calls=%fused_computation.54 | convolution fusion | flops 536870912 | bytes 8454144 | tf_op jit(solution)/shard_map/dot_general | solution.py:198
  143.0 3.5 %fusion.32 = f32[8192,128]{0,1:T(8,128)} fusion(f32[128,8192]{1,0:T(8,128)S(1)} %fusion.34, bf16[128,256]{1,0:T(8,128)(2,1)S(1)} %copy.46, bf16[8192,256]{1,0:T(8,128)(2,1)S(1)} %copy-done.3), kind=kOutput, calls=%fused_computation.43 | convolution fusion | flops 537919488 | bytes 12648448 | tf_op jit(solution)/shard_map/dot_general | solution.py:199
  149.1 48.3 %reduce-scatter.2.cloned.1.call-done = f32[2048,128]{0,1:T(8,128)} async-done(((f32[8192,128]{0,1:T(8,128)}), f32[2048,128]{0,1:T(8,128)}) %reduce-scatter.2.cloned.1.call-update) | async-done | bytes 1048592 | tf_op jit(solution)/shard_map/reduce_scatter | solution.py:197
  (123 shorter events, 63.5 us)
Async XLA Ops:
  7.2 190.2 %reduce-scatter.2.cloned.1.call-start = ((), (), s32[]{:S(2)}) async-start(), calls=%async_computation.1 | async-start | bytes 5242880 | tf_op jit(solution)/shard_map/reduce_scatter | solution.py:197
  48.6 1.9 copy-start.1
  59.7 15.8 %collective-permute-start = (bf16[128,256]{1,0:T(8,128)(2,1)}, bf16[128,256]{1,0:T(8,128)(2,1)}, u32[]{:S(2)}, u32[]{:S(2)}) collective-permute-start(bf16[128,256]{1,0:T(8,128)(2,1)} %copy.113), channel_id=1, source_target_pairs={{0,4},{4,8},{8,12},{12,0},{1,5},{5,9},{9,13},{13,1},{2,6},{6,10},{... | collective-permute-start | bytes 196616 | tf_op jit(solution)/shard_map/while/body/eval_jaxpr/ppermute | solution.py:18
  62.6 12.9 %collective-permute-start.1 = (bf16[128,256]{1,0:T(8,128)(2,1)}, bf16[128,256]{1,0:T(8,128)(2,1)}, u32[]{:S(2)}, u32[]{:S(2)}) collective-permute-start(bf16[128,256]{1,0:T(8,128)(2,1)} %copy.114), channel_id=1, source_target_pairs={{0,4},{4,8},{8,12},{12,0},{1,5},{5,9},{9,13},{13,1},{2,6},{6,10},{... | collective-permute-start | bytes 196616 | tf_op jit(solution)/shard_map/while/body/eval_jaxpr/ppermute | solution.py:18
  69.9 6.8 %collective-permute-start.2 = (f32[128,256]{0,1:T(8,128)S(1)}, f32[128,256]{0,1:T(8,128)S(1)}, u32[]{:S(2)}, u32[]{:S(2)}) collective-permute-start(f32[128,256]{0,1:T(8,128)S(1)} %add.149), channel_id=1, source_target_pairs={{0,4},{4,8},{8,12},{12,0},{1,5},{5,9},{9,13},{13,1},{2,6},{6,10},{... | collective-permute-start | bytes 393224 | tf_op jit(solution)/shard_map/while/body/eval_jaxpr/ppermute | solution.py:18
  73.9 7.8 %collective-permute-start.3 = (f32[128,256]{0,1:T(8,128)S(1)}, f32[128,256]{0,1:T(8,128)S(1)}, u32[]{:S(2)}, u32[]{:S(2)}) collective-permute-start(f32[128,256]{0,1:T(8,128)S(1)} %add.150), channel_id=1, source_target_pairs={{0,4},{4,8},{8,12},{12,0},{1,5},{5,9},{9,13},{13,1},{2,6},{6,10},{... | collective-permute-start | bytes 393224 | tf_op jit(solution)/shard_map/while/body/eval_jaxpr/ppermute | solution.py:18
  81.6 0.7 copy-start.2
  83.7 13.8 %collective-permute-start = (bf16[128,256]{1,0:T(8,128)(2,1)}, bf16[128,256]{1,0:T(8,128)(2,1)}, u32[]{:S(2)}, u32[]{:S(2)}) collective-permute-start(bf16[128,256]{1,0:T(8,128)(2,1)} %copy.113), channel_id=1, source_target_pairs={{0,4},{4,8},{8,12},{12,0},{1,5},{5,9},{9,13},{13,1},{2,6},{6,10},{... | collective-permute-start | bytes 196616 | tf_op jit(solution)/shard_map/while/body/eval_jaxpr/ppermute | solution.py:18
  85.2 12.4 %collective-permute-start.1 = (bf16[128,256]{1,0:T(8,128)(2,1)}, bf16[128,256]{1,0:T(8,128)(2,1)}, u32[]{:S(2)}, u32[]{:S(2)}) collective-permute-start(bf16[128,256]{1,0:T(8,128)(2,1)} %copy.114), channel_id=1, source_target_pairs={{0,4},{4,8},{8,12},{12,0},{1,5},{5,9},{9,13},{13,1},{2,6},{6,10},{... | collective-permute-start | bytes 196616 | tf_op jit(solution)/shard_map/while/body/eval_jaxpr/ppermute | solution.py:18
  92.5 6.9 %collective-permute-start.2 = (f32[128,256]{0,1:T(8,128)S(1)}, f32[128,256]{0,1:T(8,128)S(1)}, u32[]{:S(2)}, u32[]{:S(2)}) collective-permute-start(f32[128,256]{0,1:T(8,128)S(1)} %add.149), channel_id=1, source_target_pairs={{0,4},{4,8},{8,12},{12,0},{1,5},{5,9},{9,13},{13,1},{2,6},{6,10},{... | collective-permute-start | bytes 393224 | tf_op jit(solution)/shard_map/while/body/eval_jaxpr/ppermute | solution.py:18
  94.1 8.0 %collective-permute-start.3 = (f32[128,256]{0,1:T(8,128)S(1)}, f32[128,256]{0,1:T(8,128)S(1)}, u32[]{:S(2)}, u32[]{:S(2)}) collective-permute-start(f32[128,256]{0,1:T(8,128)S(1)} %add.150), channel_id=1, source_target_pairs={{0,4},{4,8},{8,12},{12,0},{1,5},{5,9},{9,13},{13,1},{2,6},{6,10},{... | collective-permute-start | bytes 393224 | tf_op jit(solution)/shard_map/while/body/eval_jaxpr/ppermute | solution.py:18
  104.3 13.8 %collective-permute-start = (bf16[128,256]{1,0:T(8,128)(2,1)}, bf16[128,256]{1,0:T(8,128)(2,1)}, u32[]{:S(2)}, u32[]{:S(2)}) collective-permute-start(bf16[128,256]{1,0:T(8,128)(2,1)} %copy.113), channel_id=1, source_target_pairs={{0,4},{4,8},{8,12},{12,0},{1,5},{5,9},{9,13},{13,1},{2,6},{6,10},{... | collective-permute-start | bytes 196616 | tf_op jit(solution)/shard_map/while/body/eval_jaxpr/ppermute | solution.py:18
  105.7 12.4 %collective-permute-start.1 = (bf16[128,256]{1,0:T(8,128)(2,1)}, bf16[128,256]{1,0:T(8,128)(2,1)}, u32[]{:S(2)}, u32[]{:S(2)}) collective-permute-start(bf16[128,256]{1,0:T(8,128)(2,1)} %copy.114), channel_id=1, source_target_pairs={{0,4},{4,8},{8,12},{12,0},{1,5},{5,9},{9,13},{13,1},{2,6},{6,10},{... | collective-permute-start | bytes 196616 | tf_op jit(solution)/shard_map/while/body/eval_jaxpr/ppermute | solution.py:18
  109.8 8.3 %collective-permute-start.2 = (f32[128,256]{0,1:T(8,128)S(1)}, f32[128,256]{0,1:T(8,128)S(1)}, u32[]{:S(2)}, u32[]{:S(2)}) collective-permute-start(f32[128,256]{0,1:T(8,128)S(1)} %add.149), channel_id=1, source_target_pairs={{0,4},{4,8},{8,12},{12,0},{1,5},{5,9},{9,13},{13,1},{2,6},{6,10},{... | collective-permute-start | bytes 393224 | tf_op jit(solution)/shard_map/while/body/eval_jaxpr/ppermute | solution.py:18
  112.1 7.1 %collective-permute-start.3 = (f32[128,256]{0,1:T(8,128)S(1)}, f32[128,256]{0,1:T(8,128)S(1)}, u32[]{:S(2)}, u32[]{:S(2)}) collective-permute-start(f32[128,256]{0,1:T(8,128)S(1)} %add.150), channel_id=1, source_target_pairs={{0,4},{4,8},{8,12},{12,0},{1,5},{5,9},{9,13},{13,1},{2,6},{6,10},{... | collective-permute-start | bytes 393224 | tf_op jit(solution)/shard_map/while/body/eval_jaxpr/ppermute | solution.py:18
  119.2 0.7 copy-start.2
  121.4 13.8 %collective-permute-start = (bf16[128,256]{1,0:T(8,128)(2,1)}, bf16[128,256]{1,0:T(8,128)(2,1)}, u32[]{:S(2)}, u32[]{:S(2)}) collective-permute-start(bf16[128,256]{1,0:T(8,128)(2,1)} %copy.113), channel_id=1, source_target_pairs={{0,4},{4,8},{8,12},{12,0},{1,5},{5,9},{9,13},{13,1},{2,6},{6,10},{... | collective-permute-start | bytes 196616 | tf_op jit(solution)/shard_map/while/body/eval_jaxpr/ppermute | solution.py:18
  124.4 10.9 %collective-permute-start.1 = (bf16[128,256]{1,0:T(8,128)(2,1)}, bf16[128,256]{1,0:T(8,128)(2,1)}, u32[]{:S(2)}, u32[]{:S(2)}) collective-permute-start(bf16[128,256]{1,0:T(8,128)(2,1)} %copy.114), channel_id=1, source_target_pairs={{0,4},{4,8},{8,12},{12,0},{1,5},{5,9},{9,13},{13,1},{2,6},{6,10},{... | collective-permute-start | bytes 196616 | tf_op jit(solution)/shard_map/while/body/eval_jaxpr/ppermute | solution.py:18
  128.9 6.8 %collective-permute-start.2 = (f32[128,256]{0,1:T(8,128)S(1)}, f32[128,256]{0,1:T(8,128)S(1)}, u32[]{:S(2)}, u32[]{:S(2)}) collective-permute-start(f32[128,256]{0,1:T(8,128)S(1)} %add.149), channel_id=1, source_target_pairs={{0,4},{4,8},{8,12},{12,0},{1,5},{5,9},{9,13},{13,1},{2,6},{6,10},{... | collective-permute-start | bytes 393224 | tf_op jit(solution)/shard_map/while/body/eval_jaxpr/ppermute | solution.py:18
  130.5 6.8 %collective-permute-start.3 = (f32[128,256]{0,1:T(8,128)S(1)}, f32[128,256]{0,1:T(8,128)S(1)}, u32[]{:S(2)}, u32[]{:S(2)}) collective-permute-start(f32[128,256]{0,1:T(8,128)S(1)} %add.150), channel_id=1, source_target_pairs={{0,4},{4,8},{8,12},{12,0},{1,5},{5,9},{9,13},{13,1},{2,6},{6,10},{... | collective-permute-start | bytes 393224 | tf_op jit(solution)/shard_map/while/body/eval_jaxpr/ppermute | solution.py:18
  138.1 4.9 %copy-start.4 = (bf16[128,256]{1,0:T(8,128)(2,1)}, bf16[128,256]{1,0:T(8,128)(2,1)S(1)}, u32[]{:S(2)}) copy-start(bf16[128,256]{1,0:T(8,128)(2,1)S(1)} %copy.45) | copy-start | bytes 196612
  139.2 3.9 %copy-start.5 = (bf16[128,256]{1,0:T(8,128)(2,1)}, bf16[128,256]{1,0:T(8,128)(2,1)S(1)}, u32[]{:S(2)}) copy-start(bf16[128,256]{1,0:T(8,128)(2,1)S(1)} %copy.46) | copy-start | bytes 196612
  139.2 3.9 %copy-start.3 = (bf16[8192,256]{1,0:T(8,128)(2,1)S(1)}, bf16[8192,256]{1,0:T(8,128)(2,1)}, u32[]{:S(2)}) copy-start(bf16[8192,256]{1,0:T(8,128)(2,1)} %param.21) | copy-start | bytes 12582916
  146.5 1.2 copy-start
  (2 other events, 1.3 us)
Sparse Core Ops, SparseCore 0:
  146.7 50.7 reduce-scatter.1
where the time goes:
time: 207 us
  waiting for transfers between devices  62.2 us (30%)
  local copies, waits for them, and re-layouts  37.6 us (18%)
  blocking collectives  30.7 us (15%)
  other arithmetic  25.9 us (13%)
  starting transfers between devices  17.1 us (8%)
  matrix products  15 us (7%)
  between operations  14.9 us (7%)
  loops' own time  3.15 us (2%)
    reduce_scatter x1, waiting for transfers between devices, local(): lax.psum_scatter(lax.dot_general(key_proj, key_grad, contraction, preferr...  48.3 us
    ppermute x16, starting transfers between devices, from_behind(): return lax.ppermute(value, axis, pairs)  17 us
    all_gather x1, blocking collectives, local(): key_rows = lax.all_gather(key_states, 'ctx', axis=0, tiled=True)  15.8 us
    all_gather x1, blocking collectives, local(): value_rows = lax.all_gather(value_states, 'ctx', axis=0, tiled=True)  14.8 us
    while x16, local copies, waits for them, and re-layouts  14.4 us
    ppermute x16, waiting for transfers between devices, from_behind(): return lax.ppermute(value, axis, pairs)  13.9 us
    unnamed x15, local copies, waits for them, and re-layouts  9.02 us
    reduce_sum x5, other arithmetic, select_cols(): return jnp.sum(lookup[:, None, :] * onehot[None, :, :], axis=2)  8.71 us
  transfers between devices with their start and end apart: 17, of which 8 were waited for; matrix products, arithmetic and copies ran while one was open for 19% of the time, Pallas kernels for 0%

commit v1 on v0

v1 whole, which is shorter than its diff:
```python
import math

import jax
import jax.numpy as jnp
from jax import lax
from jax.sharding import PartitionSpec as P

HD = 128
BLK = 128


masked_score = -1e30


def select_rows(lookup, picked):
    onehot = (picked[:, None] == lax.iota(jnp.int32, lookup.shape[0])[None, :]).astype(jnp.int32)
    return jnp.sum(onehot[:, :, None] * lookup[None, :, :], axis=1)


def select_cols(lookup, picked):
    onehot = (picked[:, None] == lax.iota(jnp.int32, lookup.shape[1])[None, :]).astype(jnp.int32)
    return jnp.sum(lookup[:, None, :] * onehot[None, :, :], axis=2)


def local(
    queries, key_states, value_states, out_grad, mask_flags, shard_blocks, key_proj, value_proj
):
    rows_here = queries.shape[0]
    kv_cols = key_states.shape[1]
    kv_heads = kv_cols // HD
    group_size = queries.shape[1] // kv_cols
    inv_root = HD ** (-0.5)
    position = lax.axis_index("ctx")
    query_heads = queries.reshape(rows_here, kv_heads, group_size, HD)
    grad_heads = out_grad.reshape(rows_here, kv_heads, group_size, HD)
    own_blocks = lax.dynamic_slice_in_dim(
        shard_blocks, position * (rows_here // BLK), rows_here // BLK
    )
    own_flags = select_rows(mask_flags, own_blocks)

    kv_rows = lax.all_gather(
        jnp.concatenate([key_states, value_states], axis=1), "ctx", axis=0, tiled=True
    )
    row_count = kv_rows.shape[0]
    step_rows = math.gcd(row_count, 512)
    steps = row_count // step_rows

    def chunk(offset):
        block = lax.dynamic_slice_in_dim(kv_rows, offset, step_rows)
        key_heads = block[:, :kv_cols].reshape(step_rows, kv_heads, HD)
        value_heads = block[:, kv_cols:].reshape(step_rows, kv_heads, HD)
        their_blocks = lax.dynamic_slice_in_dim(shard_blocks, offset // BLK, step_rows // BLK)
        pair_flags = select_cols(own_flags, their_blocks) > 0
        allowed = jnp.repeat(jnp.repeat(pair_flags, BLK, axis=0), BLK, axis=1)
        scores = (
            jnp.einsum("qkgd,tkd->kgqt", query_heads, key_heads, preferred_element_type=jnp.float32)
            * inv_root
        )
        scores = jnp.where(allowed[None, None], scores, masked_score)
        return key_heads, value_heads, allowed, scores

    def forward_stats(offset, current):
        row_max, row_sum, weighted = current
        key_heads, value_heads, allowed, scores = chunk(offset)
        new_max = jnp.maximum(row_max, jnp.max(scores, axis=-1))
        rescale = jnp.exp(row_max - new_max)
        shifted = jnp.where(allowed[None, None], jnp.exp(scores - new_max[..., None]), 0.0)
        row_sum = row_sum * rescale + jnp.sum(shifted, axis=-1)
        weighted = weighted * rescale[..., None] + jnp.einsum(
            "kgqt,tkd->kgqd",
            shifted.astype(jnp.bfloat16),
            value_heads,
            preferred_element_type=jnp.float32,
        )
        return (new_max, row_sum, weighted)

    def backward_chunk(offset, log_total, row_delta, scores_given=None):
        key_heads, value_heads, allowed, scores = chunk(offset)
        if scores_given is not None:
            scores = scores_given
        probs = jnp.exp(scores - log_total[..., None])
        dprobs = jnp.einsum(
            "qkgd,tkd->kgqt", grad_heads, value_heads, preferred_element_type=jnp.float32
        )
        dscores = (probs * (dprobs - row_delta[..., None])).astype(jnp.bfloat16)
        probs_low = probs.astype(jnp.bfloat16)
        query_term = (
            jnp.einsum("kgqt,tkd->qkgd", dscores, key_heads, preferred_element_type=jnp.float32)
            * inv_root
        )
        key_term = (
            jnp.einsum("kgqt,qkgd->tkd", dscores, query_heads, preferred_element_type=jnp.float32)
            * inv_root
        )
        value_term = jnp.einsum(
            "kgqt,qkgd->tkd", probs_low, grad_heads, preferred_element_type=jnp.float32
        )
        kv_term = jnp.concatenate(
            [key_term.reshape(step_rows, kv_cols), value_term.reshape(step_rows, kv_cols)], axis=1
        )
        return query_term, kv_term

    start_stats = (
        jnp.full((kv_heads, group_size, rows_here), masked_score, jnp.float32),
        jnp.zeros((kv_heads, group_size, rows_here), jnp.float32),
        jnp.zeros((kv_heads, group_size, rows_here, HD), jnp.float32),
    )
    if steps == 1:
        key_heads, value_heads, allowed, scores = chunk(0)
        row_max = jnp.max(scores, axis=-1)
        shifted = jnp.exp(scores - row_max[..., None])
        row_sum = jnp.sum(shifted, axis=-1)
        weighted = jnp.einsum(
            "kgqt,tkd->kgqd",
            shifted.astype(jnp.bfloat16),
            value_heads,
            preferred_element_type=jnp.float32,
        )
    else:
        row_max, row_sum, weighted = lax.fori_loop(
            0, steps, lambda i, c: forward_stats(i * step_rows, c), start_stats
        )
        scores = None
    log_total = row_max + jnp.log(row_sum)
    attended = (weighted / row_sum[..., None]).astype(jnp.bfloat16)
    row_delta = jnp.einsum(
        "kgqd,qkgd->kgq", attended, grad_heads, preferred_element_type=jnp.float32
    )

    if steps == 1:
        query_acc, kv_acc = backward_chunk(0, log_total, row_delta, scores)
    else:

        def backward_visit(turn_index, current):
            query_now, kv_now = current
            offset = turn_index * step_rows
            query_term, kv_term = backward_chunk(offset, log_total, row_delta)
            kv_now = lax.dynamic_update_slice_in_dim(kv_now, kv_term, offset, 0)
            return (query_now + query_term, kv_now)

        query_acc, kv_acc = lax.fori_loop(
            0,
            steps,
            backward_visit,
            (
                jnp.zeros((rows_here, kv_heads, group_size, HD), jnp.float32),
                jnp.zeros((row_count, 2 * kv_cols), jnp.float32),
            ),
        )

    kv_grad = lax.psum_scatter(kv_acc, "ctx", scatter_dimension=0, tiled=True)
    query_grad = query_acc.reshape(rows_here, -1).astype(jnp.bfloat16)
    key_grad = kv_grad[:, :kv_cols].astype(jnp.bfloat16)
    value_grad = kv_grad[:, kv_cols:].astype(jnp.bfloat16)
    contraction = (((1,), (1,)), ((), ()))
    partial = (
        lax.dot_general(key_proj, key_grad, contraction, preferred_element_type=jnp.float32)
        + lax.dot_general(value_proj, value_grad, contraction, preferred_element_type=jnp.float32)
    ).astype(jnp.bfloat16)
    input_grad_t = lax.psum_scatter(partial, "head", scatter_dimension=0, tiled=True)
    return (query_grad, key_grad, value_grad, input_grad_t)


def solution(mesh):
    return jax.shard_map(
        local,
        mesh=mesh,
        in_specs=(
            P(("groups", "ctx"), "head"),
            P(("groups", "ctx"), "head"),
            P(("groups", "ctx"), "head"),
            P(("groups", "ctx"), "head"),
            P("groups", None),
            P("groups"),
            P(None, "head"),
            P(None, "head"),
        ),
        out_specs=(
            P(("groups", "ctx"), "head"),
            P(("groups", "ctx"), "head"),
            P(("groups", "ctx"), "head"),
            P("head", ("groups", "ctx")),
        ),
        check_vma=False,
    )
```

time: 207 us -> 123 us (0.59)
  local copies, waits for them, and re-layouts: 37.6 us -> 11.9 us
  other arithmetic: 25.9 us -> 6.11 us
  starting transfers between devices: 17.1 us -> 0.08 us
  blocking collectives: 30.7 us -> 16.7 us
  waiting for transfers between devices: 62.2 us -> 56.1 us
  loops' own time: 3.15 us -> 0 us
    ppermute x16 -> x0, starting transfers between devices: 17 us -> none  [from_behind(): return lax.ppermute(value, axis, pairs)]
    while x18 -> x0, local copies, waits for them, and re-layouts: 15.5 us -> none
    all_gather x2 -> x1, blocking collectives: 30.7 us -> 16.7 us  [local(): lax.all_gather(jnp.concatenate([key_states, value_states], axis=1), 'ctx'...]
    ppermute x16 -> x0, waiting for transfers between devices: 13.9 us -> none  [from_behind(): return lax.ppermute(value, axis, pairs)]
    add x14 -> x1, other arithmetic: 11.8 us -> 0.01 us  [local(): log_total = row_max + jnp.log(row_sum)]
    reduce_sum x5 -> x1, other arithmetic: 8.71 us -> 0.84 us  [select_cols(): return jnp.sum(lookup[:, None, :] * onehot[None, :, :], axis=2)]
    reduce_scatter x1 -> x2, waiting for transfers between devices: 48.3 us -> 56.1 us  [the longest x1 28.8 us: local(): lax.psum_scatter(partial, 'head', scatter_dimension=0, tiled=True)]
    dynamic_slice x4 -> x0, local copies, waits for them, and re-layouts: 4.92 us -> none  [pair_mask(): lax.dynamic_slice_in_dim(shard_blocks, first_row // BLK, row_count // BLK)]
  transfers between devices with their start and end apart: 17 -> 2, of which waited for: 8 -> 2; matrix products, arithmetic and copies ran while one was open for 19% -> 1% of each run, Pallas kernels for 0% -> 0%
where the time goes in v1:
time: 123 us; the launch traced here: 122 us
  waiting for transfers between devices  56.1 us (46%)
  matrix products  17 us (14%)
  blocking collectives  16.7 us (14%)
  between operations  14.3 us (12%)
  local copies, waits for them, and re-layouts  11.9 us (10%)
  other arithmetic  6.11 us (5%)
    reduce_scatter x1, waiting for transfers between devices, local(): lax.psum_scatter(partial, 'head', scatter_dimension=0, tiled=True)  28.8 us
    reduce_scatter x1, waiting for transfers between devices, local(): kv_grad = lax.psum_scatter(kv_acc, 'ctx', scatter_dimension=0, tiled=True)  27.3 us
    all_gather x1, blocking collectives, local(): lax.all_gather(jnp.concatenate([key_states, value_states], axis=1), 'ctx'...  16.7 us
    unnamed x19, local copies, waits for them, and re-layouts  6.14 us
    dot_general x1, matrix products, backward_chunk(): jnp.einsum('kgqt,qkgd->tkd', probs_low, grad_heads, preferred_element_typ...  4.37 us
    dot_general x1, matrix products, local(): lax.dot_general(key_proj, key_grad, contraction, preferred_element_type=j...  3.82 us
    dot_general x1, matrix products, local(): lax.dot_general(value_proj, value_grad, contraction, preferred_element_ty...  2.88 us
  transfers between devices with their start and end apart: 2, of which 2 were waited for; matrix products, arithmetic and copies ran while one was open for 1% of the time, Pallas kernels for 0%

profile of v1, /device:TPU:0, one launch (start us, length us, event | category | flops | bytes accessed | tf_op | source)
XLA Modules:
  0.0 122.1 jit_solution(17790013261463771431)
XLA Ops:
  7.2 0.9 copy.40
  8.2 1.0 copy.39
  9.2 16.7 %all_gather.3 = bf16[512,512]{0,1:T(8,128)(2,1)S(1)} all-gather(bf16[128,512]{0,1:T(8,128)(2,1)S(1)} %pad_maximum_fusion.1), channel_id=1, replica_groups=mesh['groups'=2,'ctx'=4,'head'=4] {'ctx'}, dimensions={0}, use_global_device_ids=true | all-gather | bytes 655360 | tf_op jit(solution)/shard_map/all_gather | solution.py:41
  25.9 1.3 %dynamic_slice.3 = s32[1]{0:T(128)} dynamic-slice(s32[4]{0:T(128)} %param.13, s32[]{:T(128)S(6)} %select_n.10), dynamic_slice_sizes={1} | dynamic-slice | bytes 12 | tf_op jit(solution)/shard_map/dynamic_slice | solution.py:36
  28.6 0.8 select_reduce_fusion
  29.5 1.3 %copy.78 = bf16[128,2048]{0,1:T(8,128)(2,1)S(1)} copy(bf16[128,2048]{1,0:T(8,128)(2,1)} %param.8) | data formatting | bytes 1048576 | tf_op jit(solution)/shard_map/reshape | solution.py:34
  30.8 1.1 copy.79
  32.4 0.8 bitcast_reduce_fusion
  33.3 0.9 fusion.8
  34.3 1.5 %fusion.22 = f32[2,8,128,128]{3,2,1,0:T(8,128)S(1)} fusion(bf16[512,2,128,1]{0,2,3,1:T(8,128)(2,1)S(1)} %bitcast.94, f32[2,512,128,8]{2,1,3,0:T(8,128)S(1)} %get-tuple-element.21, f32[2,8,128]{2,1,0:T(8,128)S(1)} %get-tuple-element.20, pred[512]{0:T(512)(128)(4,1)S(1)} %broadcast_bitcast_fusion, f32[2,8,128]{2,1,0:T(8,128)S(1)} %fusion.8), kind=kOutput, calls=%fused_computation.29 | convolution fusion | flops 273416192 | bytes 5521920 | tf_op jit(solution)/shard_map/kgqt,tkd->kgqd/dot_general | solution.py:113
  35.8 0.8 multiply_reduce_fusion
  36.6 4.4 %fusion.14 = f32[2,512,128,1]{1,2,3,0:T(8,128)} fusion(bf16[128,2,8,128]{0,3,2,1:T(8,128)(2,1)S(1)} %copy.51, f32[2,512,128,8]{2,1,3,0:T(8,128)} %copy-done, f32[2,8,128]{2,1,0:T(8,128)S(1)} %log_add_fusion, pred[512]{0:T(512)(128)(4,1)S(1)} %broadcast_bitcast_fusion), kind=kOutput, calls=%fused_computation.19 | convolution fusion | flops 272629760 | bytes 5251584 | tf_op jit(solution)/shard_map/kgqt,qkgd->tkd/dot_general | solution.py:95
  41.0 1.5 %fusion.3 = bf16[2,8,128,512]{2,3,1,0:T(8,128)(2,1)S(1)} fusion(f32[2,512,128,8]{2,1,3,0:T(8,128)S(1)} %copy-done.1, bf16[512,2,128,1]{0,2,3,1:T(8,128)(2,1)S(1)} %bitcast.95, bf16[128,2,8,128]{0,3,2,1:T(8,128)(2,1)S(1)} %copy.51, f32[2,8,128]{2,1,0:T(8,128)S(1)} %copy.65, f32[2,8,128]{2,1,0:T(8,128)S(1)} %log_add_fusion, ...), kind=kOutput, calls=%fused_computation.5 | convolution fusion | flops 274726912 | bytes 7094784 | tf_op jit(solution)/shard_map/qkgd,tkd->kgqt/dot_general | solution.py:82
  42.5 1.2 %copy.53 = f32[512,256]{1,0:T(8,128)S(1)} copy(f32[512,256]{0,1:T(8,128)} %bitcast.93) | data formatting | bytes 1048576 | tf_op jit(solution)/shard_map/reshape | solution.py:99
  43.8 1.6 %fusion.19 = f32[2,512,128]{1,2,0:T(8,128)} fusion(bf16[2,8,128,512]{2,3,1,0:T(8,128)(2,1)S(1)} %fusion.3, bf16[128,2,8,128]{0,3,2,1:T(8,128)(2,1)S(1)} %bitcast.87), kind=kOutput, calls=%fused_computation.25 | convolution fusion | flops 268566528 | bytes 3145728 | tf_op jit(solution)/shard_map/kgqt,qkgd->tkd/dot_general | solution.py:92
  45.4 1.2 %copy.52 = f32[512,256]{1,0:T(8,128)S(1)} copy(f32[512,256]{0,1:T(8,128)} %bitcast.91) | data formatting | bytes 1048576 | tf_op jit(solution)/shard_map/reshape | solution.py:99
  46.6 1.1 pad_maximum_fusion
  47.9 27.3 %reduce-scatter.3.cloned.1.call-done = f32[128,512]{1,0:T(8,128)} async-done(((f32[512,512]{1,0:T(8,128)}), f32[128,512]{1,0:T(8,128)}) %reduce-scatter.3.cloned.1.call-update) | async-done | bytes 262160 | tf_op jit(solution)/shard_map/reduce_scatter | solution.py:151
  75.2 1.0 convert.4
  76.2 3.8 %fusion.31 = f32[128,8192]{1,0:T(8,128)S(1)} fusion(bf16[128,256]{1,0:T(8,128)(2,1)S(1)} %get-tuple-element.19, bf16[8192,256]{1,0:T(8,128)(2,1)} %param.14), kind=kOutput, calls=%fused_computation.44 | convolution fusion | flops 536870912 | bytes 8454144 | tf_op jit(solution)/shard_map/dot_general | solution.py:157
  80.1 2.9 %fusion.1 = bf16[8192,128]{0,1:T(8,128)(2,1)} fusion(f32[128,8192]{1,0:T(8,128)S(1)} %fusion.31, bf16[128,256]{1,0:T(8,128)(2,1)S(1)} %get-tuple-element.18, bf16[8192,256]{1,0:T(8,128)(2,1)S(1)} %copy-done.2), kind=kOutput, calls=%fused_computation.2 | convolution fusion | flops 538968064 | bytes 10551296 | tf_op jit(solution)/shard_map/dot_general | solution.py:158
  83.5 1.0 copy.54
  84.5 28.8 %reduce-scatter.5.cloned.1.call-done = bf16[2048,128]{0,1:T(8,128)(2,1)} async-done(((bf16[8192,128]{0,1:T(8,128)(2,1)}), bf16[2048,128]{0,1:T(8,128)(2,1)}) %reduce-scatter.5.cloned.1.call-update) | async-done | bytes 524304 | tf_op jit(solution)/shard_map/reduce_scatter | solution.py:160
  113.2 2.0 %copy.55 = bf16[2048,128]{1,0:T(8,128)(2,1)} copy(bf16[2048,128]{0,1:T(8,128)(2,1)} %reduce-scatter.5.cloned.1.call-done) | data formatting | bytes 1048576
  (29 shorter events, 2.7 us)
Async XLA Ops:
  7.2 68.0 %reduce-scatter.3.cloned.1.call-start = ((), (), s32[]{:S(2)}) async-start(), calls=%async_computation.2 | async-start | bytes 1310720 | tf_op jit(solution)/shard_map/reduce_scatter | solution.py:151
  25.9 8.4 %copy-start.5 = (bf16[512,256]{0,1:T(8,128)(2,1)}, bf16[512,256]{0,1:T(8,128)(2,1)S(1)}, u32[]{:S(2)}) copy-start(bf16[512,256]{0,1:T(8,128)(2,1)S(1)} %get-tuple-element.16) | copy-start | bytes 786436
  33.3 2.5 %copy-start = (f32[2,512,128,8]{2,1,3,0:T(8,128)}, f32[2,512,128,8]{2,1,3,0:T(8,128)S(1)}, u32[]{:S(2)}) copy-start(f32[2,512,128,8]{2,1,3,0:T(8,128)S(1)} %get-tuple-element.21) | copy-start | bytes 12582916
  36.6 4.4 %copy-start.1 = (f32[2,512,128,8]{2,1,3,0:T(8,128)S(1)}, f32[2,512,128,8]{2,1,3,0:T(8,128)}, u32[]{:S(2)}) copy-start(f32[2,512,128,8]{2,1,3,0:T(8,128)} %copy-done) | copy-start | bytes 12582916
  36.6 4.4 %copy-start.6 = (bf16[512,256]{0,1:T(8,128)(2,1)S(1)}, bf16[512,256]{0,1:T(8,128)(2,1)}, u32[]{:S(2)}) copy-start(bf16[512,256]{0,1:T(8,128)(2,1)} %copy-done.5) | copy-start | bytes 786436
  47.8 65.4 %reduce-scatter.5.cloned.1.call-start = ((), (), s32[]{:S(2)}) async-start(), calls=%async_computation.3 | async-start | bytes 2621440 | tf_op jit(solution)/shard_map/reduce_scatter | solution.py:160
  76.2 3.9 %copy-start.4 = (bf16[128,256]{1,0:T(8,128)(2,1)}, bf16[128,256]{1,0:T(8,128)(2,1)S(1)}, u32[]{:S(2)}) copy-start(bf16[128,256]{1,0:T(8,128)(2,1)S(1)} %get-tuple-element.19) | copy-start | bytes 196612
  76.2 3.9 %copy-start.3 = (bf16[128,256]{1,0:T(8,128)(2,1)}, bf16[128,256]{1,0:T(8,128)(2,1)S(1)}, u32[]{:S(2)}) copy-start(bf16[128,256]{1,0:T(8,128)(2,1)S(1)} %get-tuple-element.18) | copy-start | bytes 196612
  76.2 3.9 %copy-start.2 = (bf16[8192,256]{1,0:T(8,128)(2,1)S(1)}, bf16[8192,256]{1,0:T(8,128)(2,1)}, u32[]{:S(2)}) copy-start(bf16[8192,256]{1,0:T(8,128)(2,1)} %param.15) | copy-start | bytes 12582916
Sparse Core Ops, SparseCore 0:
  47.9 27.2 reduce-scatter.2
  83.1 30.0 reduce-scatter.4

commit v2 on v1

--- a/solution.py
+++ b/solution.py
@@ -20,6 +20,86 @@
 def select_cols(lookup, picked):
     onehot = (picked[:, None] == lax.iota(jnp.int32, lookup.shape[1])[None, :]).astype(jnp.int32)
     return jnp.sum(lookup[:, None, :] * onehot[None, :, :], axis=2)
+
+
+def pick(vector, picked):
+    onehot = (picked[:, None] == lax.iota(jnp.int32, vector.shape[0])[None, :]).astype(jnp.int32)
+    return jnp.sum(onehot * vector[None, :], axis=1)
+
+
+def shifted_pairs(count, steps):
+    return [(source, (source + steps) % count) for source in range(count)]
+
+
+def gather_slots(block, axis):
+    count = lax.axis_size(axis)
+    position = lax.axis_index(axis)
+    if count > 8:
+        gathered = lax.all_gather(block, axis, axis=0, tiled=True)
+        return gathered, lax.iota(jnp.int32, count)
+    pieces = [block] + [
+        lax.ppermute(block, axis, shifted_pairs(count, steps)) for steps in range(1, count)
+    ]
+    sources = (position - lax.iota(jnp.int32, count)) % count
+    return jnp.concatenate(pieces, axis=0), sources
+
+
+def scatter_slots(slots, axis):
+    count = lax.axis_size(axis)
+    if count > 8:
+        return lax.psum_scatter(slots, axis, scatter_dimension=0, tiled=True)
+    rows = slots.shape[0] // count
+    total = slots[:rows]
+    for steps in range(1, count):
+        total = total + lax.ppermute(
+            slots[steps * rows : (steps + 1) * rows], axis, shifted_pairs(count, -steps)
+        )
+    return total
+
+
+def head_reduce(key_proj, value_proj, key_grad, value_grad):
+    count = lax.axis_size("head")
+    position = lax.axis_index("head")
+    depth = count.bit_length() - 1
+    contraction = (((1,), (1,)), ((), ()))
+    if count == 1 or count != 1 << depth:
+        partial = lax.dot_general(
+            key_proj, key_grad, contraction, preferred_element_type=jnp.float32
+        ) + lax.dot_general(value_proj, value_grad, contraction, preferred_element_type=jnp.float32)
+        return lax.psum_scatter(partial, "head", scatter_dimension=0, tiled=True).astype(
+            jnp.bfloat16
+        )
+    block = key_proj.shape[0] // count
+    key_split = key_proj.reshape(count // 2, 2, block, key_proj.shape[1])
+    value_split = value_proj.reshape(count // 2, 2, block, value_proj.shape[1])
+
+    def project(half):
+        return jnp.einsum(
+            "arf,tf->art",
+            lax.dynamic_index_in_dim(key_split, half, 1, keepdims=False),
+            key_grad,
+            preferred_element_type=jnp.float32,
+        ) + jnp.einsum(
+            "arf,tf->art",
+            lax.dynamic_index_in_dim(value_split, half, 1, keepdims=False),
+            value_grad,
+            preferred_element_type=jnp.float32,
+        )
+
+    own_bit = position % 2
+    sent = project(1 - own_bit)
+    kept = project(own_bit)
+    current = kept + lax.ppermute(sent, "head", [(i, i ^ 1) for i in range(count)])
+    for level in range(1, depth):
+        current = current.reshape(-1, 2, block, current.shape[-1])
+        own_bit = (position // (1 << level)) % 2
+        kept = lax.dynamic_index_in_dim(current, own_bit, 1, keepdims=False)
+        sent = lax.dynamic_index_in_dim(current, 1 - own_bit, 1, keepdims=False)
+        arrived = lax.ppermute(
+            sent.astype(jnp.bfloat16), "head", [(i, i ^ (1 << level)) for i in range(count)]
+        )
+        current = kept + arrived.astype(jnp.float32)
+    return current.reshape(block, -1).astype(jnp.bfloat16)
 
 
 def local(
@@ -38,10 +118,16 @@
     )
     own_flags = select_rows(mask_flags, own_blocks)
 
-    kv_rows = lax.all_gather(
-        jnp.concatenate([key_states, value_states], axis=1), "ctx", axis=0, tiled=True
+    kv_rows, sources = gather_slots(
+        jnp.concatenate([key_states, value_states], axis=1), "ctx"
     )
     row_count = kv_rows.shape[0]
+    blocks_here = rows_here // BLK
+    key_blocks = lax.iota(jnp.int32, row_count // BLK)
+    key_doc_blocks = pick(
+        shard_blocks,
+        pick(sources, key_blocks // blocks_here) * blocks_here + key_blocks % blocks_here,
+    )
     step_rows = math.gcd(row_count, 512)
     steps = row_count // step_rows
 
@@ -49,7 +135,7 @@
         block = lax.dynamic_slice_in_dim(kv_rows, offset, step_rows)
         key_heads = block[:, :kv_cols].reshape(step_rows, kv_heads, HD)
         value_heads = block[:, kv_cols:].reshape(step_rows, kv_heads, HD)
-        their_blocks = lax.dynamic_slice_in_dim(shard_blocks, offset // BLK, step_rows // BLK)
+        their_blocks = lax.dynamic_slice_in_dim(key_doc_blocks, offset // BLK, step_rows // BLK)
         pair_flags = select_cols(own_flags, their_blocks) > 0
         allowed = jnp.repeat(jnp.repeat(pair_flags, BLK, axis=0), BLK, axis=1)
         scores = (
@@ -148,16 +234,11 @@
             ),
         )
 
-    kv_grad = lax.psum_scatter(kv_acc, "ctx", scatter_dimension=0, tiled=True)
+    kv_grad = scatter_slots(kv_acc, "ctx")
     query_grad = query_acc.reshape(rows_here, -1).astype(jnp.bfloat16)
     key_grad = kv_grad[:, :kv_cols].astype(jnp.bfloat16)
     value_grad = kv_grad[:, kv_cols:].astype(jnp.bfloat16)
-    contraction = (((1,), (1,)), ((), ()))
-    partial = (
-        lax.dot_general(key_proj, key_grad, contraction, preferred_element_type=jnp.float32)
-        + lax.dot_general(value_proj, value_grad, contraction, preferred_element_type=jnp.float32)
-    ).astype(jnp.bfloat16)
-    input_grad_t = lax.psum_scatter(partial, "head", scatter_dimension=0, tiled=True)
+    input_grad_t = head_reduce(key_proj, value_proj, key_grad, value_grad)
     return (query_grad, key_grad, value_grad, input_grad_t)
 
 

time: 123 us -> 87.3 us (0.71)
  the two profiles are of different devices: /device:TPU:0 before, /device:TPU:8 now
where the time goes in v2:
time: 87.3 us; the launch traced here: 86.7 us
  waiting for transfers between devices  37.5 us (43%)
  matrix products  18.7 us (21%)
  starting transfers between devices  11 us (13%)
  local copies, waits for them, and re-layouts  10.9 us (12%)
  other arithmetic  7.82 us (9%)
    ppermute x3, waiting for transfers between devices, scatter_slots(): lax.ppermute(slots[steps * rows:(steps + 1) * rows], axis, shifted_pairs(...  21.9 us
    ppermute x1, waiting for transfers between devices, head_reduce(): lax.ppermute(sent.astype(jnp.bfloat16), 'head', [(i, i ^ 1 << level) for...  11.2 us
    ppermute x3, starting transfers between devices, gather_slots(): lax.ppermute(block, axis, shifted_pairs(count, steps))  5.56 us
    unnamed x22, local copies, waits for them, and re-layouts  5.44 us
    dot_general x2, matrix products, project(): jnp.einsum('arf,tf->art', lax.dynamic_index_in_dim(value_split, half, 1,...  4.76 us
    dot_general x2, matrix products, project(): jnp.einsum('arf,tf->art', lax.dynamic_index_in_dim(key_split, half, 1, ke...  4.4 us
    dot_general x1, matrix products, backward_chunk(): jnp.einsum('kgqt,qkgd->tkd', probs_low, grad_heads, preferred_element_typ...  4.37 us
    ppermute x3, starting transfers between devices, scatter_slots(): lax.ppermute(slots[steps * rows:(steps + 1) * rows], axis, shifted_pairs(...  3.94 us
  transfers between devices with their start and end apart: 8, of which 7 were waited for; matrix products, arithmetic and copies ran while one was open for 12% of the time, Pallas kernels for 0%

profile of v2, /device:TPU:8, one launch (start us, length us, event | category | flops | bytes accessed | tf_op | source)
XLA Modules:
  0.0 86.7 jit_solution(17011218242459345934)
XLA Ops:
  2.6 3.0 %collective-permute-start.1 = (bf16[128,512]{0,1:T(8,128)(2,1)S(1)}, bf16[128,512]{0,1:T(8,128)(2,1)S(1)}, u32[]{:S(2)}, u32[]{:S(2)}) collective-permute-start(bf16[128,512]{0,1:T(8,128)(2,1)S(1)} %pad_maximum_fusion.2), channel_id=1, source_target_pairs={{0,8},{4,12},{8,0},{12,4},{1,9},{5,13},{9,1},{13,5},{2,10},{6,14},... | collective-permute-start | bytes 393224 | tf_op jit(solution)/shard_map/ppermute | solution.py:41
  5.7 2.5 %collective-permute-start = (bf16[128,512]{0,1:T(8,128)(2,1)S(1)}, bf16[128,512]{0,1:T(8,128)(2,1)S(1)}, u32[]{:S(2)}, u32[]{:S(2)}) collective-permute-start(bf16[128,512]{0,1:T(8,128)(2,1)S(1)} %pad_maximum_fusion.2), channel_id=1, source_target_pairs={{0,4},{4,8},{8,12},{12,0},{1,5},{5,9},{9,13},{13,1},{2,6},{6,10},{... | collective-permute-start | bytes 393224 | tf_op jit(solution)/shard_map/ppermute | solution.py:41
  8.1 1.2 %dynamic_slice.19 = s32[1]{0:T(128)} dynamic-slice(s32[4]{0:T(128)} %param.13, s32[]{:T(128)S(6)} %select_n.60), dynamic_slice_sizes={1} | dynamic-slice | bytes 12 | tf_op jit(solution)/shard_map/dynamic_slice | solution.py:116
  11.2 1.3 %copy.91 = bf16[128,2048]{0,1:T(8,128)(2,1)S(1)} copy(bf16[128,2048]{1,0:T(8,128)(2,1)} %param.8) | data formatting | bytes 1048576 | tf_op jit(solution)/shard_map/reshape | solution.py:114
  14.6 1.9 %collective-permute-done = bf16[128,512]{0,1:T(8,128)(2,1)S(1)} collective-permute-done((bf16[128,512]{0,1:T(8,128)(2,1)S(1)}, bf16[128,512]{0,1:T(8,128)(2,1)S(1)}, u32[]{:S(2)}, u32[]{:S(2)}) %collective-permute-start) | collective-permute-done | bytes 131104 | tf_op jit(solution)/shard_map/ppermute | solution.py:41
  18.5 1.5 %fusion.31 = f32[2,8,128,128]{3,2,1,0:T(8,128)S(1)} fusion(bf16[512,2,128,1]{0,2,3,1:T(8,128)(2,1)S(1)} %bitcast.126, f32[2,512,128,8]{2,1,3,0:T(8,128)S(1)} %get-tuple-element.24, f32[2,8,128]{2,1,0:T(8,128)S(1)} %get-tuple-element.23, pred[512]{0:T(512)(128)(4,1)S(1)} %broadcast_bitcast_fusion, f32[2,8,128]{2,1,0:T(8,128)S(1)} %fusion.6), kind=kOutput, calls=%fused_computation.46 | convolution fusion | flops 273416192 | bytes 5521920 | tf_op jit(solution)/shard_map/kgqt,tkd->kgqd/dot_general | solution.py:199
  20.8 4.4 %fusion.23 = f32[2,512,128,1]{1,2,3,0:T(8,128)} fusion(bf16[128,2,8,128]{0,3,2,1:T(8,128)(2,1)S(1)} %copy.57, f32[2,512,128,8]{2,1,3,0:T(8,128)} %copy-done, f32[2,8,128]{2,1,0:T(8,128)S(1)} %log_add_fusion, pred[512]{0:T(512)(128)(4,1)S(1)} %broadcast_bitcast_fusion), kind=kOutput, calls=%fused_computation.29 | convolution fusion | flops 272629760 | bytes 5251584 | tf_op jit(solution)/shard_map/kgqt,qkgd->tkd/dot_general | solution.py:181
  25.2 1.5 %fusion.1 = bf16[2,8,128,512]{2,3,1,0:T(8,128)(2,1)S(1)} fusion(f32[2,512,128,8]{2,1,3,0:T(8,128)S(1)} %copy-done.1, bf16[512,2,128,1]{0,2,3,1:T(8,128)(2,1)S(1)} %bitcast.127, bf16[128,2,8,128]{0,3,2,1:T(8,128)(2,1)S(1)} %copy.57, f32[2,8,128]{2,1,0:T(8,128)S(1)} %copy.74, f32[2,8,128]{2,1,0:T(8,128)S(1)} %log_add_fusion, ...), kind=kOutput, calls=%fused_computation.2 | convolution fusion | flops 274726912 | bytes 7094784 | tf_op jit(solution)/shard_map/qkgd,tkd->kgqt/dot_general | solution.py:168
  27.8 1.2 %copy.59 = f32[512,256]{1,0:T(8,128)S(1)} copy(f32[512,256]{0,1:T(8,128)} %bitcast.125) | data formatting | bytes 1048576 | tf_op jit(solution)/shard_map/reshape | solution.py:185
  29.9 2.5 %collective-permute-start.5 = (f32[128,512]{1,0:T(8,128)}, f32[128,512]{1,0:T(8,128)}, u32[]{:S(2)}, u32[]{:S(2)}) collective-permute-start(f32[128,512]{1,0:T(8,128)} %get-tuple-element.17), channel_id=1, source_target_pairs={{0,4},{4,8},{8,12},{12,0},{1,5},{5,9},{9,13},{13,1},{2,6},{6,10},{... | collective-permute-start | bytes 786440 | tf_op jit(solution)/shard_map/ppermute | solution.py:54
  32.4 1.2 %collective-permute-start.4 = (f32[128,512]{1,0:T(8,128)}, f32[128,512]{1,0:T(8,128)}, u32[]{:S(2)}, u32[]{:S(2)}) collective-permute-start(f32[128,512]{1,0:T(8,128)} %get-tuple-element.18), channel_id=1, source_target_pairs={{0,8},{4,12},{8,0},{12,4},{1,9},{5,13},{9,1},{13,5},{2,10},{6,14},... | collective-permute-start | bytes 786440 | tf_op jit(solution)/shard_map/ppermute | solution.py:54
  33.9 16.8 %collective-permute-done.5 = f32[128,512]{1,0:T(8,128)} collective-permute-done((f32[128,512]{1,0:T(8,128)}, f32[128,512]{1,0:T(8,128)}, u32[]{:S(2)}, u32[]{:S(2)}) %collective-permute-start.5) | collective-permute-done | bytes 262176 | tf_op jit(solution)/shard_map/ppermute | solution.py:54
  50.7 3.8 %collective-permute-done.4 = f32[128,512]{1,0:T(8,128)} collective-permute-done((f32[128,512]{1,0:T(8,128)}, f32[128,512]{1,0:T(8,128)}, u32[]{:S(2)}, u32[]{:S(2)}) %collective-permute-start.4) | collective-permute-done | bytes 262176 | tf_op jit(solution)/shard_map/ppermute | solution.py:54
  54.5 1.2 %collective-permute-done.3 = f32[128,512]{1,0:T(8,128)} collective-permute-done((f32[128,512]{1,0:T(8,128)}, f32[128,512]{1,0:T(8,128)}, u32[]{:S(2)}, u32[]{:S(2)}) %collective-permute-start.3) | collective-permute-done | bytes 262176 | tf_op jit(solution)/shard_map/ppermute | solution.py:54
  55.8 1.2 %fusion.40 = bf16[128,512]{1,0:T(8,128)(2,1)S(1)} fusion(f32[128,512]{1,0:T(8,128)} %collective-permute-done.5, f32[128,512]{1,0:T(8,128)} %collective-permute-done.4, f32[128,512]{1,0:T(8,128)} %collective-permute-done.3, f32[512,256]{1,0:T(8,128)S(1)} %copy.58, f32[512,256]{1,0:T(8,128)S(1)} %copy.59), kind=kLoop, calls=%fused_computation.54 | loop fusion | flops 327680 | bytes 1966080 | tf_op jit(solution)/shard_map/convert.1
  57.0 2.3 %fusion.10 = f32[2,2048,128]{2,1,0:T(8,128)S(1)} fusion(bf16[2,2,2048,256]{3,2,1,0:T(8,128)(2,1)} %bitcast.116, s32[]{:T(128)S(6)} %select_n.65, bf16[128,256]{1,0:T(8,128)(2,1)S(1)} %get-tuple-element.21), kind=kOutput, calls=%fused_computation.16 | convolution fusion | flops 268435456 | bytes 4259844 | tf_op jit(solution)/shard_map/arf,tf->art/dot_general | solution.py:82
  59.3 2.1 %convolution_add_fusion = f32[2,2048,128]{2,1,0:T(8,128)} fusion(f32[2,2048,128]{2,1,0:T(8,128)S(1)} %fusion.10, bf16[2,2,2048,256]{3,2,1,0:T(8,128)(2,1)S(1)} %bitcast.118, s32[]{:T(128)S(6)} %select_n.65, bf16[128,256]{1,0:T(8,128)(2,1)S(1)} %get-tuple-element.22), kind=kOutput, calls=%fused_computation.12 | convolution fusion | flops 268959744 | bytes 6356996 | tf_op jit(solution)/shard_map/arf,tf->art/dot_general | solution.py:77
  61.4 2.4 %fusion.13 = f32[2,2048,128]{2,1,0:T(8,128)S(1)} fusion(bf16[2,2,2048,256]{3,2,1,0:T(8,128)(2,1)} %bitcast.117, s32[]{:T(128)S(6)} %select_n.64, bf16[128,256]{1,0:T(8,128)(2,1)S(1)} %get-tuple-element.21), kind=kOutput, calls=%fused_computation.19 | convolution fusion | flops 268435456 | bytes 4259844 | tf_op jit(solution)/shard_map/arf,tf->art/dot_general | solution.py:82
  63.9 2.1 %collective-permute-done.6 = f32[2,2048,128]{2,1,0:T(8,128)} collective-permute-done((f32[2,2048,128]{2,1,0:T(8,128)}, f32[2,2048,128]{2,1,0:T(8,128)}, u32[]{:S(2)}, u32[]{:S(2)}) %collective-permute-start.6) | collective-permute-done | bytes 2097184 | tf_op jit(solution)/shard_map/ppermute | solution.py:92
  65.9 2.3 %fusion.7 = f32[2,2048,128]{2,1,0:T(8,128)S(1)} fusion(f32[2,2048,128]{2,1,0:T(8,128)} %collective-permute-done.6, f32[2,2048,128]{2,1,0:T(8,128)S(1)} %fusion.13, bf16[2,2,2048,256]{3,2,1,0:T(8,128)(2,1)S(1)} %bitcast.119, s32[]{:T(128)S(6)} %select_n.64, bf16[128,256]{1,0:T(8,128)(2,1)S(1)} %get-tuple-element.22), kind=kOutput, calls=%fused_computation.14 | convolution fusion | flops 269484032 | bytes 8454148 | tf_op jit(solution)/shard_map/arf,tf->art/dot_general | solution.py:77
  68.3 1.3 %copy-done.2 = f32[2,2048,128]{2,1,0:T(8,128)} copy-done((f32[2,2048,128]{2,1,0:T(8,128)}, f32[2,2048,128]{2,1,0:T(8,128)S(1)}, u32[]{:S(2)}) %copy-start.2) | copy-done | bytes 2097176
  70.4 1.5 %collective-permute-start.7 = (bf16[1,2048,128]{2,1,0:T(8,128)(2,1)}, bf16[1,2048,128]{2,1,0:T(8,128)(2,1)S(1)}, u32[]{:S(2)}, u32[]{:S(2)}) collective-permute-start(bf16[1,2048,128]{2,1,0:T(8,128)(2,1)} %dynamic-slice_convert_fusion), channel_id=1, source_target_pairs={{0,2},{1,3},{2,0},{3,1},{4,6},{5,7},{6,4},{7,5},{8,10},{9,11},{10,... | collective-permute-start | bytes 1572872 | tf_op jit(solution)/shard_map/ppermute | solution.py:98
  73.4 11.2 %collective-permute-done.7 = bf16[1,2048,128]{2,1,0:T(8,128)(2,1)S(1)} collective-permute-done((bf16[1,2048,128]{2,1,0:T(8,128)(2,1)}, bf16[1,2048,128]{2,1,0:T(8,128)(2,1)S(1)}, u32[]{:S(2)}, u32[]{:S(2)}) %collective-permute-start.7) | collective-permute-done | bytes 524320 | tf_op jit(solution)/shard_map/ppermute | solution.py:98
  84.6 2.1 %fusion.34 = bf16[2048,128]{1,0:T(8,128)(2,1)} fusion(bf16[1,2048,128]{2,1,0:T(8,128)(2,1)S(1)} %collective-permute-done.7, f32[2,2048,128]{2,1,0:T(8,128)} %copy-done.2, s32[]{:T(128)S(6)} %select_n.68), kind=kLoop, calls=%fused_computation.47 | loop fusion | flops 786432 | bytes 2097156 | tf_op jit(solution)/shard_map/convert_element_type | solution.py:102
  (48 shorter events, 13.1 us)
Async XLA Ops:
  2.6 11.7 %collective-permute-start.2 = (bf16[128,512]{0,1:T(8,128)(2,1)S(1)}, bf16[128,512]{0,1:T(8,128)(2,1)S(1)}, u32[]{:S(2)}, u32[]{:S(2)}) collective-permute-start(bf16[128,512]{0,1:T(8,128)(2,1)S(1)} %pad_maximum_fusion.2), channel_id=1, source_target_pairs={{0,12},{4,0},{8,4},{12,8},{1,13},{5,1},{9,5},{13,9},{2,14},{6,2},{... | collective-permute-start | bytes 393224 | tf_op jit(solution)/shard_map/ppermute | solution.py:41
  2.6 12.0 %collective-permute-start.1 = (bf16[128,512]{0,1:T(8,128)(2,1)S(1)}, bf16[128,512]{0,1:T(8,128)(2,1)S(1)}, u32[]{:S(2)}, u32[]{:S(2)}) collective-permute-start(bf16[128,512]{0,1:T(8,128)(2,1)S(1)} %pad_maximum_fusion.2), channel_id=1, source_target_pairs={{0,8},{4,12},{8,0},{12,4},{1,9},{5,13},{9,1},{13,5},{2,10},{6,14},... | collective-permute-start | bytes 393224 | tf_op jit(solution)/shard_map/ppermute | solution.py:41
  5.7 10.9 %collective-permute-start = (bf16[128,512]{0,1:T(8,128)(2,1)S(1)}, bf16[128,512]{0,1:T(8,128)(2,1)S(1)}, u32[]{:S(2)}, u32[]{:S(2)}) collective-permute-start(bf16[128,512]{0,1:T(8,128)(2,1)S(1)} %pad_maximum_fusion.2), channel_id=1, source_target_pairs={{0,4},{4,8},{8,12},{12,0},{1,5},{5,9},{9,13},{13,1},{2,6},{6,10},{... | collective-permute-start | bytes 393224 | tf_op jit(solution)/shard_map/ppermute | solution.py:41
  16.7 1.8 %copy-start.7 = (bf16[512,256]{0,1:T(8,128)(2,1)}, bf16[512,256]{0,1:T(8,128)(2,1)S(1)}, u32[]{:S(2)}) copy-start(bf16[512,256]{0,1:T(8,128)(2,1)S(1)} %get-tuple-element.19) | copy-start | bytes 786436
  17.5 2.5 %copy-start = (f32[2,512,128,8]{2,1,3,0:T(8,128)}, f32[2,512,128,8]{2,1,3,0:T(8,128)S(1)}, u32[]{:S(2)}) copy-start(f32[2,512,128,8]{2,1,3,0:T(8,128)S(1)} %get-tuple-element.24) | copy-start | bytes 12582916
  20.8 4.4 %copy-start.1 = (f32[2,512,128,8]{2,1,3,0:T(8,128)S(1)}, f32[2,512,128,8]{2,1,3,0:T(8,128)}, u32[]{:S(2)}) copy-start(f32[2,512,128,8]{2,1,3,0:T(8,128)} %copy-done) | copy-start | bytes 12582916
  20.8 4.4 %copy-start.8 = (bf16[512,256]{0,1:T(8,128)(2,1)S(1)}, bf16[512,256]{0,1:T(8,128)(2,1)}, u32[]{:S(2)}) copy-start(bf16[512,256]{0,1:T(8,128)(2,1)} %copy-done.7) | copy-start | bytes 786436
  29.9 20.8 %collective-permute-start.5 = (f32[128,512]{1,0:T(8,128)}, f32[128,512]{1,0:T(8,128)}, u32[]{:S(2)}, u32[]{:S(2)}) collective-permute-start(f32[128,512]{1,0:T(8,128)} %get-tuple-element.17), channel_id=1, source_target_pairs={{0,4},{4,8},{8,12},{12,0},{1,5},{5,9},{9,13},{13,1},{2,6},{6,10},{... | collective-permute-start | bytes 786440 | tf_op jit(solution)/shard_map/ppermute | solution.py:54
  32.4 22.1 %collective-permute-start.4 = (f32[128,512]{1,0:T(8,128)}, f32[128,512]{1,0:T(8,128)}, u32[]{:S(2)}, u32[]{:S(2)}) collective-permute-start(f32[128,512]{1,0:T(8,128)} %get-tuple-element.18), channel_id=1, source_target_pairs={{0,8},{4,12},{8,0},{12,4},{1,9},{5,13},{9,1},{13,5},{2,10},{6,14},... | collective-permute-start | bytes 786440 | tf_op jit(solution)/shard_map/ppermute | solution.py:54
  33.6 22.2 %collective-permute-start.3 = (f32[128,512]{1,0:T(8,128)}, f32[128,512]{1,0:T(8,128)}, u32[]{:S(2)}, u32[]{:S(2)}) collective-permute-start(f32[128,512]{1,0:T(8,128)} %get-tuple-element.16), channel_id=1, source_target_pairs={{0,12},{4,0},{8,4},{12,8},{1,13},{5,1},{9,5},{13,9},{2,14},{6,2},{... | collective-permute-start | bytes 786440 | tf_op jit(solution)/shard_map/ppermute | solution.py:54
  33.9 25.4 %copy-start.3 = (bf16[8192,256]{1,0:T(8,128)(2,1)S(1)}, bf16[8192,256]{1,0:T(8,128)(2,1)}, u32[]{:S(2)}) copy-start(bf16[8192,256]{1,0:T(8,128)(2,1)} %param.14) | copy-start | bytes 12582916
  57.0 4.4 %copy-start.5 = (bf16[128,256]{1,0:T(8,128)(2,1)}, bf16[128,256]{1,0:T(8,128)(2,1)S(1)}, u32[]{:S(2)}) copy-start(bf16[128,256]{1,0:T(8,128)(2,1)S(1)} %get-tuple-element.21) | copy-start | bytes 196612
  57.0 8.9 %copy-start.6 = (bf16[128,256]{1,0:T(8,128)(2,1)}, bf16[128,256]{1,0:T(8,128)(2,1)S(1)}, u32[]{:S(2)}) copy-start(bf16[128,256]{1,0:T(8,128)(2,1)S(1)} %get-tuple-element.22) | copy-start | bytes 196612
  61.4 4.5 %collective-permute-start.6 = (f32[2,2048,128]{2,1,0:T(8,128)}, f32[2,2048,128]{2,1,0:T(8,128)}, u32[]{:S(2)}, u32[]{:S(2)}) collective-permute-start(f32[2,2048,128]{2,1,0:T(8,128)} %convolution_add_fusion), channel_id=1, source_target_pairs={{0,1},{1,0},{2,3},{3,2},{4,5},{5,4},{6,7},{7,6},{8,9},{9,8},{10,11... | collective-permute-start | bytes 6291464 | tf_op jit(solution)/shard_map/ppermute | solution.py:92
  61.4 4.5 %copy-start.4 = (bf16[8192,256]{1,0:T(8,128)(2,1)S(1)}, bf16[8192,256]{1,0:T(8,128)(2,1)}, u32[]{:S(2)}) copy-start(bf16[8192,256]{1,0:T(8,128)(2,1)} %param.14) | copy-start | bytes 12582916
  68.2 1.3 %copy-start.2 = (f32[2,2048,128]{2,1,0:T(8,128)}, f32[2,2048,128]{2,1,0:T(8,128)S(1)}, u32[]{:S(2)}) copy-start(f32[2,2048,128]{2,1,0:T(8,128)S(1)} %fusion.7) | copy-start | bytes 6291460
  70.4 14.2 %collective-permute-start.7 = (bf16[1,2048,128]{2,1,0:T(8,128)(2,1)}, bf16[1,2048,128]{2,1,0:T(8,128)(2,1)S(1)}, u32[]{:S(2)}, u32[]{:S(2)}) collective-permute-start(bf16[1,2048,128]{2,1,0:T(8,128)(2,1)} %dynamic-slice_convert_fusion), channel_id=1, source_target_pairs={{0,2},{1,3},{2,0},{3,1},{4,6},{5,7},{6,4},{7,5},{8,10},{9,11},{10,... | collective-permute-start | bytes 1572872 | tf_op jit(solution)/shard_map/ppermute | solution.py:98

commit v3 on v2

--- a/solution.py
+++ b/solution.py
@@ -52,8 +52,10 @@
     total = slots[:rows]
     for steps in range(1, count):
         total = total + lax.ppermute(
-            slots[steps * rows : (steps + 1) * rows], axis, shifted_pairs(count, -steps)
-        )
+            slots[steps * rows : (steps + 1) * rows].astype(jnp.bfloat16),
+            axis,
+            shifted_pairs(count, -steps),
+        ).astype(jnp.float32)
     return total
 
 

time: 87.3 us -> 76.1 us (0.87)
  the two profiles are of different devices: /device:TPU:8 before, /device:TPU:0 now
where the time goes in v3:
time: 76.1 us; the launch traced here: 75.6 us
  waiting for transfers between devices  24.4 us (32%)
  matrix products  18.7 us (25%)
  starting transfers between devices  13.2 us (17%)
  local copies, waits for them, and re-layouts  11.6 us (15%)
  other arithmetic  6.84 us (9%)
  between operations  0.88 us (1%)
    ppermute x1, waiting for transfers between devices, head_reduce(): lax.ppermute(sent.astype(jnp.bfloat16), 'head', [(i, i ^ 1 << level) for...  11.2 us
    ppermute x3, waiting for transfers between devices, scatter_slots(): lax.ppermute(slots[steps * rows:(steps + 1) * rows].astype(jnp.bfloat16),...  7.09 us
    ppermute x3, starting transfers between devices, gather_slots(): lax.ppermute(block, axis, shifted_pairs(count, steps))  6.11 us
    ppermute x3, starting transfers between devices, scatter_slots(): lax.ppermute(slots[steps * rows:(steps + 1) * rows].astype(jnp.bfloat16),...  5.56 us
    unnamed x22, local copies, waits for them, and re-layouts  5.44 us
    dot_general x2, matrix products, project(): jnp.einsum('arf,tf->art', lax.dynamic_index_in_dim(key_split, half, 1, ke...  4.77 us
    dot_general x2, matrix products, project(): jnp.einsum('arf,tf->art', lax.dynamic_index_in_dim(value_split, half, 1,...  4.4 us
    dot_general x1, matrix products, backward_chunk(): jnp.einsum('kgqt,qkgd->tkd', probs_low, grad_heads, preferred_element_typ...  4.37 us
  transfers between devices with their start and end apart: 8, of which 5 were waited for; matrix products, arithmetic and copies ran while one was open for 13% of the time, Pallas kernels for 0%

profile of v3, /device:TPU:0, one launch (start us, length us, event | category | flops | bytes accessed | tf_op | source)
XLA Modules:
  0.0 75.6 jit_solution(156462472508812662)
XLA Ops:
  2.6 5.1 %collective-permute-start.2 = (bf16[128,512]{0,1:T(8,128)(2,1)S(1)}, bf16[128,512]{0,1:T(8,128)(2,1)S(1)}, u32[]{:S(2)}, u32[]{:S(2)}) collective-permute-start(bf16[128,512]{0,1:T(8,128)(2,1)S(1)} %pad_maximum_fusion.2), channel_id=1, source_target_pairs={{0,12},{4,0},{8,4},{12,8},{1,13},{5,1},{9,5},{13,9},{2,14},{6,2},{... | collective-permute-start | bytes 393224 | tf_op jit(solution)/shard_map/ppermute | solution.py:41
  7.7 1.0 %collective-permute-start = (bf16[128,512]{0,1:T(8,128)(2,1)S(1)}, bf16[128,512]{0,1:T(8,128)(2,1)S(1)}, u32[]{:S(2)}, u32[]{:S(2)}) collective-permute-start(bf16[128,512]{0,1:T(8,128)(2,1)S(1)} %pad_maximum_fusion.2), channel_id=1, source_target_pairs={{0,4},{4,8},{8,12},{12,0},{1,5},{5,9},{9,13},{13,1},{2,6},{6,10},{... | collective-permute-start | bytes 393224 | tf_op jit(solution)/shard_map/ppermute | solution.py:41
  8.7 1.2 %dynamic_slice.19 = s32[1]{0:T(128)} dynamic-slice(s32[4]{0:T(128)} %param.13, s32[]{:T(128)S(6)} %select_n.60), dynamic_slice_sizes={1} | dynamic-slice | bytes 12 | tf_op jit(solution)/shard_map/dynamic_slice | solution.py:118
  11.8 1.3 %copy.91 = bf16[128,2048]{0,1:T(8,128)(2,1)S(1)} copy(bf16[128,2048]{1,0:T(8,128)(2,1)} %param.8) | data formatting | bytes 1048576 | tf_op jit(solution)/shard_map/reshape | solution.py:116
  13.1 1.1 %copy.92 = bf16[16,8,16,128]{3,2,1,0:T(8,128)(2,1)S(1)} copy(bf16[16,8,16,128]{3,1,2,0:T(8,128)(2,1)} %bitcast.124) | data formatting | bytes 1048576
  14.8 4.1 %collective-permute-done.1 = bf16[128,512]{0,1:T(8,128)(2,1)S(1)} collective-permute-done((bf16[128,512]{0,1:T(8,128)(2,1)S(1)}, bf16[128,512]{0,1:T(8,128)(2,1)S(1)}, u32[]{:S(2)}, u32[]{:S(2)}) %collective-permute-start.1) | collective-permute-done | bytes 131104 | tf_op jit(solution)/shard_map/ppermute | solution.py:41
  20.8 1.5 %fusion.32 = f32[2,8,128,128]{3,2,1,0:T(8,128)S(1)} fusion(bf16[512,2,128,1]{0,2,3,1:T(8,128)(2,1)S(1)} %bitcast.126, f32[2,512,128,8]{2,1,3,0:T(8,128)S(1)} %get-tuple-element.24, f32[2,8,128]{2,1,0:T(8,128)S(1)} %get-tuple-element.23, pred[512]{0:T(512)(128)(4,1)S(1)} %broadcast_bitcast_fusion, f32[2,8,128]{2,1,0:T(8,128)S(1)} %fusion.6), kind=kOutput, calls=%fused_computation.44 | convolution fusion | flops 273416192 | bytes 5521920 | tf_op jit(solution)/shard_map/kgqt,tkd->kgqd/dot_general | solution.py:201
  23.1 4.4 %fusion.23 = f32[2,512,128,1]{1,2,3,0:T(8,128)} fusion(bf16[128,2,8,128]{0,3,2,1:T(8,128)(2,1)S(1)} %copy.57, f32[2,512,128,8]{2,1,3,0:T(8,128)} %copy-done, f32[2,8,128]{2,1,0:T(8,128)S(1)} %log_add_fusion, pred[512]{0:T(512)(128)(4,1)S(1)} %broadcast_bitcast_fusion), kind=kOutput, calls=%fused_computation.29 | convolution fusion | flops 272629760 | bytes 5251584 | tf_op jit(solution)/shard_map/kgqt,qkgd->tkd/dot_general | solution.py:183
  27.5 1.5 %fusion.1 = bf16[2,8,128,512]{2,3,1,0:T(8,128)(2,1)S(1)} fusion(f32[2,512,128,8]{2,1,3,0:T(8,128)S(1)} %copy-done.1, bf16[512,2,128,1]{0,2,3,1:T(8,128)(2,1)S(1)} %bitcast.127, bf16[128,2,8,128]{0,3,2,1:T(8,128)(2,1)S(1)} %copy.57, f32[2,8,128]{2,1,0:T(8,128)S(1)} %copy.74, f32[2,8,128]{2,1,0:T(8,128)S(1)} %log_add_fusion, ...), kind=kOutput, calls=%fused_computation.2 | convolution fusion | flops 274726912 | bytes 7094784 | tf_op jit(solution)/shard_map/qkgd,tkd->kgqt/dot_general | solution.py:170
  30.1 1.2 %copy.59 = f32[512,256]{1,0:T(8,128)S(1)} copy(f32[512,256]{0,1:T(8,128)} %bitcast.125) | data formatting | bytes 1048576 | tf_op jit(solution)/shard_map/reshape | solution.py:187
  32.9 1.9 %collective-permute-start.4 = (bf16[128,512]{1,0:T(8,128)(2,1)}, bf16[128,512]{1,0:T(8,128)(2,1)}, u32[]{:S(2)}, u32[]{:S(2)}) collective-permute-start(bf16[128,512]{1,0:T(8,128)(2,1)} %get-tuple-element.18), channel_id=1, source_target_pairs={{0,8},{4,12},{8,0},{12,4},{1,9},{5,13},{9,1},{13,5},{2,10},{6,14},... | collective-permute-start | bytes 393224 | tf_op jit(solution)/shard_map/ppermute | solution.py:54
  34.8 2.9 %collective-permute-start.3 = (bf16[128,512]{1,0:T(8,128)(2,1)}, bf16[128,512]{1,0:T(8,128)(2,1)}, u32[]{:S(2)}, u32[]{:S(2)}) collective-permute-start(bf16[128,512]{1,0:T(8,128)(2,1)} %get-tuple-element.16), channel_id=1, source_target_pairs={{0,12},{4,0},{8,4},{12,8},{1,13},{5,1},{9,5},{13,9},{2,14},{6,2},{... | collective-permute-start | bytes 393224 | tf_op jit(solution)/shard_map/ppermute | solution.py:54
  37.7 2.9 %collective-permute-done.5 = bf16[128,512]{1,0:T(8,128)(2,1)S(1)} collective-permute-done((bf16[128,512]{1,0:T(8,128)(2,1)}, bf16[128,512]{1,0:T(8,128)(2,1)S(1)}, u32[]{:S(2)}, u32[]{:S(2)}) %collective-permute-start.5) | collective-permute-done | bytes 131104 | tf_op jit(solution)/shard_map/ppermute | solution.py:54
  40.6 4.2 %collective-permute-done.4 = bf16[128,512]{1,0:T(8,128)(2,1)} collective-permute-done((bf16[128,512]{1,0:T(8,128)(2,1)}, bf16[128,512]{1,0:T(8,128)(2,1)}, u32[]{:S(2)}, u32[]{:S(2)}) %collective-permute-start.4) | collective-permute-done | bytes 131104 | tf_op jit(solution)/shard_map/ppermute | solution.py:54
  44.8 1.0 %fusion.40 = bf16[128,512]{1,0:T(8,128)(2,1)S(1)} fusion(f32[512,256]{1,0:T(8,128)S(1)} %copy.58, f32[512,256]{1,0:T(8,128)S(1)} %copy.59, bf16[128,512]{1,0:T(8,128)(2,1)S(1)} %collective-permute-done.5, bf16[128,512]{1,0:T(8,128)(2,1)} %collective-permute-done.4, bf16[128,512]{1,0:T(8,128)(2,1)} %collective-permute-done.3), kind=kLoop, calls=%fused_computation.51 | loop fusion | flops 524288 | bytes 1572864 | tf_op jit(solution)/shard_map/convert.1
  45.9 2.3 %fusion.11 = f32[2,2048,128]{2,1,0:T(8,128)S(1)} fusion(bf16[2,2,2048,256]{3,2,1,0:T(8,128)(2,1)} %bitcast.116, s32[]{:T(128)S(6)} %select_n.65, bf16[128,256]{1,0:T(8,128)(2,1)S(1)} %get-tuple-element.22), kind=kOutput, calls=%fused_computation.17 | convolution fusion | flops 268435456 | bytes 4259844 | tf_op jit(solution)/shard_map/arf,tf->art/dot_general | solution.py:79
  48.2 2.1 %convolution_add_fusion = f32[2,2048,128]{2,1,0:T(8,128)} fusion(f32[2,2048,128]{2,1,0:T(8,128)S(1)} %fusion.11, bf16[2,2,2048,256]{3,2,1,0:T(8,128)(2,1)S(1)} %bitcast.118, s32[]{:T(128)S(6)} %select_n.65, bf16[128,256]{1,0:T(8,128)(2,1)S(1)} %get-tuple-element.21), kind=kOutput, calls=%fused_computation.12 | convolution fusion | flops 268959744 | bytes 6356996 | tf_op jit(solution)/shard_map/arf,tf->art/dot_general | solution.py:84
  50.3 2.4 %fusion.14 = f32[2,2048,128]{2,1,0:T(8,128)S(1)} fusion(bf16[2,2,2048,256]{3,2,1,0:T(8,128)(2,1)} %bitcast.117, s32[]{:T(128)S(6)} %select_n.64, bf16[128,256]{1,0:T(8,128)(2,1)S(1)} %get-tuple-element.22), kind=kOutput, calls=%fused_computation.20 | convolution fusion | flops 268435456 | bytes 4259844 | tf_op jit(solution)/shard_map/arf,tf->art/dot_general | solution.py:79
  52.7 2.0 %collective-permute-done.6 = f32[2,2048,128]{2,1,0:T(8,128)} collective-permute-done((f32[2,2048,128]{2,1,0:T(8,128)}, f32[2,2048,128]{2,1,0:T(8,128)}, u32[]{:S(2)}, u32[]{:S(2)}) %collective-permute-start.6) | collective-permute-done | bytes 2097184 | tf_op jit(solution)/shard_map/ppermute | solution.py:94
  54.8 2.3 %fusion.7 = f32[2,2048,128]{2,1,0:T(8,128)S(1)} fusion(f32[2,2048,128]{2,1,0:T(8,128)} %collective-permute-done.6, f32[2,2048,128]{2,1,0:T(8,128)S(1)} %fusion.14, bf16[2,2,2048,256]{3,2,1,0:T(8,128)(2,1)S(1)} %bitcast.119, s32[]{:T(128)S(6)} %select_n.64, bf16[128,256]{1,0:T(8,128)(2,1)S(1)} %get-tuple-element.21), kind=kOutput, calls=%fused_computation.14 | convolution fusion | flops 269484032 | bytes 8454148 | tf_op jit(solution)/shard_map/arf,tf->art/dot_general | solution.py:84
  57.1 1.3 %copy-done.2 = f32[2,2048,128]{2,1,0:T(8,128)} copy-done((f32[2,2048,128]{2,1,0:T(8,128)}, f32[2,2048,128]{2,1,0:T(8,128)S(1)}, u32[]{:S(2)}) %copy-start.2) | copy-done | bytes 2097176
  59.3 1.5 %collective-permute-start.7 = (bf16[1,2048,128]{2,1,0:T(8,128)(2,1)}, bf16[1,2048,128]{2,1,0:T(8,128)(2,1)S(1)}, u32[]{:S(2)}, u32[]{:S(2)}) collective-permute-start(bf16[1,2048,128]{2,1,0:T(8,128)(2,1)} %dynamic-slice_convert_fusion), channel_id=1, source_target_pairs={{0,2},{1,3},{2,0},{3,1},{4,6},{5,7},{6,4},{7,5},{8,10},{9,11},{10,... | collective-permute-start | bytes 1572872 | tf_op jit(solution)/shard_map/ppermute | solution.py:100
  62.3 11.2 %collective-permute-done.7 = bf16[1,2048,128]{2,1,0:T(8,128)(2,1)S(1)} collective-permute-done((bf16[1,2048,128]{2,1,0:T(8,128)(2,1)}, bf16[1,2048,128]{2,1,0:T(8,128)(2,1)S(1)}, u32[]{:S(2)}, u32[]{:S(2)}) %collective-permute-start.7) | collective-permute-done | bytes 524320 | tf_op jit(solution)/shard_map/ppermute | solution.py:100
  73.5 2.1 %fusion.35 = bf16[2048,128]{1,0:T(8,128)(2,1)} fusion(bf16[1,2048,128]{2,1,0:T(8,128)(2,1)S(1)} %collective-permute-done.7, f32[2,2048,128]{2,1,0:T(8,128)} %copy-done.2, s32[]{:T(128)S(6)} %select_n.68), kind=kLoop, calls=%fused_computation.45 | loop fusion | flops 786432 | bytes 2097156 | tf_op jit(solution)/shard_map/convert_element_type | solution.py:104
  (49 shorter events, 11.9 us)
Async XLA Ops:
  2.6 12.2 %collective-permute-start.2 = (bf16[128,512]{0,1:T(8,128)(2,1)S(1)}, bf16[128,512]{0,1:T(8,128)(2,1)S(1)}, u32[]{:S(2)}, u32[]{:S(2)}) collective-permute-start(bf16[128,512]{0,1:T(8,128)(2,1)S(1)} %pad_maximum_fusion.2), channel_id=1, source_target_pairs={{0,12},{4,0},{8,4},{12,8},{1,13},{5,1},{9,5},{13,9},{2,14},{6,2},{... | collective-permute-start | bytes 393224 | tf_op jit(solution)/shard_map/ppermute | solution.py:41
  7.7 11.2 %collective-permute-start.1 = (bf16[128,512]{0,1:T(8,128)(2,1)S(1)}, bf16[128,512]{0,1:T(8,128)(2,1)S(1)}, u32[]{:S(2)}, u32[]{:S(2)}) collective-permute-start(bf16[128,512]{0,1:T(8,128)(2,1)S(1)} %pad_maximum_fusion.2), channel_id=1, source_target_pairs={{0,8},{4,12},{8,0},{12,4},{1,9},{5,13},{9,1},{13,5},{2,10},{6,14},... | collective-permute-start | bytes 393224 | tf_op jit(solution)/shard_map/ppermute | solution.py:41
  7.7 11.2 %collective-permute-start = (bf16[128,512]{0,1:T(8,128)(2,1)S(1)}, bf16[128,512]{0,1:T(8,128)(2,1)S(1)}, u32[]{:S(2)}, u32[]{:S(2)}) collective-permute-start(bf16[128,512]{0,1:T(8,128)(2,1)S(1)} %pad_maximum_fusion.2), channel_id=1, source_target_pairs={{0,4},{4,8},{8,12},{12,0},{1,5},{5,9},{9,13},{13,1},{2,6},{6,10},{... | collective-permute-start | bytes 393224 | tf_op jit(solution)/shard_map/ppermute | solution.py:41
  19.0 1.8 %copy-start.7 = (bf16[512,256]{0,1:T(8,128)(2,1)}, bf16[512,256]{0,1:T(8,128)(2,1)S(1)}, u32[]{:S(2)}) copy-start(bf16[512,256]{0,1:T(8,128)(2,1)S(1)} %get-tuple-element.19) | copy-start | bytes 786436
  19.8 2.5 %copy-start = (f32[2,512,128,8]{2,1,3,0:T(8,128)}, f32[2,512,128,8]{2,1,3,0:T(8,128)S(1)}, u32[]{:S(2)}) copy-start(f32[2,512,128,8]{2,1,3,0:T(8,128)S(1)} %get-tuple-element.24) | copy-start | bytes 12582916
  23.1 4.4 %copy-start.1 = (f32[2,512,128,8]{2,1,3,0:T(8,128)S(1)}, f32[2,512,128,8]{2,1,3,0:T(8,128)}, u32[]{:S(2)}) copy-start(f32[2,512,128,8]{2,1,3,0:T(8,128)} %copy-done) | copy-start | bytes 12582916
  23.1 4.4 %copy-start.8 = (bf16[512,256]{0,1:T(8,128)(2,1)S(1)}, bf16[512,256]{0,1:T(8,128)(2,1)}, u32[]{:S(2)}) copy-start(bf16[512,256]{0,1:T(8,128)(2,1)} %copy-done.7) | copy-start | bytes 786436
  32.1 8.5 %collective-permute-start.5 = (bf16[128,512]{1,0:T(8,128)(2,1)}, bf16[128,512]{1,0:T(8,128)(2,1)S(1)}, u32[]{:S(2)}, u32[]{:S(2)}) collective-permute-start(bf16[128,512]{1,0:T(8,128)(2,1)} %get-tuple-element.17), channel_id=1, source_target_pairs={{0,4},{4,8},{8,12},{12,0},{1,5},{5,9},{9,13},{13,1},{2,6},{6,10},{... | collective-permute-start | bytes 393224 | tf_op jit(solution)/shard_map/ppermute | solution.py:54
  32.9 11.9 %collective-permute-start.4 = (bf16[128,512]{1,0:T(8,128)(2,1)}, bf16[128,512]{1,0:T(8,128)(2,1)}, u32[]{:S(2)}, u32[]{:S(2)}) collective-permute-start(bf16[128,512]{1,0:T(8,128)(2,1)} %get-tuple-element.18), channel_id=1, source_target_pairs={{0,8},{4,12},{8,0},{12,4},{1,9},{5,13},{9,1},{13,5},{2,10},{6,14},... | collective-permute-start | bytes 393224 | tf_op jit(solution)/shard_map/ppermute | solution.py:54
  34.8 10.0 %collective-permute-start.3 = (bf16[128,512]{1,0:T(8,128)(2,1)}, bf16[128,512]{1,0:T(8,128)(2,1)}, u32[]{:S(2)}, u32[]{:S(2)}) collective-permute-start(bf16[128,512]{1,0:T(8,128)(2,1)} %get-tuple-element.16), channel_id=1, source_target_pairs={{0,12},{4,0},{8,4},{12,8},{1,13},{5,1},{9,5},{13,9},{2,14},{6,2},{... | collective-permute-start | bytes 393224 | tf_op jit(solution)/shard_map/ppermute | solution.py:54
  37.7 10.5 %copy-start.3 = (bf16[8192,256]{1,0:T(8,128)(2,1)S(1)}, bf16[8192,256]{1,0:T(8,128)(2,1)}, u32[]{:S(2)}) copy-start(bf16[8192,256]{1,0:T(8,128)(2,1)} %param.15) | copy-start | bytes 12582916
  45.8 4.4 %copy-start.6 = (bf16[128,256]{1,0:T(8,128)(2,1)}, bf16[128,256]{1,0:T(8,128)(2,1)S(1)}, u32[]{:S(2)}) copy-start(bf16[128,256]{1,0:T(8,128)(2,1)S(1)} %get-tuple-element.22) | copy-start | bytes 196612
  45.9 8.9 %copy-start.5 = (bf16[128,256]{1,0:T(8,128)(2,1)}, bf16[128,256]{1,0:T(8,128)(2,1)S(1)}, u32[]{:S(2)}) copy-start(bf16[128,256]{1,0:T(8,128)(2,1)S(1)} %get-tuple-element.21) | copy-start | bytes 196612
  50.3 4.5 %collective-permute-start.6 = (f32[2,2048,128]{2,1,0:T(8,128)}, f32[2,2048,128]{2,1,0:T(8,128)}, u32[]{:S(2)}, u32[]{:S(2)}) collective-permute-start(f32[2,2048,128]{2,1,0:T(8,128)} %convolution_add_fusion), channel_id=1, source_target_pairs={{0,1},{1,0},{2,3},{3,2},{4,5},{5,4},{6,7},{7,6},{8,9},{9,8},{10,11... | collective-permute-start | bytes 6291464 | tf_op jit(solution)/shard_map/ppermute | solution.py:94
  50.3 4.5 %copy-start.4 = (bf16[8192,256]{1,0:T(8,128)(2,1)S(1)}, bf16[8192,256]{1,0:T(8,128)(2,1)}, u32[]{:S(2)}) copy-start(bf16[8192,256]{1,0:T(8,128)(2,1)} %param.15) | copy-start | bytes 12582916
  57.1 1.3 %copy-start.2 = (f32[2,2048,128]{2,1,0:T(8,128)}, f32[2,2048,128]{2,1,0:T(8,128)S(1)}, u32[]{:S(2)}) copy-start(f32[2,2048,128]{2,1,0:T(8,128)S(1)} %fusion.7) | copy-start | bytes 6291460
  59.3 14.2 %collective-permute-start.7 = (bf16[1,2048,128]{2,1,0:T(8,128)(2,1)}, bf16[1,2048,128]{2,1,0:T(8,128)(2,1)S(1)}, u32[]{:S(2)}, u32[]{:S(2)}) collective-permute-start(bf16[1,2048,128]{2,1,0:T(8,128)(2,1)} %dynamic-slice_convert_fusion), channel_id=1, source_target_pairs={{0,2},{1,3},{2,0},{3,1},{4,6},{5,7},{6,4},{7,5},{8,10},{9,11},{10,... | collective-permute-start | bytes 1572872 | tf_op jit(solution)/shard_map/ppermute | solution.py:100

commit v4 on v3

--- a/solution.py
+++ b/solution.py
@@ -236,11 +236,23 @@
             ),
         )
 
-    kv_grad = scatter_slots(kv_acc, "ctx")
     query_grad = query_acc.reshape(rows_here, -1).astype(jnp.bfloat16)
-    key_grad = kv_grad[:, :kv_cols].astype(jnp.bfloat16)
-    value_grad = kv_grad[:, kv_cols:].astype(jnp.bfloat16)
-    input_grad_t = head_reduce(key_proj, value_proj, key_grad, value_grad)
+    slot_count = row_count // rows_here
+    parts = 2 if rows_here % 16 == 0 else 1
+    part_rows = rows_here // parts
+    slots = kv_acc.reshape(slot_count, rows_here, 2 * kv_cols)
+    key_parts, value_parts, input_parts = [], [], []
+    for part in range(parts):
+        sending = slots[:, part * part_rows : (part + 1) * part_rows].reshape(-1, 2 * kv_cols)
+        if key_parts:
+            sending, _ = lax.optimization_barrier((sending, key_parts[-1]))
+        kv_grad = scatter_slots(sending, "ctx")
+        key_parts.append(kv_grad[:, :kv_cols].astype(jnp.bfloat16))
+        value_parts.append(kv_grad[:, kv_cols:].astype(jnp.bfloat16))
+        input_parts.append(head_reduce(key_proj, value_proj, key_parts[-1], value_parts[-1]))
+    key_grad = jnp.concatenate(key_parts, axis=0)
+    value_grad = jnp.concatenate(value_parts, axis=0)
+    input_grad_t = jnp.concatenate(input_parts, axis=1)
     return (query_grad, key_grad, value_grad, input_grad_t)
 
 

time: 76.1 us -> 79 us (1.038)
  waiting for transfers between devices: 24.4 us -> 16.4 us
  local copies, waits for them, and re-layouts: 11.6 us -> 17.8 us
  starting transfers between devices: 13.2 us -> 17.9 us
    ppermute x3 -> x6, waiting for transfers between devices: 7.09 us -> 0.42 us  [scatter_slots(): lax.ppermute(slots[steps * rows:(steps + 1) * rows].astype(jnp.bfloat16),...]
    concatenate x0 -> x3, local copies, waits for them, and re-layouts: none -> 4.57 us  [backward_chunk(): jnp.concatenate([key_term.reshape(step_rows, kv_cols), value_term.reshape...]
    ppermute x3 -> x6, starting transfers between devices: 5.56 us -> 9.44 us  [scatter_slots(): lax.ppermute(slots[steps * rows:(steps + 1) * rows].astype(jnp.bfloat16),...]
    reshape x4 -> x0, local copies, waits for them, and re-layouts: 3.22 us -> none  [the longest x1 1.31 us: local(): query_heads = queries.reshape(rows_here, kv_heads, group_size, HD)]
    unnamed x22 -> x17, local copies, waits for them, and re-layouts: 5.44 us -> 8.36 us
    transpose x0 -> x1, local copies, waits for them, and re-layouts: none -> 2.25 us  [backward_chunk(): jnp.einsum('kgqt,qkgd->tkd', probs_low, grad_heads, preferred_element_typ...]
    ppermute x1 -> x2, waiting for transfers between devices: 2.04 us -> 0.01 us  [head_reduce(): lax.ppermute(sent, 'head', [(i, i ^ 1) for i in range(count)])]
    convert_element_type x1 -> x2, other arithmetic: 2.12 us -> 0.11 us  [head_reduce(): return current.reshape(block, -1).astype(jnp.bfloat16)]
  transfers between devices with their start and end apart: 8 -> 13, of which waited for: 5 -> 4; matrix products, arithmetic and copies ran while one was open for 13% -> 23% of each run, Pallas kernels for 0% -> 0%
where the time goes in v4:
time: 79 us; the launch traced here: 78.4 us
  matrix products  19 us (24%)
  starting transfers between devices  17.9 us (23%)
  local copies, waits for them, and re-layouts  17.8 us (23%)
  waiting for transfers between devices  16.4 us (21%)
  other arithmetic  6.23 us (8%)
  between operations  0.97 us (1%)
    ppermute x2, waiting for transfers between devices, head_reduce(): lax.ppermute(sent.astype(jnp.bfloat16), 'head', [(i, i ^ 1 << level) for...  11.3 us
    ppermute x6, starting transfers between devices, scatter_slots(): lax.ppermute(slots[steps * rows:(steps + 1) * rows].astype(jnp.bfloat16),...  9.44 us
    unnamed x17, local copies, waits for them, and re-layouts  8.36 us
    ppermute x3, starting transfers between devices, gather_slots(): lax.ppermute(block, axis, shifted_pairs(count, steps))  6.11 us
    ppermute x3, waiting for transfers between devices, gather_slots(): lax.ppermute(block, axis, shifted_pairs(count, steps))  4.69 us
    dot_general x4, matrix products, project(): jnp.einsum('arf,tf->art', lax.dynamic_index_in_dim(key_split, half, 1, ke...  4.59 us
    concatenate x3, local copies, waits for them, and re-layouts, backward_chunk(): jnp.concatenate([key_term.reshape(step_rows, kv_cols), value_term.reshape...  4.57 us
    dot_general x1, matrix products, backward_chunk(): jnp.einsum('kgqt,qkgd->tkd', probs_low, grad_heads, preferred_element_typ...  4.22 us
  transfers between devices with their start and end apart: 13, of which 4 were waited for; matrix products, arithmetic and copies ran while one was open for 23% of the time, Pallas kernels for 0%

profile of v4, /device:TPU:0, one launch (start us, length us, event | category | flops | bytes accessed | tf_op | source)
XLA Modules:
  0.0 78.4 jit_solution(6189305367314085240)
XLA Ops:
  2.6 5.1 %collective-permute-start.2 = (bf16[128,512]{0,1:T(8,128)(2,1)S(1)}, bf16[128,512]{0,1:T(8,128)(2,1)S(1)}, u32[]{:S(2)}, u32[]{:S(2)}) collective-permute-start(bf16[128,512]{0,1:T(8,128)(2,1)S(1)} %pad_maximum_fusion.2), channel_id=1, source_target_pairs={{0,12},{4,0},{8,4},{12,8},{1,13},{5,1},{9,5},{13,9},{2,14},{6,2},{... | collective-permute-start | bytes 393224 | tf_op jit(solution)/shard_map/ppermute | solution.py:41
  8.7 1.2 %dynamic_slice.25 = s32[1]{0:T(128)} dynamic-slice(s32[4]{0:T(128)} %param.13, s32[]{:T(128)S(6)} %select_n.71), dynamic_slice_sizes={1} | dynamic-slice | bytes 12 | tf_op jit(solution)/shard_map/dynamic_slice | solution.py:118
  11.8 1.1 %copy.84 = bf16[16,8,16,128]{3,2,1,0:T(8,128)(2,1)S(1)} copy(bf16[16,8,16,128]{3,1,2,0:T(8,128)(2,1)} %bitcast.167) | data formatting | bytes 1048576
  12.9 1.1 %copy.85 = bf16[16,8,16,128]{3,2,1,0:T(8,128)(2,1)S(1)} copy(bf16[16,8,16,128]{3,1,2,0:T(8,128)(2,1)} %bitcast.168) | data formatting | bytes 1048576
  14.2 4.7 %collective-permute-done.1 = bf16[128,512]{0,1:T(8,128)(2,1)S(1)} collective-permute-done((bf16[128,512]{0,1:T(8,128)(2,1)S(1)}, bf16[128,512]{0,1:T(8,128)(2,1)S(1)}, u32[]{:S(2)}, u32[]{:S(2)}) %collective-permute-start.1) | collective-permute-done | bytes 131104 | tf_op jit(solution)/shard_map/ppermute | solution.py:41
  19.0 1.1 %bitcast_reduce_fusion = (f32[2,8,128]{2,1,0:T(8,128)S(1)}, f32[2,512,128,8]{2,1,3,0:T(8,128)S(1)}) fusion(pred[512]{0:T(512)(128)(4,1)S(1)} %broadcast_bitcast_fusion, bf16[512,2,128,1]{0,2,3,1:T(8,128)(2,1)S(1)} %bitcast.161, bf16[128,2,8,128]{3,2,1,0:T(8,128)(2,1)S(1)} %bitcast.157), kind=kOutput, calls=%fused_computation.5 | convolution fusion | flops 271579136 | bytes 4989440 | tf_op jit(solution)/shard_map/qkgd,tkd->kgqt/dot_general | solution.py:144
  21.0 1.5 %fusion.46 = f32[2,8,128,128]{3,2,1,0:T(8,128)S(1)} fusion(bf16[512,2,128,1]{0,2,3,1:T(8,128)(2,1)S(1)} %bitcast.169, f32[2,512,128,8]{2,1,3,0:T(8,128)S(1)} %get-tuple-element.31, f32[2,8,128]{2,1,0:T(8,128)S(1)} %get-tuple-element.30, pred[512]{0:T(512)(128)(4,1)S(1)} %broadcast_bitcast_fusion, f32[2,8,128]{2,1,0:T(8,128)S(1)} %fusion.6), kind=kOutput, calls=%fused_computation.53 | convolution fusion | flops 273416192 | bytes 5521920 | tf_op jit(solution)/shard_map/kgqt,tkd->kgqd/dot_general | solution.py:201
  23.4 4.2 %fusion.41 = f32[512,2,128]{2,0,1:T(8,128)} fusion(f32[2,512,128,8]{2,1,3,0:T(8,128)} %copy-done, f32[2,8,128]{2,1,0:T(8,128)S(1)} %log_add_fusion, pred[512]{0:T(512)(128)(4,1)S(1)} %broadcast_bitcast_fusion, bf16[128,2,8,128]{3,2,1,0:T(8,128)(2,1)S(1)} %bitcast.164), kind=kOutput, calls=%fused_computation.50 | convolution fusion | flops 272629760 | bytes 5251584 | tf_op jit(solution)/shard_map/kgqt,qkgd->tkd/dot_general | solution.py:183
  27.6 2.6 %fusion.1 = bf16[2,8,128,512]{2,3,1,0:T(8,128)(2,1)S(1)} fusion(f32[2,512,128,8]{2,1,3,0:T(8,128)S(1)} %copy-done.1, bf16[512,2,128,1]{0,2,3,1:T(8,128)(2,1)} %bitcast.170, f32[2,8,128]{2,1,0:T(8,128)S(1)} %copy.69, f32[2,8,128]{2,1,0:T(8,128)S(1)} %log_add_fusion, pred[512]{0:T(512)(128)(4,1)S(1)} %broadcast_bitcast_fusion, ...), kind=kOutput, calls=%fused_computation.2 | convolution fusion | flops 274726912 | bytes 7094784 | tf_op jit(solution)/shard_map/qkgd,tkd->kgqt/dot_general | solution.py:170
  31.4 1.2 %concatenate.25 = f32[4,128,256]{2,1,0:T(8,128)} reshape(f32[512,2,128]{2,1,0:T(2,128)S(1)} %copy.51) | data formatting | bytes 1048576 | tf_op jit(solution)/shard_map/concatenate | solution.py:186
  32.6 1.1 %constant_dynamic-update-slice_fusion.1 = f32[4,128,512]{2,1,0:T(8,128)S(1)} fusion(f32[4,128,256]{2,1,0:T(8,128)} %concatenate.25), kind=kLoop, calls=%fused_computation.89 | loop fusion | bytes 1048576
  33.7 2.2 %copy.53 = f32[512,2,128]{2,1,0:T(2,128)} copy(f32[512,2,128]{2,0,1:T(8,128)} %fusion.41) | data formatting | bytes 1048576 | tf_op jit(solution)/shard_map/kgqt,qkgd->tkd/transpose | solution.py:183
  36.0 2.3 %concatenate.26 = f32[4,128,256]{2,1,0:T(8,128)} reshape(f32[512,2,128]{2,1,0:T(2,128)} %copy.53) | data formatting | bytes 1048576 | tf_op jit(solution)/shard_map/concatenate | solution.py:186
  38.2 1.1 %constant_dynamic-update-slice_fusion = f32[4,128,512]{2,1,0:T(8,128)S(1)} fusion(f32[4,128,512]{2,1,0:T(8,128)S(1)} %constant_dynamic-update-slice_fusion.1, f32[4,128,256]{2,1,0:T(8,128)} %concatenate.26), kind=kLoop, calls=%fused_computation.88 | loop fusion | bytes 1048576 | tf_op jit(solution)/shard_map/concatenate | solution.py:186
  40.8 1.9 %collective-permute-start.4 = (bf16[64,512]{1,0:T(8,128)(2,1)}, bf16[64,512]{1,0:T(8,128)(2,1)}, u32[]{:S(2)}, u32[]{:S(2)}) collective-permute-start(bf16[64,512]{1,0:T(8,128)(2,1)} %get-tuple-element.20), channel_id=1, source_target_pairs={{0,8},{4,12},{8,0},{12,4},{1,9},{5,13},{9,1},{13,5},{2,10},{6,14},... | collective-permute-start | bytes 196616 | tf_op jit(solution)/shard_map/ppermute | solution.py:54
  42.7 2.9 %collective-permute-start.3 = (bf16[64,512]{1,0:T(8,128)(2,1)S(1)}, bf16[64,512]{1,0:T(8,128)(2,1)}, u32[]{:S(2)}, u32[]{:S(2)}) collective-permute-start(bf16[64,512]{1,0:T(8,128)(2,1)S(1)} %get-tuple-element.18), channel_id=1, source_target_pairs={{0,12},{4,0},{8,4},{12,8},{1,13},{5,1},{9,5},{13,9},{2,14},{6,2},{... | collective-permute-start | bytes 196616 | tf_op jit(solution)/shard_map/ppermute | solution.py:54
  45.6 1.3 %fusion.38 = bf16[2,128,8,128]{3,1,2,0:T(8,128)(2,1)} fusion(bf16[512,2,128,1]{0,2,3,1:T(8,128)(2,1)S(1)} %bitcast.162, bf16[2,8,128,512]{2,3,1,0:T(8,128)(2,1)S(1)} %fusion.1), kind=kOutput, calls=%fused_computation.46 | convolution fusion | flops 268959744 | bytes 2883584 | tf_op jit(solution)/shard_map/kgqt,tkd->qkgd/dot_general | solution.py:176
  46.9 2.0 %copy.58 = bf16[128,2048]{1,0:T(8,128)(2,1)} copy(bf16[128,2048]{0,1:T(8,128)(2,1)} %bitcast.166) | data formatting | bytes 1048576
  50.1 1.1 %collective-permute-start.8 = (bf16[64,512]{1,0:T(8,128)(2,1)S(1)}, bf16[64,512]{1,0:T(8,128)(2,1)S(1)}, u32[]{:S(2)}, u32[]{:S(2)}) collective-permute-start(bf16[64,512]{1,0:T(8,128)(2,1)S(1)} %get-tuple-element.24), channel_id=1, source_target_pairs={{0,4},{4,8},{8,12},{12,0},{1,5},{5,9},{9,13},{13,1},{2,6},{6,10},{... | collective-permute-start | bytes 196616 | tf_op jit(solution)/shard_map/ppermute | solution.py:54
  51.2 2.2 %collective-permute-start.7 = (bf16[64,512]{1,0:T(8,128)(2,1)S(1)}, bf16[64,512]{1,0:T(8,128)(2,1)S(1)}, u32[]{:S(2)}, u32[]{:S(2)}) collective-permute-start(bf16[64,512]{1,0:T(8,128)(2,1)S(1)} %get-tuple-element.25), channel_id=1, source_target_pairs={{0,8},{4,12},{8,0},{12,4},{1,9},{5,13},{9,1},{13,5},{2,10},{6,14},... | collective-permute-start | bytes 196616 | tf_op jit(solution)/shard_map/ppermute | solution.py:54
  54.0 2.3 %fusion.15 = f32[2,2048,64]{1,2,0:T(8,128)S(1)} fusion(bf16[2,2,2048,256]{3,2,1,0:T(8,128)(2,1)} %bitcast.149, s32[]{:T(128)S(6)} %select_n.76, bf16[64,512]{1,0:T(8,128)(2,1)S(1)} %fusion.59), kind=kOutput, calls=%fused_computation.23 | convolution fusion | flops 134217728 | bytes 3178500 | tf_op jit(solution)/shard_map/arf,tf->art/dot_general | solution.py:79
  62.9 1.6 %collective-permute-start.10 = (bf16[1,2048,64]{1,2,0:T(8,128)(2,1)S(1)}, bf16[1,2048,64]{1,2,0:T(8,128)(2,1)S(1)}, u32[]{:S(2)}, u32[]{:S(2)}) collective-permute-start(bf16[1,2048,64]{1,2,0:T(8,128)(2,1)S(1)} %dynamic-slice_convert_fusion.1), channel_id=1, source_target_pairs={{0,2},{1,3},{2,0},{3,1},{4,6},{5,7},{6,4},{7,5},{8,10},{9,11},{10,... | collective-permute-start | bytes 786440 | tf_op jit(solution)/shard_map/ppermute | solution.py:100
  65.9 6.2 %collective-permute-done.10 = bf16[1,2048,64]{1,2,0:T(8,128)(2,1)S(1)} collective-permute-done((bf16[1,2048,64]{1,2,0:T(8,128)(2,1)S(1)}, bf16[1,2048,64]{1,2,0:T(8,128)(2,1)S(1)}, u32[]{:S(2)}, u32[]{:S(2)}) %collective-permute-start.10) | collective-permute-done | bytes 262176 | tf_op jit(solution)/shard_map/ppermute | solution.py:100
  72.2 5.1 %collective-permute-done.12 = bf16[1,2048,64]{1,2,0:T(8,128)(2,1)S(1)} collective-permute-done((bf16[1,2048,64]{1,2,0:T(8,128)(2,1)S(1)}, bf16[1,2048,64]{1,2,0:T(8,128)(2,1)S(1)}, u32[]{:S(2)}, u32[]{:S(2)}) %collective-permute-start.12) | collective-permute-done | bytes 262176 | tf_op jit(solution)/shard_map/ppermute | solution.py:100
  (69 shorter events, 20.1 us)
Async XLA Ops:
  2.6 11.6 %collective-permute-start.2 = (bf16[128,512]{0,1:T(8,128)(2,1)S(1)}, bf16[128,512]{0,1:T(8,128)(2,1)S(1)}, u32[]{:S(2)}, u32[]{:S(2)}) collective-permute-start(bf16[128,512]{0,1:T(8,128)(2,1)S(1)} %pad_maximum_fusion.2), channel_id=1, source_target_pairs={{0,12},{4,0},{8,4},{12,8},{1,13},{5,1},{9,5},{13,9},{2,14},{6,2},{... | collective-permute-start | bytes 393224 | tf_op jit(solution)/shard_map/ppermute | solution.py:41
  7.7 11.2 %collective-permute-start.1 = (bf16[128,512]{0,1:T(8,128)(2,1)S(1)}, bf16[128,512]{0,1:T(8,128)(2,1)S(1)}, u32[]{:S(2)}, u32[]{:S(2)}) collective-permute-start(bf16[128,512]{0,1:T(8,128)(2,1)S(1)} %pad_maximum_fusion.2), channel_id=1, source_target_pairs={{0,8},{4,12},{8,0},{12,4},{1,9},{5,13},{9,1},{13,5},{2,10},{6,14},... | collective-permute-start | bytes 393224 | tf_op jit(solution)/shard_map/ppermute | solution.py:41
  7.7 11.2 %collective-permute-start = (bf16[128,512]{0,1:T(8,128)(2,1)S(1)}, bf16[128,512]{0,1:T(8,128)(2,1)S(1)}, u32[]{:S(2)}, u32[]{:S(2)}) collective-permute-start(bf16[128,512]{0,1:T(8,128)(2,1)S(1)} %pad_maximum_fusion.2), channel_id=1, source_target_pairs={{0,4},{4,8},{8,12},{12,0},{1,5},{5,9},{9,13},{13,1},{2,6},{6,10},{... | collective-permute-start | bytes 393224 | tf_op jit(solution)/shard_map/ppermute | solution.py:41
  19.0 2.1 %copy-start.4 = (bf16[512,256]{0,1:T(8,128)(2,1)}, bf16[512,256]{0,1:T(8,128)(2,1)S(1)}, u32[]{:S(2)}) copy-start(bf16[512,256]{0,1:T(8,128)(2,1)S(1)} %get-tuple-element.21) | copy-start | bytes 786436
  20.1 2.4 %copy-start = (f32[2,512,128,8]{2,1,3,0:T(8,128)}, f32[2,512,128,8]{2,1,3,0:T(8,128)S(1)}, u32[]{:S(2)}) copy-start(f32[2,512,128,8]{2,1,3,0:T(8,128)S(1)} %get-tuple-element.31) | copy-start | bytes 12582916
  23.4 4.2 %copy-start.1 = (f32[2,512,128,8]{2,1,3,0:T(8,128)S(1)}, f32[2,512,128,8]{2,1,3,0:T(8,128)}, u32[]{:S(2)}) copy-start(f32[2,512,128,8]{2,1,3,0:T(8,128)} %copy-done) | copy-start | bytes 12582916
  40.1 8.9 %collective-permute-start.5 = (bf16[64,512]{1,0:T(8,128)(2,1)}, bf16[64,512]{1,0:T(8,128)(2,1)S(1)}, u32[]{:S(2)}, u32[]{:S(2)}) collective-permute-start(bf16[64,512]{1,0:T(8,128)(2,1)} %get-tuple-element.19), channel_id=1, source_target_pairs={{0,4},{4,8},{8,12},{12,0},{1,5},{5,9},{9,13},{13,1},{2,6},{6,10},{... | collective-permute-start | bytes 196616 | tf_op jit(solution)/shard_map/ppermute | solution.py:54
  40.8 8.2 %collective-permute-start.4 = (bf16[64,512]{1,0:T(8,128)(2,1)}, bf16[64,512]{1,0:T(8,128)(2,1)}, u32[]{:S(2)}, u32[]{:S(2)}) collective-permute-start(bf16[64,512]{1,0:T(8,128)(2,1)} %get-tuple-element.20), channel_id=1, source_target_pairs={{0,8},{4,12},{8,0},{12,4},{1,9},{5,13},{9,1},{13,5},{2,10},{6,14},... | collective-permute-start | bytes 196616 | tf_op jit(solution)/shard_map/ppermute | solution.py:54
  42.7 6.3 %collective-permute-start.3 = (bf16[64,512]{1,0:T(8,128)(2,1)S(1)}, bf16[64,512]{1,0:T(8,128)(2,1)}, u32[]{:S(2)}, u32[]{:S(2)}) collective-permute-start(bf16[64,512]{1,0:T(8,128)(2,1)S(1)} %get-tuple-element.18), channel_id=1, source_target_pairs={{0,12},{4,0},{8,4},{12,8},{1,13},{5,1},{9,5},{13,9},{2,14},{6,2},{... | collective-permute-start | bytes 196616 | tf_op jit(solution)/shard_map/ppermute | solution.py:54
  49.0 7.4 %copy-start.3 = (bf16[8192,256]{1,0:T(8,128)(2,1)S(1)}, bf16[8192,256]{1,0:T(8,128)(2,1)}, u32[]{:S(2)}) copy-start(bf16[8192,256]{1,0:T(8,128)(2,1)} %param.15) | copy-start | bytes 12582916
  50.1 7.1 %copy-start.2 = (bf16[8192,256]{1,0:T(8,128)(2,1)S(1)}, bf16[8192,256]{1,0:T(8,128)(2,1)}, u32[]{:S(2)}) copy-start(bf16[8192,256]{1,0:T(8,128)(2,1)} %param.14) | copy-start | bytes 12582916
  50.1 7.8 %collective-permute-start.8 = (bf16[64,512]{1,0:T(8,128)(2,1)S(1)}, bf16[64,512]{1,0:T(8,128)(2,1)S(1)}, u32[]{:S(2)}, u32[]{:S(2)}) collective-permute-start(bf16[64,512]{1,0:T(8,128)(2,1)S(1)} %get-tuple-element.24), channel_id=1, source_target_pairs={{0,4},{4,8},{8,12},{12,0},{1,5},{5,9},{9,13},{13,1},{2,6},{6,10},{... | collective-permute-start | bytes 196616 | tf_op jit(solution)/shard_map/ppermute | solution.py:54
  51.2 6.8 %collective-permute-start.7 = (bf16[64,512]{1,0:T(8,128)(2,1)S(1)}, bf16[64,512]{1,0:T(8,128)(2,1)S(1)}, u32[]{:S(2)}, u32[]{:S(2)}) collective-permute-start(bf16[64,512]{1,0:T(8,128)(2,1)S(1)} %get-tuple-element.25), channel_id=1, source_target_pairs={{0,8},{4,12},{8,0},{12,4},{1,9},{5,13},{9,1},{13,5},{2,10},{6,14},... | collective-permute-start | bytes 196616 | tf_op jit(solution)/shard_map/ppermute | solution.py:54
  53.4 5.0 %collective-permute-start.6 = (bf16[64,512]{1,0:T(8,128)(2,1)S(1)}, bf16[64,512]{1,0:T(8,128)(2,1)S(1)}, u32[]{:S(2)}, u32[]{:S(2)}) collective-permute-start(bf16[64,512]{1,0:T(8,128)(2,1)S(1)} %get-tuple-element.23), channel_id=1, source_target_pairs={{0,12},{4,0},{8,4},{12,8},{1,13},{5,1},{9,5},{13,9},{2,14},{6,2},{... | collective-permute-start | bytes 196616 | tf_op jit(solution)/shard_map/ppermute | solution.py:54
  57.1 5.0 %collective-permute-start.9 = (f32[2,2048,64]{1,2,0:T(8,128)S(1)}, f32[2,2048,64]{1,2,0:T(8,128)S(1)}, u32[]{:S(2)}, u32[]{:S(2)}) collective-permute-start(f32[2,2048,64]{1,2,0:T(8,128)S(1)} %convolution_add_fusion.2), channel_id=1, source_target_pairs={{0,1},{1,0},{2,3},{3,2},{4,5},{5,4},{6,7},{7,6},{8,9},{9,8},{10,11... | collective-permute-start | bytes 3145736 | tf_op jit(solution)/shard_map/ppermute | solution.py:94
  59.9 4.6 %collective-permute-start.11 = (f32[2,2048,64]{1,2,0:T(8,128)S(1)}, f32[2,2048,64]{1,2,0:T(8,128)S(1)}, u32[]{:S(2)}, u32[]{:S(2)}) collective-permute-start(f32[2,2048,64]{1,2,0:T(8,128)S(1)} %convolution_add_fusion), channel_id=1, source_target_pairs={{0,1},{1,0},{2,3},{3,2},{4,5},{5,4},{6,7},{7,6},{8,9},{9,8},{10,11... | collective-permute-start | bytes 3145736 | tf_op jit(solution)/shard_map/ppermute | solution.py:94
  62.9 9.2 %collective-permute-start.10 = (bf16[1,2048,64]{1,2,0:T(8,128)(2,1)S(1)}, bf16[1,2048,64]{1,2,0:T(8,128)(2,1)S(1)}, u32[]{:S(2)}, u32[]{:S(2)}) collective-permute-start(bf16[1,2048,64]{1,2,0:T(8,128)(2,1)S(1)} %dynamic-slice_convert_fusion.1), channel_id=1, source_target_pairs={{0,2},{1,3},{2,0},{3,1},{4,6},{5,7},{6,4},{7,5},{8,10},{9,11},{10,... | collective-permute-start | bytes 786440 | tf_op jit(solution)/shard_map/ppermute | solution.py:100
  65.3 12.0 %collective-permute-start.12 = (bf16[1,2048,64]{1,2,0:T(8,128)(2,1)S(1)}, bf16[1,2048,64]{1,2,0:T(8,128)(2,1)S(1)}, u32[]{:S(2)}, u32[]{:S(2)}) collective-permute-start(bf16[1,2048,64]{1,2,0:T(8,128)(2,1)S(1)} %dynamic-slice_convert_fusion), channel_id=1, source_target_pairs={{0,2},{1,3},{2,0},{3,1},{4,6},{5,7},{6,4},{7,5},{8,10},{9,11},{10,... | collective-permute-start | bytes 786440 | tf_op jit(solution)/shard_map/ppermute | solution.py:100

commit v5 on v3

--- a/solution.py
+++ b/solution.py
@@ -3,6 +3,7 @@
 import jax
 import jax.numpy as jnp
 from jax import lax
+from jax.experimental import pallas as pl
 from jax.sharding import PartitionSpec as P
 
 HD = 128
@@ -102,6 +103,68 @@
         )
         current = kept + arrived.astype(jnp.float32)
     return current.reshape(block, -1).astype(jnp.bfloat16)
+
+
+def attention_kernel(query_ref, grad_ref, kv_ref, mask_ref, query_out, kv_out):
+    inv_root = HD ** (-0.5)
+    kv_cols = kv_ref.shape[1] // 2
+    kv_heads = kv_cols // HD
+    group_size = query_ref.shape[1] // kv_cols
+    allowed = mask_ref[...] > 0
+    across = (((1,), (1,)), ((), ()))
+    for kv_head in range(kv_heads):
+        key_head = kv_ref[:, kv_head * HD : (kv_head + 1) * HD]
+        value_head = kv_ref[:, kv_cols + kv_head * HD : kv_cols + (kv_head + 1) * HD]
+        key_sum = jnp.zeros(key_head.shape, jnp.float32)
+        value_sum = jnp.zeros(value_head.shape, jnp.float32)
+        for member in range(group_size):
+            first = (kv_head * group_size + member) * HD
+            query_head = query_ref[:, first : first + HD]
+            grad_head = grad_ref[:, first : first + HD]
+            scores = (
+                lax.dot_general(query_head, key_head, across, preferred_element_type=jnp.float32)
+                * inv_root
+            )
+            scores = jnp.where(allowed, scores, masked_score)
+            row_max = jnp.max(scores, axis=1, keepdims=True)
+            shifted = jnp.exp(scores - row_max)
+            row_sum = jnp.sum(shifted, axis=1, keepdims=True)
+            weighted = jnp.dot(
+                shifted.astype(jnp.bfloat16), value_head, preferred_element_type=jnp.float32
+            )
+            attended = (weighted / row_sum).astype(jnp.bfloat16)
+            probs = jnp.exp(scores - (row_max + jnp.log(row_sum)))
+            row_delta = jnp.sum(
+                grad_head.astype(jnp.float32) * attended.astype(jnp.float32), axis=1, keepdims=True
+            )
+            dprobs = lax.dot_general(
+                grad_head, value_head, across, preferred_element_type=jnp.float32
+            )
+            dscores = probs * (dprobs - row_delta)
+            query_term = (
+                jnp.dot(dscores.astype(jnp.bfloat16), key_head, preferred_element_type=jnp.float32)
+                * inv_root
+            )
+            query_out[:, first : first + HD] = query_term.astype(jnp.bfloat16)
+            key_sum = key_sum + jnp.dot(
+                dscores.T.astype(jnp.bfloat16), query_head, preferred_element_type=jnp.float32
+            )
+            value_sum = value_sum + jnp.dot(
+                probs.T.astype(jnp.bfloat16), grad_head, preferred_element_type=jnp.float32
+            )
+        kv_out[:, kv_head * HD : (kv_head + 1) * HD] = key_sum * inv_root
+        kv_out[:, kv_cols + kv_head * HD : kv_cols + (kv_head + 1) * HD] = value_sum
+
+
+def attention_block(queries, out_grad, kv_rows, allowed, interpret=False):
+    return pl.pallas_call(
+        attention_kernel,
+        out_shape=(
+            jax.ShapeDtypeStruct(queries.shape, jnp.bfloat16),
+            jax.ShapeDtypeStruct(kv_rows.shape, jnp.float32),
+        ),
+        interpret=interpret,
+    )(queries, out_grad, kv_rows, allowed.astype(jnp.int32))
 
 
 def local(
@@ -188,36 +251,23 @@
         )
         return query_term, kv_term
 
-    start_stats = (
-        jnp.full((kv_heads, group_size, rows_here), masked_score, jnp.float32),
-        jnp.zeros((kv_heads, group_size, rows_here), jnp.float32),
-        jnp.zeros((kv_heads, group_size, rows_here, HD), jnp.float32),
-    )
     if steps == 1:
-        key_heads, value_heads, allowed, scores = chunk(0)
-        row_max = jnp.max(scores, axis=-1)
-        shifted = jnp.exp(scores - row_max[..., None])
-        row_sum = jnp.sum(shifted, axis=-1)
-        weighted = jnp.einsum(
-            "kgqt,tkd->kgqd",
-            shifted.astype(jnp.bfloat16),
-            value_heads,
-            preferred_element_type=jnp.float32,
-        )
+        allowed = chunk(0)[2]
+        query_grad, kv_acc = attention_block(queries, out_grad, kv_rows, allowed)
     else:
+        start_stats = (
+            jnp.full((kv_heads, group_size, rows_here), masked_score, jnp.float32),
+            jnp.zeros((kv_heads, group_size, rows_here), jnp.float32),
+            jnp.zeros((kv_heads, group_size, rows_here, HD), jnp.float32),
+        )
         row_max, row_sum, weighted = lax.fori_loop(
             0, steps, lambda i, c: forward_stats(i * step_rows, c), start_stats
         )
-        scores = None
-    log_total = row_max + jnp.log(row_sum)
-    attended = (weighted / row_sum[..., None]).astype(jnp.bfloat16)
-    row_delta = jnp.einsum(
-        "kgqd,qkgd->kgq", attended, grad_heads, preferred_element_type=jnp.float32
-    )
-
-    if steps == 1:
-        query_acc, kv_acc = backward_chunk(0, log_total, row_delta, scores)
-    else:
+        log_total = row_max + jnp.log(row_sum)
+        attended = (weighted / row_sum[..., None]).astype(jnp.bfloat16)
+        row_delta = jnp.einsum(
+            "kgqd,qkgd->kgq", attended, grad_heads, preferred_element_type=jnp.float32
+        )
 
         def backward_visit(turn_index, current):
             query_now, kv_now = current
@@ -235,9 +285,9 @@
                 jnp.zeros((row_count, 2 * kv_cols), jnp.float32),
             ),
         )
+        query_grad = query_acc.reshape(rows_here, -1).astype(jnp.bfloat16)
 
     kv_grad = scatter_slots(kv_acc, "ctx")
-    query_grad = query_acc.reshape(rows_here, -1).astype(jnp.bfloat16)
     key_grad = kv_grad[:, :kv_cols].astype(jnp.bfloat16)
     value_grad = kv_grad[:, kv_cols:].astype(jnp.bfloat16)
     input_grad_t = head_reduce(key_proj, value_proj, key_grad, value_grad)

time: 76.1 us -> 73.4 us (0.965)
  Pallas kernels: 0 us -> 12.8 us
  matrix products: 18.7 us -> 7.92 us
  local copies, waits for them, and re-layouts: 11.6 us -> 4.25 us
  waiting for transfers between devices: 24.4 us -> 28 us
  other arithmetic: 6.84 us -> 5.87 us
    pallas_call x0 -> x1, Pallas kernels: none -> 12.8 us  [attention_block(): pl.pallas_call(attention_kernel, out_shape=(jax.ShapeDtypeStruct(queries....]
    dot_general x6 -> x0, matrix products: 9.49 us -> none  [the longest x1 4.37 us: backward_chunk(): jnp.einsum('kgqt,qkgd->tkd', probs_low, grad_heads, preferred_element_typ...]
    unnamed x22 -> x9, local copies, waits for them, and re-layouts: 5.44 us -> 1.28 us
    reshape x4 -> x0, local copies, waits for them, and re-layouts: 3.22 us -> none  [the longest x1 1.31 us: local(): query_heads = queries.reshape(rows_here, kv_heads, group_size, HD)]
    ppermute x3, waiting for transfers between devices: 4.08 us -> 7.03 us  [gather_slots(): lax.ppermute(block, axis, shifted_pairs(count, steps))]
    dot_general x2, matrix products: 4.4 us -> 3.05 us  [project(): jnp.einsum('arf,tf->art', lax.dynamic_index_in_dim(value_split, half, 1,...]
    ppermute x1, waiting for transfers between devices: 11.2 us -> 12.5 us  [head_reduce(): lax.ppermute(sent.astype(jnp.bfloat16), 'head', [(i, i ^ 1 << level) for...]
    convert_element_type x1, other arithmetic: 2.12 us -> 0.9 us  [head_reduce(): return current.reshape(block, -1).astype(jnp.bfloat16)]
  transfers between devices with their start and end apart: 8 -> 8, of which waited for: 5 -> 5; matrix products, arithmetic and copies ran while one was open for 13% -> 8% of each run, Pallas kernels for 0% -> 0%
where the time goes in v5:
time: 73.4 us; the launch traced here: 73 us
  waiting for transfers between devices  28 us (38%)
  starting transfers between devices  13.3 us (18%)
  Pallas kernels  12.8 us (17%)
  matrix products  7.92 us (11%)
  other arithmetic  5.87 us (8%)
  local copies, waits for them, and re-layouts  4.25 us (6%)
  between operations  0.8 us (1%)
    pallas_call x1, Pallas kernels, attention_block(): pl.pallas_call(attention_kernel, out_shape=(jax.ShapeDtypeStruct(queries....  12.8 us
    ppermute x1, waiting for transfers between devices, head_reduce(): lax.ppermute(sent.astype(jnp.bfloat16), 'head', [(i, i ^ 1 << level) for...  12.5 us
    ppermute x3, waiting for transfers between devices, gather_slots(): lax.ppermute(block, axis, shifted_pairs(count, steps))  7.03 us
    ppermute x3, waiting for transfers between devices, scatter_slots(): lax.ppermute(slots[steps * rows:(steps + 1) * rows].astype(jnp.bfloat16),...  6.78 us
    ppermute x3, starting transfers between devices, gather_slots(): lax.ppermute(block, axis, shifted_pairs(count, steps))  6.06 us
    ppermute x3, starting transfers between devices, scatter_slots(): lax.ppermute(slots[steps * rows:(steps + 1) * rows].astype(jnp.bfloat16),...  5.59 us
    dot_general x2, matrix products, project(): jnp.einsum('arf,tf->art', lax.dynamic_index_in_dim(key_split, half, 1, ke...  4.88 us
    dot_general x2, matrix products, project(): jnp.einsum('arf,tf->art', lax.dynamic_index_in_dim(value_split, half, 1,...  3.05 us
  transfers between devices with their start and end apart: 8, of which 5 were waited for; matrix products, arithmetic and copies ran while one was open for 8% of the time, Pallas kernels for 0%

profile of v5, /device:TPU:0, one launch (start us, length us, event | category | flops | bytes accessed | tf_op | source)
XLA Modules:
  0.0 73.0 jit_solution(18173410916963272917)
XLA Ops:
  0.6 0.8 %constant_dynamic-update-slice_fusion.1 = bf16[128,512]{1,0:T(8,128)(2,1)S(1)} fusion(bf16[128,256]{1,0:T(8,128)(2,1)} %param.9), kind=kLoop, calls=%fused_computation.23 | loop fusion | bytes 131072
  1.5 0.8 %constant_dynamic-update-slice_fusion = bf16[128,512]{1,0:T(8,128)(2,1)S(1)} fusion(bf16[128,512]{1,0:T(8,128)(2,1)S(1)} %constant_dynamic-update-slice_fusion.1, bf16[128,256]{1,0:T(8,128)(2,1)} %param.10), kind=kLoop, calls=%fused_computation.22 | loop fusion | bytes 131072 | tf_op jit(solution)/shard_map/concatenate | solution.py:187
  2.3 5.0 %collective-permute-start.2 = (bf16[128,512]{1,0:T(8,128)(2,1)S(1)}, bf16[128,512]{1,0:T(8,128)(2,1)S(1)}, u32[]{:S(2)}, u32[]{:S(2)}) collective-permute-start(bf16[128,512]{1,0:T(8,128)(2,1)S(1)} %constant_dynamic-update-slice_fusion), channel_id=1, source_target_pairs={{0,12},{4,0},{8,4},{12,8},{1,13},{5,1},{9,5},{13,9},{2,14},{6,2},{... | collective-permute-start | bytes 393224 | tf_op jit(solution)/shard_map/ppermute | solution.py:42
  7.4 1.0 %collective-permute-start = (bf16[128,512]{1,0:T(8,128)(2,1)S(1)}, bf16[128,512]{1,0:T(8,128)(2,1)S(1)}, u32[]{:S(2)}, u32[]{:S(2)}) collective-permute-start(bf16[128,512]{1,0:T(8,128)(2,1)S(1)} %constant_dynamic-update-slice_fusion), channel_id=1, source_target_pairs={{0,4},{4,8},{8,12},{12,0},{1,5},{5,9},{9,13},{13,1},{2,6},{6,10},{... | collective-permute-start | bytes 393224 | tf_op jit(solution)/shard_map/ppermute | solution.py:42
  8.4 1.2 %dynamic_slice.19 = s32[1]{0:T(128)} dynamic-slice(s32[4]{0:T(128)} %param.13, s32[]{:T(128)S(6)} %select_n.53), dynamic_slice_sizes={1} | dynamic-slice | bytes 12 | tf_op jit(solution)/shard_map/dynamic_slice | solution.py:181
  10.4 0.9 %multiply_reduce_fusion = (s32[4]{0:T(128)S(1)}, s32[4]{0:T(128)S(1)}) fusion(s32[4,4]{1,0:T(4,128)} %param.12, s32[4]{0:T(128)S(1)} %compare_convert_fusion.1, s32[4]{0:T(128)} %param.13, s32[4]{0:T(128)S(1)} %select_reduce_fusion.2), kind=kLoop, calls=%fused_computation.27 | loop fusion | flops 72 | bytes 144 | tf_op jit(solution)/shard_map/reduce_sum | solution.py:18
  11.5 7.0 %collective-permute-done.1 = bf16[128,512]{1,0:T(8,128)(2,1)S(1)} collective-permute-done((bf16[128,512]{1,0:T(8,128)(2,1)S(1)}, bf16[128,512]{1,0:T(8,128)(2,1)S(1)}, u32[]{:S(2)}, u32[]{:S(2)}) %collective-permute-start.1) | collective-permute-done | bytes 131104 | tf_op jit(solution)/shard_map/ppermute | solution.py:42
  18.6 0.8 %pad_maximum_fusion.kv_ref = bf16[512,512]{1,0:T(8,128)(2,1)} fusion(bf16[128,512]{1,0:T(8,128)(2,1)S(1)} %collective-permute-done.2, bf16[128,512]{1,0:T(8,128)(2,1)S(1)} %collective-permute-done.1, bf16[128,512]{1,0:T(8,128)(2,1)S(1)} %collective-permute-done, bf16[128,512]{1,0:T(8,128)(2,1)S(1)} %constant_dynamic-update-slice_fusion), kind=kLoop, calls=%fused_computation.16 | loop fusion | flops 2097152 | bytes 1048576 | tf_op jit(solution)/shard_map/concatenate | solution.py:45
  19.4 0.7 broadcast_in_dim.5.mask_ref
  20.1 12.8 %shard_map.111 = (bf16[128,2048]{1,0:T(8,128)(2,1)}, f32[512,512]{1,0:T(8,128)}) custom-call(bf16[128,2048]{1,0:T(8,128)(2,1)} %query_ref.1, bf16[128,2048]{1,0:T(8,128)(2,1)} %grad_ref.1, bf16[512,512]{1,0:T(8,128)(2,1)} %pad_maximum_fusion.kv_ref, s32[128,512]{1,0:T(8,128)} %broadcast_in_dim.5.mask_ref), custom_call_target="tpu_custom_call" | custom-call | tf_op jit(solution)/shard_map/pallas_call | solution.py:160
  33.0 1.3 %convert.9 = bf16[512,512]{1,0:T(8,128)(2,1)S(1)} convert(f32[512,512]{1,0:T(8,128)} %get-tuple-element.7) | non-fusion elementwise | flops 262144 | bytes 1572864 | tf_op jit(solution)/shard_map/convert.4
  34.3 0.8 %collective-permute-start.5 = (bf16[128,512]{1,0:T(8,128)(2,1)S(1)}, bf16[128,512]{1,0:T(8,128)(2,1)S(1)}, u32[]{:S(2)}, u32[]{:S(2)}) collective-permute-start(bf16[128,512]{1,0:T(8,128)(2,1)S(1)} %get-tuple-element.9), channel_id=1, source_target_pairs={{0,4},{4,8},{8,12},{12,0},{1,5},{5,9},{9,13},{13,1},{2,6},{6,10},{... | collective-permute-start | bytes 393224 | tf_op jit(solution)/shard_map/ppermute | solution.py:55
  35.0 2.0 %collective-permute-start.4 = (bf16[128,512]{1,0:T(8,128)(2,1)S(1)}, bf16[128,512]{1,0:T(8,128)(2,1)S(1)}, u32[]{:S(2)}, u32[]{:S(2)}) collective-permute-start(bf16[128,512]{1,0:T(8,128)(2,1)S(1)} %get-tuple-element.10), channel_id=1, source_target_pairs={{0,8},{4,12},{8,0},{12,4},{1,9},{5,13},{9,1},{13,5},{2,10},{6,14},... | collective-permute-start | bytes 393224 | tf_op jit(solution)/shard_map/ppermute | solution.py:55
  37.0 2.8 %collective-permute-start.3 = (bf16[128,512]{1,0:T(8,128)(2,1)S(1)}, bf16[128,512]{1,0:T(8,128)(2,1)S(1)}, u32[]{:S(2)}, u32[]{:S(2)}) collective-permute-start(bf16[128,512]{1,0:T(8,128)(2,1)S(1)} %get-tuple-element.8), channel_id=1, source_target_pairs={{0,12},{4,0},{8,4},{12,8},{1,13},{5,1},{9,5},{13,9},{2,14},{6,2},{... | collective-permute-start | bytes 393224 | tf_op jit(solution)/shard_map/ppermute | solution.py:55
  39.9 2.7 %collective-permute-done.5 = bf16[128,512]{1,0:T(8,128)(2,1)S(1)} collective-permute-done((bf16[128,512]{1,0:T(8,128)(2,1)S(1)}, bf16[128,512]{1,0:T(8,128)(2,1)S(1)}, u32[]{:S(2)}, u32[]{:S(2)}) %collective-permute-start.5) | collective-permute-done | bytes 131104 | tf_op jit(solution)/shard_map/ppermute | solution.py:55
  42.6 4.0 %collective-permute-done.4 = bf16[128,512]{1,0:T(8,128)(2,1)S(1)} collective-permute-done((bf16[128,512]{1,0:T(8,128)(2,1)S(1)}, bf16[128,512]{1,0:T(8,128)(2,1)S(1)}, u32[]{:S(2)}, u32[]{:S(2)}) %collective-permute-start.4) | collective-permute-done | bytes 131104 | tf_op jit(solution)/shard_map/ppermute | solution.py:55
  46.7 1.0 %add_convert_fusion.1 = bf16[128,512]{1,0:T(8,128)(2,1)S(1)} fusion(bf16[128,512]{1,0:T(8,128)(2,1)S(1)} %collective-permute-done.5, bf16[128,512]{1,0:T(8,128)(2,1)S(1)} %collective-permute-done.4, bf16[128,512]{1,0:T(8,128)(2,1)S(1)} %collective-permute-done.3, f32[512,512]{1,0:T(8,128)} %get-tuple-element.7), kind=kLoop, calls=%fused_computation.17 | loop fusion | flops 458752 | bytes 786432 | tf_op jit(solution)/shard_map/convert.1
  47.7 2.4 %fusion.2 = f32[2,2048,128]{2,1,0:T(8,128)S(1)} fusion(bf16[2,2,2048,256]{3,2,1,0:T(8,128)(2,1)} %bitcast.37, s32[]{:T(128)S(6)} %select_n.56, bf16[128,256]{1,0:T(8,128)(2,1)S(1)} %get-tuple-element.12), kind=kOutput, calls=%fused_computation.4 | convolution fusion | flops 268435456 | bytes 4259844 | tf_op jit(solution)/shard_map/arf,tf->art/dot_general | solution.py:80
  51.4 2.4 %fusion.5 = f32[2,2048,128]{2,1,0:T(8,128)S(1)} fusion(bf16[2,2,2048,256]{3,2,1,0:T(8,128)(2,1)} %bitcast.38, s32[]{:T(128)S(6)} %select_n.55, bf16[128,256]{1,0:T(8,128)(2,1)S(1)} %get-tuple-element.12), kind=kOutput, calls=%fused_computation.7 | convolution fusion | flops 268435456 | bytes 4259844 | tf_op jit(solution)/shard_map/arf,tf->art/dot_general | solution.py:80
  53.9 1.8 %collective-permute-done.6 = f32[2,2048,128]{2,1,0:T(8,128)} collective-permute-done((f32[2,2048,128]{2,1,0:T(8,128)S(1)}, f32[2,2048,128]{2,1,0:T(8,128)}, u32[]{:S(2)}, u32[]{:S(2)}) %collective-permute-start.6) | collective-permute-done | bytes 2097184 | tf_op jit(solution)/shard_map/ppermute | solution.py:95
  55.7 2.3 %fusion = f32[2,2048,128]{2,1,0:T(8,128)S(1)} fusion(f32[2,2048,128]{2,1,0:T(8,128)} %collective-permute-done.6, f32[2,2048,128]{2,1,0:T(8,128)S(1)} %fusion.5, bf16[2,2,2048,256]{3,2,1,0:T(8,128)(2,1)S(1)} %bitcast.40, s32[]{:T(128)S(6)} %select_n.55, bf16[128,256]{1,0:T(8,128)(2,1)S(1)} %get-tuple-element.11), kind=kOutput, calls=%fused_computation.2 | convolution fusion | flops 269484032 | bytes 8454148 | tf_op jit(solution)/shard_map/arf,tf->art/dot_general | solution.py:85
  58.1 1.6 %collective-permute-start.7 = (bf16[1,2048,128]{2,1,0:T(8,128)(2,1)S(1)}, bf16[1,2048,128]{2,1,0:T(8,128)(2,1)S(1)}, u32[]{:S(2)}, u32[]{:S(2)}) collective-permute-start(bf16[1,2048,128]{2,1,0:T(8,128)(2,1)S(1)} %dynamic-slice_convert_fusion), channel_id=1, source_target_pairs={{0,2},{1,3},{2,0},{3,1},{4,6},{5,7},{6,4},{7,5},{8,10},{9,11},{10,... | collective-permute-start | bytes 1572872 | tf_op jit(solution)/shard_map/ppermute | solution.py:101
  59.6 12.5 %collective-permute-done.7 = bf16[1,2048,128]{2,1,0:T(8,128)(2,1)S(1)} collective-permute-done((bf16[1,2048,128]{2,1,0:T(8,128)(2,1)S(1)}, bf16[1,2048,128]{2,1,0:T(8,128)(2,1)S(1)}, u32[]{:S(2)}, u32[]{:S(2)}) %collective-permute-start.7) | collective-permute-done | bytes 524320 | tf_op jit(solution)/shard_map/ppermute | solution.py:101
  72.1 0.9 %fusion.11 = bf16[2048,128]{1,0:T(8,128)(2,1)} fusion(bf16[1,2048,128]{2,1,0:T(8,128)(2,1)S(1)} %collective-permute-done.7, f32[2,2048,128]{2,1,0:T(8,128)S(1)} %fusion, s32[]{:T(128)S(6)} %select_n.59), kind=kLoop, calls=%fused_computation.15 | loop fusion | flops 786432 | bytes 2097156 | tf_op jit(solution)/shard_map/convert_element_type | solution.py:105
  (23 shorter events, 2.4 us)
Async XLA Ops:
  2.3 9.2 %collective-permute-start.2 = (bf16[128,512]{1,0:T(8,128)(2,1)S(1)}, bf16[128,512]{1,0:T(8,128)(2,1)S(1)}, u32[]{:S(2)}, u32[]{:S(2)}) collective-permute-start(bf16[128,512]{1,0:T(8,128)(2,1)S(1)} %constant_dynamic-update-slice_fusion), channel_id=1, source_target_pairs={{0,12},{4,0},{8,4},{12,8},{1,13},{5,1},{9,5},{13,9},{2,14},{6,2},{... | collective-permute-start | bytes 393224 | tf_op jit(solution)/shard_map/ppermute | solution.py:42
  7.4 11.2 %collective-permute-start.1 = (bf16[128,512]{1,0:T(8,128)(2,1)S(1)}, bf16[128,512]{1,0:T(8,128)(2,1)S(1)}, u32[]{:S(2)}, u32[]{:S(2)}) collective-permute-start(bf16[128,512]{1,0:T(8,128)(2,1)S(1)} %constant_dynamic-update-slice_fusion), channel_id=1, source_target_pairs={{0,8},{4,12},{8,0},{12,4},{1,9},{5,13},{9,1},{13,5},{2,10},{6,14},... | collective-permute-start | bytes 393224 | tf_op jit(solution)/shard_map/ppermute | solution.py:42
  7.4 11.2 %collective-permute-start = (bf16[128,512]{1,0:T(8,128)(2,1)S(1)}, bf16[128,512]{1,0:T(8,128)(2,1)S(1)}, u32[]{:S(2)}, u32[]{:S(2)}) collective-permute-start(bf16[128,512]{1,0:T(8,128)(2,1)S(1)} %constant_dynamic-update-slice_fusion), channel_id=1, source_target_pairs={{0,4},{4,8},{8,12},{12,0},{1,5},{5,9},{9,13},{13,1},{2,6},{6,10},{... | collective-permute-start | bytes 393224 | tf_op jit(solution)/shard_map/ppermute | solution.py:42
  34.3 8.3 %collective-permute-start.5 = (bf16[128,512]{1,0:T(8,128)(2,1)S(1)}, bf16[128,512]{1,0:T(8,128)(2,1)S(1)}, u32[]{:S(2)}, u32[]{:S(2)}) collective-permute-start(bf16[128,512]{1,0:T(8,128)(2,1)S(1)} %get-tuple-element.9), channel_id=1, source_target_pairs={{0,4},{4,8},{8,12},{12,0},{1,5},{5,9},{9,13},{13,1},{2,6},{6,10},{... | collective-permute-start | bytes 393224 | tf_op jit(solution)/shard_map/ppermute | solution.py:55
  35.0 11.6 %collective-permute-start.4 = (bf16[128,512]{1,0:T(8,128)(2,1)S(1)}, bf16[128,512]{1,0:T(8,128)(2,1)S(1)}, u32[]{:S(2)}, u32[]{:S(2)}) collective-permute-start(bf16[128,512]{1,0:T(8,128)(2,1)S(1)} %get-tuple-element.10), channel_id=1, source_target_pairs={{0,8},{4,12},{8,0},{12,4},{1,9},{5,13},{9,1},{13,5},{2,10},{6,14},... | collective-permute-start | bytes 393224 | tf_op jit(solution)/shard_map/ppermute | solution.py:55
  37.0 9.6 %collective-permute-start.3 = (bf16[128,512]{1,0:T(8,128)(2,1)S(1)}, bf16[128,512]{1,0:T(8,128)(2,1)S(1)}, u32[]{:S(2)}, u32[]{:S(2)}) collective-permute-start(bf16[128,512]{1,0:T(8,128)(2,1)S(1)} %get-tuple-element.8), channel_id=1, source_target_pairs={{0,12},{4,0},{8,4},{12,8},{1,13},{5,1},{9,5},{13,9},{2,14},{6,2},{... | collective-permute-start | bytes 393224 | tf_op jit(solution)/shard_map/ppermute | solution.py:55
  47.7 3.7 %copy-start.3 = (bf16[128,256]{1,0:T(8,128)(2,1)}, bf16[128,256]{1,0:T(8,128)(2,1)S(1)}, u32[]{:S(2)}) copy-start(bf16[128,256]{1,0:T(8,128)(2,1)S(1)} %get-tuple-element.12) | copy-start | bytes 196612
  47.7 7.9 %copy-start.2 = (bf16[128,256]{1,0:T(8,128)(2,1)}, bf16[128,256]{1,0:T(8,128)(2,1)S(1)}, u32[]{:S(2)}) copy-start(bf16[128,256]{1,0:T(8,128)(2,1)S(1)} %get-tuple-element.11) | copy-start | bytes 196612
  47.7 2.9 %copy-start = (bf16[8192,256]{1,0:T(8,128)(2,1)S(1)}, bf16[8192,256]{1,0:T(8,128)(2,1)}, u32[]{:S(2)}) copy-start(bf16[8192,256]{1,0:T(8,128)(2,1)} %param.15) | copy-start | bytes 12582916
  51.3 4.4 %collective-permute-start.6 = (f32[2,2048,128]{2,1,0:T(8,128)S(1)}, f32[2,2048,128]{2,1,0:T(8,128)}, u32[]{:S(2)}, u32[]{:S(2)}) collective-permute-start(f32[2,2048,128]{2,1,0:T(8,128)S(1)} %convolution_add_fusion), channel_id=1, source_target_pairs={{0,1},{1,0},{2,3},{3,2},{4,5},{5,4},{6,7},{7,6},{8,9},{9,8},{10,11... | collective-permute-start | bytes 6291464 | tf_op jit(solution)/shard_map/ppermute | solution.py:95
  51.4 4.2 %copy-start.1 = (bf16[8192,256]{1,0:T(8,128)(2,1)S(1)}, bf16[8192,256]{1,0:T(8,128)(2,1)}, u32[]{:S(2)}) copy-start(bf16[8192,256]{1,0:T(8,128)(2,1)} %param.15) | copy-start | bytes 12582916
  58.1 14.0 %collective-permute-start.7 = (bf16[1,2048,128]{2,1,0:T(8,128)(2,1)S(1)}, bf16[1,2048,128]{2,1,0:T(8,128)(2,1)S(1)}, u32[]{:S(2)}, u32[]{:S(2)}) collective-permute-start(bf16[1,2048,128]{2,1,0:T(8,128)(2,1)S(1)} %dynamic-slice_convert_fusion), channel_id=1, source_target_pairs={{0,2},{1,3},{2,0},{3,1},{4,6},{5,7},{6,4},{7,5},{8,10},{9,11},{10,... | collective-permute-start | bytes 1572872 | tf_op jit(solution)/shard_map/ppermute | solution.py:101

commit v6 on v5

--- a/solution.py
+++ b/solution.py
@@ -112,6 +112,7 @@
     group_size = query_ref.shape[1] // kv_cols
     allowed = mask_ref[...] > 0
     across = (((1,), (1,)), ((), ()))
+    down = (((0,), (0,)), ((), ()))
     for kv_head in range(kv_heads):
         key_head = kv_ref[:, kv_head * HD : (kv_head + 1) * HD]
         value_head = kv_ref[:, kv_cols + kv_head * HD : kv_cols + (kv_head + 1) * HD]
@@ -133,7 +134,7 @@
                 shifted.astype(jnp.bfloat16), value_head, preferred_element_type=jnp.float32
             )
             attended = (weighted / row_sum).astype(jnp.bfloat16)
-            probs = jnp.exp(scores - (row_max + jnp.log(row_sum)))
+            probs = shifted * (1.0 / row_sum)
             row_delta = jnp.sum(
                 grad_head.astype(jnp.float32) * attended.astype(jnp.float32), axis=1, keepdims=True
             )
@@ -146,11 +147,11 @@
                 * inv_root
             )
             query_out[:, first : first + HD] = query_term.astype(jnp.bfloat16)
-            key_sum = key_sum + jnp.dot(
-                dscores.T.astype(jnp.bfloat16), query_head, preferred_element_type=jnp.float32
-            )
-            value_sum = value_sum + jnp.dot(
-                probs.T.astype(jnp.bfloat16), grad_head, preferred_element_type=jnp.float32
+            key_sum = key_sum + lax.dot_general(
+                dscores.astype(jnp.bfloat16), query_head, down, preferred_element_type=jnp.float32
+            )
+            value_sum = value_sum + lax.dot_general(
+                probs.astype(jnp.bfloat16), grad_head, down, preferred_element_type=jnp.float32
             )
         kv_out[:, kv_head * HD : (kv_head + 1) * HD] = key_sum * inv_root
         kv_out[:, kv_cols + kv_head * HD : kv_cols + (kv_head + 1) * HD] = value_sum

time: 73.4 us -> 72.6 us (0.989)
  Pallas kernels: 12.8 us -> 12 us
    pallas_call x1, Pallas kernels: 12.8 us -> 12 us  [attention_block(): pl.pallas_call(attention_kernel, out_shape=(jax.ShapeDtypeStruct(queries....]
where the time goes in v6:
time: 72.6 us; the launch traced here: 72.2 us
  waiting for transfers between devices  28.1 us (39%)
  starting transfers between devices  13.3 us (18%)
  Pallas kernels  12 us (17%)
  matrix products  7.91 us (11%)
  other arithmetic  5.87 us (8%)
  local copies, waits for them, and re-layouts  4.25 us (6%)
  between operations  0.8 us (1%)
    ppermute x1, waiting for transfers between devices, head_reduce(): lax.ppermute(sent.astype(jnp.bfloat16), 'head', [(i, i ^ 1 << level) for...  12.5 us
    pallas_call x1, Pallas kernels, attention_block(): pl.pallas_call(attention_kernel, out_shape=(jax.ShapeDtypeStruct(queries....  12 us
    ppermute x3, waiting for transfers between devices, gather_slots(): lax.ppermute(block, axis, shifted_pairs(count, steps))  7.03 us
    ppermute x3, waiting for transfers between devices, scatter_slots(): lax.ppermute(slots[steps * rows:(steps + 1) * rows].astype(jnp.bfloat16),...  6.79 us
    ppermute x3, starting transfers between devices, gather_slots(): lax.ppermute(block, axis, shifted_pairs(count, steps))  6.06 us
    ppermute x3, starting transfers between devices, scatter_slots(): lax.ppermute(slots[steps * rows:(steps + 1) * rows].astype(jnp.bfloat16),...  5.61 us
    dot_general x2, matrix products, project(): jnp.einsum('arf,tf->art', lax.dynamic_index_in_dim(key_split, half, 1, ke...  4.88 us
    dot_general x2, matrix products, project(): jnp.einsum('arf,tf->art', lax.dynamic_index_in_dim(value_split, half, 1,...  3.03 us
  transfers between devices with their start and end apart: 8, of which 5 were waited for; matrix products, arithmetic and copies ran while one was open for 8% of the time, Pallas kernels for 0%

profile of v6, /device:TPU:0, one launch (start us, length us, event | category | flops | bytes accessed | tf_op | source)
XLA Modules:
  0.0 72.2 jit_solution(14562183278976474915)
XLA Ops:
  0.6 0.8 %constant_dynamic-update-slice_fusion.1 = bf16[128,512]{1,0:T(8,128)(2,1)S(1)} fusion(bf16[128,256]{1,0:T(8,128)(2,1)} %param.9), kind=kLoop, calls=%fused_computation.23 | loop fusion | bytes 131072
  1.5 0.8 %constant_dynamic-update-slice_fusion = bf16[128,512]{1,0:T(8,128)(2,1)S(1)} fusion(bf16[128,512]{1,0:T(8,128)(2,1)S(1)} %constant_dynamic-update-slice_fusion.1, bf16[128,256]{1,0:T(8,128)(2,1)} %param.10), kind=kLoop, calls=%fused_computation.22 | loop fusion | bytes 131072 | tf_op jit(solution)/shard_map/concatenate | solution.py:188
  2.3 5.0 %collective-permute-start.2 = (bf16[128,512]{1,0:T(8,128)(2,1)S(1)}, bf16[128,512]{1,0:T(8,128)(2,1)S(1)}, u32[]{:S(2)}, u32[]{:S(2)}) collective-permute-start(bf16[128,512]{1,0:T(8,128)(2,1)S(1)} %constant_dynamic-update-slice_fusion), channel_id=1, source_target_pairs={{0,12},{4,0},{8,4},{12,8},{1,13},{5,1},{9,5},{13,9},{2,14},{6,2},{... | collective-permute-start | bytes 393224 | tf_op jit(solution)/shard_map/ppermute | solution.py:42
  7.4 1.0 %collective-permute-start = (bf16[128,512]{1,0:T(8,128)(2,1)S(1)}, bf16[128,512]{1,0:T(8,128)(2,1)S(1)}, u32[]{:S(2)}, u32[]{:S(2)}) collective-permute-start(bf16[128,512]{1,0:T(8,128)(2,1)S(1)} %constant_dynamic-update-slice_fusion), channel_id=1, source_target_pairs={{0,4},{4,8},{8,12},{12,0},{1,5},{5,9},{9,13},{13,1},{2,6},{6,10},{... | collective-permute-start | bytes 393224 | tf_op jit(solution)/shard_map/ppermute | solution.py:42
  8.4 1.2 %dynamic_slice.19 = s32[1]{0:T(128)} dynamic-slice(s32[4]{0:T(128)} %param.13, s32[]{:T(128)S(6)} %select_n.53), dynamic_slice_sizes={1} | dynamic-slice | bytes 12 | tf_op jit(solution)/shard_map/dynamic_slice | solution.py:182
  10.4 0.9 %multiply_reduce_fusion = (s32[4]{0:T(128)S(1)}, s32[4]{0:T(128)S(1)}) fusion(s32[4,4]{1,0:T(4,128)} %param.12, s32[4]{0:T(128)S(1)} %compare_convert_fusion.1, s32[4]{0:T(128)} %param.13, s32[4]{0:T(128)S(1)} %select_reduce_fusion.2), kind=kLoop, calls=%fused_computation.27 | loop fusion | flops 72 | bytes 144 | tf_op jit(solution)/shard_map/reduce_sum | solution.py:18
  11.5 7.0 %collective-permute-done.1 = bf16[128,512]{1,0:T(8,128)(2,1)S(1)} collective-permute-done((bf16[128,512]{1,0:T(8,128)(2,1)S(1)}, bf16[128,512]{1,0:T(8,128)(2,1)S(1)}, u32[]{:S(2)}, u32[]{:S(2)}) %collective-permute-start.1) | collective-permute-done | bytes 131104 | tf_op jit(solution)/shard_map/ppermute | solution.py:42
  18.6 0.8 %pad_maximum_fusion.kv_ref = bf16[512,512]{1,0:T(8,128)(2,1)} fusion(bf16[128,512]{1,0:T(8,128)(2,1)S(1)} %collective-permute-done.2, bf16[128,512]{1,0:T(8,128)(2,1)S(1)} %collective-permute-done.1, bf16[128,512]{1,0:T(8,128)(2,1)S(1)} %collective-permute-done, bf16[128,512]{1,0:T(8,128)(2,1)S(1)} %constant_dynamic-update-slice_fusion), kind=kLoop, calls=%fused_computation.16 | loop fusion | flops 2097152 | bytes 1048576 | tf_op jit(solution)/shard_map/concatenate | solution.py:45
  19.4 0.7 broadcast_in_dim.5.mask_ref
  20.1 12.0 %shard_map.111 = (bf16[128,2048]{1,0:T(8,128)(2,1)}, f32[512,512]{1,0:T(8,128)}) custom-call(bf16[128,2048]{1,0:T(8,128)(2,1)} %query_ref.1, bf16[128,2048]{1,0:T(8,128)(2,1)} %grad_ref.1, bf16[512,512]{1,0:T(8,128)(2,1)} %pad_maximum_fusion.kv_ref, s32[128,512]{1,0:T(8,128)} %broadcast_in_dim.5.mask_ref), custom_call_target="tpu_custom_call" | custom-call | tf_op jit(solution)/shard_map/pallas_call | solution.py:161
  32.2 1.3 %convert.9 = bf16[512,512]{1,0:T(8,128)(2,1)S(1)} convert(f32[512,512]{1,0:T(8,128)} %get-tuple-element.7) | non-fusion elementwise | flops 262144 | bytes 1572864 | tf_op jit(solution)/shard_map/convert.4
  33.5 0.8 %collective-permute-start.5 = (bf16[128,512]{1,0:T(8,128)(2,1)S(1)}, bf16[128,512]{1,0:T(8,128)(2,1)S(1)}, u32[]{:S(2)}, u32[]{:S(2)}) collective-permute-start(bf16[128,512]{1,0:T(8,128)(2,1)S(1)} %get-tuple-element.9), channel_id=1, source_target_pairs={{0,4},{4,8},{8,12},{12,0},{1,5},{5,9},{9,13},{13,1},{2,6},{6,10},{... | collective-permute-start | bytes 393224 | tf_op jit(solution)/shard_map/ppermute | solution.py:55
  34.3 2.0 %collective-permute-start.4 = (bf16[128,512]{1,0:T(8,128)(2,1)S(1)}, bf16[128,512]{1,0:T(8,128)(2,1)S(1)}, u32[]{:S(2)}, u32[]{:S(2)}) collective-permute-start(bf16[128,512]{1,0:T(8,128)(2,1)S(1)} %get-tuple-element.10), channel_id=1, source_target_pairs={{0,8},{4,12},{8,0},{12,4},{1,9},{5,13},{9,1},{13,5},{2,10},{6,14},... | collective-permute-start | bytes 393224 | tf_op jit(solution)/shard_map/ppermute | solution.py:55
  36.3 2.8 %collective-permute-start.3 = (bf16[128,512]{1,0:T(8,128)(2,1)S(1)}, bf16[128,512]{1,0:T(8,128)(2,1)S(1)}, u32[]{:S(2)}, u32[]{:S(2)}) collective-permute-start(bf16[128,512]{1,0:T(8,128)(2,1)S(1)} %get-tuple-element.8), channel_id=1, source_target_pairs={{0,12},{4,0},{8,4},{12,8},{1,13},{5,1},{9,5},{13,9},{2,14},{6,2},{... | collective-permute-start | bytes 393224 | tf_op jit(solution)/shard_map/ppermute | solution.py:55
  39.1 2.7 %collective-permute-done.5 = bf16[128,512]{1,0:T(8,128)(2,1)S(1)} collective-permute-done((bf16[128,512]{1,0:T(8,128)(2,1)S(1)}, bf16[128,512]{1,0:T(8,128)(2,1)S(1)}, u32[]{:S(2)}, u32[]{:S(2)}) %collective-permute-start.5) | collective-permute-done | bytes 131104 | tf_op jit(solution)/shard_map/ppermute | solution.py:55
  41.8 4.1 %collective-permute-done.4 = bf16[128,512]{1,0:T(8,128)(2,1)S(1)} collective-permute-done((bf16[128,512]{1,0:T(8,128)(2,1)S(1)}, bf16[128,512]{1,0:T(8,128)(2,1)S(1)}, u32[]{:S(2)}, u32[]{:S(2)}) %collective-permute-start.4) | collective-permute-done | bytes 131104 | tf_op jit(solution)/shard_map/ppermute | solution.py:55
  45.9 1.0 %add_convert_fusion.1 = bf16[128,512]{1,0:T(8,128)(2,1)S(1)} fusion(bf16[128,512]{1,0:T(8,128)(2,1)S(1)} %collective-permute-done.5, bf16[128,512]{1,0:T(8,128)(2,1)S(1)} %collective-permute-done.4, bf16[128,512]{1,0:T(8,128)(2,1)S(1)} %collective-permute-done.3, f32[512,512]{1,0:T(8,128)} %get-tuple-element.7), kind=kLoop, calls=%fused_computation.17 | loop fusion | flops 458752 | bytes 786432 | tf_op jit(solution)/shard_map/convert.1
  47.0 2.4 %fusion.2 = f32[2,2048,128]{2,1,0:T(8,128)S(1)} fusion(bf16[2,2,2048,256]{3,2,1,0:T(8,128)(2,1)} %bitcast.37, s32[]{:T(128)S(6)} %select_n.56, bf16[128,256]{1,0:T(8,128)(2,1)S(1)} %get-tuple-element.12), kind=kOutput, calls=%fused_computation.4 | convolution fusion | flops 268435456 | bytes 4259844 | tf_op jit(solution)/shard_map/arf,tf->art/dot_general | solution.py:80
  50.7 2.4 %fusion.5 = f32[2,2048,128]{2,1,0:T(8,128)S(1)} fusion(bf16[2,2,2048,256]{3,2,1,0:T(8,128)(2,1)} %bitcast.38, s32[]{:T(128)S(6)} %select_n.55, bf16[128,256]{1,0:T(8,128)(2,1)S(1)} %get-tuple-element.12), kind=kOutput, calls=%fused_computation.7 | convolution fusion | flops 268435456 | bytes 4259844 | tf_op jit(solution)/shard_map/arf,tf->art/dot_general | solution.py:80
  53.1 1.8 %collective-permute-done.6 = f32[2,2048,128]{2,1,0:T(8,128)} collective-permute-done((f32[2,2048,128]{2,1,0:T(8,128)S(1)}, f32[2,2048,128]{2,1,0:T(8,128)}, u32[]{:S(2)}, u32[]{:S(2)}) %collective-permute-start.6) | collective-permute-done | bytes 2097184 | tf_op jit(solution)/shard_map/ppermute | solution.py:95
  54.9 2.3 %fusion = f32[2,2048,128]{2,1,0:T(8,128)S(1)} fusion(f32[2,2048,128]{2,1,0:T(8,128)} %collective-permute-done.6, f32[2,2048,128]{2,1,0:T(8,128)S(1)} %fusion.5, bf16[2,2,2048,256]{3,2,1,0:T(8,128)(2,1)S(1)} %bitcast.40, s32[]{:T(128)S(6)} %select_n.55, bf16[128,256]{1,0:T(8,128)(2,1)S(1)} %get-tuple-element.11), kind=kOutput, calls=%fused_computation.2 | convolution fusion | flops 269484032 | bytes 8454148 | tf_op jit(solution)/shard_map/arf,tf->art/dot_general | solution.py:85
  57.3 1.6 %collective-permute-start.7 = (bf16[1,2048,128]{2,1,0:T(8,128)(2,1)S(1)}, bf16[1,2048,128]{2,1,0:T(8,128)(2,1)S(1)}, u32[]{:S(2)}, u32[]{:S(2)}) collective-permute-start(bf16[1,2048,128]{2,1,0:T(8,128)(2,1)S(1)} %dynamic-slice_convert_fusion), channel_id=1, source_target_pairs={{0,2},{1,3},{2,0},{3,1},{4,6},{5,7},{6,4},{7,5},{8,10},{9,11},{10,... | collective-permute-start | bytes 1572872 | tf_op jit(solution)/shard_map/ppermute | solution.py:101
  58.9 12.5 %collective-permute-done.7 = bf16[1,2048,128]{2,1,0:T(8,128)(2,1)S(1)} collective-permute-done((bf16[1,2048,128]{2,1,0:T(8,128)(2,1)S(1)}, bf16[1,2048,128]{2,1,0:T(8,128)(2,1)S(1)}, u32[]{:S(2)}, u32[]{:S(2)}) %collective-permute-start.7) | collective-permute-done | bytes 524320 | tf_op jit(solution)/shard_map/ppermute | solution.py:101
  71.3 0.9 %fusion.11 = bf16[2048,128]{1,0:T(8,128)(2,1)} fusion(bf16[1,2048,128]{2,1,0:T(8,128)(2,1)S(1)} %collective-permute-done.7, f32[2,2048,128]{2,1,0:T(8,128)S(1)} %fusion, s32[]{:T(128)S(6)} %select_n.59), kind=kLoop, calls=%fused_computation.15 | loop fusion | flops 786432 | bytes 2097156 | tf_op jit(solution)/shard_map/convert_element_type | solution.py:105
  (23 shorter events, 2.3 us)
Async XLA Ops:
  2.3 9.2 %collective-permute-start.2 = (bf16[128,512]{1,0:T(8,128)(2,1)S(1)}, bf16[128,512]{1,0:T(8,128)(2,1)S(1)}, u32[]{:S(2)}, u32[]{:S(2)}) collective-permute-start(bf16[128,512]{1,0:T(8,128)(2,1)S(1)} %constant_dynamic-update-slice_fusion), channel_id=1, source_target_pairs={{0,12},{4,0},{8,4},{12,8},{1,13},{5,1},{9,5},{13,9},{2,14},{6,2},{... | collective-permute-start | bytes 393224 | tf_op jit(solution)/shard_map/ppermute | solution.py:42
  7.4 11.2 %collective-permute-start.1 = (bf16[128,512]{1,0:T(8,128)(2,1)S(1)}, bf16[128,512]{1,0:T(8,128)(2,1)S(1)}, u32[]{:S(2)}, u32[]{:S(2)}) collective-permute-start(bf16[128,512]{1,0:T(8,128)(2,1)S(1)} %constant_dynamic-update-slice_fusion), channel_id=1, source_target_pairs={{0,8},{4,12},{8,0},{12,4},{1,9},{5,13},{9,1},{13,5},{2,10},{6,14},... | collective-permute-start | bytes 393224 | tf_op jit(solution)/shard_map/ppermute | solution.py:42
  7.4 11.2 %collective-permute-start = (bf16[128,512]{1,0:T(8,128)(2,1)S(1)}, bf16[128,512]{1,0:T(8,128)(2,1)S(1)}, u32[]{:S(2)}, u32[]{:S(2)}) collective-permute-start(bf16[128,512]{1,0:T(8,128)(2,1)S(1)} %constant_dynamic-update-slice_fusion), channel_id=1, source_target_pairs={{0,4},{4,8},{8,12},{12,0},{1,5},{5,9},{9,13},{13,1},{2,6},{6,10},{... | collective-permute-start | bytes 393224 | tf_op jit(solution)/shard_map/ppermute | solution.py:42
  33.5 8.3 %collective-permute-start.5 = (bf16[128,512]{1,0:T(8,128)(2,1)S(1)}, bf16[128,512]{1,0:T(8,128)(2,1)S(1)}, u32[]{:S(2)}, u32[]{:S(2)}) collective-permute-start(bf16[128,512]{1,0:T(8,128)(2,1)S(1)} %get-tuple-element.9), channel_id=1, source_target_pairs={{0,4},{4,8},{8,12},{12,0},{1,5},{5,9},{9,13},{13,1},{2,6},{6,10},{... | collective-permute-start | bytes 393224 | tf_op jit(solution)/shard_map/ppermute | solution.py:55
  34.3 11.6 %collective-permute-start.4 = (bf16[128,512]{1,0:T(8,128)(2,1)S(1)}, bf16[128,512]{1,0:T(8,128)(2,1)S(1)}, u32[]{:S(2)}, u32[]{:S(2)}) collective-permute-start(bf16[128,512]{1,0:T(8,128)(2,1)S(1)} %get-tuple-element.10), channel_id=1, source_target_pairs={{0,8},{4,12},{8,0},{12,4},{1,9},{5,13},{9,1},{13,5},{2,10},{6,14},... | collective-permute-start | bytes 393224 | tf_op jit(solution)/shard_map/ppermute | solution.py:55
  36.3 9.6 %collective-permute-start.3 = (bf16[128,512]{1,0:T(8,128)(2,1)S(1)}, bf16[128,512]{1,0:T(8,128)(2,1)S(1)}, u32[]{:S(2)}, u32[]{:S(2)}) collective-permute-start(bf16[128,512]{1,0:T(8,128)(2,1)S(1)} %get-tuple-element.8), channel_id=1, source_target_pairs={{0,12},{4,0},{8,4},{12,8},{1,13},{5,1},{9,5},{13,9},{2,14},{6,2},{... | collective-permute-start | bytes 393224 | tf_op jit(solution)/shard_map/ppermute | solution.py:55
  46.9 3.7 %copy-start.3 = (bf16[128,256]{1,0:T(8,128)(2,1)}, bf16[128,256]{1,0:T(8,128)(2,1)S(1)}, u32[]{:S(2)}) copy-start(bf16[128,256]{1,0:T(8,128)(2,1)S(1)} %get-tuple-element.12) | copy-start | bytes 196612
  46.9 7.9 %copy-start.2 = (bf16[128,256]{1,0:T(8,128)(2,1)}, bf16[128,256]{1,0:T(8,128)(2,1)S(1)}, u32[]{:S(2)}) copy-start(bf16[128,256]{1,0:T(8,128)(2,1)S(1)} %get-tuple-element.11) | copy-start | bytes 196612
  47.0 2.9 %copy-start = (bf16[8192,256]{1,0:T(8,128)(2,1)S(1)}, bf16[8192,256]{1,0:T(8,128)(2,1)}, u32[]{:S(2)}) copy-start(bf16[8192,256]{1,0:T(8,128)(2,1)} %param.15) | copy-start | bytes 12582916
  50.5 4.4 %collective-permute-start.6 = (f32[2,2048,128]{2,1,0:T(8,128)S(1)}, f32[2,2048,128]{2,1,0:T(8,128)}, u32[]{:S(2)}, u32[]{:S(2)}) collective-permute-start(f32[2,2048,128]{2,1,0:T(8,128)S(1)} %convolution_add_fusion), channel_id=1, source_target_pairs={{0,1},{1,0},{2,3},{3,2},{4,5},{5,4},{6,7},{7,6},{8,9},{9,8},{10,11... | collective-permute-start | bytes 6291464 | tf_op jit(solution)/shard_map/ppermute | solution.py:95
  50.6 4.2 %copy-start.1 = (bf16[8192,256]{1,0:T(8,128)(2,1)S(1)}, bf16[8192,256]{1,0:T(8,128)(2,1)}, u32[]{:S(2)}) copy-start(bf16[8192,256]{1,0:T(8,128)(2,1)} %param.15) | copy-start | bytes 12582916
  57.3 14.0 %collective-permute-start.7 = (bf16[1,2048,128]{2,1,0:T(8,128)(2,1)S(1)}, bf16[1,2048,128]{2,1,0:T(8,128)(2,1)S(1)}, u32[]{:S(2)}, u32[]{:S(2)}) collective-permute-start(bf16[1,2048,128]{2,1,0:T(8,128)(2,1)S(1)} %dynamic-slice_convert_fusion), channel_id=1, source_target_pairs={{0,2},{1,3},{2,0},{3,1},{4,6},{5,7},{6,4},{7,5},{8,10},{9,11},{10,... | collective-permute-start | bytes 1572872 | tf_op jit(solution)/shard_map/ppermute | solution.py:101

commit v7 on v6

--- a/solution.py
+++ b/solution.py
@@ -4,6 +4,7 @@
 import jax.numpy as jnp
 from jax import lax
 from jax.experimental import pallas as pl
+from jax.experimental.pallas import tpu as pltpu
 from jax.sharding import PartitionSpec as P
 
 HD = 128
@@ -60,6 +61,45 @@
     return total
 
 
+def projection_kernel(order_ref, key_ref, value_ref, key_grad_ref, value_grad_ref, out_ref):
+    across = (((1,), (1,)), ((), ()))
+    out_ref[...] = lax.dot_general(
+        key_ref[...], key_grad_ref[...], across, preferred_element_type=jnp.float32
+    ) + lax.dot_general(
+        value_ref[...], value_grad_ref[...], across, preferred_element_type=jnp.float32
+    )
+
+
+def project_rows(key_proj, value_proj, key_grad, value_grad, blocks, block_rows):
+    sub = math.gcd(block_rows, 1024)
+    per = block_rows // sub
+    features = key_proj.shape[1]
+    tokens = key_grad.shape[0]
+
+    def weight_rows(i, j, order):
+        return (order[i] * per + j, 0)
+
+    def whole(i, j, order):
+        return (0, 0)
+
+    grid_spec = pltpu.PrefetchScalarGridSpec(
+        num_scalar_prefetch=1,
+        grid=(blocks.shape[0], per),
+        in_specs=[
+            pl.BlockSpec((sub, features), weight_rows),
+            pl.BlockSpec((sub, features), weight_rows),
+            pl.BlockSpec((tokens, features), whole),
+            pl.BlockSpec((tokens, features), whole),
+        ],
+        out_specs=pl.BlockSpec((sub, tokens), lambda i, j, order: (i * per + j, 0)),
+    )
+    return pl.pallas_call(
+        projection_kernel,
+        grid_spec=grid_spec,
+        out_shape=jax.ShapeDtypeStruct((blocks.shape[0] * block_rows, tokens), jnp.float32),
+    )(blocks, key_proj, value_proj, key_grad, value_grad)
+
+
 def head_reduce(key_proj, value_proj, key_grad, value_grad):
     count = lax.axis_size("head")
     position = lax.axis_index("head")
@@ -73,20 +113,11 @@
             jnp.bfloat16
         )
     block = key_proj.shape[0] // count
-    key_split = key_proj.reshape(count // 2, 2, block, key_proj.shape[1])
-    value_split = value_proj.reshape(count // 2, 2, block, value_proj.shape[1])
+    upper = lax.iota(jnp.int32, count // 2) * 2
 
     def project(half):
-        return jnp.einsum(
-            "arf,tf->art",
-            lax.dynamic_index_in_dim(key_split, half, 1, keepdims=False),
-            key_grad,
-            preferred_element_type=jnp.float32,
-        ) + jnp.einsum(
-            "arf,tf->art",
-            lax.dynamic_index_in_dim(value_split, half, 1, keepdims=False),
-            value_grad,
-            preferred_element_type=jnp.float32,
+        return project_rows(key_proj, value_proj, key_grad, value_grad, upper + half, block).reshape(
+            count // 2, block, -1
         )
 
     own_bit = position % 2

time: 72.6 us -> 81.2 us (1.12)
  Pallas kernels: 12 us -> 23.3 us
  matrix products: 7.91 us -> 0 us
  other arithmetic: 5.87 us -> 9.33 us
  local copies, waits for them, and re-layouts: 4.25 us -> 5.79 us
    pallas_call x0 -> x2, Pallas kernels: none -> 11.3 us  [project_rows(): pl.pallas_call(projection_kernel, grid_spec=grid_spec, out_shape=jax.Shap...]
    dot_general x4 -> x0, matrix products: 7.91 us -> none  [the longest x2 4.88 us: project(): jnp.einsum('arf,tf->art', lax.dynamic_index_in_dim(key_split, half, 1, ke...]
    ppermute x3, waiting for transfers between devices: 6.79 us -> 11.1 us  [scatter_slots(): lax.ppermute(slots[steps * rows:(steps + 1) * rows].astype(jnp.bfloat16),...]
    add x0 -> x3, other arithmetic: none -> 3.46 us  [the longest x1 2.43 us: head_reduce(): kept + lax.ppermute(sent, 'head', [(i, i ^ 1) for i in range(count)])]
    ppermute x3, waiting for transfers between devices: 7.03 us -> 4.13 us  [gather_slots(): lax.ppermute(block, axis, shifted_pairs(count, steps))]
    ppermute x1, waiting for transfers between devices: 1.76 us -> 0.01 us  [head_reduce(): lax.ppermute(sent, 'head', [(i, i ^ 1) for i in range(count)])]
    ppermute x3, starting transfers between devices: 6.06 us -> 6.96 us  [gather_slots(): lax.ppermute(block, axis, shifted_pairs(count, steps))]
    unnamed x9 -> x3, local copies, waits for them, and re-layouts: 1.28 us -> 2.14 us
  transfers between devices with their start and end apart: 8 -> 8, of which waited for: 5 -> 4; matrix products, arithmetic and copies ran while one was open for 8% -> 5% of each run, Pallas kernels for 0% -> 7%
where the time goes in v7:
time: 81.2 us; the launch traced here: 80.7 us
  waiting for transfers between devices  28 us (34%)
  Pallas kernels  23.3 us (29%)
  starting transfers between devices  13.6 us (17%)
  other arithmetic  9.33 us (11%)
  local copies, waits for them, and re-layouts  5.79 us (7%)
    ppermute x1, waiting for transfers between devices, head_reduce(): lax.ppermute(sent.astype(jnp.bfloat16), 'head', [(i, i ^ 1 << level) for...  12.8 us
    pallas_call x1, Pallas kernels, attention_block(): pl.pallas_call(attention_kernel, out_shape=(jax.ShapeDtypeStruct(queries....  12.1 us
    pallas_call x2, Pallas kernels, project_rows(): pl.pallas_call(projection_kernel, grid_spec=grid_spec, out_shape=jax.Shap...  11.3 us
    ppermute x3, waiting for transfers between devices, scatter_slots(): lax.ppermute(slots[steps * rows:(steps + 1) * rows].astype(jnp.bfloat16),...  11.1 us
    ppermute x3, starting transfers between devices, gather_slots(): lax.ppermute(block, axis, shifted_pairs(count, steps))  6.96 us
    ppermute x3, starting transfers between devices, scatter_slots(): lax.ppermute(slots[steps * rows:(steps + 1) * rows].astype(jnp.bfloat16),...  5.04 us
    ppermute x3, waiting for transfers between devices, gather_slots(): lax.ppermute(block, axis, shifted_pairs(count, steps))  4.13 us
    add x1, other arithmetic, head_reduce(): kept + lax.ppermute(sent, 'head', [(i, i ^ 1) for i in range(count)])  2.43 us
  transfers between devices with their start and end apart: 8, of which 4 were waited for; matrix products, arithmetic and copies ran while one was open for 5% of the time, Pallas kernels for 7%

profile of v7, /device:TPU:0, one launch (start us, length us, event | category | flops | bytes accessed | tf_op | source)
XLA Modules:
  0.0 80.7 jit_solution(1067948313490738603)
XLA Ops:
  0.6 0.8 %constant_dynamic-update-slice_fusion.1 = bf16[128,512]{1,0:T(8,128)(2,1)S(1)} fusion(bf16[128,256]{1,0:T(8,128)(2,1)} %param.9), kind=kLoop, calls=%fused_computation.6 | loop fusion | bytes 131072
  1.5 0.8 %constant_dynamic-update-slice_fusion = bf16[128,512]{1,0:T(8,128)(2,1)S(1)} fusion(bf16[128,512]{1,0:T(8,128)(2,1)S(1)} %constant_dynamic-update-slice_fusion.1, bf16[128,256]{1,0:T(8,128)(2,1)} %param.10), kind=kLoop, calls=%fused_computation.5 | loop fusion | bytes 131072 | tf_op jit(solution)/shard_map/concatenate | solution.py:219
  2.3 3.0 %collective-permute-start = (bf16[128,512]{1,0:T(8,128)(2,1)S(1)}, bf16[128,512]{1,0:T(8,128)(2,1)S(1)}, u32[]{:S(2)}, u32[]{:S(2)}) collective-permute-start(bf16[128,512]{1,0:T(8,128)(2,1)S(1)} %constant_dynamic-update-slice_fusion), channel_id=1, source_target_pairs={{0,4},{4,8},{8,12},{12,0},{1,5},{5,9},{9,13},{13,1},{2,6},{6,10},{... | collective-permute-start | bytes 393224 | tf_op jit(solution)/shard_map/ppermute | solution.py:43
  5.3 2.6 %collective-permute-start.1 = (bf16[128,512]{1,0:T(8,128)(2,1)S(1)}, bf16[128,512]{1,0:T(8,128)(2,1)S(1)}, u32[]{:S(2)}, u32[]{:S(2)}) collective-permute-start(bf16[128,512]{1,0:T(8,128)(2,1)S(1)} %constant_dynamic-update-slice_fusion), channel_id=1, source_target_pairs={{0,8},{4,12},{8,0},{12,4},{1,9},{5,13},{9,1},{13,5},{2,10},{6,14},... | collective-permute-start | bytes 393224 | tf_op jit(solution)/shard_map/ppermute | solution.py:43
  7.9 1.3 %collective-permute-start.2 = (bf16[128,512]{1,0:T(8,128)(2,1)S(1)}, bf16[128,512]{1,0:T(8,128)(2,1)S(1)}, u32[]{:S(2)}, u32[]{:S(2)}) collective-permute-start(bf16[128,512]{1,0:T(8,128)(2,1)S(1)} %constant_dynamic-update-slice_fusion), channel_id=1, source_target_pairs={{0,12},{4,0},{8,4},{12,8},{1,13},{5,1},{9,5},{13,9},{2,14},{6,2},{... | collective-permute-start | bytes 393224 | tf_op jit(solution)/shard_map/ppermute | solution.py:43
  9.3 1.2 %dynamic_slice.6 = s32[1]{0:T(128)} dynamic-slice(s32[4]{0:T(128)} %param.13, s32[]{:T(128)S(6)} %select_n.44), dynamic_slice_sizes={1} | dynamic-slice | bytes 12 | tf_op jit(solution)/shard_map/dynamic_slice | solution.py:213
  11.3 0.9 %multiply_reduce_fusion = (s32[4]{0:T(128)S(1)}, s32[4]{0:T(128)S(1)}) fusion(s32[4,4]{1,0:T(4,128)} %param.12, s32[4]{0:T(128)S(1)} %compare_convert_fusion.1, s32[4]{0:T(128)} %param.13, s32[4]{0:T(128)S(1)} %select_reduce_fusion.2), kind=kLoop, calls=%fused_computation.10 | loop fusion | flops 72 | bytes 144 | tf_op jit(solution)/shard_map/reduce_sum | solution.py:19
  12.4 4.1 %collective-permute-done.1 = bf16[128,512]{1,0:T(8,128)(2,1)S(1)} collective-permute-done((bf16[128,512]{1,0:T(8,128)(2,1)S(1)}, bf16[128,512]{1,0:T(8,128)(2,1)S(1)}, u32[]{:S(2)}, u32[]{:S(2)}) %collective-permute-start.1) | collective-permute-done | bytes 131104 | tf_op jit(solution)/shard_map/ppermute | solution.py:43
  16.6 0.8 %pad_maximum_fusion.kv_ref = bf16[512,512]{1,0:T(8,128)(2,1)} fusion(bf16[128,512]{1,0:T(8,128)(2,1)S(1)} %collective-permute-done.2, bf16[128,512]{1,0:T(8,128)(2,1)S(1)} %collective-permute-done.1, bf16[128,512]{1,0:T(8,128)(2,1)S(1)} %collective-permute-done, bf16[128,512]{1,0:T(8,128)(2,1)S(1)} %constant_dynamic-update-slice_fusion), kind=kLoop, calls=%fused_computation.3 | loop fusion | flops 2097152 | bytes 1048576 | tf_op jit(solution)/shard_map/concatenate | solution.py:46
  17.4 0.7 broadcast_in_dim.5.mask_ref
  18.2 12.1 %shard_map.111 = (bf16[128,2048]{1,0:T(8,128)(2,1)}, f32[512,512]{1,0:T(8,128)}) custom-call(bf16[128,2048]{1,0:T(8,128)(2,1)} %query_ref.1, bf16[128,2048]{1,0:T(8,128)(2,1)} %grad_ref.1, bf16[512,512]{1,0:T(8,128)(2,1)} %pad_maximum_fusion.kv_ref, s32[128,512]{1,0:T(8,128)} %broadcast_in_dim.5.mask_ref), custom_call_target="tpu_custom_call" | custom-call | tf_op jit(solution)/shard_map/pallas_call | solution.py:192
  30.2 1.3 %convert.9 = bf16[512,512]{1,0:T(8,128)(2,1)S(1)} convert(f32[512,512]{1,0:T(8,128)} %get-tuple-element.7) | non-fusion elementwise | flops 262144 | bytes 1572864 | tf_op jit(solution)/shard_map/convert.4
  31.5 4.4 %collective-permute-start.3 = (bf16[128,512]{1,0:T(8,128)(2,1)S(1)}, bf16[128,512]{1,0:T(8,128)(2,1)S(1)}, u32[]{:S(2)}, u32[]{:S(2)}) collective-permute-start(bf16[128,512]{1,0:T(8,128)(2,1)S(1)} %get-tuple-element.8), channel_id=1, source_target_pairs={{0,12},{4,0},{8,4},{12,8},{1,13},{5,1},{9,5},{13,9},{2,14},{6,2},{... | collective-permute-start | bytes 393224 | tf_op jit(solution)/shard_map/ppermute | solution.py:56
  37.1 2.8 %collective-permute-done.3 = bf16[128,512]{1,0:T(8,128)(2,1)S(1)} collective-permute-done((bf16[128,512]{1,0:T(8,128)(2,1)S(1)}, bf16[128,512]{1,0:T(8,128)(2,1)S(1)}, u32[]{:S(2)}, u32[]{:S(2)}) %collective-permute-start.3) | collective-permute-done | bytes 131104 | tf_op jit(solution)/shard_map/ppermute | solution.py:56
  39.9 8.3 %collective-permute-done.4 = bf16[128,512]{1,0:T(8,128)(2,1)S(1)} collective-permute-done((bf16[128,512]{1,0:T(8,128)(2,1)S(1)}, bf16[128,512]{1,0:T(8,128)(2,1)S(1)}, u32[]{:S(2)}, u32[]{:S(2)}) %collective-permute-start.4) | collective-permute-done | bytes 131104 | tf_op jit(solution)/shard_map/ppermute | solution.py:56
  48.1 1.0 %add_convert_fusion.1 = bf16[128,512]{1,0:T(8,128)(2,1)S(1)} fusion(bf16[128,512]{1,0:T(8,128)(2,1)S(1)} %collective-permute-done.5, bf16[128,512]{1,0:T(8,128)(2,1)S(1)} %collective-permute-done.4, bf16[128,512]{1,0:T(8,128)(2,1)S(1)} %collective-permute-done.3, f32[512,512]{1,0:T(8,128)} %get-tuple-element.7), kind=kLoop, calls=%fused_computation.4 | loop fusion | flops 458752 | bytes 786432 | tf_op jit(solution)/shard_map/convert.1
  49.2 0.7 fusion.5
  49.8 5.6 %shard_map.113 = f32[4096,128]{1,0:T(8,128)} custom-call(s32[2]{0:T(128)} %fusion.2.order_ref, bf16[8192,256]{1,0:T(8,128)(2,1)} %key_ref.3, bf16[8192,256]{1,0:T(8,128)(2,1)} %value_ref.3, bf16[128,256]{1,0:T(8,128)(2,1)} %get-tuple-element.12.key_grad_ref, bf16[128,256]{1,0:T(8,128)(2,1)} %get-tuple-element.11.value_grad_ref), custom_call_target="tpu_custom_call" | custom-call | tf_op jit(solution)/shard_map/pallas_call | solution.py:96
  56.0 5.6 %shard_map.112 = f32[4096,128]{1,0:T(8,128)} custom-call(s32[2]{0:T(128)} %fusion.3.order_ref, bf16[8192,256]{1,0:T(8,128)(2,1)} %key_ref.3, bf16[8192,256]{1,0:T(8,128)(2,1)} %value_ref.3, bf16[128,256]{1,0:T(8,128)(2,1)} %get-tuple-element.12.key_grad_ref, bf16[128,256]{1,0:T(8,128)(2,1)} %get-tuple-element.11.value_grad_ref), custom_call_target="tpu_custom_call" | custom-call | tf_op jit(solution)/shard_map/pallas_call | solution.py:96
  61.6 1.3 %copy-done = f32[2,2048,128]{2,1,0:T(8,128)} copy-done((f32[2,2048,128]{2,1,0:T(8,128)}, f32[2,2048,128]{2,1,0:T(8,128)S(1)}, u32[]{:S(2)}) %copy-start) | copy-done | bytes 2097176
  62.9 2.4 %add.72 = f32[2,2048,128]{2,1,0:T(8,128)S(1)} add(f32[2,2048,128]{2,1,0:T(8,128)} %bitcast.7, f32[2,2048,128]{2,1,0:T(8,128)} %copy-done) | non-fusion elementwise | flops 524288 | bytes 6291456 | tf_op jit(solution)/shard_map/add | solution.py:126
  65.4 1.6 %collective-permute-start.7 = (bf16[1,2048,128]{2,1,0:T(8,128)(2,1)S(1)}, bf16[1,2048,128]{2,1,0:T(8,128)(2,1)S(1)}, u32[]{:S(2)}, u32[]{:S(2)}) collective-permute-start(bf16[1,2048,128]{2,1,0:T(8,128)(2,1)S(1)} %dynamic-slice_convert_fusion), channel_id=1, source_target_pairs={{0,2},{1,3},{2,0},{3,1},{4,6},{5,7},{6,4},{7,5},{8,10},{9,11},{10,... | collective-permute-start | bytes 1572872 | tf_op jit(solution)/shard_map/ppermute | solution.py:132
  67.0 12.8 %collective-permute-done.7 = bf16[1,2048,128]{2,1,0:T(8,128)(2,1)S(1)} collective-permute-done((bf16[1,2048,128]{2,1,0:T(8,128)(2,1)S(1)}, bf16[1,2048,128]{2,1,0:T(8,128)(2,1)S(1)}, u32[]{:S(2)}, u32[]{:S(2)}) %collective-permute-start.7) | collective-permute-done | bytes 524320 | tf_op jit(solution)/shard_map/ppermute | solution.py:132
  79.8 0.9 %fusion = bf16[2048,128]{1,0:T(8,128)(2,1)} fusion(bf16[1,2048,128]{2,1,0:T(8,128)(2,1)S(1)} %collective-permute-done.7, f32[2,2048,128]{2,1,0:T(8,128)S(1)} %add.72, s32[]{:T(128)S(6)} %select_n.48), kind=kLoop, calls=%fused_computation.2 | loop fusion | flops 786432 | bytes 2097156 | tf_op jit(solution)/shard_map/convert_element_type | solution.py:136
  (18 shorter events, 2.8 us)
Async XLA Ops:
  2.3 10.1 %collective-permute-start = (bf16[128,512]{1,0:T(8,128)(2,1)S(1)}, bf16[128,512]{1,0:T(8,128)(2,1)S(1)}, u32[]{:S(2)}, u32[]{:S(2)}) collective-permute-start(bf16[128,512]{1,0:T(8,128)(2,1)S(1)} %constant_dynamic-update-slice_fusion), channel_id=1, source_target_pairs={{0,4},{4,8},{8,12},{12,0},{1,5},{5,9},{9,13},{13,1},{2,6},{6,10},{... | collective-permute-start | bytes 393224 | tf_op jit(solution)/shard_map/ppermute | solution.py:43
  5.3 11.2 %collective-permute-start.1 = (bf16[128,512]{1,0:T(8,128)(2,1)S(1)}, bf16[128,512]{1,0:T(8,128)(2,1)S(1)}, u32[]{:S(2)}, u32[]{:S(2)}) collective-permute-start(bf16[128,512]{1,0:T(8,128)(2,1)S(1)} %constant_dynamic-update-slice_fusion), channel_id=1, source_target_pairs={{0,8},{4,12},{8,0},{12,4},{1,9},{5,13},{9,1},{13,5},{2,10},{6,14},... | collective-permute-start | bytes 393224 | tf_op jit(solution)/shard_map/ppermute | solution.py:43
  7.9 8.6 %collective-permute-start.2 = (bf16[128,512]{1,0:T(8,128)(2,1)S(1)}, bf16[128,512]{1,0:T(8,128)(2,1)S(1)}, u32[]{:S(2)}, u32[]{:S(2)}) collective-permute-start(bf16[128,512]{1,0:T(8,128)(2,1)S(1)} %constant_dynamic-update-slice_fusion), channel_id=1, source_target_pairs={{0,12},{4,0},{8,4},{12,8},{1,13},{5,1},{9,5},{13,9},{2,14},{6,2},{... | collective-permute-start | bytes 393224 | tf_op jit(solution)/shard_map/ppermute | solution.py:43
  31.5 8.4 %collective-permute-start.3 = (bf16[128,512]{1,0:T(8,128)(2,1)S(1)}, bf16[128,512]{1,0:T(8,128)(2,1)S(1)}, u32[]{:S(2)}, u32[]{:S(2)}) collective-permute-start(bf16[128,512]{1,0:T(8,128)(2,1)S(1)} %get-tuple-element.8), channel_id=1, source_target_pairs={{0,12},{4,0},{8,4},{12,8},{1,13},{5,1},{9,5},{13,9},{2,14},{6,2},{... | collective-permute-start | bytes 393224 | tf_op jit(solution)/shard_map/ppermute | solution.py:56
  35.9 12.2 %collective-permute-start.4 = (bf16[128,512]{1,0:T(8,128)(2,1)S(1)}, bf16[128,512]{1,0:T(8,128)(2,1)S(1)}, u32[]{:S(2)}, u32[]{:S(2)}) collective-permute-start(bf16[128,512]{1,0:T(8,128)(2,1)S(1)} %get-tuple-element.10), channel_id=1, source_target_pairs={{0,8},{4,12},{8,0},{12,4},{1,9},{5,13},{9,1},{13,5},{2,10},{6,14},... | collective-permute-start | bytes 393224 | tf_op jit(solution)/shard_map/ppermute | solution.py:56
  36.3 11.8 %collective-permute-start.5 = (bf16[128,512]{1,0:T(8,128)(2,1)S(1)}, bf16[128,512]{1,0:T(8,128)(2,1)S(1)}, u32[]{:S(2)}, u32[]{:S(2)}) collective-permute-start(bf16[128,512]{1,0:T(8,128)(2,1)S(1)} %get-tuple-element.9), channel_id=1, source_target_pairs={{0,4},{4,8},{8,12},{12,0},{1,5},{5,9},{9,13},{13,1},{2,6},{6,10},{... | collective-permute-start | bytes 393224 | tf_op jit(solution)/shard_map/ppermute | solution.py:56
  55.5 6.1 %collective-permute-start.6 = (f32[2,2048,128]{2,1,0:T(8,128)}, f32[2,2048,128]{2,1,0:T(8,128)S(1)}, u32[]{:S(2)}, u32[]{:S(2)}) collective-permute-start(f32[2,2048,128]{2,1,0:T(8,128)} %bitcast.8), channel_id=1, source_target_pairs={{0,1},{1,0},{2,3},{3,2},{4,5},{5,4},{6,7},{7,6},{8,9},{9,8},{10,11... | collective-permute-start | bytes 6291464 | tf_op jit(solution)/shard_map/ppermute | solution.py:126
  61.6 1.3 %copy-start = (f32[2,2048,128]{2,1,0:T(8,128)}, f32[2,2048,128]{2,1,0:T(8,128)S(1)}, u32[]{:S(2)}) copy-start(f32[2,2048,128]{2,1,0:T(8,128)S(1)} %collective-permute-done.6) | copy-start | bytes 6291460
  65.4 14.4 %collective-permute-start.7 = (bf16[1,2048,128]{2,1,0:T(8,128)(2,1)S(1)}, bf16[1,2048,128]{2,1,0:T(8,128)(2,1)S(1)}, u32[]{:S(2)}, u32[]{:S(2)}) collective-permute-start(bf16[1,2048,128]{2,1,0:T(8,128)(2,1)S(1)} %dynamic-slice_convert_fusion), channel_id=1, source_target_pairs={{0,2},{1,3},{2,0},{3,1},{4,6},{5,7},{6,4},{7,5},{8,10},{9,11},{10,... | collective-permute-start | bytes 1572872 | tf_op jit(solution)/shard_map/ppermute | solution.py:132

commit v8 on v7

--- a/solution.py
+++ b/solution.py
@@ -62,16 +62,13 @@
 
 
 def projection_kernel(order_ref, key_ref, value_ref, key_grad_ref, value_grad_ref, out_ref):
-    across = (((1,), (1,)), ((), ()))
-    out_ref[...] = lax.dot_general(
-        key_ref[...], key_grad_ref[...], across, preferred_element_type=jnp.float32
-    ) + lax.dot_general(
-        value_ref[...], value_grad_ref[...], across, preferred_element_type=jnp.float32
-    )
+    out_ref[...] = jnp.dot(
+        key_ref[...], key_grad_ref[...], preferred_element_type=jnp.float32
+    ) + jnp.dot(value_ref[...], value_grad_ref[...], preferred_element_type=jnp.float32)
 
 
 def project_rows(key_proj, value_proj, key_grad, value_grad, blocks, block_rows):
-    sub = math.gcd(block_rows, 1024)
+    sub = math.gcd(block_rows, 2048)
     per = block_rows // sub
     features = key_proj.shape[1]
     tokens = key_grad.shape[0]
@@ -88,8 +85,8 @@
         in_specs=[
             pl.BlockSpec((sub, features), weight_rows),
             pl.BlockSpec((sub, features), weight_rows),
-            pl.BlockSpec((tokens, features), whole),
-            pl.BlockSpec((tokens, features), whole),
+            pl.BlockSpec((features, tokens), whole),
+            pl.BlockSpec((features, tokens), whole),
         ],
         out_specs=pl.BlockSpec((sub, tokens), lambda i, j, order: (i * per + j, 0)),
     )
@@ -97,7 +94,7 @@
         projection_kernel,
         grid_spec=grid_spec,
         out_shape=jax.ShapeDtypeStruct((blocks.shape[0] * block_rows, tokens), jnp.float32),
-    )(blocks, key_proj, value_proj, key_grad, value_grad)
+    )(blocks, key_proj, value_proj, key_grad.T, value_grad.T)
 
 
 def head_reduce(key_proj, value_proj, key_grad, value_grad):

time: 81.2 us -> 78.6 us (0.968)
  local copies, waits for them, and re-layouts: 5.79 us -> 8.9 us
  other arithmetic: 9.33 us -> 7.15 us
  Pallas kernels: 23.3 us -> 21.4 us
  waiting for transfers between devices: 28 us -> 26.5 us
    another operation x2, other arithmetic: 2.3 us -> 0.13 us
    pallas_call x2, Pallas kernels: 11.3 us -> 9.38 us  [project_rows(): pl.pallas_call(projection_kernel, grid_spec=grid_spec, out_shape=jax.Shap...]
    pallas_call x0 -> x1, local copies, waits for them, and re-layouts: none -> 1.55 us  [attention_block(): pl.pallas_call(attention_kernel, out_shape=(jax.ShapeDtypeStruct(queries....]
    ppermute x1, waiting for transfers between devices: 12.8 us -> 11.3 us  [head_reduce(): lax.ppermute(sent.astype(jnp.bfloat16), 'head', [(i, i ^ 1 << level) for...]
    unnamed x3 -> x5, local copies, waits for them, and re-layouts: 2.14 us -> 3.63 us
  transfers between devices with their start and end apart: 8 -> 8, of which waited for: 4 -> 4; matrix products, arithmetic and copies ran while one was open for 5% -> 7% of each run, Pallas kernels for 7% -> 6%
where the time goes in v8:
time: 78.6 us; the launch traced here: 78.3 us
  waiting for transfers between devices  26.5 us (34%)
  Pallas kernels  21.4 us (27%)
  starting transfers between devices  13.6 us (17%)
  local copies, waits for them, and re-layouts  8.9 us (11%)
  other arithmetic  7.15 us (9%)
    pallas_call x1, Pallas kernels, attention_block(): pl.pallas_call(attention_kernel, out_shape=(jax.ShapeDtypeStruct(queries....  12.1 us
    ppermute x1, waiting for transfers between devices, head_reduce(): lax.ppermute(sent.astype(jnp.bfloat16), 'head', [(i, i ^ 1 << level) for...  11.3 us
    ppermute x3, waiting for transfers between devices, scatter_slots(): lax.ppermute(slots[steps * rows:(steps + 1) * rows].astype(jnp.bfloat16),...  11.1 us
    pallas_call x2, Pallas kernels, project_rows(): pl.pallas_call(projection_kernel, grid_spec=grid_spec, out_shape=jax.Shap...  9.38 us
    ppermute x3, starting transfers between devices, gather_slots(): lax.ppermute(block, axis, shifted_pairs(count, steps))  6.96 us
    ppermute x3, starting transfers between devices, scatter_slots(): lax.ppermute(slots[steps * rows:(steps + 1) * rows].astype(jnp.bfloat16),...  5.04 us
    ppermute x3, waiting for transfers between devices, gather_slots(): lax.ppermute(block, axis, shifted_pairs(count, steps))  4.13 us
    unnamed x5, local copies, waits for them, and re-layouts  3.63 us
  transfers between devices with their start and end apart: 8, of which 4 were waited for; matrix products, arithmetic and copies ran while one was open for 7% of the time, Pallas kernels for 6%

profile of v8, /device:TPU:0, one launch (start us, length us, event | category | flops | bytes accessed | tf_op | source)
XLA Modules:
  0.0 78.3 jit_solution(5744861186122981205)
XLA Ops:
  0.6 0.8 %constant_dynamic-update-slice_fusion.1 = bf16[128,512]{1,0:T(8,128)(2,1)S(1)} fusion(bf16[128,256]{1,0:T(8,128)(2,1)} %param.9), kind=kLoop, calls=%fused_computation.9 | loop fusion | bytes 131072
  1.5 0.8 %constant_dynamic-update-slice_fusion = bf16[128,512]{1,0:T(8,128)(2,1)S(1)} fusion(bf16[128,512]{1,0:T(8,128)(2,1)S(1)} %constant_dynamic-update-slice_fusion.1, bf16[128,256]{1,0:T(8,128)(2,1)} %param.10), kind=kLoop, calls=%fused_computation.8 | loop fusion | bytes 131072 | tf_op jit(solution)/shard_map/concatenate | solution.py:216
  2.3 3.0 %collective-permute-start = (bf16[128,512]{1,0:T(8,128)(2,1)S(1)}, bf16[128,512]{1,0:T(8,128)(2,1)S(1)}, u32[]{:S(2)}, u32[]{:S(2)}) collective-permute-start(bf16[128,512]{1,0:T(8,128)(2,1)S(1)} %constant_dynamic-update-slice_fusion), channel_id=1, source_target_pairs={{0,4},{4,8},{8,12},{12,0},{1,5},{5,9},{9,13},{13,1},{2,6},{6,10},{... | collective-permute-start | bytes 393224 | tf_op jit(solution)/shard_map/ppermute | solution.py:43
  5.3 2.6 %collective-permute-start.1 = (bf16[128,512]{1,0:T(8,128)(2,1)S(1)}, bf16[128,512]{1,0:T(8,128)(2,1)S(1)}, u32[]{:S(2)}, u32[]{:S(2)}) collective-permute-start(bf16[128,512]{1,0:T(8,128)(2,1)S(1)} %constant_dynamic-update-slice_fusion), channel_id=1, source_target_pairs={{0,8},{4,12},{8,0},{12,4},{1,9},{5,13},{9,1},{13,5},{2,10},{6,14},... | collective-permute-start | bytes 393224 | tf_op jit(solution)/shard_map/ppermute | solution.py:43
  7.9 1.3 %collective-permute-start.2 = (bf16[128,512]{1,0:T(8,128)(2,1)S(1)}, bf16[128,512]{1,0:T(8,128)(2,1)S(1)}, u32[]{:S(2)}, u32[]{:S(2)}) collective-permute-start(bf16[128,512]{1,0:T(8,128)(2,1)S(1)} %constant_dynamic-update-slice_fusion), channel_id=1, source_target_pairs={{0,12},{4,0},{8,4},{12,8},{1,13},{5,1},{9,5},{13,9},{2,14},{6,2},{... | collective-permute-start | bytes 393224 | tf_op jit(solution)/shard_map/ppermute | solution.py:43
  9.3 1.2 %dynamic_slice.6 = s32[1]{0:T(128)} dynamic-slice(s32[4]{0:T(128)} %param.13, s32[]{:T(128)S(6)} %select_n.44), dynamic_slice_sizes={1} | dynamic-slice | bytes 12 | tf_op jit(solution)/shard_map/dynamic_slice | solution.py:210
  11.3 0.9 %multiply_reduce_fusion = (s32[4]{0:T(128)S(1)}, s32[4]{0:T(128)S(1)}) fusion(s32[4,4]{1,0:T(4,128)} %param.12, s32[4]{0:T(128)S(1)} %compare_convert_fusion.1, s32[4]{0:T(128)} %param.13, s32[4]{0:T(128)S(1)} %select_reduce_fusion.2), kind=kLoop, calls=%fused_computation.13 | loop fusion | flops 72 | bytes 144 | tf_op jit(solution)/shard_map/reduce_sum | solution.py:19
  12.4 4.1 %collective-permute-done.1 = bf16[128,512]{1,0:T(8,128)(2,1)S(1)} collective-permute-done((bf16[128,512]{1,0:T(8,128)(2,1)S(1)}, bf16[128,512]{1,0:T(8,128)(2,1)S(1)}, u32[]{:S(2)}, u32[]{:S(2)}) %collective-permute-start.1) | collective-permute-done | bytes 131104 | tf_op jit(solution)/shard_map/ppermute | solution.py:43
  16.6 0.8 %pad_maximum_fusion.kv_ref = bf16[512,512]{1,0:T(8,128)(2,1)} fusion(bf16[128,512]{1,0:T(8,128)(2,1)S(1)} %collective-permute-done.2, bf16[128,512]{1,0:T(8,128)(2,1)S(1)} %collective-permute-done.1, bf16[128,512]{1,0:T(8,128)(2,1)S(1)} %collective-permute-done, bf16[128,512]{1,0:T(8,128)(2,1)S(1)} %constant_dynamic-update-slice_fusion), kind=kLoop, calls=%fused_computation.3 | loop fusion | flops 2097152 | bytes 1048576 | tf_op jit(solution)/shard_map/concatenate | solution.py:46
  17.4 0.7 broadcast_in_dim.5.mask_ref
  18.2 12.1 %shard_map.111 = (bf16[128,2048]{1,0:T(8,128)(2,1)}, f32[512,512]{1,0:T(8,128)}) custom-call(bf16[128,2048]{1,0:T(8,128)(2,1)} %query_ref.1, bf16[128,2048]{1,0:T(8,128)(2,1)} %grad_ref.1, bf16[512,512]{1,0:T(8,128)(2,1)} %pad_maximum_fusion.kv_ref, s32[128,512]{1,0:T(8,128)} %broadcast_in_dim.5.mask_ref), custom_call_target="tpu_custom_call" | custom-call | tf_op jit(solution)/shard_map/pallas_call | solution.py:189
  30.2 1.6 %copy.16 = f32[512,512]{0,1:T(8,128)S(1)} copy(f32[512,512]{1,0:T(8,128)} %get-tuple-element.7) | data formatting | bytes 2097152 | tf_op jit(solution)/shard_map/pallas_call | solution.py:189
  31.9 4.4 %collective-permute-start.3 = (bf16[128,512]{0,1:T(8,128)(2,1)S(1)}, bf16[128,512]{0,1:T(8,128)(2,1)S(1)}, u32[]{:S(2)}, u32[]{:S(2)}) collective-permute-start(bf16[128,512]{0,1:T(8,128)(2,1)S(1)} %get-tuple-element.16), channel_id=1, source_target_pairs={{0,12},{4,0},{8,4},{12,8},{1,13},{5,1},{9,5},{13,9},{2,14},{6,2},{... | collective-permute-start | bytes 393224 | tf_op jit(solution)/shard_map/ppermute | solution.py:56
  37.5 2.8 %collective-permute-done.3 = bf16[128,512]{0,1:T(8,128)(2,1)S(1)} collective-permute-done((bf16[128,512]{0,1:T(8,128)(2,1)S(1)}, bf16[128,512]{0,1:T(8,128)(2,1)S(1)}, u32[]{:S(2)}, u32[]{:S(2)}) %collective-permute-start.3) | collective-permute-done | bytes 131104 | tf_op jit(solution)/shard_map/ppermute | solution.py:56
  40.3 8.3 %collective-permute-done.4 = bf16[128,512]{0,1:T(8,128)(2,1)S(1)} collective-permute-done((bf16[128,512]{0,1:T(8,128)(2,1)S(1)}, bf16[128,512]{0,1:T(8,128)(2,1)S(1)}, u32[]{:S(2)}, u32[]{:S(2)}) %collective-permute-start.4) | collective-permute-done | bytes 131104 | tf_op jit(solution)/shard_map/ppermute | solution.py:56
  49.3 4.7 %shard_map.113 = f32[4096,128]{1,0:T(8,128)} custom-call(s32[2]{0:T(128)} %fusion.5.order_ref, bf16[8192,256]{1,0:T(8,128)(2,1)} %key_ref.3, bf16[8192,256]{1,0:T(8,128)(2,1)} %value_ref.3, bf16[256,128]{1,0:T(8,128)(2,1)} %get-tuple-element.20.key_grad_ref, bf16[256,128]{1,0:T(8,128)(2,1)} %get-tuple-element.19.value_grad_ref), custom_call_target="tpu_custom_call" | custom-call | tf_op jit(solution)/shard_map/pallas_call | solution.py:93
  54.5 4.7 %shard_map.112 = f32[4096,128]{1,0:T(8,128)} custom-call(s32[2]{0:T(128)} %fusion.6.order_ref, bf16[8192,256]{1,0:T(8,128)(2,1)} %key_ref.3, bf16[8192,256]{1,0:T(8,128)(2,1)} %value_ref.3, bf16[256,128]{1,0:T(8,128)(2,1)} %get-tuple-element.20.key_grad_ref, bf16[256,128]{1,0:T(8,128)(2,1)} %get-tuple-element.19.value_grad_ref), custom_call_target="tpu_custom_call" | custom-call | tf_op jit(solution)/shard_map/pallas_call | solution.py:93
  59.2 1.3 %copy-done = f32[2,2048,128]{2,1,0:T(8,128)} copy-done((f32[2,2048,128]{2,1,0:T(8,128)}, f32[2,2048,128]{2,1,0:T(8,128)S(1)}, u32[]{:S(2)}) %copy-start) | copy-done | bytes 2097176
  60.5 2.4 %add.72 = f32[2,2048,128]{2,1,0:T(8,128)S(1)} add(f32[2,2048,128]{2,1,0:T(8,128)} %bitcast.11, f32[2,2048,128]{2,1,0:T(8,128)} %copy-done) | non-fusion elementwise | flops 524288 | bytes 6291456 | tf_op jit(solution)/shard_map/add | solution.py:123
  63.0 1.6 %collective-permute-start.7 = (bf16[1,2048,128]{2,1,0:T(8,128)(2,1)S(1)}, bf16[1,2048,128]{2,1,0:T(8,128)(2,1)S(1)}, u32[]{:S(2)}, u32[]{:S(2)}) collective-permute-start(bf16[1,2048,128]{2,1,0:T(8,128)(2,1)S(1)} %dynamic-slice_convert_fusion), channel_id=1, source_target_pairs={{0,2},{1,3},{2,0},{3,1},{4,6},{5,7},{6,4},{7,5},{8,10},{9,11},{10,... | collective-permute-start | bytes 1572872 | tf_op jit(solution)/shard_map/ppermute | solution.py:129
  64.5 0.7 copy.18
  65.3 0.7 copy.19
  66.0 11.3 %collective-permute-done.7 = bf16[1,2048,128]{2,1,0:T(8,128)(2,1)S(1)} collective-permute-done((bf16[1,2048,128]{2,1,0:T(8,128)(2,1)S(1)}, bf16[1,2048,128]{2,1,0:T(8,128)(2,1)S(1)}, u32[]{:S(2)}, u32[]{:S(2)}) %collective-permute-start.7) | collective-permute-done | bytes 524320 | tf_op jit(solution)/shard_map/ppermute | solution.py:129
  77.4 0.9 %fusion = bf16[2048,128]{1,0:T(8,128)(2,1)} fusion(bf16[1,2048,128]{2,1,0:T(8,128)(2,1)S(1)} %collective-permute-done.7, f32[2,2048,128]{2,1,0:T(8,128)S(1)} %add.72, s32[]{:T(128)S(6)} %select_n.48), kind=kLoop, calls=%fused_computation.2 | loop fusion | flops 786432 | bytes 2097156 | tf_op jit(solution)/shard_map/convert_element_type | solution.py:133
  (21 shorter events, 3.7 us)
Async XLA Ops:
  2.3 10.1 %collective-permute-start = (bf16[128,512]{1,0:T(8,128)(2,1)S(1)}, bf16[128,512]{1,0:T(8,128)(2,1)S(1)}, u32[]{:S(2)}, u32[]{:S(2)}) collective-permute-start(bf16[128,512]{1,0:T(8,128)(2,1)S(1)} %constant_dynamic-update-slice_fusion), channel_id=1, source_target_pairs={{0,4},{4,8},{8,12},{12,0},{1,5},{5,9},{9,13},{13,1},{2,6},{6,10},{... | collective-permute-start | bytes 393224 | tf_op jit(solution)/shard_map/ppermute | solution.py:43
  5.3 11.2 %collective-permute-start.1 = (bf16[128,512]{1,0:T(8,128)(2,1)S(1)}, bf16[128,512]{1,0:T(8,128)(2,1)S(1)}, u32[]{:S(2)}, u32[]{:S(2)}) collective-permute-start(bf16[128,512]{1,0:T(8,128)(2,1)S(1)} %constant_dynamic-update-slice_fusion), channel_id=1, source_target_pairs={{0,8},{4,12},{8,0},{12,4},{1,9},{5,13},{9,1},{13,5},{2,10},{6,14},... | collective-permute-start | bytes 393224 | tf_op jit(solution)/shard_map/ppermute | solution.py:43
  7.9 8.6 %collective-permute-start.2 = (bf16[128,512]{1,0:T(8,128)(2,1)S(1)}, bf16[128,512]{1,0:T(8,128)(2,1)S(1)}, u32[]{:S(2)}, u32[]{:S(2)}) collective-permute-start(bf16[128,512]{1,0:T(8,128)(2,1)S(1)} %constant_dynamic-update-slice_fusion), channel_id=1, source_target_pairs={{0,12},{4,0},{8,4},{12,8},{1,13},{5,1},{9,5},{13,9},{2,14},{6,2},{... | collective-permute-start | bytes 393224 | tf_op jit(solution)/shard_map/ppermute | solution.py:43
  31.9 8.4 %collective-permute-start.3 = (bf16[128,512]{0,1:T(8,128)(2,1)S(1)}, bf16[128,512]{0,1:T(8,128)(2,1)S(1)}, u32[]{:S(2)}, u32[]{:S(2)}) collective-permute-start(bf16[128,512]{0,1:T(8,128)(2,1)S(1)} %get-tuple-element.16), channel_id=1, source_target_pairs={{0,12},{4,0},{8,4},{12,8},{1,13},{5,1},{9,5},{13,9},{2,14},{6,2},{... | collective-permute-start | bytes 393224 | tf_op jit(solution)/shard_map/ppermute | solution.py:56
  36.3 12.2 %collective-permute-start.4 = (bf16[128,512]{0,1:T(8,128)(2,1)S(1)}, bf16[128,512]{0,1:T(8,128)(2,1)S(1)}, u32[]{:S(2)}, u32[]{:S(2)}) collective-permute-start(bf16[128,512]{0,1:T(8,128)(2,1)S(1)} %get-tuple-element.18), channel_id=1, source_target_pairs={{0,8},{4,12},{8,0},{12,4},{1,9},{5,13},{9,1},{13,5},{2,10},{6,14},... | collective-permute-start | bytes 393224 | tf_op jit(solution)/shard_map/ppermute | solution.py:56
  36.7 11.8 %collective-permute-start.5 = (bf16[128,512]{0,1:T(8,128)(2,1)S(1)}, bf16[128,512]{0,1:T(8,128)(2,1)S(1)}, u32[]{:S(2)}, u32[]{:S(2)}) collective-permute-start(bf16[128,512]{0,1:T(8,128)(2,1)S(1)} %get-tuple-element.17), channel_id=1, source_target_pairs={{0,4},{4,8},{8,12},{12,0},{1,5},{5,9},{9,13},{13,1},{2,6},{6,10},{... | collective-permute-start | bytes 393224 | tf_op jit(solution)/shard_map/ppermute | solution.py:56
  53.9 5.2 %collective-permute-start.6 = (f32[2,2048,128]{2,1,0:T(8,128)}, f32[2,2048,128]{2,1,0:T(8,128)S(1)}, u32[]{:S(2)}, u32[]{:S(2)}) collective-permute-start(f32[2,2048,128]{2,1,0:T(8,128)} %bitcast.12), channel_id=1, source_target_pairs={{0,1},{1,0},{2,3},{3,2},{4,5},{5,4},{6,7},{7,6},{8,9},{9,8},{10,11... | collective-permute-start | bytes 6291464 | tf_op jit(solution)/shard_map/ppermute | solution.py:123
  59.2 1.3 %copy-start = (f32[2,2048,128]{2,1,0:T(8,128)}, f32[2,2048,128]{2,1,0:T(8,128)S(1)}, u32[]{:S(2)}) copy-start(f32[2,2048,128]{2,1,0:T(8,128)S(1)} %collective-permute-done.6) | copy-start | bytes 6291460
  63.0 14.4 %collective-permute-start.7 = (bf16[1,2048,128]{2,1,0:T(8,128)(2,1)S(1)}, bf16[1,2048,128]{2,1,0:T(8,128)(2,1)S(1)}, u32[]{:S(2)}, u32[]{:S(2)}) collective-permute-start(bf16[1,2048,128]{2,1,0:T(8,128)(2,1)S(1)} %dynamic-slice_convert_fusion), channel_id=1, source_target_pairs={{0,2},{1,3},{2,0},{3,1},{4,6},{5,7},{6,4},{7,5},{8,10},{9,11},{10,... | collective-permute-start | bytes 1572872 | tf_op jit(solution)/shard_map/ppermute | solution.py:129

commit v9 on v6

--- a/solution.py
+++ b/solution.py
@@ -109,50 +109,48 @@
     inv_root = HD ** (-0.5)
     kv_cols = kv_ref.shape[1] // 2
     kv_heads = kv_cols // HD
+    rows = query_ref.shape[0]
     group_size = query_ref.shape[1] // kv_cols
-    allowed = mask_ref[...] > 0
+    allowed = jnp.concatenate([mask_ref[...]] * group_size, axis=0) > 0
     across = (((1,), (1,)), ((), ()))
     down = (((0,), (0,)), ((), ()))
     for kv_head in range(kv_heads):
         key_head = kv_ref[:, kv_head * HD : (kv_head + 1) * HD]
         value_head = kv_ref[:, kv_cols + kv_head * HD : kv_cols + (kv_head + 1) * HD]
-        key_sum = jnp.zeros(key_head.shape, jnp.float32)
-        value_sum = jnp.zeros(value_head.shape, jnp.float32)
-        for member in range(group_size):
-            first = (kv_head * group_size + member) * HD
-            query_head = query_ref[:, first : first + HD]
-            grad_head = grad_ref[:, first : first + HD]
-            scores = (
-                lax.dot_general(query_head, key_head, across, preferred_element_type=jnp.float32)
-                * inv_root
-            )
-            scores = jnp.where(allowed, scores, masked_score)
-            row_max = jnp.max(scores, axis=1, keepdims=True)
-            shifted = jnp.exp(scores - row_max)
-            row_sum = jnp.sum(shifted, axis=1, keepdims=True)
-            weighted = jnp.dot(
-                shifted.astype(jnp.bfloat16), value_head, preferred_element_type=jnp.float32
-            )
-            attended = (weighted / row_sum).astype(jnp.bfloat16)
-            probs = shifted * (1.0 / row_sum)
-            row_delta = jnp.sum(
-                grad_head.astype(jnp.float32) * attended.astype(jnp.float32), axis=1, keepdims=True
-            )
-            dprobs = lax.dot_general(
-                grad_head, value_head, across, preferred_element_type=jnp.float32
-            )
-            dscores = probs * (dprobs - row_delta)
-            query_term = (
-                jnp.dot(dscores.astype(jnp.bfloat16), key_head, preferred_element_type=jnp.float32)
-                * inv_root
-            )
-            query_out[:, first : first + HD] = query_term.astype(jnp.bfloat16)
-            key_sum = key_sum + lax.dot_general(
-                dscores.astype(jnp.bfloat16), query_head, down, preferred_element_type=jnp.float32
-            )
-            value_sum = value_sum + lax.dot_general(
-                probs.astype(jnp.bfloat16), grad_head, down, preferred_element_type=jnp.float32
-            )
+        base = kv_head * group_size * HD
+        query_stack = jnp.concatenate(
+            [query_ref[:, base + m * HD : base + (m + 1) * HD] for m in range(group_size)], axis=0
+        )
+        grad_stack = jnp.concatenate(
+            [grad_ref[:, base + m * HD : base + (m + 1) * HD] for m in range(group_size)], axis=0
+        )
+        scores = (
+            lax.dot_general(query_stack, key_head, across, preferred_element_type=jnp.float32)
+            * inv_root
+        )
+        scores = jnp.where(allowed, scores, masked_score)
+        row_max = jnp.max(scores, axis=1, keepdims=True)
+        shifted = jnp.exp(scores - row_max)
+        row_sum = jnp.sum(shifted, axis=1, keepdims=True)
+        weighted = jnp.dot(
+            shifted.astype(jnp.bfloat16), value_head, preferred_element_type=jnp.float32
+        )
+        attended = (weighted / row_sum).astype(jnp.bfloat16)
+        probs = shifted * (1.0 / row_sum)
+        row_delta = jnp.sum(
+            grad_stack.astype(jnp.float32) * attended.astype(jnp.float32), axis=1, keepdims=True
+        )
+        dprobs = lax.dot_general(grad_stack, value_head, across, preferred_element_type=jnp.float32)
+        dscores = (probs * (dprobs - row_delta)).astype(jnp.bfloat16)
+        query_term = jnp.dot(dscores, key_head, preferred_element_type=jnp.float32) * inv_root
+        for m in range(group_size):
+            query_out[:, base + m * HD : base + (m + 1) * HD] = query_term[
+                m * rows : (m + 1) * rows
+            ].astype(jnp.bfloat16)
+        key_sum = lax.dot_general(dscores, query_stack, down, preferred_element_type=jnp.float32)
+        value_sum = lax.dot_general(
+            probs.astype(jnp.bfloat16), grad_stack, down, preferred_element_type=jnp.float32
+        )
         kv_out[:, kv_head * HD : (kv_head + 1) * HD] = key_sum * inv_root
         kv_out[:, kv_cols + kv_head * HD : kv_cols + (kv_head + 1) * HD] = value_sum
 

time: 72.6 us -> 67.6 us (0.931)
  Pallas kernels: 12 us -> 7.09 us
    pallas_call x1, Pallas kernels: 12 us -> 7.09 us  [attention_block(): pl.pallas_call(attention_kernel, out_shape=(jax.ShapeDtypeStruct(queries....]
where the time goes in v9:
time: 67.6 us; the launch traced here: 67.3 us
  waiting for transfers between devices  28 us (41%)
  starting transfers between devices  13.3 us (20%)
  matrix products  7.94 us (12%)
  Pallas kernels  7.09 us (10%)
  other arithmetic  5.87 us (9%)
  local copies, waits for them, and re-layouts  4.24 us (6%)
  between operations  0.8 us (1%)
    ppermute x1, waiting for transfers between devices, head_reduce(): lax.ppermute(sent.astype(jnp.bfloat16), 'head', [(i, i ^ 1 << level) for...  12.5 us
    pallas_call x1, Pallas kernels, attention_block(): pl.pallas_call(attention_kernel, out_shape=(jax.ShapeDtypeStruct(queries....  7.09 us
    ppermute x3, waiting for transfers between devices, gather_slots(): lax.ppermute(block, axis, shifted_pairs(count, steps))  7.03 us
    ppermute x3, waiting for transfers between devices, scatter_slots(): lax.ppermute(slots[steps * rows:(steps + 1) * rows].astype(jnp.bfloat16),...  6.78 us
    ppermute x3, starting transfers between devices, gather_slots(): lax.ppermute(block, axis, shifted_pairs(count, steps))  6.06 us
    ppermute x3, starting transfers between devices, scatter_slots(): lax.ppermute(slots[steps * rows:(steps + 1) * rows].astype(jnp.bfloat16),...  5.6 us
    dot_general x2, matrix products, project(): jnp.einsum('arf,tf->art', lax.dynamic_index_in_dim(key_split, half, 1, ke...  4.9 us
    dot_general x2, matrix products, project(): jnp.einsum('arf,tf->art', lax.dynamic_index_in_dim(value_split, half, 1,...  3.04 us
  transfers between devices with their start and end apart: 8, of which 5 were waited for; matrix products, arithmetic and copies ran while one was open for 8% of the time, Pallas kernels for 0%

profile of v9, /device:TPU:0, one launch (start us, length us, event | category | flops | bytes accessed | tf_op | source)
XLA Modules:
  0.0 67.3 jit_solution(3035539724160257940)
XLA Ops:
  0.6 0.8 %constant_dynamic-update-slice_fusion.1 = bf16[128,512]{1,0:T(8,128)(2,1)S(1)} fusion(bf16[128,256]{1,0:T(8,128)(2,1)} %param.9), kind=kLoop, calls=%fused_computation.23 | loop fusion | bytes 131072
  1.5 0.8 %constant_dynamic-update-slice_fusion = bf16[128,512]{1,0:T(8,128)(2,1)S(1)} fusion(bf16[128,512]{1,0:T(8,128)(2,1)S(1)} %constant_dynamic-update-slice_fusion.1, bf16[128,256]{1,0:T(8,128)(2,1)} %param.10), kind=kLoop, calls=%fused_computation.22 | loop fusion | bytes 131072 | tf_op jit(solution)/shard_map/concatenate | solution.py:186
  2.3 5.0 %collective-permute-start.2 = (bf16[128,512]{1,0:T(8,128)(2,1)S(1)}, bf16[128,512]{1,0:T(8,128)(2,1)S(1)}, u32[]{:S(2)}, u32[]{:S(2)}) collective-permute-start(bf16[128,512]{1,0:T(8,128)(2,1)S(1)} %constant_dynamic-update-slice_fusion), channel_id=1, source_target_pairs={{0,12},{4,0},{8,4},{12,8},{1,13},{5,1},{9,5},{13,9},{2,14},{6,2},{... | collective-permute-start | bytes 393224 | tf_op jit(solution)/shard_map/ppermute | solution.py:42
  7.4 1.0 %collective-permute-start = (bf16[128,512]{1,0:T(8,128)(2,1)S(1)}, bf16[128,512]{1,0:T(8,128)(2,1)S(1)}, u32[]{:S(2)}, u32[]{:S(2)}) collective-permute-start(bf16[128,512]{1,0:T(8,128)(2,1)S(1)} %constant_dynamic-update-slice_fusion), channel_id=1, source_target_pairs={{0,4},{4,8},{8,12},{12,0},{1,5},{5,9},{9,13},{13,1},{2,6},{6,10},{... | collective-permute-start | bytes 393224 | tf_op jit(solution)/shard_map/ppermute | solution.py:42
  8.4 1.2 %dynamic_slice.19 = s32[1]{0:T(128)} dynamic-slice(s32[4]{0:T(128)} %param.13, s32[]{:T(128)S(6)} %select_n.53), dynamic_slice_sizes={1} | dynamic-slice | bytes 12 | tf_op jit(solution)/shard_map/dynamic_slice | solution.py:180
  10.4 0.9 %multiply_reduce_fusion = (s32[4]{0:T(128)S(1)}, s32[4]{0:T(128)S(1)}) fusion(s32[4,4]{1,0:T(4,128)} %param.12, s32[4]{0:T(128)S(1)} %compare_convert_fusion.1, s32[4]{0:T(128)} %param.13, s32[4]{0:T(128)S(1)} %select_reduce_fusion.2), kind=kLoop, calls=%fused_computation.27 | loop fusion | flops 72 | bytes 144 | tf_op jit(solution)/shard_map/reduce_sum | solution.py:18
  11.5 7.0 %collective-permute-done.1 = bf16[128,512]{1,0:T(8,128)(2,1)S(1)} collective-permute-done((bf16[128,512]{1,0:T(8,128)(2,1)S(1)}, bf16[128,512]{1,0:T(8,128)(2,1)S(1)}, u32[]{:S(2)}, u32[]{:S(2)}) %collective-permute-start.1) | collective-permute-done | bytes 131104 | tf_op jit(solution)/shard_map/ppermute | solution.py:42
  18.6 0.8 %pad_maximum_fusion.kv_ref = bf16[512,512]{1,0:T(8,128)(2,1)} fusion(bf16[128,512]{1,0:T(8,128)(2,1)S(1)} %collective-permute-done.2, bf16[128,512]{1,0:T(8,128)(2,1)S(1)} %collective-permute-done.1, bf16[128,512]{1,0:T(8,128)(2,1)S(1)} %collective-permute-done, bf16[128,512]{1,0:T(8,128)(2,1)S(1)} %constant_dynamic-update-slice_fusion), kind=kLoop, calls=%fused_computation.16 | loop fusion | flops 2097152 | bytes 1048576 | tf_op jit(solution)/shard_map/concatenate | solution.py:45
  19.4 0.7 %broadcast_in_dim.5.mask_ref = s32[128,512]{1,0:T(8,128)} broadcast(s32[512]{0:T(512)S(1)} %broadcast_bitcast_fusion), dimensions={1} | broadcast | bytes 264192 | tf_op jit(solution)/shard_map/broadcast_in_dim | solution.py:204
  20.1 7.1 %shard_map.111 = (bf16[128,2048]{1,0:T(8,128)(2,1)}, f32[512,512]{1,0:T(8,128)}) custom-call(bf16[128,2048]{1,0:T(8,128)(2,1)} %query_ref.1, bf16[128,2048]{1,0:T(8,128)(2,1)} %grad_ref.1, bf16[512,512]{1,0:T(8,128)(2,1)} %pad_maximum_fusion.kv_ref, s32[128,512]{1,0:T(8,128)} %broadcast_in_dim.5.mask_ref), custom_call_target="tpu_custom_call" | custom-call | tf_op jit(solution)/shard_map/pallas_call | solution.py:159
  27.2 1.3 %convert.9 = bf16[512,512]{1,0:T(8,128)(2,1)S(1)} convert(f32[512,512]{1,0:T(8,128)} %get-tuple-element.7) | non-fusion elementwise | flops 262144 | bytes 1572864 | tf_op jit(solution)/shard_map/convert.4
  28.5 0.8 %collective-permute-start.5 = (bf16[128,512]{1,0:T(8,128)(2,1)S(1)}, bf16[128,512]{1,0:T(8,128)(2,1)S(1)}, u32[]{:S(2)}, u32[]{:S(2)}) collective-permute-start(bf16[128,512]{1,0:T(8,128)(2,1)S(1)} %get-tuple-element.9), channel_id=1, source_target_pairs={{0,4},{4,8},{8,12},{12,0},{1,5},{5,9},{9,13},{13,1},{2,6},{6,10},{... | collective-permute-start | bytes 393224 | tf_op jit(solution)/shard_map/ppermute | solution.py:55
  29.3 2.0 %collective-permute-start.4 = (bf16[128,512]{1,0:T(8,128)(2,1)S(1)}, bf16[128,512]{1,0:T(8,128)(2,1)S(1)}, u32[]{:S(2)}, u32[]{:S(2)}) collective-permute-start(bf16[128,512]{1,0:T(8,128)(2,1)S(1)} %get-tuple-element.10), channel_id=1, source_target_pairs={{0,8},{4,12},{8,0},{12,4},{1,9},{5,13},{9,1},{13,5},{2,10},{6,14},... | collective-permute-start | bytes 393224 | tf_op jit(solution)/shard_map/ppermute | solution.py:55
  31.3 2.8 %collective-permute-start.3 = (bf16[128,512]{1,0:T(8,128)(2,1)S(1)}, bf16[128,512]{1,0:T(8,128)(2,1)S(1)}, u32[]{:S(2)}, u32[]{:S(2)}) collective-permute-start(bf16[128,512]{1,0:T(8,128)(2,1)S(1)} %get-tuple-element.8), channel_id=1, source_target_pairs={{0,12},{4,0},{8,4},{12,8},{1,13},{5,1},{9,5},{13,9},{2,14},{6,2},{... | collective-permute-start | bytes 393224 | tf_op jit(solution)/shard_map/ppermute | solution.py:55
  34.1 2.7 %collective-permute-done.5 = bf16[128,512]{1,0:T(8,128)(2,1)S(1)} collective-permute-done((bf16[128,512]{1,0:T(8,128)(2,1)S(1)}, bf16[128,512]{1,0:T(8,128)(2,1)S(1)}, u32[]{:S(2)}, u32[]{:S(2)}) %collective-permute-start.5) | collective-permute-done | bytes 131104 | tf_op jit(solution)/shard_map/ppermute | solution.py:55
  36.9 4.0 %collective-permute-done.4 = bf16[128,512]{1,0:T(8,128)(2,1)S(1)} collective-permute-done((bf16[128,512]{1,0:T(8,128)(2,1)S(1)}, bf16[128,512]{1,0:T(8,128)(2,1)S(1)}, u32[]{:S(2)}, u32[]{:S(2)}) %collective-permute-start.4) | collective-permute-done | bytes 131104 | tf_op jit(solution)/shard_map/ppermute | solution.py:55
  40.9 1.0 %add_convert_fusion.1 = bf16[128,512]{1,0:T(8,128)(2,1)S(1)} fusion(bf16[128,512]{1,0:T(8,128)(2,1)S(1)} %collective-permute-done.5, bf16[128,512]{1,0:T(8,128)(2,1)S(1)} %collective-permute-done.4, bf16[128,512]{1,0:T(8,128)(2,1)S(1)} %collective-permute-done.3, f32[512,512]{1,0:T(8,128)} %get-tuple-element.7), kind=kLoop, calls=%fused_computation.17 | loop fusion | flops 458752 | bytes 786432 | tf_op jit(solution)/shard_map/convert.1
  42.0 2.4 %fusion.2 = f32[2,2048,128]{2,1,0:T(8,128)S(1)} fusion(bf16[2,2,2048,256]{3,2,1,0:T(8,128)(2,1)} %bitcast.37, s32[]{:T(128)S(6)} %select_n.56, bf16[128,256]{1,0:T(8,128)(2,1)S(1)} %get-tuple-element.12), kind=kOutput, calls=%fused_computation.4 | convolution fusion | flops 268435456 | bytes 4259844 | tf_op jit(solution)/shard_map/arf,tf->art/dot_general | solution.py:80
  45.7 2.4 %fusion.5 = f32[2,2048,128]{2,1,0:T(8,128)S(1)} fusion(bf16[2,2,2048,256]{3,2,1,0:T(8,128)(2,1)} %bitcast.38, s32[]{:T(128)S(6)} %select_n.55, bf16[128,256]{1,0:T(8,128)(2,1)S(1)} %get-tuple-element.12), kind=kOutput, calls=%fused_computation.7 | convolution fusion | flops 268435456 | bytes 4259844 | tf_op jit(solution)/shard_map/arf,tf->art/dot_general | solution.py:80
  48.2 1.8 %collective-permute-done.6 = f32[2,2048,128]{2,1,0:T(8,128)} collective-permute-done((f32[2,2048,128]{2,1,0:T(8,128)S(1)}, f32[2,2048,128]{2,1,0:T(8,128)}, u32[]{:S(2)}, u32[]{:S(2)}) %collective-permute-start.6) | collective-permute-done | bytes 2097184 | tf_op jit(solution)/shard_map/ppermute | solution.py:95
  49.9 2.3 %fusion = f32[2,2048,128]{2,1,0:T(8,128)S(1)} fusion(f32[2,2048,128]{2,1,0:T(8,128)} %collective-permute-done.6, f32[2,2048,128]{2,1,0:T(8,128)S(1)} %fusion.5, bf16[2,2,2048,256]{3,2,1,0:T(8,128)(2,1)S(1)} %bitcast.40, s32[]{:T(128)S(6)} %select_n.55, bf16[128,256]{1,0:T(8,128)(2,1)S(1)} %get-tuple-element.11), kind=kOutput, calls=%fused_computation.2 | convolution fusion | flops 269484032 | bytes 8454148 | tf_op jit(solution)/shard_map/arf,tf->art/dot_general | solution.py:85
  52.3 1.6 %collective-permute-start.7 = (bf16[1,2048,128]{2,1,0:T(8,128)(2,1)S(1)}, bf16[1,2048,128]{2,1,0:T(8,128)(2,1)S(1)}, u32[]{:S(2)}, u32[]{:S(2)}) collective-permute-start(bf16[1,2048,128]{2,1,0:T(8,128)(2,1)S(1)} %dynamic-slice_convert_fusion), channel_id=1, source_target_pairs={{0,2},{1,3},{2,0},{3,1},{4,6},{5,7},{6,4},{7,5},{8,10},{9,11},{10,... | collective-permute-start | bytes 1572872 | tf_op jit(solution)/shard_map/ppermute | solution.py:101
  53.9 12.5 %collective-permute-done.7 = bf16[1,2048,128]{2,1,0:T(8,128)(2,1)S(1)} collective-permute-done((bf16[1,2048,128]{2,1,0:T(8,128)(2,1)S(1)}, bf16[1,2048,128]{2,1,0:T(8,128)(2,1)S(1)}, u32[]{:S(2)}, u32[]{:S(2)}) %collective-permute-start.7) | collective-permute-done | bytes 524320 | tf_op jit(solution)/shard_map/ppermute | solution.py:101
  66.4 0.9 %fusion.11 = bf16[2048,128]{1,0:T(8,128)(2,1)} fusion(bf16[1,2048,128]{2,1,0:T(8,128)(2,1)S(1)} %collective-permute-done.7, f32[2,2048,128]{2,1,0:T(8,128)S(1)} %fusion, s32[]{:T(128)S(6)} %select_n.59), kind=kLoop, calls=%fused_computation.15 | loop fusion | flops 786432 | bytes 2097156 | tf_op jit(solution)/shard_map/convert_element_type | solution.py:105
  (23 shorter events, 2.3 us)
Async XLA Ops:
  2.3 9.2 %collective-permute-start.2 = (bf16[128,512]{1,0:T(8,128)(2,1)S(1)}, bf16[128,512]{1,0:T(8,128)(2,1)S(1)}, u32[]{:S(2)}, u32[]{:S(2)}) collective-permute-start(bf16[128,512]{1,0:T(8,128)(2,1)S(1)} %constant_dynamic-update-slice_fusion), channel_id=1, source_target_pairs={{0,12},{4,0},{8,4},{12,8},{1,13},{5,1},{9,5},{13,9},{2,14},{6,2},{... | collective-permute-start | bytes 393224 | tf_op jit(solution)/shard_map/ppermute | solution.py:42
  7.4 11.2 %collective-permute-start.1 = (bf16[128,512]{1,0:T(8,128)(2,1)S(1)}, bf16[128,512]{1,0:T(8,128)(2,1)S(1)}, u32[]{:S(2)}, u32[]{:S(2)}) collective-permute-start(bf16[128,512]{1,0:T(8,128)(2,1)S(1)} %constant_dynamic-update-slice_fusion), channel_id=1, source_target_pairs={{0,8},{4,12},{8,0},{12,4},{1,9},{5,13},{9,1},{13,5},{2,10},{6,14},... | collective-permute-start | bytes 393224 | tf_op jit(solution)/shard_map/ppermute | solution.py:42
  7.4 11.2 %collective-permute-start = (bf16[128,512]{1,0:T(8,128)(2,1)S(1)}, bf16[128,512]{1,0:T(8,128)(2,1)S(1)}, u32[]{:S(2)}, u32[]{:S(2)}) collective-permute-start(bf16[128,512]{1,0:T(8,128)(2,1)S(1)} %constant_dynamic-update-slice_fusion), channel_id=1, source_target_pairs={{0,4},{4,8},{8,12},{12,0},{1,5},{5,9},{9,13},{13,1},{2,6},{6,10},{... | collective-permute-start | bytes 393224 | tf_op jit(solution)/shard_map/ppermute | solution.py:42
  28.5 8.3 %collective-permute-start.5 = (bf16[128,512]{1,0:T(8,128)(2,1)S(1)}, bf16[128,512]{1,0:T(8,128)(2,1)S(1)}, u32[]{:S(2)}, u32[]{:S(2)}) collective-permute-start(bf16[128,512]{1,0:T(8,128)(2,1)S(1)} %get-tuple-element.9), channel_id=1, source_target_pairs={{0,4},{4,8},{8,12},{12,0},{1,5},{5,9},{9,13},{13,1},{2,6},{6,10},{... | collective-permute-start | bytes 393224 | tf_op jit(solution)/shard_map/ppermute | solution.py:55
  29.3 11.6 %collective-permute-start.4 = (bf16[128,512]{1,0:T(8,128)(2,1)S(1)}, bf16[128,512]{1,0:T(8,128)(2,1)S(1)}, u32[]{:S(2)}, u32[]{:S(2)}) collective-permute-start(bf16[128,512]{1,0:T(8,128)(2,1)S(1)} %get-tuple-element.10), channel_id=1, source_target_pairs={{0,8},{4,12},{8,0},{12,4},{1,9},{5,13},{9,1},{13,5},{2,10},{6,14},... | collective-permute-start | bytes 393224 | tf_op jit(solution)/shard_map/ppermute | solution.py:55
  31.3 9.6 %collective-permute-start.3 = (bf16[128,512]{1,0:T(8,128)(2,1)S(1)}, bf16[128,512]{1,0:T(8,128)(2,1)S(1)}, u32[]{:S(2)}, u32[]{:S(2)}) collective-permute-start(bf16[128,512]{1,0:T(8,128)(2,1)S(1)} %get-tuple-element.8), channel_id=1, source_target_pairs={{0,12},{4,0},{8,4},{12,8},{1,13},{5,1},{9,5},{13,9},{2,14},{6,2},{... | collective-permute-start | bytes 393224 | tf_op jit(solution)/shard_map/ppermute | solution.py:55
  42.0 3.7 %copy-start.3 = (bf16[128,256]{1,0:T(8,128)(2,1)}, bf16[128,256]{1,0:T(8,128)(2,1)S(1)}, u32[]{:S(2)}) copy-start(bf16[128,256]{1,0:T(8,128)(2,1)S(1)} %get-tuple-element.12) | copy-start | bytes 196612
  42.0 7.9 %copy-start.2 = (bf16[128,256]{1,0:T(8,128)(2,1)}, bf16[128,256]{1,0:T(8,128)(2,1)S(1)}, u32[]{:S(2)}) copy-start(bf16[128,256]{1,0:T(8,128)(2,1)S(1)} %get-tuple-element.11) | copy-start | bytes 196612
  42.0 2.9 %copy-start = (bf16[8192,256]{1,0:T(8,128)(2,1)S(1)}, bf16[8192,256]{1,0:T(8,128)(2,1)}, u32[]{:S(2)}) copy-start(bf16[8192,256]{1,0:T(8,128)(2,1)} %param.15) | copy-start | bytes 12582916
  45.6 4.4 %collective-permute-start.6 = (f32[2,2048,128]{2,1,0:T(8,128)S(1)}, f32[2,2048,128]{2,1,0:T(8,128)}, u32[]{:S(2)}, u32[]{:S(2)}) collective-permute-start(f32[2,2048,128]{2,1,0:T(8,128)S(1)} %convolution_add_fusion), channel_id=1, source_target_pairs={{0,1},{1,0},{2,3},{3,2},{4,5},{5,4},{6,7},{7,6},{8,9},{9,8},{10,11... | collective-permute-start | bytes 6291464 | tf_op jit(solution)/shard_map/ppermute | solution.py:95
  45.7 4.2 %copy-start.1 = (bf16[8192,256]{1,0:T(8,128)(2,1)S(1)}, bf16[8192,256]{1,0:T(8,128)(2,1)}, u32[]{:S(2)}) copy-start(bf16[8192,256]{1,0:T(8,128)(2,1)} %param.15) | copy-start | bytes 12582916
  52.3 14.0 %collective-permute-start.7 = (bf16[1,2048,128]{2,1,0:T(8,128)(2,1)S(1)}, bf16[1,2048,128]{2,1,0:T(8,128)(2,1)S(1)}, u32[]{:S(2)}, u32[]{:S(2)}) collective-permute-start(bf16[1,2048,128]{2,1,0:T(8,128)(2,1)S(1)} %dynamic-slice_convert_fusion), channel_id=1, source_target_pairs={{0,2},{1,3},{2,0},{3,1},{4,6},{5,7},{6,4},{7,5},{8,10},{9,11},{10,... | collective-permute-start | bytes 1572872 | tf_op jit(solution)/shard_map/ppermute | solution.py:101

commit v10 on v9

--- a/solution.py
+++ b/solution.py
@@ -60,6 +60,35 @@
     return total
 
 
+def two_level_reduce(key_proj, value_proj, key_grad, value_grad, block, position):
+    across = (((1,), (1,)), ((), ()))
+    core_bit = position % 2
+    chip_bit = position // 2
+
+    def project(chip, core):
+        first = (chip * 2 + core) * block
+        return lax.dot_general(
+            lax.dynamic_slice_in_dim(key_proj, first, block, 0),
+            key_grad,
+            across,
+            preferred_element_type=jnp.float32,
+        ) + lax.dot_general(
+            lax.dynamic_slice_in_dim(value_proj, first, block, 0),
+            value_grad,
+            across,
+            preferred_element_type=jnp.float32,
+        )
+
+    sibling = [(i, i ^ 1) for i in range(4)]
+    partner = [(i, i ^ 2) for i in range(4)]
+    for_sibling_send = lax.ppermute(project(1 - chip_bit, 1 - core_bit), "head", sibling)
+    chip_sum = project(1 - chip_bit, core_bit) + for_sibling_send
+    from_other_chip = lax.ppermute(chip_sum.astype(jnp.bfloat16), "head", partner)
+    from_sibling = lax.ppermute(project(chip_bit, 1 - core_bit), "head", sibling)
+    total = project(chip_bit, core_bit) + from_sibling + from_other_chip.astype(jnp.float32)
+    return total.astype(jnp.bfloat16)
+
+
 def head_reduce(key_proj, value_proj, key_grad, value_grad):
     count = lax.axis_size("head")
     position = lax.axis_index("head")
@@ -89,6 +118,8 @@
             preferred_element_type=jnp.float32,
         )
 
+    if depth == 2:
+        return two_level_reduce(key_proj, value_proj, key_grad, value_grad, block, position)
     own_bit = position % 2
     sent = project(1 - own_bit)
     kept = project(own_bit)

time: 67.6 us -> 72.3 us (1.070)
  matrix products: 7.94 us -> 14.5 us
  waiting for transfers between devices: 28 us -> 26.4 us
  other arithmetic: 5.87 us -> 4.97 us
  starting transfers between devices: 13.3 us -> 14.2 us
    dot_general x4 -> x8, matrix products: 7.94 us -> 14.5 us  [the longest x4 7.83 us: project(): lax.dot_general(lax.dynamic_slice_in_dim(key_proj, first, block, 0), key_...]
    ppermute x3, waiting for transfers between devices: 6.78 us -> 11.6 us  [scatter_slots(): lax.ppermute(slots[steps * rows:(steps + 1) * rows].astype(jnp.bfloat16),...]
    ppermute x2 -> x3, waiting for transfers between devices: 14.2 us -> 10.7 us  [the longest x1 10.7 us: two_level_reduce(): lax.ppermute(chip_sum.astype(jnp.bfloat16), 'head', partner)]
    ppermute x3, waiting for transfers between devices: 7.03 us -> 4.13 us  [gather_slots(): lax.ppermute(block, axis, shifted_pairs(count, steps))]
    ppermute x3, starting transfers between devices: 6.06 us -> 6.96 us  [gather_slots(): lax.ppermute(block, axis, shifted_pairs(count, steps))]
    convert_element_type x1 -> x0, other arithmetic: 0.9 us -> none  [head_reduce(): return current.reshape(block, -1).astype(jnp.bfloat16)]
    ppermute x2 -> x3, starting transfers between devices: 1.63 us -> 2.16 us  [the longest x1 1.55 us: two_level_reduce(): lax.ppermute(chip_sum.astype(jnp.bfloat16), 'head', partner)]
  transfers between devices with their start and end apart: 8 -> 9, of which waited for: 5 -> 4; matrix products, arithmetic and copies ran while one was open for 8% -> 16% of each run, Pallas kernels for 0% -> 0%
where the time goes in v10:
time: 72.3 us; the launch traced here: 71.6 us
  waiting for transfers between devices  26.4 us (37%)
  matrix products  14.5 us (20%)
  starting transfers between devices  14.2 us (20%)
  Pallas kernels  7.09 us (10%)
  other arithmetic  4.97 us (7%)
  local copies, waits for them, and re-layouts  3.77 us (5%)
  between operations  0.78 us (1%)
    ppermute x3, waiting for transfers between devices, scatter_slots(): lax.ppermute(slots[steps * rows:(steps + 1) * rows].astype(jnp.bfloat16),...  11.6 us
    ppermute x1, waiting for transfers between devices, two_level_reduce(): lax.ppermute(chip_sum.astype(jnp.bfloat16), 'head', partner)  10.7 us
    dot_general x4, matrix products, project(): lax.dot_general(lax.dynamic_slice_in_dim(key_proj, first, block, 0), key_...  7.83 us
    pallas_call x1, Pallas kernels, attention_block(): pl.pallas_call(attention_kernel, out_shape=(jax.ShapeDtypeStruct(queries....  7.09 us
    ppermute x3, starting transfers between devices, gather_slots(): lax.ppermute(block, axis, shifted_pairs(count, steps))  6.96 us
    dot_general x4, matrix products, project(): lax.dot_general(lax.dynamic_slice_in_dim(value_proj, first, block, 0), va...  6.62 us
    ppermute x3, starting transfers between devices, scatter_slots(): lax.ppermute(slots[steps * rows:(steps + 1) * rows].astype(jnp.bfloat16),...  5.04 us
    ppermute x3, waiting for transfers between devices, gather_slots(): lax.ppermute(block, axis, shifted_pairs(count, steps))  4.13 us
  transfers between devices with their start and end apart: 9, of which 4 were waited for; matrix products, arithmetic and copies ran while one was open for 16% of the time, Pallas kernels for 0%

profile of v10, /device:TPU:0, one launch (start us, length us, event | category | flops | bytes accessed | tf_op | source)
XLA Modules:
  0.0 71.6 jit_solution(6908117391755042435)
XLA Ops:
  0.6 0.8 %constant_dynamic-update-slice_fusion.1 = bf16[128,512]{1,0:T(8,128)(2,1)S(1)} fusion(bf16[128,256]{1,0:T(8,128)(2,1)} %param.9), kind=kLoop, calls=%fused_computation.24 | loop fusion | bytes 131072
  1.5 0.8 %constant_dynamic-update-slice_fusion = bf16[128,512]{1,0:T(8,128)(2,1)S(1)} fusion(bf16[128,512]{1,0:T(8,128)(2,1)S(1)} %constant_dynamic-update-slice_fusion.1, bf16[128,256]{1,0:T(8,128)(2,1)} %param.10), kind=kLoop, calls=%fused_computation.23 | loop fusion | bytes 131072 | tf_op jit(solution)/shard_map/concatenate | solution.py:217
  2.3 3.0 %collective-permute-start = (bf16[128,512]{1,0:T(8,128)(2,1)S(1)}, bf16[128,512]{1,0:T(8,128)(2,1)S(1)}, u32[]{:S(2)}, u32[]{:S(2)}) collective-permute-start(bf16[128,512]{1,0:T(8,128)(2,1)S(1)} %constant_dynamic-update-slice_fusion), channel_id=1, source_target_pairs={{0,4},{4,8},{8,12},{12,0},{1,5},{5,9},{9,13},{13,1},{2,6},{6,10},{... | collective-permute-start | bytes 393224 | tf_op jit(solution)/shard_map/ppermute | solution.py:42
  5.3 2.6 %collective-permute-start.1 = (bf16[128,512]{1,0:T(8,128)(2,1)S(1)}, bf16[128,512]{1,0:T(8,128)(2,1)S(1)}, u32[]{:S(2)}, u32[]{:S(2)}) collective-permute-start(bf16[128,512]{1,0:T(8,128)(2,1)S(1)} %constant_dynamic-update-slice_fusion), channel_id=1, source_target_pairs={{0,8},{4,12},{8,0},{12,4},{1,9},{5,13},{9,1},{13,5},{2,10},{6,14},... | collective-permute-start | bytes 393224 | tf_op jit(solution)/shard_map/ppermute | solution.py:42
  7.9 1.3 %collective-permute-start.2 = (bf16[128,512]{1,0:T(8,128)(2,1)S(1)}, bf16[128,512]{1,0:T(8,128)(2,1)S(1)}, u32[]{:S(2)}, u32[]{:S(2)}) collective-permute-start(bf16[128,512]{1,0:T(8,128)(2,1)S(1)} %constant_dynamic-update-slice_fusion), channel_id=1, source_target_pairs={{0,12},{4,0},{8,4},{12,8},{1,13},{5,1},{9,5},{13,9},{2,14},{6,2},{... | collective-permute-start | bytes 393224 | tf_op jit(solution)/shard_map/ppermute | solution.py:42
  9.3 1.2 %dynamic_slice.27 = s32[1]{0:T(128)} dynamic-slice(s32[4]{0:T(128)} %param.13, s32[]{:T(128)S(6)} %select_n.49), dynamic_slice_sizes={1} | dynamic-slice | bytes 12 | tf_op jit(solution)/shard_map/dynamic_slice | solution.py:211
  11.3 0.9 %multiply_reduce_fusion = (s32[4]{0:T(128)S(1)}, s32[4]{0:T(128)S(1)}) fusion(s32[4,4]{1,0:T(4,128)} %param.12, s32[4]{0:T(128)S(1)} %compare_convert_fusion.1, s32[4]{0:T(128)} %param.13, s32[4]{0:T(128)S(1)} %select_reduce_fusion.2), kind=kLoop, calls=%fused_computation.28 | loop fusion | flops 72 | bytes 144 | tf_op jit(solution)/shard_map/reduce_sum | solution.py:18
  12.4 4.1 %collective-permute-done.1 = bf16[128,512]{1,0:T(8,128)(2,1)S(1)} collective-permute-done((bf16[128,512]{1,0:T(8,128)(2,1)S(1)}, bf16[128,512]{1,0:T(8,128)(2,1)S(1)}, u32[]{:S(2)}, u32[]{:S(2)}) %collective-permute-start.1) | collective-permute-done | bytes 131104 | tf_op jit(solution)/shard_map/ppermute | solution.py:42
  18.1 7.1 %shard_map.111 = (bf16[128,2048]{1,0:T(8,128)(2,1)}, f32[512,512]{1,0:T(8,128)}) custom-call(bf16[128,2048]{1,0:T(8,128)(2,1)} %query_ref.1, bf16[128,2048]{1,0:T(8,128)(2,1)} %grad_ref.1, bf16[512,512]{1,0:T(8,128)(2,1)} %pad_maximum_fusion.kv_ref, s32[128,512]{1,0:T(8,128)} %broadcast_in_dim.5.mask_ref), custom_call_target="tpu_custom_call" | custom-call | tf_op jit(solution)/shard_map/pallas_call | solution.py:190
  25.2 1.3 %convert.9 = bf16[512,512]{1,0:T(8,128)(2,1)S(1)} convert(f32[512,512]{1,0:T(8,128)} %get-tuple-element.7) | non-fusion elementwise | flops 262144 | bytes 1572864 | tf_op jit(solution)/shard_map/convert.4
  26.5 4.4 %collective-permute-start.3 = (bf16[128,512]{1,0:T(8,128)(2,1)S(1)}, bf16[128,512]{1,0:T(8,128)(2,1)S(1)}, u32[]{:S(2)}, u32[]{:S(2)}) collective-permute-start(bf16[128,512]{1,0:T(8,128)(2,1)S(1)} %get-tuple-element.8), channel_id=1, source_target_pairs={{0,12},{4,0},{8,4},{12,8},{1,13},{5,1},{9,5},{13,9},{2,14},{6,2},{... | collective-permute-start | bytes 393224 | tf_op jit(solution)/shard_map/ppermute | solution.py:55
  31.6 3.3 %collective-permute-done.3 = bf16[128,512]{1,0:T(8,128)(2,1)S(1)} collective-permute-done((bf16[128,512]{1,0:T(8,128)(2,1)S(1)}, bf16[128,512]{1,0:T(8,128)(2,1)S(1)}, u32[]{:S(2)}, u32[]{:S(2)}) %collective-permute-start.3) | collective-permute-done | bytes 131104 | tf_op jit(solution)/shard_map/ppermute | solution.py:55
  34.9 8.3 %collective-permute-done.4 = bf16[128,512]{1,0:T(8,128)(2,1)S(1)} collective-permute-done((bf16[128,512]{1,0:T(8,128)(2,1)S(1)}, bf16[128,512]{1,0:T(8,128)(2,1)S(1)}, u32[]{:S(2)}, u32[]{:S(2)}) %collective-permute-start.4) | collective-permute-done | bytes 131104 | tf_op jit(solution)/shard_map/ppermute | solution.py:55
  43.2 1.0 %add_convert_fusion = bf16[128,512]{1,0:T(8,128)(2,1)S(1)} fusion(bf16[128,512]{1,0:T(8,128)(2,1)S(1)} %collective-permute-done.5, bf16[128,512]{1,0:T(8,128)(2,1)S(1)} %collective-permute-done.4, bf16[128,512]{1,0:T(8,128)(2,1)S(1)} %collective-permute-done.3, f32[512,512]{1,0:T(8,128)} %get-tuple-element.7), kind=kLoop, calls=%fused_computation.22 | loop fusion | flops 458752 | bytes 786432 | tf_op jit(solution)/shard_map/convert.1
  44.2 1.7 %fusion.5 = f32[2048,128]{1,0:T(8,128)S(1)} fusion(bf16[128,256]{1,0:T(8,128)(2,1)S(1)} %get-tuple-element.11, bf16[8192,256]{1,0:T(8,128)(2,1)} %param.15, s32[]{:T(128)S(6)} %select_n.55), kind=kOutput, calls=%fused_computation.9 | convolution fusion | flops 134217728 | bytes 2162692 | tf_op jit(solution)/shard_map/dot_general | solution.py:75
  45.9 1.7 %convolution_add_fusion = f32[2048,128]{1,0:T(8,128)S(1)} fusion(f32[2048,128]{1,0:T(8,128)S(1)} %fusion.5, bf16[128,256]{1,0:T(8,128)(2,1)S(1)} %get-tuple-element.12, bf16[8192,256]{1,0:T(8,128)(2,1)} %param.14, s32[]{:T(128)S(6)} %select_n.55), kind=kOutput, calls=%fused_computation | convolution fusion | flops 134479872 | bytes 3211268 | tf_op jit(solution)/shard_map/dot_general | solution.py:70
  47.7 1.6 %fusion.11 = f32[2048,128]{1,0:T(8,128)S(1)} fusion(bf16[128,256]{1,0:T(8,128)(2,1)S(1)} %get-tuple-element.11, bf16[8192,256]{1,0:T(8,128)(2,1)} %param.15, s32[]{:T(128)S(6)} %select_n.53), kind=kOutput, calls=%fused_computation.15 | convolution fusion | flops 134217728 | bytes 2162692 | tf_op jit(solution)/shard_map/dot_general | solution.py:75
  49.3 1.7 %convolution_add_fusion.2 = f32[2048,128]{1,0:T(8,128)S(1)} fusion(f32[2048,128]{1,0:T(8,128)S(1)} %fusion.11, bf16[128,256]{1,0:T(8,128)(2,1)S(1)} %get-tuple-element.12, bf16[8192,256]{1,0:T(8,128)(2,1)} %param.14, s32[]{:T(128)S(6)} %select_n.53), kind=kOutput, calls=%fused_computation.3 | convolution fusion | flops 134479872 | bytes 3211268 | tf_op jit(solution)/shard_map/dot_general | solution.py:70
  51.5 1.6 %fusion.8 = f32[2048,128]{1,0:T(8,128)S(1)} fusion(bf16[128,256]{1,0:T(8,128)(2,1)S(1)} %get-tuple-element.11, bf16[8192,256]{1,0:T(8,128)(2,1)} %param.15, s32[]{:T(128)S(6)} %select_n.54), kind=kOutput, calls=%fused_computation.12 | convolution fusion | flops 134217728 | bytes 2162692 | tf_op jit(solution)/shard_map/dot_general | solution.py:75
  53.2 2.0 %fusion.4 = bf16[2048,128]{1,0:T(8,128)(2,1)S(1)} fusion(f32[2048,128]{1,0:T(8,128)} %collective-permute-done.7, f32[2048,128]{1,0:T(8,128)S(1)} %fusion.8, bf16[128,256]{1,0:T(8,128)(2,1)S(1)} %get-tuple-element.12, bf16[8192,256]{1,0:T(8,128)(2,1)} %param.14, s32[]{:T(128)S(6)} %select_n.54), kind=kOutput, calls=%fused_computation.8 | convolution fusion | flops 135004160 | bytes 3735556 | tf_op jit(solution)/shard_map/dot_general | solution.py:70
  55.2 1.6 %collective-permute-start.8 = (bf16[2048,128]{1,0:T(8,128)(2,1)S(1)}, bf16[2048,128]{1,0:T(8,128)(2,1)S(1)}, u32[]{:S(2)}, u32[]{:S(2)}) collective-permute-start(bf16[2048,128]{1,0:T(8,128)(2,1)S(1)} %fusion.4), channel_id=1, source_target_pairs={{0,2},{1,3},{2,0},{3,1},{4,6},{5,7},{6,4},{7,5},{8,10},{9,11},{10,... | collective-permute-start | bytes 1572872 | tf_op jit(solution)/shard_map/ppermute | solution.py:86
  56.7 1.6 %fusion.14 = f32[2048,128]{1,0:T(8,128)S(1)} fusion(bf16[128,256]{1,0:T(8,128)(2,1)S(1)} %get-tuple-element.11, bf16[8192,256]{1,0:T(8,128)(2,1)} %param.15, s32[]{:T(128)S(6)} %select_n.52), kind=kOutput, calls=%fused_computation.18 | convolution fusion | flops 134217728 | bytes 2162692 | tf_op jit(solution)/shard_map/dot_general | solution.py:75
  58.4 10.7 %collective-permute-done.8 = bf16[2048,128]{1,0:T(8,128)(2,1)S(1)} collective-permute-done((bf16[2048,128]{1,0:T(8,128)(2,1)S(1)}, bf16[2048,128]{1,0:T(8,128)(2,1)S(1)}, u32[]{:S(2)}, u32[]{:S(2)}) %collective-permute-start.8) | collective-permute-done | bytes 524320 | tf_op jit(solution)/shard_map/ppermute | solution.py:86
  69.1 2.5 %fusion.3 = bf16[2048,128]{1,0:T(8,128)(2,1)} fusion(f32[2048,128]{1,0:T(8,128)S(1)} %collective-permute-done.6, f32[2048,128]{1,0:T(8,128)S(1)} %fusion.14, bf16[128,256]{1,0:T(8,128)(2,1)S(1)} %get-tuple-element.12, bf16[2048,128]{1,0:T(8,128)(2,1)S(1)} %collective-permute-done.8, bf16[8192,256]{1,0:T(8,128)(2,1)} %param.14, s32[]{:T(128)S(6)} %select_n.52), kind=kOutput, calls=%fused_computation.7 | convolution fusion | flops 135528448 | bytes 4259844 | tf_op jit(solution)/shard_map/dot_general | solution.py:70
  (23 shorter events, 3.9 us)
Async XLA Ops:
  2.3 10.1 %collective-permute-start = (bf16[128,512]{1,0:T(8,128)(2,1)S(1)}, bf16[128,512]{1,0:T(8,128)(2,1)S(1)}, u32[]{:S(2)}, u32[]{:S(2)}) collective-permute-start(bf16[128,512]{1,0:T(8,128)(2,1)S(1)} %constant_dynamic-update-slice_fusion), channel_id=1, source_target_pairs={{0,4},{4,8},{8,12},{12,0},{1,5},{5,9},{9,13},{13,1},{2,6},{6,10},{... | collective-permute-start | bytes 393224 | tf_op jit(solution)/shard_map/ppermute | solution.py:42
  5.3 11.2 %collective-permute-start.1 = (bf16[128,512]{1,0:T(8,128)(2,1)S(1)}, bf16[128,512]{1,0:T(8,128)(2,1)S(1)}, u32[]{:S(2)}, u32[]{:S(2)}) collective-permute-start(bf16[128,512]{1,0:T(8,128)(2,1)S(1)} %constant_dynamic-update-slice_fusion), channel_id=1, source_target_pairs={{0,8},{4,12},{8,0},{12,4},{1,9},{5,13},{9,1},{13,5},{2,10},{6,14},... | collective-permute-start | bytes 393224 | tf_op jit(solution)/shard_map/ppermute | solution.py:42
  7.9 8.6 %collective-permute-start.2 = (bf16[128,512]{1,0:T(8,128)(2,1)S(1)}, bf16[128,512]{1,0:T(8,128)(2,1)S(1)}, u32[]{:S(2)}, u32[]{:S(2)}) collective-permute-start(bf16[128,512]{1,0:T(8,128)(2,1)S(1)} %constant_dynamic-update-slice_fusion), channel_id=1, source_target_pairs={{0,12},{4,0},{8,4},{12,8},{1,13},{5,1},{9,5},{13,9},{2,14},{6,2},{... | collective-permute-start | bytes 393224 | tf_op jit(solution)/shard_map/ppermute | solution.py:42
  26.5 8.3 %collective-permute-start.3 = (bf16[128,512]{1,0:T(8,128)(2,1)S(1)}, bf16[128,512]{1,0:T(8,128)(2,1)S(1)}, u32[]{:S(2)}, u32[]{:S(2)}) collective-permute-start(bf16[128,512]{1,0:T(8,128)(2,1)S(1)} %get-tuple-element.8), channel_id=1, source_target_pairs={{0,12},{4,0},{8,4},{12,8},{1,13},{5,1},{9,5},{13,9},{2,14},{6,2},{... | collective-permute-start | bytes 393224 | tf_op jit(solution)/shard_map/ppermute | solution.py:55
  30.9 12.2 %collective-permute-start.4 = (bf16[128,512]{1,0:T(8,128)(2,1)S(1)}, bf16[128,512]{1,0:T(8,128)(2,1)S(1)}, u32[]{:S(2)}, u32[]{:S(2)}) collective-permute-start(bf16[128,512]{1,0:T(8,128)(2,1)S(1)} %get-tuple-element.10), channel_id=1, source_target_pairs={{0,8},{4,12},{8,0},{12,4},{1,9},{5,13},{9,1},{13,5},{2,10},{6,14},... | collective-permute-start | bytes 393224 | tf_op jit(solution)/shard_map/ppermute | solution.py:55
  31.3 11.8 %collective-permute-start.5 = (bf16[128,512]{1,0:T(8,128)(2,1)S(1)}, bf16[128,512]{1,0:T(8,128)(2,1)S(1)}, u32[]{:S(2)}, u32[]{:S(2)}) collective-permute-start(bf16[128,512]{1,0:T(8,128)(2,1)S(1)} %get-tuple-element.9), channel_id=1, source_target_pairs={{0,4},{4,8},{8,12},{12,0},{1,5},{5,9},{9,13},{13,1},{2,6},{6,10},{... | collective-permute-start | bytes 393224 | tf_op jit(solution)/shard_map/ppermute | solution.py:55
  44.2 12.5 %copy-start.1 = (bf16[128,256]{1,0:T(8,128)(2,1)}, bf16[128,256]{1,0:T(8,128)(2,1)S(1)}, u32[]{:S(2)}) copy-start(bf16[128,256]{1,0:T(8,128)(2,1)S(1)} %get-tuple-element.11) | copy-start | bytes 196612
  44.2 24.9 %copy-start = (bf16[128,256]{1,0:T(8,128)(2,1)}, bf16[128,256]{1,0:T(8,128)(2,1)S(1)}, u32[]{:S(2)}) copy-start(bf16[128,256]{1,0:T(8,128)(2,1)S(1)} %get-tuple-element.12) | copy-start | bytes 196612
  47.6 5.6 %collective-permute-start.7 = (f32[2048,128]{1,0:T(8,128)S(1)}, f32[2048,128]{1,0:T(8,128)}, u32[]{:S(2)}, u32[]{:S(2)}) collective-permute-start(f32[2048,128]{1,0:T(8,128)S(1)} %convolution_add_fusion), channel_id=1, source_target_pairs={{0,1},{1,0},{2,3},{3,2},{4,5},{5,4},{6,7},{7,6},{8,9},{9,8},{10,11... | collective-permute-start | bytes 3145736 | tf_op jit(solution)/shard_map/ppermute | solution.py:84
  51.0 7.4 %collective-permute-start.6 = (f32[2048,128]{1,0:T(8,128)S(1)}, f32[2048,128]{1,0:T(8,128)S(1)}, u32[]{:S(2)}, u32[]{:S(2)}) collective-permute-start(f32[2048,128]{1,0:T(8,128)S(1)} %convolution_add_fusion.2), channel_id=1, source_target_pairs={{0,1},{1,0},{2,3},{3,2},{4,5},{5,4},{6,7},{7,6},{8,9},{9,8},{10,11... | collective-permute-start | bytes 3145736 | tf_op jit(solution)/shard_map/ppermute | solution.py:87
  55.2 13.9 %collective-permute-start.8 = (bf16[2048,128]{1,0:T(8,128)(2,1)S(1)}, bf16[2048,128]{1,0:T(8,128)(2,1)S(1)}, u32[]{:S(2)}, u32[]{:S(2)}) collective-permute-start(bf16[2048,128]{1,0:T(8,128)(2,1)S(1)} %fusion.4), channel_id=1, source_target_pairs={{0,2},{1,3},{2,0},{3,1},{4,6},{5,7},{6,4},{7,5},{8,10},{9,11},{10,... | collective-permute-start | bytes 1572872 | tf_op jit(solution)/shard_map/ppermute | solution.py:86

commit v11 on v9

--- a/solution.py
+++ b/solution.py
@@ -60,6 +60,17 @@
     return total
 
 
+def scatter_parts(own, sent, axis):
+    count = lax.axis_size(axis)
+    rows = own.shape[0]
+    total = own
+    for steps in range(1, count):
+        total = total + lax.ppermute(
+            sent[(steps - 1) * rows : steps * rows], axis, shifted_pairs(count, -steps)
+        ).astype(jnp.float32)
+    return total
+
+
 def head_reduce(key_proj, value_proj, key_grad, value_grad):
     count = lax.axis_size("head")
     position = lax.axis_index("head")
@@ -105,13 +116,16 @@
     return current.reshape(block, -1).astype(jnp.bfloat16)
 
 
-def attention_kernel(query_ref, grad_ref, kv_ref, mask_ref, query_out, kv_out):
+def attention_kernel(query_ref, grad_ref, kv_ref, mask_ref, query_out, own_out, sent_out):
     inv_root = HD ** (-0.5)
     kv_cols = kv_ref.shape[1] // 2
     kv_heads = kv_cols // HD
     rows = query_ref.shape[0]
     group_size = query_ref.shape[1] // kv_cols
-    allowed = jnp.concatenate([mask_ref[...]] * group_size, axis=0) > 0
+    if mask_ref.shape[0] == 1:
+        allowed = mask_ref[...] > 0
+    else:
+        allowed = jnp.concatenate([mask_ref[...]] * group_size, axis=0) > 0
     across = (((1,), (1,)), ((), ()))
     down = (((0,), (0,)), ((), ()))
     for kv_head in range(kv_heads):
@@ -151,16 +165,23 @@
         value_sum = lax.dot_general(
             probs.astype(jnp.bfloat16), grad_stack, down, preferred_element_type=jnp.float32
         )
-        kv_out[:, kv_head * HD : (kv_head + 1) * HD] = key_sum * inv_root
-        kv_out[:, kv_cols + kv_head * HD : kv_cols + (kv_head + 1) * HD] = value_sum
+        key_sum = key_sum * inv_root
+        key_cols = slice(kv_head * HD, (kv_head + 1) * HD)
+        value_cols = slice(kv_cols + kv_head * HD, kv_cols + (kv_head + 1) * HD)
+        own_out[:, key_cols] = key_sum[:rows]
+        own_out[:, value_cols] = value_sum[:rows]
+        sent_out[:, key_cols] = key_sum[rows:].astype(jnp.bfloat16)
+        sent_out[:, value_cols] = value_sum[rows:].astype(jnp.bfloat16)
 
 
 def attention_block(queries, out_grad, kv_rows, allowed, interpret=False):
+    rows = queries.shape[0]
     return pl.pallas_call(
         attention_kernel,
         out_shape=(
             jax.ShapeDtypeStruct(queries.shape, jnp.bfloat16),
-            jax.ShapeDtypeStruct(kv_rows.shape, jnp.float32),
+            jax.ShapeDtypeStruct((rows, kv_rows.shape[1]), jnp.float32),
+            jax.ShapeDtypeStruct((kv_rows.shape[0] - rows, kv_rows.shape[1]), jnp.bfloat16),
         ),
         interpret=interpret,
     )(queries, out_grad, kv_rows, allowed.astype(jnp.int32))
@@ -250,9 +271,14 @@
         )
         return query_term, kv_term
 
-    if steps == 1:
-        allowed = chunk(0)[2]
-        query_grad, kv_acc = attention_block(queries, out_grad, kv_rows, allowed)
+    if steps == 1 and lax.axis_size("ctx") <= 8:
+        if rows_here == BLK:
+            column_flags = select_cols(own_flags, key_doc_blocks) > 0
+            allowed = jnp.repeat(column_flags, BLK, axis=1)
+        else:
+            allowed = chunk(0)[2]
+        query_grad, own_part, sent_part = attention_block(queries, out_grad, kv_rows, allowed)
+        kv_grad = scatter_parts(own_part, sent_part, "ctx")
     else:
         start_stats = (
             jnp.full((kv_heads, group_size, rows_here), masked_score, jnp.float32),
@@ -285,8 +311,8 @@
             ),
         )
         query_grad = query_acc.reshape(rows_here, -1).astype(jnp.bfloat16)
-
-    kv_grad = scatter_slots(kv_acc, "ctx")
+        kv_grad = scatter_slots(kv_acc, "ctx")
+
     key_grad = kv_grad[:, :kv_cols].astype(jnp.bfloat16)
     value_grad = kv_grad[:, kv_cols:].astype(jnp.bfloat16)
     input_grad_t = head_reduce(key_proj, value_proj, key_grad, value_grad)

time: 67.6 us -> 66.9 us (0.990)
  other arithmetic: 5.87 us -> 4.58 us
  local copies, waits for them, and re-layouts: 4.24 us -> 5.13 us
    another operation x2 -> x1, other arithmetic: 2.3 us -> 1.01 us
    slice x1, local copies, waits for them, and re-layouts: 0.03 us -> 1.06 us  [scatter_parts(): sent[(steps - 1) * rows:steps * rows]]
where the time goes in v11:
time: 66.9 us; the launch traced here: 66.5 us
  waiting for transfers between devices  28.1 us (42%)
  starting transfers between devices  13.3 us (20%)
  matrix products  7.91 us (12%)
  Pallas kernels  6.69 us (10%)
  local copies, waits for them, and re-layouts  5.13 us (8%)
  other arithmetic  4.58 us (7%)
  between operations  0.8 us (1%)
    ppermute x1, waiting for transfers between devices, head_reduce(): lax.ppermute(sent.astype(jnp.bfloat16), 'head', [(i, i ^ 1 << level) for...  12.5 us
    ppermute x3, waiting for transfers between devices, gather_slots(): lax.ppermute(block, axis, shifted_pairs(count, steps))  7.1 us
    ppermute x3, waiting for transfers between devices, scatter_parts(): lax.ppermute(sent[(steps - 1) * rows:steps * rows], axis, shifted_pairs(c...  6.78 us
    pallas_call x1, Pallas kernels, attention_block(): pl.pallas_call(attention_kernel, out_shape=(jax.ShapeDtypeStruct(queries....  6.69 us
    ppermute x3, starting transfers between devices, gather_slots(): lax.ppermute(block, axis, shifted_pairs(count, steps))  6.06 us
    ppermute x3, starting transfers between devices, scatter_parts(): lax.ppermute(sent[(steps - 1) * rows:steps * rows], axis, shifted_pairs(c...  5.6 us
    dot_general x2, matrix products, project(): jnp.einsum('arf,tf->art', lax.dynamic_index_in_dim(key_split, half, 1, ke...  4.88 us
    dot_general x2, matrix products, project(): jnp.einsum('arf,tf->art', lax.dynamic_index_in_dim(value_split, half, 1,...  3.03 us
  transfers between devices with their start and end apart: 8, of which 5 were waited for; matrix products, arithmetic and copies ran while one was open for 8% of the time, Pallas kernels for 0%

profile of v11, /device:TPU:0, one launch (start us, length us, event | category | flops | bytes accessed | tf_op | source)
XLA Modules:
  0.0 66.5 jit_solution(9834493933735678421)
XLA Ops:
  0.6 0.8 %constant_dynamic-update-slice_fusion.1 = bf16[128,512]{1,0:T(8,128)(2,1)S(1)} fusion(bf16[128,256]{1,0:T(8,128)(2,1)} %param.9), kind=kLoop, calls=%fused_computation.23 | loop fusion | bytes 131072
  1.5 0.8 %constant_dynamic-update-slice_fusion = bf16[128,512]{1,0:T(8,128)(2,1)S(1)} fusion(bf16[128,512]{1,0:T(8,128)(2,1)S(1)} %constant_dynamic-update-slice_fusion.1, bf16[128,256]{1,0:T(8,128)(2,1)} %param.10), kind=kLoop, calls=%fused_computation.22 | loop fusion | bytes 131072 | tf_op jit(solution)/shard_map/concatenate | solution.py:207
  2.3 5.0 %collective-permute-start.2 = (bf16[128,512]{1,0:T(8,128)(2,1)S(1)}, bf16[128,512]{1,0:T(8,128)(2,1)S(1)}, u32[]{:S(2)}, u32[]{:S(2)}) collective-permute-start(bf16[128,512]{1,0:T(8,128)(2,1)S(1)} %constant_dynamic-update-slice_fusion), channel_id=1, source_target_pairs={{0,12},{4,0},{8,4},{12,8},{1,13},{5,1},{9,5},{13,9},{2,14},{6,2},{... | collective-permute-start | bytes 393224 | tf_op jit(solution)/shard_map/ppermute | solution.py:42
  7.4 1.0 %collective-permute-start = (bf16[128,512]{1,0:T(8,128)(2,1)S(1)}, bf16[128,512]{1,0:T(8,128)(2,1)S(1)}, u32[]{:S(2)}, u32[]{:S(2)}) collective-permute-start(bf16[128,512]{1,0:T(8,128)(2,1)S(1)} %constant_dynamic-update-slice_fusion), channel_id=1, source_target_pairs={{0,4},{4,8},{8,12},{12,0},{1,5},{5,9},{9,13},{13,1},{2,6},{6,10},{... | collective-permute-start | bytes 393224 | tf_op jit(solution)/shard_map/ppermute | solution.py:42
  8.4 1.2 %dynamic_slice.19 = s32[1]{0:T(128)} dynamic-slice(s32[4]{0:T(128)} %param.13, s32[]{:T(128)S(6)} %select_n.53), dynamic_slice_sizes={1} | dynamic-slice | bytes 12 | tf_op jit(solution)/shard_map/dynamic_slice | solution.py:201
  10.4 0.9 %multiply_reduce_fusion = (s32[4]{0:T(128)S(1)}, s32[4]{0:T(128)S(1)}) fusion(s32[4,4]{1,0:T(4,128)} %param.12, s32[4]{0:T(128)S(1)} %compare_convert_fusion.1, s32[4]{0:T(128)} %param.13, s32[4]{0:T(128)S(1)} %select_reduce_fusion.2), kind=kLoop, calls=%fused_computation.27 | loop fusion | flops 72 | bytes 144 | tf_op jit(solution)/shard_map/reduce_sum | solution.py:18
  11.5 7.1 %collective-permute-done.1 = bf16[128,512]{1,0:T(8,128)(2,1)S(1)} collective-permute-done((bf16[128,512]{1,0:T(8,128)(2,1)S(1)}, bf16[128,512]{1,0:T(8,128)(2,1)S(1)}, u32[]{:S(2)}, u32[]{:S(2)}) %collective-permute-start.1) | collective-permute-done | bytes 131104 | tf_op jit(solution)/shard_map/ppermute | solution.py:42
  18.6 0.8 %pad_maximum_fusion.kv_ref = bf16[512,512]{1,0:T(8,128)(2,1)} fusion(bf16[128,512]{1,0:T(8,128)(2,1)S(1)} %collective-permute-done.2, bf16[128,512]{1,0:T(8,128)(2,1)S(1)} %collective-permute-done.1, bf16[128,512]{1,0:T(8,128)(2,1)S(1)} %collective-permute-done, bf16[128,512]{1,0:T(8,128)(2,1)S(1)} %constant_dynamic-update-slice_fusion), kind=kLoop, calls=%fused_computation.16 | loop fusion | flops 2097152 | bytes 1048576 | tf_op jit(solution)/shard_map/concatenate | solution.py:45
  20.1 6.7 %shard_map.111 = (bf16[128,2048]{1,0:T(8,128)(2,1)}, f32[128,512]{1,0:T(8,128)}, bf16[384,512]{1,0:T(8,128)(2,1)}) custom-call(bf16[128,2048]{1,0:T(8,128)(2,1)} %query_ref.1, bf16[128,2048]{1,0:T(8,128)(2,1)} %grad_ref.1, bf16[512,512]{1,0:T(8,128)(2,1)} %pad_maximum_fusion.kv_ref, s32[1,512]{1,0:T(1,128)} %bitcast.40), custom_call_target="tpu_custom_call" | custom-call | tf_op jit(solution)/shard_map/pallas_call | solution.py:179
  26.7 1.1 %fusion.21 = (bf16[128,512]{1,0:T(8,128)(2,1)S(1)}, bf16[128,512]{1,0:T(8,128)(2,1)S(1)}, bf16[128,512]{1,0:T(8,128)(2,1)S(1)}) fusion(bf16[384,512]{1,0:T(8,128)(2,1)} %get-tuple-element.9), kind=kLoop, calls=%fused_computation.41 | loop fusion | bytes 786432 | tf_op jit(solution)/shard_map/slice | solution.py:69
  27.8 0.8 %collective-permute-start.5 = (bf16[128,512]{1,0:T(8,128)(2,1)S(1)}, bf16[128,512]{1,0:T(8,128)(2,1)S(1)}, u32[]{:S(2)}, u32[]{:S(2)}) collective-permute-start(bf16[128,512]{1,0:T(8,128)(2,1)S(1)} %get-tuple-element.11), channel_id=1, source_target_pairs={{0,4},{4,8},{8,12},{12,0},{1,5},{5,9},{9,13},{13,1},{2,6},{6,10},{... | collective-permute-start | bytes 393224 | tf_op jit(solution)/shard_map/ppermute | solution.py:68
  28.6 2.0 %collective-permute-start.4 = (bf16[128,512]{1,0:T(8,128)(2,1)S(1)}, bf16[128,512]{1,0:T(8,128)(2,1)S(1)}, u32[]{:S(2)}, u32[]{:S(2)}) collective-permute-start(bf16[128,512]{1,0:T(8,128)(2,1)S(1)} %get-tuple-element.12), channel_id=1, source_target_pairs={{0,8},{4,12},{8,0},{12,4},{1,9},{5,13},{9,1},{13,5},{2,10},{6,14},... | collective-permute-start | bytes 393224 | tf_op jit(solution)/shard_map/ppermute | solution.py:68
  30.6 2.8 %collective-permute-start.3 = (bf16[128,512]{1,0:T(8,128)(2,1)S(1)}, bf16[128,512]{1,0:T(8,128)(2,1)S(1)}, u32[]{:S(2)}, u32[]{:S(2)}) collective-permute-start(bf16[128,512]{1,0:T(8,128)(2,1)S(1)} %get-tuple-element.10), channel_id=1, source_target_pairs={{0,12},{4,0},{8,4},{12,8},{1,13},{5,1},{9,5},{13,9},{2,14},{6,2},{... | collective-permute-start | bytes 393224 | tf_op jit(solution)/shard_map/ppermute | solution.py:68
  33.4 2.7 %collective-permute-done.5 = bf16[128,512]{1,0:T(8,128)(2,1)S(1)} collective-permute-done((bf16[128,512]{1,0:T(8,128)(2,1)S(1)}, bf16[128,512]{1,0:T(8,128)(2,1)S(1)}, u32[]{:S(2)}, u32[]{:S(2)}) %collective-permute-start.5) | collective-permute-done | bytes 131104 | tf_op jit(solution)/shard_map/ppermute | solution.py:68
  36.1 4.0 %collective-permute-done.4 = bf16[128,512]{1,0:T(8,128)(2,1)S(1)} collective-permute-done((bf16[128,512]{1,0:T(8,128)(2,1)S(1)}, bf16[128,512]{1,0:T(8,128)(2,1)S(1)}, u32[]{:S(2)}, u32[]{:S(2)}) %collective-permute-start.4) | collective-permute-done | bytes 131104 | tf_op jit(solution)/shard_map/ppermute | solution.py:68
  40.2 1.0 %add_convert_fusion.1 = bf16[128,512]{1,0:T(8,128)(2,1)S(1)} fusion(bf16[128,512]{1,0:T(8,128)(2,1)S(1)} %collective-permute-done.5, bf16[128,512]{1,0:T(8,128)(2,1)S(1)} %collective-permute-done.4, f32[128,512]{1,0:T(8,128)} %get-tuple-element.8, bf16[128,512]{1,0:T(8,128)(2,1)S(1)} %collective-permute-done.3), kind=kLoop, calls=%fused_computation.17 | loop fusion | flops 458752 | bytes 786432 | tf_op jit(solution)/shard_map/convert.1
  41.3 2.4 %fusion.2 = f32[2,2048,128]{2,1,0:T(8,128)S(1)} fusion(bf16[2,2,2048,256]{3,2,1,0:T(8,128)(2,1)} %bitcast.36, s32[]{:T(128)S(6)} %select_n.56, bf16[128,256]{1,0:T(8,128)(2,1)S(1)} %get-tuple-element.14), kind=kOutput, calls=%fused_computation.4 | convolution fusion | flops 268435456 | bytes 4259844 | tf_op jit(solution)/shard_map/arf,tf->art/dot_general | solution.py:91
  44.1 0.7 %convolution_add_fusion = f32[2,2048,128]{2,1,0:T(8,128)S(1)} fusion(f32[2,2048,128]{2,1,0:T(8,128)S(1)} %fusion.2, bf16[2,2,2048,256]{3,2,1,0:T(8,128)(2,1)S(1)} %bitcast.38, s32[]{:T(128)S(6)} %select_n.56, bf16[128,256]{1,0:T(8,128)(2,1)S(1)} %get-tuple-element.13), kind=kOutput, calls=%fused_computation | convolution fusion | flops 268959744 | bytes 6356996 | tf_op jit(solution)/shard_map/arf,tf->art/dot_general | solution.py:96
  45.0 2.4 %fusion.5 = f32[2,2048,128]{2,1,0:T(8,128)S(1)} fusion(bf16[2,2,2048,256]{3,2,1,0:T(8,128)(2,1)} %bitcast.37, s32[]{:T(128)S(6)} %select_n.55, bf16[128,256]{1,0:T(8,128)(2,1)S(1)} %get-tuple-element.14), kind=kOutput, calls=%fused_computation.7 | convolution fusion | flops 268435456 | bytes 4259844 | tf_op jit(solution)/shard_map/arf,tf->art/dot_general | solution.py:91
  47.4 1.8 %collective-permute-done.6 = f32[2,2048,128]{2,1,0:T(8,128)} collective-permute-done((f32[2,2048,128]{2,1,0:T(8,128)S(1)}, f32[2,2048,128]{2,1,0:T(8,128)}, u32[]{:S(2)}, u32[]{:S(2)}) %collective-permute-start.6) | collective-permute-done | bytes 2097184 | tf_op jit(solution)/shard_map/ppermute | solution.py:106
  49.2 2.3 %fusion = f32[2,2048,128]{2,1,0:T(8,128)S(1)} fusion(f32[2,2048,128]{2,1,0:T(8,128)} %collective-permute-done.6, f32[2,2048,128]{2,1,0:T(8,128)S(1)} %fusion.5, bf16[2,2,2048,256]{3,2,1,0:T(8,128)(2,1)S(1)} %bitcast.39, s32[]{:T(128)S(6)} %select_n.55, bf16[128,256]{1,0:T(8,128)(2,1)S(1)} %get-tuple-element.13), kind=kOutput, calls=%fused_computation.2 | convolution fusion | flops 269484032 | bytes 8454148 | tf_op jit(solution)/shard_map/arf,tf->art/dot_general | solution.py:96
  51.6 1.6 %collective-permute-start.7 = (bf16[1,2048,128]{2,1,0:T(8,128)(2,1)S(1)}, bf16[1,2048,128]{2,1,0:T(8,128)(2,1)S(1)}, u32[]{:S(2)}, u32[]{:S(2)}) collective-permute-start(bf16[1,2048,128]{2,1,0:T(8,128)(2,1)S(1)} %dynamic-slice_convert_fusion), channel_id=1, source_target_pairs={{0,2},{1,3},{2,0},{3,1},{4,6},{5,7},{6,4},{7,5},{8,10},{9,11},{10,... | collective-permute-start | bytes 1572872 | tf_op jit(solution)/shard_map/ppermute | solution.py:112
  53.1 12.5 %collective-permute-done.7 = bf16[1,2048,128]{2,1,0:T(8,128)(2,1)S(1)} collective-permute-done((bf16[1,2048,128]{2,1,0:T(8,128)(2,1)S(1)}, bf16[1,2048,128]{2,1,0:T(8,128)(2,1)S(1)}, u32[]{:S(2)}, u32[]{:S(2)}) %collective-permute-start.7) | collective-permute-done | bytes 524320 | tf_op jit(solution)/shard_map/ppermute | solution.py:112
  65.6 0.9 %fusion.11 = bf16[2048,128]{1,0:T(8,128)(2,1)} fusion(bf16[1,2048,128]{2,1,0:T(8,128)(2,1)S(1)} %collective-permute-done.7, f32[2,2048,128]{2,1,0:T(8,128)S(1)} %fusion, s32[]{:T(128)S(6)} %select_n.59), kind=kLoop, calls=%fused_computation.15 | loop fusion | flops 786432 | bytes 2097156 | tf_op jit(solution)/shard_map/convert_element_type | solution.py:116
  (21 shorter events, 2.2 us)
Async XLA Ops:
  2.3 9.2 %collective-permute-start.2 = (bf16[128,512]{1,0:T(8,128)(2,1)S(1)}, bf16[128,512]{1,0:T(8,128)(2,1)S(1)}, u32[]{:S(2)}, u32[]{:S(2)}) collective-permute-start(bf16[128,512]{1,0:T(8,128)(2,1)S(1)} %constant_dynamic-update-slice_fusion), channel_id=1, source_target_pairs={{0,12},{4,0},{8,4},{12,8},{1,13},{5,1},{9,5},{13,9},{2,14},{6,2},{... | collective-permute-start | bytes 393224 | tf_op jit(solution)/shard_map/ppermute | solution.py:42
  7.4 11.2 %collective-permute-start.1 = (bf16[128,512]{1,0:T(8,128)(2,1)S(1)}, bf16[128,512]{1,0:T(8,128)(2,1)S(1)}, u32[]{:S(2)}, u32[]{:S(2)}) collective-permute-start(bf16[128,512]{1,0:T(8,128)(2,1)S(1)} %constant_dynamic-update-slice_fusion), channel_id=1, source_target_pairs={{0,8},{4,12},{8,0},{12,4},{1,9},{5,13},{9,1},{13,5},{2,10},{6,14},... | collective-permute-start | bytes 393224 | tf_op jit(solution)/shard_map/ppermute | solution.py:42
  7.4 11.2 %collective-permute-start = (bf16[128,512]{1,0:T(8,128)(2,1)S(1)}, bf16[128,512]{1,0:T(8,128)(2,1)S(1)}, u32[]{:S(2)}, u32[]{:S(2)}) collective-permute-start(bf16[128,512]{1,0:T(8,128)(2,1)S(1)} %constant_dynamic-update-slice_fusion), channel_id=1, source_target_pairs={{0,4},{4,8},{8,12},{12,0},{1,5},{5,9},{9,13},{13,1},{2,6},{6,10},{... | collective-permute-start | bytes 393224 | tf_op jit(solution)/shard_map/ppermute | solution.py:42
  27.8 8.3 %collective-permute-start.5 = (bf16[128,512]{1,0:T(8,128)(2,1)S(1)}, bf16[128,512]{1,0:T(8,128)(2,1)S(1)}, u32[]{:S(2)}, u32[]{:S(2)}) collective-permute-start(bf16[128,512]{1,0:T(8,128)(2,1)S(1)} %get-tuple-element.11), channel_id=1, source_target_pairs={{0,4},{4,8},{8,12},{12,0},{1,5},{5,9},{9,13},{13,1},{2,6},{6,10},{... | collective-permute-start | bytes 393224 | tf_op jit(solution)/shard_map/ppermute | solution.py:68
  28.6 11.6 %collective-permute-start.4 = (bf16[128,512]{1,0:T(8,128)(2,1)S(1)}, bf16[128,512]{1,0:T(8,128)(2,1)S(1)}, u32[]{:S(2)}, u32[]{:S(2)}) collective-permute-start(bf16[128,512]{1,0:T(8,128)(2,1)S(1)} %get-tuple-element.12), channel_id=1, source_target_pairs={{0,8},{4,12},{8,0},{12,4},{1,9},{5,13},{9,1},{13,5},{2,10},{6,14},... | collective-permute-start | bytes 393224 | tf_op jit(solution)/shard_map/ppermute | solution.py:68
  30.6 9.6 %collective-permute-start.3 = (bf16[128,512]{1,0:T(8,128)(2,1)S(1)}, bf16[128,512]{1,0:T(8,128)(2,1)S(1)}, u32[]{:S(2)}, u32[]{:S(2)}) collective-permute-start(bf16[128,512]{1,0:T(8,128)(2,1)S(1)} %get-tuple-element.10), channel_id=1, source_target_pairs={{0,12},{4,0},{8,4},{12,8},{1,13},{5,1},{9,5},{13,9},{2,14},{6,2},{... | collective-permute-start | bytes 393224 | tf_op jit(solution)/shard_map/ppermute | solution.py:68
  41.2 3.7 %copy-start.3 = (bf16[128,256]{1,0:T(8,128)(2,1)}, bf16[128,256]{1,0:T(8,128)(2,1)S(1)}, u32[]{:S(2)}) copy-start(bf16[128,256]{1,0:T(8,128)(2,1)S(1)} %get-tuple-element.14) | copy-start | bytes 196612
  41.2 7.9 %copy-start.2 = (bf16[128,256]{1,0:T(8,128)(2,1)}, bf16[128,256]{1,0:T(8,128)(2,1)S(1)}, u32[]{:S(2)}) copy-start(bf16[128,256]{1,0:T(8,128)(2,1)S(1)} %get-tuple-element.13) | copy-start | bytes 196612
  41.2 2.9 %copy-start = (bf16[8192,256]{1,0:T(8,128)(2,1)S(1)}, bf16[8192,256]{1,0:T(8,128)(2,1)}, u32[]{:S(2)}) copy-start(bf16[8192,256]{1,0:T(8,128)(2,1)} %param.15) | copy-start | bytes 12582916
  44.8 4.4 %collective-permute-start.6 = (f32[2,2048,128]{2,1,0:T(8,128)S(1)}, f32[2,2048,128]{2,1,0:T(8,128)}, u32[]{:S(2)}, u32[]{:S(2)}) collective-permute-start(f32[2,2048,128]{2,1,0:T(8,128)S(1)} %convolution_add_fusion), channel_id=1, source_target_pairs={{0,1},{1,0},{2,3},{3,2},{4,5},{5,4},{6,7},{7,6},{8,9},{9,8},{10,11... | collective-permute-start | bytes 6291464 | tf_op jit(solution)/shard_map/ppermute | solution.py:106
  44.9 4.2 %copy-start.1 = (bf16[8192,256]{1,0:T(8,128)(2,1)S(1)}, bf16[8192,256]{1,0:T(8,128)(2,1)}, u32[]{:S(2)}) copy-start(bf16[8192,256]{1,0:T(8,128)(2,1)} %param.15) | copy-start | bytes 12582916
  51.6 14.0 %collective-permute-start.7 = (bf16[1,2048,128]{2,1,0:T(8,128)(2,1)S(1)}, bf16[1,2048,128]{2,1,0:T(8,128)(2,1)S(1)}, u32[]{:S(2)}, u32[]{:S(2)}) collective-permute-start(bf16[1,2048,128]{2,1,0:T(8,128)(2,1)S(1)} %dynamic-slice_convert_fusion), channel_id=1, source_target_pairs={{0,2},{1,3},{2,0},{3,1},{4,6},{5,7},{6,4},{7,5},{8,10},{9,11},{10,... | collective-permute-start | bytes 1572872 | tf_op jit(solution)/shard_map/ppermute | solution.py:112

commit v12 on v11

--- a/solution.py
+++ b/solution.py
@@ -103,7 +103,9 @@
     own_bit = position % 2
     sent = project(1 - own_bit)
     kept = project(own_bit)
-    current = kept + lax.ppermute(sent, "head", [(i, i ^ 1) for i in range(count)])
+    current = kept + lax.ppermute(
+        sent.astype(jnp.bfloat16), "head", [(i, i ^ 1) for i in range(count)]
+    ).astype(jnp.float32)
     for level in range(1, depth):
         current = current.reshape(-1, 2, block, current.shape[-1])
         own_bit = (position // (1 << level)) % 2

time: 66.9 us -> 65.8 us (0.984)
  matrix products: 7.91 us -> 6.34 us
  waiting for transfers between devices: 28.1 us -> 29.3 us
  starting transfers between devices: 13.3 us -> 12.4 us
    ppermute x3, waiting for transfers between devices: 6.78 us -> 9.35 us  [scatter_parts(): lax.ppermute(sent[(steps - 1) * rows:steps * rows], axis, shifted_pairs(c...]
    ppermute x1, waiting for transfers between devices: 1.76 us -> 0.13 us  [head_reduce(): lax.ppermute(sent.astype(jnp.bfloat16), 'head', [(i, i ^ 1) for i in rang...]
    dot_general x2, matrix products: 3.03 us -> 1.45 us  [project(): jnp.einsum('arf,tf->art', lax.dynamic_index_in_dim(value_split, half, 1,...]
    ppermute x3, starting transfers between devices: 5.6 us -> 4.7 us  [scatter_parts(): lax.ppermute(sent[(steps - 1) * rows:steps * rows], axis, shifted_pairs(c...]
  transfers between devices with their start and end apart: 8 -> 8, of which waited for: 5 -> 6; matrix products, arithmetic and copies ran while one was open for 8% -> 8% of each run, Pallas kernels for 0% -> 0%
where the time goes in v12:
time: 65.8 us; the launch traced here: 65.5 us
  waiting for transfers between devices  29.3 us (45%)
  starting transfers between devices  12.4 us (19%)
  Pallas kernels  6.69 us (10%)
  matrix products  6.34 us (10%)
  local copies, waits for them, and re-layouts  5.35 us (8%)
  other arithmetic  4.58 us (7%)
  between operations  0.8 us (1%)
    ppermute x1, waiting for transfers between devices, head_reduce(): lax.ppermute(sent.astype(jnp.bfloat16), 'head', [(i, i ^ 1 << level) for...  12.8 us
    ppermute x3, waiting for transfers between devices, scatter_parts(): lax.ppermute(sent[(steps - 1) * rows:steps * rows], axis, shifted_pairs(c...  9.35 us
    ppermute x3, waiting for transfers between devices, gather_slots(): lax.ppermute(block, axis, shifted_pairs(count, steps))  7.1 us
    pallas_call x1, Pallas kernels, attention_block(): pl.pallas_call(attention_kernel, out_shape=(jax.ShapeDtypeStruct(queries....  6.69 us
    ppermute x3, starting transfers between devices, gather_slots(): lax.ppermute(block, axis, shifted_pairs(count, steps))  6.06 us
    dot_general x2, matrix products, project(): jnp.einsum('arf,tf->art', lax.dynamic_index_in_dim(key_split, half, 1, ke...  4.89 us
    ppermute x3, starting transfers between devices, scatter_parts(): lax.ppermute(sent[(steps - 1) * rows:steps * rows], axis, shifted_pairs(c...  4.7 us
    ppermute x1, starting transfers between devices, head_reduce(): lax.ppermute(sent.astype(jnp.bfloat16), 'head', [(i, i ^ 1 << level) for...  1.57 us
  transfers between devices with their start and end apart: 8, of which 6 were waited for; matrix products, arithmetic and copies ran while one was open for 8% of the time, Pallas kernels for 0%

profile of v12, /device:TPU:0, one launch (start us, length us, event | category | flops | bytes accessed | tf_op | source)
XLA Modules:
  0.0 65.5 jit_solution(6382316064551846560)
XLA Ops:
  0.6 0.8 %constant_dynamic-update-slice_fusion.1 = bf16[128,512]{1,0:T(8,128)(2,1)S(1)} fusion(bf16[128,256]{1,0:T(8,128)(2,1)} %param.9), kind=kLoop, calls=%fused_computation.24 | loop fusion | bytes 131072
  1.5 0.8 %constant_dynamic-update-slice_fusion = bf16[128,512]{1,0:T(8,128)(2,1)S(1)} fusion(bf16[128,512]{1,0:T(8,128)(2,1)S(1)} %constant_dynamic-update-slice_fusion.1, bf16[128,256]{1,0:T(8,128)(2,1)} %param.10), kind=kLoop, calls=%fused_computation.23 | loop fusion | bytes 131072 | tf_op jit(solution)/shard_map/concatenate | solution.py:209
  2.3 5.0 %collective-permute-start.2 = (bf16[128,512]{1,0:T(8,128)(2,1)S(1)}, bf16[128,512]{1,0:T(8,128)(2,1)S(1)}, u32[]{:S(2)}, u32[]{:S(2)}) collective-permute-start(bf16[128,512]{1,0:T(8,128)(2,1)S(1)} %constant_dynamic-update-slice_fusion), channel_id=1, source_target_pairs={{0,12},{4,0},{8,4},{12,8},{1,13},{5,1},{9,5},{13,9},{2,14},{6,2},{... | collective-permute-start | bytes 393224 | tf_op jit(solution)/shard_map/ppermute | solution.py:42
  7.4 1.0 %collective-permute-start = (bf16[128,512]{1,0:T(8,128)(2,1)S(1)}, bf16[128,512]{1,0:T(8,128)(2,1)S(1)}, u32[]{:S(2)}, u32[]{:S(2)}) collective-permute-start(bf16[128,512]{1,0:T(8,128)(2,1)S(1)} %constant_dynamic-update-slice_fusion), channel_id=1, source_target_pairs={{0,4},{4,8},{8,12},{12,0},{1,5},{5,9},{9,13},{13,1},{2,6},{6,10},{... | collective-permute-start | bytes 393224 | tf_op jit(solution)/shard_map/ppermute | solution.py:42
  8.4 1.2 %dynamic_slice.19 = s32[1]{0:T(128)} dynamic-slice(s32[4]{0:T(128)} %param.13, s32[]{:T(128)S(6)} %select_n.53), dynamic_slice_sizes={1} | dynamic-slice | bytes 12 | tf_op jit(solution)/shard_map/dynamic_slice | solution.py:203
  9.6 0.6 compare_convert_fusion.1
  10.4 0.9 %multiply_reduce_fusion = (s32[4]{0:T(128)S(1)}, s32[4]{0:T(128)S(1)}) fusion(s32[4,4]{1,0:T(4,128)} %param.12, s32[4]{0:T(128)S(1)} %compare_convert_fusion.1, s32[4]{0:T(128)} %param.13, s32[4]{0:T(128)S(1)} %select_reduce_fusion.2), kind=kLoop, calls=%fused_computation.28 | loop fusion | flops 72 | bytes 144 | tf_op jit(solution)/shard_map/reduce_sum | solution.py:18
  11.5 7.1 %collective-permute-done.1 = bf16[128,512]{1,0:T(8,128)(2,1)S(1)} collective-permute-done((bf16[128,512]{1,0:T(8,128)(2,1)S(1)}, bf16[128,512]{1,0:T(8,128)(2,1)S(1)}, u32[]{:S(2)}, u32[]{:S(2)}) %collective-permute-start.1) | collective-permute-done | bytes 131104 | tf_op jit(solution)/shard_map/ppermute | solution.py:42
  18.6 0.8 %pad_maximum_fusion.kv_ref = bf16[512,512]{1,0:T(8,128)(2,1)} fusion(bf16[128,512]{1,0:T(8,128)(2,1)S(1)} %collective-permute-done.2, bf16[128,512]{1,0:T(8,128)(2,1)S(1)} %collective-permute-done.1, bf16[128,512]{1,0:T(8,128)(2,1)S(1)} %collective-permute-done, bf16[128,512]{1,0:T(8,128)(2,1)S(1)} %constant_dynamic-update-slice_fusion), kind=kLoop, calls=%fused_computation.17 | loop fusion | flops 2097152 | bytes 1048576 | tf_op jit(solution)/shard_map/concatenate | solution.py:45
  20.1 6.7 %shard_map.111 = (bf16[128,2048]{1,0:T(8,128)(2,1)}, f32[128,512]{1,0:T(8,128)}, bf16[384,512]{1,0:T(8,128)(2,1)}) custom-call(bf16[128,2048]{1,0:T(8,128)(2,1)} %query_ref.1, bf16[128,2048]{1,0:T(8,128)(2,1)} %grad_ref.1, bf16[512,512]{1,0:T(8,128)(2,1)} %pad_maximum_fusion.kv_ref, s32[1,512]{1,0:T(1,128)} %bitcast.42), custom_call_target="tpu_custom_call" | custom-call | tf_op jit(solution)/shard_map/pallas_call | solution.py:181
  26.7 1.1 %fusion.23 = (bf16[128,512]{1,0:T(8,128)(2,1)S(1)}, bf16[128,512]{1,0:T(8,128)(2,1)S(1)}, bf16[128,512]{1,0:T(8,128)(2,1)S(1)}) fusion(bf16[384,512]{1,0:T(8,128)(2,1)} %get-tuple-element.9), kind=kLoop, calls=%fused_computation.42 | loop fusion | bytes 786432 | tf_op jit(solution)/shard_map/slice | solution.py:69
  27.8 1.7 %collective-permute-start.3 = (bf16[128,512]{1,0:T(8,128)(2,1)S(1)}, bf16[128,512]{1,0:T(8,128)(2,1)S(1)}, u32[]{:S(2)}, u32[]{:S(2)}) collective-permute-start(bf16[128,512]{1,0:T(8,128)(2,1)S(1)} %get-tuple-element.10), channel_id=1, source_target_pairs={{0,12},{4,0},{8,4},{12,8},{1,13},{5,1},{9,5},{13,9},{2,14},{6,2},{... | collective-permute-start | bytes 393224 | tf_op jit(solution)/shard_map/ppermute | solution.py:68
  29.9 2.6 %collective-permute-start.4 = (bf16[128,512]{1,0:T(8,128)(2,1)S(1)}, bf16[128,512]{1,0:T(8,128)(2,1)S(1)}, u32[]{:S(2)}, u32[]{:S(2)}) collective-permute-start(bf16[128,512]{1,0:T(8,128)(2,1)S(1)} %get-tuple-element.12), channel_id=1, source_target_pairs={{0,8},{4,12},{8,0},{12,4},{1,9},{5,13},{9,1},{13,5},{2,10},{6,14},... | collective-permute-start | bytes 393224 | tf_op jit(solution)/shard_map/ppermute | solution.py:68
  32.5 1.7 %collective-permute-done.3 = bf16[128,512]{1,0:T(8,128)(2,1)S(1)} collective-permute-done((bf16[128,512]{1,0:T(8,128)(2,1)S(1)}, bf16[128,512]{1,0:T(8,128)(2,1)S(1)}, u32[]{:S(2)}, u32[]{:S(2)}) %collective-permute-start.3) | collective-permute-done | bytes 131104 | tf_op jit(solution)/shard_map/ppermute | solution.py:68
  34.2 4.6 %collective-permute-done.5 = bf16[128,512]{1,0:T(8,128)(2,1)S(1)} collective-permute-done((bf16[128,512]{1,0:T(8,128)(2,1)S(1)}, bf16[128,512]{1,0:T(8,128)(2,1)S(1)}, u32[]{:S(2)}, u32[]{:S(2)}) %collective-permute-start.5) | collective-permute-done | bytes 131104 | tf_op jit(solution)/shard_map/ppermute | solution.py:68
  38.8 3.1 %collective-permute-done.4 = bf16[128,512]{1,0:T(8,128)(2,1)S(1)} collective-permute-done((bf16[128,512]{1,0:T(8,128)(2,1)S(1)}, bf16[128,512]{1,0:T(8,128)(2,1)S(1)}, u32[]{:S(2)}, u32[]{:S(2)}) %collective-permute-start.4) | collective-permute-done | bytes 131104 | tf_op jit(solution)/shard_map/ppermute | solution.py:68
  41.9 1.0 %add_convert_fusion.1 = bf16[128,512]{1,0:T(8,128)(2,1)S(1)} fusion(bf16[128,512]{1,0:T(8,128)(2,1)S(1)} %collective-permute-done.5, bf16[128,512]{1,0:T(8,128)(2,1)S(1)} %collective-permute-done.4, f32[128,512]{1,0:T(8,128)} %get-tuple-element.8, bf16[128,512]{1,0:T(8,128)(2,1)S(1)} %collective-permute-done.3), kind=kLoop, calls=%fused_computation.18 | loop fusion | flops 458752 | bytes 786432 | tf_op jit(solution)/shard_map/convert.1
  42.9 2.4 %fusion.2 = f32[2,2048,128]{2,1,0:T(8,128)S(1)} fusion(bf16[2,2,2048,256]{3,2,1,0:T(8,128)(2,1)} %bitcast.38, s32[]{:T(128)S(6)} %select_n.56, bf16[128,256]{1,0:T(8,128)(2,1)S(1)} %get-tuple-element.14), kind=kOutput, calls=%fused_computation.4 | convolution fusion | flops 268435456 | bytes 4259844 | tf_op jit(solution)/shard_map/arf,tf->art/dot_general | solution.py:91
  45.8 0.7 %fusion = bf16[2,2048,128]{2,1,0:T(8,128)(2,1)S(1)} fusion(f32[2,2048,128]{2,1,0:T(8,128)S(1)} %fusion.2, bf16[2,2,2048,256]{3,2,1,0:T(8,128)(2,1)S(1)} %bitcast.40, s32[]{:T(128)S(6)} %select_n.56, bf16[128,256]{1,0:T(8,128)(2,1)S(1)} %get-tuple-element.13), kind=kOutput, calls=%fused_computation.2 | convolution fusion | flops 269484032 | bytes 5308420 | tf_op jit(solution)/shard_map/arf,tf->art/dot_general | solution.py:96
  46.6 2.4 %fusion.5 = f32[2,2048,128]{2,1,0:T(8,128)S(1)} fusion(bf16[2,2,2048,256]{3,2,1,0:T(8,128)(2,1)} %bitcast.39, s32[]{:T(128)S(6)} %select_n.55, bf16[128,256]{1,0:T(8,128)(2,1)S(1)} %get-tuple-element.14), kind=kOutput, calls=%fused_computation.7 | convolution fusion | flops 268435456 | bytes 4259844 | tf_op jit(solution)/shard_map/arf,tf->art/dot_general | solution.py:91
  49.4 0.8 %convert_add_fusion = f32[2,2048,128]{2,1,0:T(8,128)S(1)} fusion(bf16[2,2048,128]{2,1,0:T(8,128)(2,1)S(1)} %collective-permute-done.6, f32[2,2048,128]{2,1,0:T(8,128)S(1)} %fusion.5, bf16[2,2,2048,256]{3,2,1,0:T(8,128)(2,1)S(1)} %bitcast.41, s32[]{:T(128)S(6)} %select_n.55, bf16[128,256]{1,0:T(8,128)(2,1)S(1)} %get-tuple-element.13), kind=kOutput, calls=%fused_computation.9 | convolution fusion | flops 270008320 | bytes 7405572 | tf_op jit(solution)/shard_map/arf,tf->art/dot_general | solution.py:96
  50.3 1.6 %collective-permute-start.7 = (bf16[1,2048,128]{2,1,0:T(8,128)(2,1)S(1)}, bf16[1,2048,128]{2,1,0:T(8,128)(2,1)S(1)}, u32[]{:S(2)}, u32[]{:S(2)}) collective-permute-start(bf16[1,2048,128]{2,1,0:T(8,128)(2,1)S(1)} %dynamic-slice_convert_fusion), channel_id=1, source_target_pairs={{0,2},{1,3},{2,0},{3,1},{4,6},{5,7},{6,4},{7,5},{8,10},{9,11},{10,... | collective-permute-start | bytes 1572872 | tf_op jit(solution)/shard_map/ppermute | solution.py:114
  51.8 12.8 %collective-permute-done.7 = bf16[1,2048,128]{2,1,0:T(8,128)(2,1)S(1)} collective-permute-done((bf16[1,2048,128]{2,1,0:T(8,128)(2,1)S(1)}, bf16[1,2048,128]{2,1,0:T(8,128)(2,1)S(1)}, u32[]{:S(2)}, u32[]{:S(2)}) %collective-permute-start.7) | collective-permute-done | bytes 524320 | tf_op jit(solution)/shard_map/ppermute | solution.py:114
  64.6 0.9 %fusion.13 = bf16[2048,128]{1,0:T(8,128)(2,1)} fusion(bf16[1,2048,128]{2,1,0:T(8,128)(2,1)S(1)} %collective-permute-done.7, f32[2,2048,128]{2,1,0:T(8,128)S(1)} %convert_add_fusion, s32[]{:T(128)S(6)} %select_n.59), kind=kLoop, calls=%fused_computation.16 | loop fusion | flops 786432 | bytes 2097156 | tf_op jit(solution)/shard_map/convert_element_type | solution.py:118
  (21 shorter events, 2.3 us)
Async XLA Ops:
  2.3 9.2 %collective-permute-start.2 = (bf16[128,512]{1,0:T(8,128)(2,1)S(1)}, bf16[128,512]{1,0:T(8,128)(2,1)S(1)}, u32[]{:S(2)}, u32[]{:S(2)}) collective-permute-start(bf16[128,512]{1,0:T(8,128)(2,1)S(1)} %constant_dynamic-update-slice_fusion), channel_id=1, source_target_pairs={{0,12},{4,0},{8,4},{12,8},{1,13},{5,1},{9,5},{13,9},{2,14},{6,2},{... | collective-permute-start | bytes 393224 | tf_op jit(solution)/shard_map/ppermute | solution.py:42
  7.4 11.2 %collective-permute-start.1 = (bf16[128,512]{1,0:T(8,128)(2,1)S(1)}, bf16[128,512]{1,0:T(8,128)(2,1)S(1)}, u32[]{:S(2)}, u32[]{:S(2)}) collective-permute-start(bf16[128,512]{1,0:T(8,128)(2,1)S(1)} %constant_dynamic-update-slice_fusion), channel_id=1, source_target_pairs={{0,8},{4,12},{8,0},{12,4},{1,9},{5,13},{9,1},{13,5},{2,10},{6,14},... | collective-permute-start | bytes 393224 | tf_op jit(solution)/shard_map/ppermute | solution.py:42
  7.4 11.2 %collective-permute-start = (bf16[128,512]{1,0:T(8,128)(2,1)S(1)}, bf16[128,512]{1,0:T(8,128)(2,1)S(1)}, u32[]{:S(2)}, u32[]{:S(2)}) collective-permute-start(bf16[128,512]{1,0:T(8,128)(2,1)S(1)} %constant_dynamic-update-slice_fusion), channel_id=1, source_target_pairs={{0,4},{4,8},{8,12},{12,0},{1,5},{5,9},{9,13},{13,1},{2,6},{6,10},{... | collective-permute-start | bytes 393224 | tf_op jit(solution)/shard_map/ppermute | solution.py:42
  27.8 6.4 %collective-permute-start.3 = (bf16[128,512]{1,0:T(8,128)(2,1)S(1)}, bf16[128,512]{1,0:T(8,128)(2,1)S(1)}, u32[]{:S(2)}, u32[]{:S(2)}) collective-permute-start(bf16[128,512]{1,0:T(8,128)(2,1)S(1)} %get-tuple-element.10), channel_id=1, source_target_pairs={{0,12},{4,0},{8,4},{12,8},{1,13},{5,1},{9,5},{13,9},{2,14},{6,2},{... | collective-permute-start | bytes 393224 | tf_op jit(solution)/shard_map/ppermute | solution.py:68
  29.5 9.3 %collective-permute-start.5 = (bf16[128,512]{1,0:T(8,128)(2,1)S(1)}, bf16[128,512]{1,0:T(8,128)(2,1)S(1)}, u32[]{:S(2)}, u32[]{:S(2)}) collective-permute-start(bf16[128,512]{1,0:T(8,128)(2,1)S(1)} %get-tuple-element.11), channel_id=1, source_target_pairs={{0,4},{4,8},{8,12},{12,0},{1,5},{5,9},{9,13},{13,1},{2,6},{6,10},{... | collective-permute-start | bytes 393224 | tf_op jit(solution)/shard_map/ppermute | solution.py:68
  29.9 12.0 %collective-permute-start.4 = (bf16[128,512]{1,0:T(8,128)(2,1)S(1)}, bf16[128,512]{1,0:T(8,128)(2,1)S(1)}, u32[]{:S(2)}, u32[]{:S(2)}) collective-permute-start(bf16[128,512]{1,0:T(8,128)(2,1)S(1)} %get-tuple-element.12), channel_id=1, source_target_pairs={{0,8},{4,12},{8,0},{12,4},{1,9},{5,13},{9,1},{13,5},{2,10},{6,14},... | collective-permute-start | bytes 393224 | tf_op jit(solution)/shard_map/ppermute | solution.py:68
  42.9 3.7 %copy-start.3 = (bf16[128,256]{1,0:T(8,128)(2,1)}, bf16[128,256]{1,0:T(8,128)(2,1)S(1)}, u32[]{:S(2)}) copy-start(bf16[128,256]{1,0:T(8,128)(2,1)S(1)} %get-tuple-element.14) | copy-start | bytes 196612
  42.9 6.3 %copy-start.2 = (bf16[128,256]{1,0:T(8,128)(2,1)}, bf16[128,256]{1,0:T(8,128)(2,1)S(1)}, u32[]{:S(2)}) copy-start(bf16[128,256]{1,0:T(8,128)(2,1)S(1)} %get-tuple-element.13) | copy-start | bytes 196612
  42.9 2.9 %copy-start = (bf16[8192,256]{1,0:T(8,128)(2,1)S(1)}, bf16[8192,256]{1,0:T(8,128)(2,1)}, u32[]{:S(2)}) copy-start(bf16[8192,256]{1,0:T(8,128)(2,1)} %param.15) | copy-start | bytes 12582916
  46.5 2.7 %collective-permute-start.6 = (bf16[2,2048,128]{2,1,0:T(8,128)(2,1)S(1)}, bf16[2,2048,128]{2,1,0:T(8,128)(2,1)S(1)}, u32[]{:S(2)}, u32[]{:S(2)}) collective-permute-start(bf16[2,2048,128]{2,1,0:T(8,128)(2,1)S(1)} %fusion), channel_id=1, source_target_pairs={{0,1},{1,0},{2,3},{3,2},{4,5},{5,4},{6,7},{7,6},{8,9},{9,8},{10,11... | collective-permute-start | bytes 3145736 | tf_op jit(solution)/shard_map/ppermute | solution.py:106
  46.6 2.8 %copy-start.1 = (bf16[8192,256]{1,0:T(8,128)(2,1)S(1)}, bf16[8192,256]{1,0:T(8,128)(2,1)}, u32[]{:S(2)}) copy-start(bf16[8192,256]{1,0:T(8,128)(2,1)} %param.15) | copy-start | bytes 12582916
  50.3 14.3 %collective-permute-start.7 = (bf16[1,2048,128]{2,1,0:T(8,128)(2,1)S(1)}, bf16[1,2048,128]{2,1,0:T(8,128)(2,1)S(1)}, u32[]{:S(2)}, u32[]{:S(2)}) collective-permute-start(bf16[1,2048,128]{2,1,0:T(8,128)(2,1)S(1)} %dynamic-slice_convert_fusion), channel_id=1, source_target_pairs={{0,2},{1,3},{2,0},{3,1},{4,6},{5,7},{6,4},{7,5},{8,10},{9,11},{10,... | collective-permute-start | bytes 1572872 | tf_op jit(solution)/shard_map/ppermute | solution.py:114

commit v13 on v12

--- a/solution.py
+++ b/solution.py
@@ -62,13 +62,14 @@
 
 def scatter_parts(own, sent, axis):
     count = lax.axis_size(axis)
+    position = lax.axis_index(axis)
     rows = own.shape[0]
-    total = own
-    for steps in range(1, count):
-        total = total + lax.ppermute(
-            sent[(steps - 1) * rows : steps * rows], axis, shifted_pairs(count, -steps)
-        ).astype(jnp.float32)
-    return total
+    slots = jnp.concatenate([jnp.zeros(own.shape, jnp.bfloat16), sent], axis=0).reshape(
+        count, rows, -1
+    )
+    by_device = jnp.take(slots, (position - lax.iota(jnp.int32, count)) % count, axis=0)
+    arrived = lax.all_to_all(by_device, axis, 0, 0, tiled=True)
+    return own + jnp.sum(arrived.astype(jnp.float32), axis=0)
 
 
 def head_reduce(key_proj, value_proj, key_grad, value_grad):

time: 65.8 us -> 70.2 us (1.067)
  waiting for transfers between devices: 29.3 us -> 33.1 us
  starting transfers between devices: 12.4 us -> 11.6 us
  other arithmetic: 4.58 us -> 5.34 us
    all_to_all x0 -> x1, waiting for transfers between devices: none -> 13.9 us  [scatter_parts(): arrived = lax.all_to_all(by_device, axis, 0, 0, tiled=True)]
    ppermute x3 -> x0, waiting for transfers between devices: 9.35 us -> none  [scatter_parts(): lax.ppermute(sent[(steps - 1) * rows:steps * rows], axis, shifted_pairs(c...]
    ppermute x3 -> x0, starting transfers between devices: 4.7 us -> none  [scatter_parts(): lax.ppermute(sent[(steps - 1) * rows:steps * rows], axis, shifted_pairs(c...]
    all_to_all x0 -> x1, starting transfers between devices: none -> 3.9 us  [scatter_parts(): arrived = lax.all_to_all(by_device, axis, 0, 0, tiled=True)]
    slice x1 -> x0, local copies, waits for them, and re-layouts: 1.06 us -> none  [scatter_parts(): sent[(steps - 1) * rows:steps * rows]]
    concatenate x0 -> x1, local copies, waits for them, and re-layouts: none -> 1.03 us  [scatter_parts(): jnp.concatenate([jnp.zeros(own.shape, jnp.bfloat16), sent], axis=0)]
    another operation x1, other arithmetic: 1.01 us -> 0.04 us
    select_n x0 -> x2, other arithmetic: none -> 0.92 us  [scatter_parts(): jnp.take(slots, (position - lax.iota(jnp.int32, count)) % count, axis=0)]
  transfers between devices with their start and end apart: 8 -> 6, of which waited for: 6 -> 4; matrix products, arithmetic and copies ran while one was open for 8% -> 9% of each run, Pallas kernels for 0% -> 0%
where the time goes in v13:
time: 70.2 us; the launch traced here: 69.8 us
  waiting for transfers between devices  33.1 us (47%)
  starting transfers between devices  11.6 us (17%)
  Pallas kernels  6.67 us (10%)
  matrix products  6.33 us (9%)
  local copies, waits for them, and re-layouts  5.9 us (8%)
  other arithmetic  5.34 us (8%)
  between operations  0.84 us (1%)
    all_to_all x1, waiting for transfers between devices, scatter_parts(): arrived = lax.all_to_all(by_device, axis, 0, 0, tiled=True)  13.9 us
    ppermute x1, waiting for transfers between devices, head_reduce(): lax.ppermute(sent.astype(jnp.bfloat16), 'head', [(i, i ^ 1 << level) for...  12.8 us
    pallas_call x1, Pallas kernels, attention_block(): pl.pallas_call(attention_kernel, out_shape=(jax.ShapeDtypeStruct(queries....  6.67 us
    ppermute x3, waiting for transfers between devices, gather_slots(): lax.ppermute(block, axis, shifted_pairs(count, steps))  6.32 us
    ppermute x3, starting transfers between devices, gather_slots(): lax.ppermute(block, axis, shifted_pairs(count, steps))  6.06 us
    dot_general x2, matrix products, project(): jnp.einsum('arf,tf->art', lax.dynamic_index_in_dim(key_split, half, 1, ke...  4.88 us
    all_to_all x1, starting transfers between devices, scatter_parts(): arrived = lax.all_to_all(by_device, axis, 0, 0, tiled=True)  3.9 us
    ppermute x1, starting transfers between devices, head_reduce(): lax.ppermute(sent.astype(jnp.bfloat16), 'head', [(i, i ^ 1 << level) for...  1.57 us
  transfers between devices with their start and end apart: 6, of which 4 were waited for; matrix products, arithmetic and copies ran while one was open for 9% of the time, Pallas kernels for 0%

profile of v13, /device:TPU:0, one launch (start us, length us, event | category | flops | bytes accessed | tf_op | source)
XLA Modules:
  0.0 69.8 jit_solution(1930709222189196220)
XLA Ops:
  0.6 0.8 %constant_dynamic-update-slice_fusion.1 = bf16[128,512]{1,0:T(8,128)(2,1)S(1)} fusion(bf16[128,256]{1,0:T(8,128)(2,1)} %param.9), kind=kLoop, calls=%fused_computation.28 | loop fusion | bytes 131072
  1.5 0.8 %constant_dynamic-update-slice_fusion = bf16[128,512]{1,0:T(8,128)(2,1)S(1)} fusion(bf16[128,512]{1,0:T(8,128)(2,1)S(1)} %constant_dynamic-update-slice_fusion.1, bf16[128,256]{1,0:T(8,128)(2,1)} %param.10), kind=kLoop, calls=%fused_computation.27 | loop fusion | bytes 131072 | tf_op jit(solution)/shard_map/concatenate | solution.py:210
  2.3 5.0 %collective-permute-start.2 = (bf16[128,512]{1,0:T(8,128)(2,1)S(1)}, bf16[128,512]{1,0:T(8,128)(2,1)S(1)}, u32[]{:S(2)}, u32[]{:S(2)}) collective-permute-start(bf16[128,512]{1,0:T(8,128)(2,1)S(1)} %constant_dynamic-update-slice_fusion), channel_id=1, source_target_pairs={{0,12},{4,0},{8,4},{12,8},{1,13},{5,1},{9,5},{13,9},{2,14},{6,2},{... | collective-permute-start | bytes 393224 | tf_op jit(solution)/shard_map/ppermute | solution.py:42
  7.4 1.0 %collective-permute-start = (bf16[128,512]{1,0:T(8,128)(2,1)S(1)}, bf16[128,512]{1,0:T(8,128)(2,1)S(1)}, u32[]{:S(2)}, u32[]{:S(2)}) collective-permute-start(bf16[128,512]{1,0:T(8,128)(2,1)S(1)} %constant_dynamic-update-slice_fusion), channel_id=1, source_target_pairs={{0,4},{4,8},{8,12},{12,0},{1,5},{5,9},{9,13},{13,1},{2,6},{6,10},{... | collective-permute-start | bytes 393224 | tf_op jit(solution)/shard_map/ppermute | solution.py:42
  8.4 1.2 %dynamic_slice.19 = s32[1]{0:T(128)} dynamic-slice(s32[4]{0:T(128)} %param.13, s32[]{:T(128)S(6)} %select_n.85), dynamic_slice_sizes={1} | dynamic-slice | bytes 12 | tf_op jit(solution)/shard_map/dynamic_slice | solution.py:204
  9.6 0.6 compare_convert_fusion.1
  10.4 0.8 %select_reduce_fusion.1 = s32[4]{0:T(128)S(1)} fusion(s32[4]{0:T(128)} %param.13, s32[4]{0:T(128)S(1)} %select_reduce_fusion.2), kind=kLoop, calls=%fused_computation.38 | loop fusion | flops 44 | bytes 48 | tf_op jit(solution)/shard_map/reduce_sum | solution.py:28
  11.2 0.8 %multiply_reduce_fusion = s32[4]{0:T(128)S(1)} fusion(s32[4,4]{1,0:T(4,128)} %param.12, s32[4]{0:T(128)S(1)} %compare_convert_fusion.1), kind=kLoop, calls=%fused_computation.36 | loop fusion | flops 28 | bytes 96 | tf_op jit(solution)/shard_map/reduce_sum | solution.py:18
  12.3 6.3 %collective-permute-done.1 = bf16[128,512]{1,0:T(8,128)(2,1)S(1)} collective-permute-done((bf16[128,512]{1,0:T(8,128)(2,1)S(1)}, bf16[128,512]{1,0:T(8,128)(2,1)S(1)}, u32[]{:S(2)}, u32[]{:S(2)}) %collective-permute-start.1) | collective-permute-done | bytes 131104 | tf_op jit(solution)/shard_map/ppermute | solution.py:42
  18.6 0.8 %pad_maximum_fusion.kv_ref = bf16[512,512]{1,0:T(8,128)(2,1)} fusion(bf16[128,512]{1,0:T(8,128)(2,1)S(1)} %collective-permute-done.2, bf16[128,512]{1,0:T(8,128)(2,1)S(1)} %collective-permute-done.1, bf16[128,512]{1,0:T(8,128)(2,1)S(1)} %collective-permute-done, bf16[128,512]{1,0:T(8,128)(2,1)S(1)} %constant_dynamic-update-slice_fusion), kind=kLoop, calls=%fused_computation.19 | loop fusion | flops 2097152 | bytes 1048576 | tf_op jit(solution)/shard_map/concatenate | solution.py:45
  19.4 0.6 broadcast_in_dim.9
  20.1 6.7 %shard_map.111 = (bf16[128,2048]{1,0:T(8,128)(2,1)}, f32[128,512]{1,0:T(8,128)}, bf16[384,512]{1,0:T(8,128)(2,1)}) custom-call(bf16[128,2048]{1,0:T(8,128)(2,1)} %query_ref.1, bf16[128,2048]{1,0:T(8,128)(2,1)} %grad_ref.1, bf16[512,512]{1,0:T(8,128)(2,1)} %pad_maximum_fusion.kv_ref, s32[1,512]{1,0:T(1,128)} %bitcast.46), custom_call_target="tpu_custom_call" | custom-call | tf_op jit(solution)/shard_map/pallas_call | solution.py:182
  26.7 1.0 %concatenate.11 = bf16[512,512]{1,0:T(8,128)(2,1)S(1)} pad(bf16[384,512]{1,0:T(8,128)(2,1)} %get-tuple-element.9, bf16[]{:T(256)} %constant.110.clone.1), padding=128_0x0_0 | pad | bytes 917506 | tf_op jit(solution)/shard_map/concatenate | solution.py:67
  27.8 0.6 gather_fusion
  28.4 0.9 %broadcast_select_fusion = bf16[4,128,512]{2,1,0:T(8,128)(2,1)} fusion(bf16[4,128,512]{2,1,0:T(8,128)(2,1)S(1)} %gather_fusion, pred[4]{0:T(512)(128)(4,1)S(1)} %get-tuple-element.12), kind=kLoop, calls=%fused_computation.20 | loop fusion | flops 262144 | bytes 1048580 | tf_op jit(solution)/shard_map/jit(_take)/select_n | solution.py:70
  29.3 3.9 %all-to-all-start = ((bf16[4,128,512]{2,1,0:T(8,128)(2,1)}), bf16[4,128,512]{2,1,0:T(8,128)(2,1)S(1)}, u32[]{:S(2)}, u32[]{:S(2)}) async-start(bf16[4,128,512]{2,1,0:T(8,128)(2,1)} %broadcast_select_fusion), calls=%async_computation | async-start | bytes 1048576 | tf_op jit(solution)/shard_map/all_to_all | solution.py:71
  33.2 13.9 %all-to-all-done = bf16[4,128,512]{2,1,0:T(8,128)(2,1)S(1)} async-done(((bf16[4,128,512]{2,1,0:T(8,128)(2,1)}), bf16[4,128,512]{2,1,0:T(8,128)(2,1)S(1)}, u32[]{:S(2)}, u32[]{:S(2)}) %all-to-all-start) | async-done | bytes 524320 | tf_op jit(solution)/shard_map/all_to_all | solution.py:71
  47.2 2.4 %fusion.2 = f32[2,2048,128]{2,1,0:T(8,128)S(1)} fusion(bf16[2,2,2048,256]{3,2,1,0:T(8,128)(2,1)} %bitcast.41, s32[]{:T(128)S(6)} %select_n.92, bf16[128,256]{1,0:T(8,128)(2,1)S(1)} %get-tuple-element.11), kind=kOutput, calls=%fused_computation.5 | convolution fusion | flops 268435456 | bytes 4259844 | tf_op jit(solution)/shard_map/arf,tf->art/dot_general | solution.py:92
  50.1 0.7 %fusion = bf16[2,2048,128]{2,1,0:T(8,128)(2,1)S(1)} fusion(f32[2,2048,128]{2,1,0:T(8,128)S(1)} %fusion.2, bf16[2,2,2048,256]{3,2,1,0:T(8,128)(2,1)S(1)} %bitcast.43, s32[]{:T(128)S(6)} %select_n.92, bf16[128,256]{1,0:T(8,128)(2,1)S(1)} %get-tuple-element.10), kind=kOutput, calls=%fused_computation.3 | convolution fusion | flops 269484032 | bytes 5308420 | tf_op jit(solution)/shard_map/arf,tf->art/dot_general | solution.py:97
  50.9 2.4 %fusion.5 = f32[2,2048,128]{2,1,0:T(8,128)S(1)} fusion(bf16[2,2,2048,256]{3,2,1,0:T(8,128)(2,1)} %bitcast.42, s32[]{:T(128)S(6)} %select_n.91, bf16[128,256]{1,0:T(8,128)(2,1)S(1)} %get-tuple-element.11), kind=kOutput, calls=%fused_computation.8 | convolution fusion | flops 268435456 | bytes 4259844 | tf_op jit(solution)/shard_map/arf,tf->art/dot_general | solution.py:92
  53.8 0.7 %convert_add_fusion = f32[2,2048,128]{2,1,0:T(8,128)S(1)} fusion(bf16[2,2048,128]{2,1,0:T(8,128)(2,1)S(1)} %collective-permute-done.3, f32[2,2048,128]{2,1,0:T(8,128)S(1)} %fusion.5, bf16[2,2,2048,256]{3,2,1,0:T(8,128)(2,1)S(1)} %bitcast.44, s32[]{:T(128)S(6)} %select_n.91, bf16[128,256]{1,0:T(8,128)(2,1)S(1)} %get-tuple-element.10), kind=kOutput, calls=%fused_computation.10 | convolution fusion | flops 270008320 | bytes 7405572 | tf_op jit(solution)/shard_map/arf,tf->art/dot_general | solution.py:97
  54.6 1.6 %collective-permute-start.4 = (bf16[1,2048,128]{2,1,0:T(8,128)(2,1)S(1)}, bf16[1,2048,128]{2,1,0:T(8,128)(2,1)S(1)}, u32[]{:S(2)}, u32[]{:S(2)}) collective-permute-start(bf16[1,2048,128]{2,1,0:T(8,128)(2,1)S(1)} %dynamic-slice_convert_fusion), channel_id=1, source_target_pairs={{0,2},{1,3},{2,0},{3,1},{4,6},{5,7},{6,4},{7,5},{8,10},{9,11},{10,... | collective-permute-start | bytes 1572872 | tf_op jit(solution)/shard_map/ppermute | solution.py:115
  56.1 12.8 %collective-permute-done.4 = bf16[1,2048,128]{2,1,0:T(8,128)(2,1)S(1)} collective-permute-done((bf16[1,2048,128]{2,1,0:T(8,128)(2,1)S(1)}, bf16[1,2048,128]{2,1,0:T(8,128)(2,1)S(1)}, u32[]{:S(2)}, u32[]{:S(2)}) %collective-permute-start.4) | collective-permute-done | bytes 524320 | tf_op jit(solution)/shard_map/ppermute | solution.py:115
  68.9 0.9 %fusion.13 = bf16[2048,128]{1,0:T(8,128)(2,1)} fusion(bf16[1,2048,128]{2,1,0:T(8,128)(2,1)S(1)} %collective-permute-done.4, f32[2,2048,128]{2,1,0:T(8,128)S(1)} %convert_add_fusion, s32[]{:T(128)S(6)} %select_n.95), kind=kLoop, calls=%fused_computation.18 | loop fusion | flops 786432 | bytes 2097156 | tf_op jit(solution)/shard_map/convert_element_type | solution.py:119
  (25 shorter events, 1.4 us)
Async XLA Ops:
  2.3 9.9 %collective-permute-start.2 = (bf16[128,512]{1,0:T(8,128)(2,1)S(1)}, bf16[128,512]{1,0:T(8,128)(2,1)S(1)}, u32[]{:S(2)}, u32[]{:S(2)}) collective-permute-start(bf16[128,512]{1,0:T(8,128)(2,1)S(1)} %constant_dynamic-update-slice_fusion), channel_id=1, source_target_pairs={{0,12},{4,0},{8,4},{12,8},{1,13},{5,1},{9,5},{13,9},{2,14},{6,2},{... | collective-permute-start | bytes 393224 | tf_op jit(solution)/shard_map/ppermute | solution.py:42
  7.4 11.2 %collective-permute-start.1 = (bf16[128,512]{1,0:T(8,128)(2,1)S(1)}, bf16[128,512]{1,0:T(8,128)(2,1)S(1)}, u32[]{:S(2)}, u32[]{:S(2)}) collective-permute-start(bf16[128,512]{1,0:T(8,128)(2,1)S(1)} %constant_dynamic-update-slice_fusion), channel_id=1, source_target_pairs={{0,8},{4,12},{8,0},{12,4},{1,9},{5,13},{9,1},{13,5},{2,10},{6,14},... | collective-permute-start | bytes 393224 | tf_op jit(solution)/shard_map/ppermute | solution.py:42
  7.4 11.2 %collective-permute-start = (bf16[128,512]{1,0:T(8,128)(2,1)S(1)}, bf16[128,512]{1,0:T(8,128)(2,1)S(1)}, u32[]{:S(2)}, u32[]{:S(2)}) collective-permute-start(bf16[128,512]{1,0:T(8,128)(2,1)S(1)} %constant_dynamic-update-slice_fusion), channel_id=1, source_target_pairs={{0,4},{4,8},{8,12},{12,0},{1,5},{5,9},{9,13},{13,1},{2,6},{6,10},{... | collective-permute-start | bytes 393224 | tf_op jit(solution)/shard_map/ppermute | solution.py:42
  27.8 19.4 %copy-start.4 = (f32[128,512]{1,0:T(8,128)S(1)}, f32[128,512]{1,0:T(8,128)}, u32[]{:S(2)}) copy-start(f32[128,512]{1,0:T(8,128)} %get-tuple-element.8) | copy-start | bytes 786436
  29.3 17.8 %all-to-all-start = ((bf16[4,128,512]{2,1,0:T(8,128)(2,1)}), bf16[4,128,512]{2,1,0:T(8,128)(2,1)S(1)}, u32[]{:S(2)}, u32[]{:S(2)}) async-start(bf16[4,128,512]{2,1,0:T(8,128)(2,1)} %broadcast_select_fusion), calls=%async_computation | async-start | bytes 1048576 | tf_op jit(solution)/shard_map/all_to_all | solution.py:71
  47.2 3.7 %copy-start.3 = (bf16[128,256]{1,0:T(8,128)(2,1)}, bf16[128,256]{1,0:T(8,128)(2,1)S(1)}, u32[]{:S(2)}) copy-start(bf16[128,256]{1,0:T(8,128)(2,1)S(1)} %get-tuple-element.11) | copy-start | bytes 196612
  47.2 6.3 %copy-start.2 = (bf16[128,256]{1,0:T(8,128)(2,1)}, bf16[128,256]{1,0:T(8,128)(2,1)S(1)}, u32[]{:S(2)}) copy-start(bf16[128,256]{1,0:T(8,128)(2,1)S(1)} %get-tuple-element.10) | copy-start | bytes 196612
  47.2 2.9 %copy-start = (bf16[8192,256]{1,0:T(8,128)(2,1)S(1)}, bf16[8192,256]{1,0:T(8,128)(2,1)}, u32[]{:S(2)}) copy-start(bf16[8192,256]{1,0:T(8,128)(2,1)} %param.15) | copy-start | bytes 12582916
  50.8 2.7 %collective-permute-start.3 = (bf16[2,2048,128]{2,1,0:T(8,128)(2,1)S(1)}, bf16[2,2048,128]{2,1,0:T(8,128)(2,1)S(1)}, u32[]{:S(2)}, u32[]{:S(2)}) collective-permute-start(bf16[2,2048,128]{2,1,0:T(8,128)(2,1)S(1)} %fusion), channel_id=1, source_target_pairs={{0,1},{1,0},{2,3},{3,2},{4,5},{5,4},{6,7},{7,6},{8,9},{9,8},{10,11... | collective-permute-start | bytes 3145736 | tf_op jit(solution)/shard_map/ppermute | solution.py:107
  50.9 2.8 %copy-start.1 = (bf16[8192,256]{1,0:T(8,128)(2,1)S(1)}, bf16[8192,256]{1,0:T(8,128)(2,1)}, u32[]{:S(2)}) copy-start(bf16[8192,256]{1,0:T(8,128)(2,1)} %param.15) | copy-start | bytes 12582916
  54.6 14.3 %collective-permute-start.4 = (bf16[1,2048,128]{2,1,0:T(8,128)(2,1)S(1)}, bf16[1,2048,128]{2,1,0:T(8,128)(2,1)S(1)}, u32[]{:S(2)}, u32[]{:S(2)}) collective-permute-start(bf16[1,2048,128]{2,1,0:T(8,128)(2,1)S(1)} %dynamic-slice_convert_fusion), channel_id=1, source_target_pairs={{0,2},{1,3},{2,0},{3,1},{4,6},{5,7},{6,4},{7,5},{8,10},{9,11},{10,... | collective-permute-start | bytes 1572872 | tf_op jit(solution)/shard_map/ppermute | solution.py:115

commit v14 on v12

--- a/solution.py
+++ b/solution.py
@@ -4,6 +4,7 @@
 import jax.numpy as jnp
 from jax import lax
 from jax.experimental import pallas as pl
+from jax.experimental.pallas import tpu as pltpu
 from jax.sharding import PartitionSpec as P
 
 HD = 128
@@ -71,6 +72,19 @@
     return total
 
 
+def copy_to_vmem(source, target):
+    pltpu.sync_copy(source, target)
+
+
+def staged(weights):
+    return pl.pallas_call(
+        copy_to_vmem,
+        out_shape=jax.ShapeDtypeStruct(weights.shape, weights.dtype),
+        in_specs=[pl.BlockSpec(memory_space=pl.ANY)],
+        out_specs=pl.BlockSpec(memory_space=pltpu.VMEM),
+    )(weights)
+
+
 def head_reduce(key_proj, value_proj, key_grad, value_grad):
     count = lax.axis_size("head")
     position = lax.axis_index("head")
@@ -84,6 +98,8 @@
             jnp.bfloat16
         )
     block = key_proj.shape[0] // count
+    key_proj = staged(key_proj)
+    value_proj = staged(value_proj)
     key_split = key_proj.reshape(count // 2, 2, block, key_proj.shape[1])
     value_split = value_proj.reshape(count // 2, 2, block, value_proj.shape[1])
 

time: 65.8 us -> 64.9 us (0.986)
  Pallas kernels: 6.69 us -> 15 us
  waiting for transfers between devices: 29.3 us -> 21 us
  other arithmetic: 4.58 us -> 3.63 us
    ppermute x3, waiting for transfers between devices: 9.35 us -> 1.02 us  [scatter_parts(): lax.ppermute(sent[(steps - 1) * rows:steps * rows], axis, shifted_pairs(c...]
    pallas_call x0 -> x2, Pallas kernels: none -> 8.32 us  [staged(): pl.pallas_call(copy_to_vmem, out_shape=jax.ShapeDtypeStruct(weights.shape...]
    another operation x1, other arithmetic: 1.01 us -> 0.06 us
    unnamed x9 -> x11, local copies, waits for them, and re-layouts: 1.5 us -> 1.5 us
  transfers between devices with their start and end apart: 8 -> 8, of which waited for: 6 -> 4; matrix products, arithmetic and copies ran while one was open for 8% -> 9% of each run, Pallas kernels for 0% -> 13%
where the time goes in v14:
time: 64.9 us; the launch traced here: 64.5 us
  waiting for transfers between devices  21 us (32%)
  Pallas kernels  15 us (23%)
  starting transfers between devices  12.4 us (19%)
  matrix products  6.32 us (10%)
  local copies, waits for them, and re-layouts  5.35 us (8%)
  other arithmetic  3.63 us (6%)
  between operations  0.8 us (1%)
    ppermute x1, waiting for transfers between devices, head_reduce(): lax.ppermute(sent.astype(jnp.bfloat16), 'head', [(i, i ^ 1 << level) for...  12.8 us
    pallas_call x2, Pallas kernels, staged(): pl.pallas_call(copy_to_vmem, out_shape=jax.ShapeDtypeStruct(weights.shape...  8.32 us
    ppermute x3, waiting for transfers between devices, gather_slots(): lax.ppermute(block, axis, shifted_pairs(count, steps))  7.1 us
    pallas_call x1, Pallas kernels, attention_block(): pl.pallas_call(attention_kernel, out_shape=(jax.ShapeDtypeStruct(queries....  6.68 us
    ppermute x3, starting transfers between devices, gather_slots(): lax.ppermute(block, axis, shifted_pairs(count, steps))  6.06 us
    dot_general x2, matrix products, project(): jnp.einsum('arf,tf->art', lax.dynamic_index_in_dim(key_split, half, 1, ke...  4.88 us
    ppermute x3, starting transfers between devices, scatter_parts(): lax.ppermute(sent[(steps - 1) * rows:steps * rows], axis, shifted_pairs(c...  4.7 us
    ppermute x1, starting transfers between devices, head_reduce(): lax.ppermute(sent.astype(jnp.bfloat16), 'head', [(i, i ^ 1 << level) for...  1.57 us
  transfers between devices with their start and end apart: 8, of which 4 were waited for; matrix products, arithmetic and copies ran while one was open for 9% of the time, Pallas kernels for 13%

profile of v14, /device:TPU:0, one launch (start us, length us, event | category | flops | bytes accessed | tf_op | source)
XLA Modules:
  0.0 64.5 jit_solution(179489748058280085)
XLA Ops:
  0.6 0.8 %constant_dynamic-update-slice_fusion.1 = bf16[128,512]{1,0:T(8,128)(2,1)S(1)} fusion(bf16[128,256]{1,0:T(8,128)(2,1)} %param.9), kind=kLoop, calls=%fused_computation.24 | loop fusion | bytes 131072
  1.5 0.8 %constant_dynamic-update-slice_fusion = bf16[128,512]{1,0:T(8,128)(2,1)S(1)} fusion(bf16[128,512]{1,0:T(8,128)(2,1)S(1)} %constant_dynamic-update-slice_fusion.1, bf16[128,256]{1,0:T(8,128)(2,1)} %param.10), kind=kLoop, calls=%fused_computation.23 | loop fusion | bytes 131072 | tf_op jit(solution)/shard_map/concatenate | solution.py:225
  2.3 5.0 %collective-permute-start.2 = (bf16[128,512]{1,0:T(8,128)(2,1)S(1)}, bf16[128,512]{1,0:T(8,128)(2,1)S(1)}, u32[]{:S(2)}, u32[]{:S(2)}) collective-permute-start(bf16[128,512]{1,0:T(8,128)(2,1)S(1)} %constant_dynamic-update-slice_fusion), channel_id=1, source_target_pairs={{0,12},{4,0},{8,4},{12,8},{1,13},{5,1},{9,5},{13,9},{2,14},{6,2},{... | collective-permute-start | bytes 393224 | tf_op jit(solution)/shard_map/ppermute | solution.py:43
  7.4 1.0 %collective-permute-start = (bf16[128,512]{1,0:T(8,128)(2,1)S(1)}, bf16[128,512]{1,0:T(8,128)(2,1)S(1)}, u32[]{:S(2)}, u32[]{:S(2)}) collective-permute-start(bf16[128,512]{1,0:T(8,128)(2,1)S(1)} %constant_dynamic-update-slice_fusion), channel_id=1, source_target_pairs={{0,4},{4,8},{8,12},{12,0},{1,5},{5,9},{9,13},{13,1},{2,6},{6,10},{... | collective-permute-start | bytes 393224 | tf_op jit(solution)/shard_map/ppermute | solution.py:43
  8.4 1.2 %dynamic_slice.19 = s32[1]{0:T(128)} dynamic-slice(s32[4]{0:T(128)} %param.13, s32[]{:T(128)S(6)} %select_n.53), dynamic_slice_sizes={1} | dynamic-slice | bytes 12 | tf_op jit(solution)/shard_map/dynamic_slice | solution.py:219
  9.6 0.6 %compare_convert_fusion.1 = s32[4]{0:T(128)S(1)} fusion(s32[]{:T(128)} %bitcast), kind=kLoop, calls=%fused_computation.35 | loop fusion | flops 8 | bytes 20 | tf_op jit(solution)/shard_map/convert_element_type | solution.py:18
  10.4 0.9 %multiply_reduce_fusion = (s32[4]{0:T(128)S(1)}, s32[4]{0:T(128)S(1)}) fusion(s32[4,4]{1,0:T(4,128)} %param.12, s32[4]{0:T(128)S(1)} %compare_convert_fusion.1, s32[4]{0:T(128)} %param.13, s32[4]{0:T(128)S(1)} %select_reduce_fusion.2), kind=kLoop, calls=%fused_computation.28 | loop fusion | flops 72 | bytes 144 | tf_op jit(solution)/shard_map/reduce_sum | solution.py:19
  11.5 7.1 %collective-permute-done.1 = bf16[128,512]{1,0:T(8,128)(2,1)S(1)} collective-permute-done((bf16[128,512]{1,0:T(8,128)(2,1)S(1)}, bf16[128,512]{1,0:T(8,128)(2,1)S(1)}, u32[]{:S(2)}, u32[]{:S(2)}) %collective-permute-start.1) | collective-permute-done | bytes 131104 | tf_op jit(solution)/shard_map/ppermute | solution.py:43
  18.6 0.8 %pad_maximum_fusion.kv_ref = bf16[512,512]{1,0:T(8,128)(2,1)} fusion(bf16[128,512]{1,0:T(8,128)(2,1)S(1)} %collective-permute-done.2, bf16[128,512]{1,0:T(8,128)(2,1)S(1)} %collective-permute-done.1, bf16[128,512]{1,0:T(8,128)(2,1)S(1)} %collective-permute-done, bf16[128,512]{1,0:T(8,128)(2,1)S(1)} %constant_dynamic-update-slice_fusion), kind=kLoop, calls=%fused_computation.17 | loop fusion | flops 2097152 | bytes 1048576 | tf_op jit(solution)/shard_map/concatenate | solution.py:46
  19.4 0.6 broadcast_in_dim.2
  20.1 6.7 %shard_map.111 = (bf16[128,2048]{1,0:T(8,128)(2,1)}, f32[128,512]{1,0:T(8,128)}, bf16[384,512]{1,0:T(8,128)(2,1)}) custom-call(bf16[128,2048]{1,0:T(8,128)(2,1)} %query_ref.1, bf16[128,2048]{1,0:T(8,128)(2,1)} %grad_ref.1, bf16[512,512]{1,0:T(8,128)(2,1)} %pad_maximum_fusion.kv_ref, s32[1,512]{1,0:T(1,128)} %bitcast.34), custom_call_target="tpu_custom_call" | custom-call | tf_op jit(solution)/shard_map/pallas_call | solution.py:197
  26.7 1.1 %fusion.23 = (bf16[128,512]{1,0:T(8,128)(2,1)S(1)}, bf16[128,512]{1,0:T(8,128)(2,1)S(1)}, bf16[128,512]{1,0:T(8,128)(2,1)S(1)}) fusion(bf16[384,512]{1,0:T(8,128)(2,1)} %get-tuple-element.9), kind=kLoop, calls=%fused_computation.42 | loop fusion | bytes 786432 | tf_op jit(solution)/shard_map/slice | solution.py:70
  27.8 1.7 %collective-permute-start.3 = (bf16[128,512]{1,0:T(8,128)(2,1)S(1)}, bf16[128,512]{1,0:T(8,128)(2,1)S(1)}, u32[]{:S(2)}, u32[]{:S(2)}) collective-permute-start(bf16[128,512]{1,0:T(8,128)(2,1)S(1)} %get-tuple-element.10), channel_id=1, source_target_pairs={{0,12},{4,0},{8,4},{12,8},{1,13},{5,1},{9,5},{13,9},{2,14},{6,2},{... | collective-permute-start | bytes 393224 | tf_op jit(solution)/shard_map/ppermute | solution.py:69
  29.9 2.6 %collective-permute-start.4 = (bf16[128,512]{1,0:T(8,128)(2,1)S(1)}, bf16[128,512]{1,0:T(8,128)(2,1)S(1)}, u32[]{:S(2)}, u32[]{:S(2)}) collective-permute-start(bf16[128,512]{1,0:T(8,128)(2,1)S(1)} %get-tuple-element.12), channel_id=1, source_target_pairs={{0,8},{4,12},{8,0},{12,4},{1,9},{5,13},{9,1},{13,5},{2,10},{6,14},... | collective-permute-start | bytes 393224 | tf_op jit(solution)/shard_map/ppermute | solution.py:69
  32.5 4.1 %shard_map.112 = bf16[8192,256]{1,0:T(8,128)(2,1)} custom-call(bf16[8192,256]{1,0:T(8,128)(2,1)} %source.2), custom_call_target="tpu_custom_call" | custom-call | tf_op jit(solution)/shard_map/pallas_call | solution.py:80
  36.6 4.2 %shard_map.113 = bf16[8192,256]{1,0:T(8,128)(2,1)} custom-call(bf16[8192,256]{1,0:T(8,128)(2,1)} %source.3), custom_call_target="tpu_custom_call" | custom-call | tf_op jit(solution)/shard_map/pallas_call | solution.py:80
  40.8 1.0 %collective-permute-done.4 = bf16[128,512]{1,0:T(8,128)(2,1)S(1)} collective-permute-done((bf16[128,512]{1,0:T(8,128)(2,1)S(1)}, bf16[128,512]{1,0:T(8,128)(2,1)S(1)}, u32[]{:S(2)}, u32[]{:S(2)}) %collective-permute-start.4) | collective-permute-done | bytes 131104 | tf_op jit(solution)/shard_map/ppermute | solution.py:69
  42.0 2.4 %fusion.2 = f32[2,2048,128]{2,1,0:T(8,128)S(1)} fusion(bf16[2,2,2048,256]{3,2,1,0:T(8,128)(2,1)} %bitcast.30, s32[]{:T(128)S(6)} %select_n.56, bf16[128,256]{1,0:T(8,128)(2,1)S(1)} %get-tuple-element.14), kind=kOutput, calls=%fused_computation.4 | convolution fusion | flops 268435456 | bytes 4259844 | tf_op jit(solution)/shard_map/arf,tf->art/dot_general | solution.py:107
  44.8 0.7 %fusion = bf16[2,2048,128]{2,1,0:T(8,128)(2,1)S(1)} fusion(f32[2,2048,128]{2,1,0:T(8,128)S(1)} %fusion.2, bf16[2,2,2048,256]{3,2,1,0:T(8,128)(2,1)S(1)} %bitcast.32, s32[]{:T(128)S(6)} %select_n.56, bf16[128,256]{1,0:T(8,128)(2,1)S(1)} %get-tuple-element.13), kind=kOutput, calls=%fused_computation.2 | convolution fusion | flops 269484032 | bytes 5308420 | tf_op jit(solution)/shard_map/arf,tf->art/dot_general | solution.py:112
  45.7 2.4 %fusion.5 = f32[2,2048,128]{2,1,0:T(8,128)S(1)} fusion(bf16[2,2,2048,256]{3,2,1,0:T(8,128)(2,1)} %bitcast.31, s32[]{:T(128)S(6)} %select_n.55, bf16[128,256]{1,0:T(8,128)(2,1)S(1)} %get-tuple-element.14), kind=kOutput, calls=%fused_computation.7 | convolution fusion | flops 268435456 | bytes 4259844 | tf_op jit(solution)/shard_map/arf,tf->art/dot_general | solution.py:107
  48.5 0.7 %convert_add_fusion = f32[2,2048,128]{2,1,0:T(8,128)S(1)} fusion(bf16[2,2048,128]{2,1,0:T(8,128)(2,1)S(1)} %collective-permute-done.6, f32[2,2048,128]{2,1,0:T(8,128)S(1)} %fusion.5, bf16[2,2,2048,256]{3,2,1,0:T(8,128)(2,1)S(1)} %bitcast.33, s32[]{:T(128)S(6)} %select_n.55, bf16[128,256]{1,0:T(8,128)(2,1)S(1)} %get-tuple-element.13), kind=kOutput, calls=%fused_computation.9 | convolution fusion | flops 270008320 | bytes 7405572 | tf_op jit(solution)/shard_map/arf,tf->art/dot_general | solution.py:112
  49.3 1.6 %collective-permute-start.7 = (bf16[1,2048,128]{2,1,0:T(8,128)(2,1)S(1)}, bf16[1,2048,128]{2,1,0:T(8,128)(2,1)S(1)}, u32[]{:S(2)}, u32[]{:S(2)}) collective-permute-start(bf16[1,2048,128]{2,1,0:T(8,128)(2,1)S(1)} %dynamic-slice_convert_fusion), channel_id=1, source_target_pairs={{0,2},{1,3},{2,0},{3,1},{4,6},{5,7},{6,4},{7,5},{8,10},{9,11},{10,... | collective-permute-start | bytes 1572872 | tf_op jit(solution)/shard_map/ppermute | solution.py:130
  50.9 12.8 %collective-permute-done.7 = bf16[1,2048,128]{2,1,0:T(8,128)(2,1)S(1)} collective-permute-done((bf16[1,2048,128]{2,1,0:T(8,128)(2,1)S(1)}, bf16[1,2048,128]{2,1,0:T(8,128)(2,1)S(1)}, u32[]{:S(2)}, u32[]{:S(2)}) %collective-permute-start.7) | collective-permute-done | bytes 524320 | tf_op jit(solution)/shard_map/ppermute | solution.py:130
  63.6 0.9 %fusion.13 = bf16[2048,128]{1,0:T(8,128)(2,1)} fusion(bf16[1,2048,128]{2,1,0:T(8,128)(2,1)S(1)} %collective-permute-done.7, f32[2,2048,128]{2,1,0:T(8,128)S(1)} %convert_add_fusion, s32[]{:T(128)S(6)} %select_n.59), kind=kLoop, calls=%fused_computation.16 | loop fusion | flops 786432 | bytes 2097156 | tf_op jit(solution)/shard_map/convert_element_type | solution.py:134
  (25 shorter events, 1.8 us)
Async XLA Ops:
  2.3 9.2 %collective-permute-start.2 = (bf16[128,512]{1,0:T(8,128)(2,1)S(1)}, bf16[128,512]{1,0:T(8,128)(2,1)S(1)}, u32[]{:S(2)}, u32[]{:S(2)}) collective-permute-start(bf16[128,512]{1,0:T(8,128)(2,1)S(1)} %constant_dynamic-update-slice_fusion), channel_id=1, source_target_pairs={{0,12},{4,0},{8,4},{12,8},{1,13},{5,1},{9,5},{13,9},{2,14},{6,2},{... | collective-permute-start | bytes 393224 | tf_op jit(solution)/shard_map/ppermute | solution.py:43
  7.4 11.2 %collective-permute-start.1 = (bf16[128,512]{1,0:T(8,128)(2,1)S(1)}, bf16[128,512]{1,0:T(8,128)(2,1)S(1)}, u32[]{:S(2)}, u32[]{:S(2)}) collective-permute-start(bf16[128,512]{1,0:T(8,128)(2,1)S(1)} %constant_dynamic-update-slice_fusion), channel_id=1, source_target_pairs={{0,8},{4,12},{8,0},{12,4},{1,9},{5,13},{9,1},{13,5},{2,10},{6,14},... | collective-permute-start | bytes 393224 | tf_op jit(solution)/shard_map/ppermute | solution.py:43
  7.4 11.2 %collective-permute-start = (bf16[128,512]{1,0:T(8,128)(2,1)S(1)}, bf16[128,512]{1,0:T(8,128)(2,1)S(1)}, u32[]{:S(2)}, u32[]{:S(2)}) collective-permute-start(bf16[128,512]{1,0:T(8,128)(2,1)S(1)} %constant_dynamic-update-slice_fusion), channel_id=1, source_target_pairs={{0,4},{4,8},{8,12},{12,0},{1,5},{5,9},{9,13},{13,1},{2,6},{6,10},{... | collective-permute-start | bytes 393224 | tf_op jit(solution)/shard_map/ppermute | solution.py:43
  27.8 13.0 %collective-permute-start.3 = (bf16[128,512]{1,0:T(8,128)(2,1)S(1)}, bf16[128,512]{1,0:T(8,128)(2,1)S(1)}, u32[]{:S(2)}, u32[]{:S(2)}) collective-permute-start(bf16[128,512]{1,0:T(8,128)(2,1)S(1)} %get-tuple-element.10), channel_id=1, source_target_pairs={{0,12},{4,0},{8,4},{12,8},{1,13},{5,1},{9,5},{13,9},{2,14},{6,2},{... | collective-permute-start | bytes 393224 | tf_op jit(solution)/shard_map/ppermute | solution.py:69
  29.4 11.4 %collective-permute-start.5 = (bf16[128,512]{1,0:T(8,128)(2,1)S(1)}, bf16[128,512]{1,0:T(8,128)(2,1)S(1)}, u32[]{:S(2)}, u32[]{:S(2)}) collective-permute-start(bf16[128,512]{1,0:T(8,128)(2,1)S(1)} %get-tuple-element.11), channel_id=1, source_target_pairs={{0,4},{4,8},{8,12},{12,0},{1,5},{5,9},{9,13},{13,1},{2,6},{6,10},{... | collective-permute-start | bytes 393224 | tf_op jit(solution)/shard_map/ppermute | solution.py:69
  29.9 12.0 %collective-permute-start.4 = (bf16[128,512]{1,0:T(8,128)(2,1)S(1)}, bf16[128,512]{1,0:T(8,128)(2,1)S(1)}, u32[]{:S(2)}, u32[]{:S(2)}) collective-permute-start(bf16[128,512]{1,0:T(8,128)(2,1)S(1)} %get-tuple-element.12), channel_id=1, source_target_pairs={{0,8},{4,12},{8,0},{12,4},{1,9},{5,13},{9,1},{13,5},{2,10},{6,14},... | collective-permute-start | bytes 393224 | tf_op jit(solution)/shard_map/ppermute | solution.py:69
  36.6 5.2 %copy-start.4 = (f32[128,512]{1,0:T(8,128)S(1)}, f32[128,512]{1,0:T(8,128)}, u32[]{:S(2)}) copy-start(f32[128,512]{1,0:T(8,128)} %get-tuple-element.8) | copy-start | bytes 786436
  41.9 3.7 %copy-start.3 = (bf16[128,256]{1,0:T(8,128)(2,1)}, bf16[128,256]{1,0:T(8,128)(2,1)S(1)}, u32[]{:S(2)}) copy-start(bf16[128,256]{1,0:T(8,128)(2,1)S(1)} %get-tuple-element.14) | copy-start | bytes 196612
  41.9 6.3 %copy-start.2 = (bf16[128,256]{1,0:T(8,128)(2,1)}, bf16[128,256]{1,0:T(8,128)(2,1)S(1)}, u32[]{:S(2)}) copy-start(bf16[128,256]{1,0:T(8,128)(2,1)S(1)} %get-tuple-element.13) | copy-start | bytes 196612
  42.0 2.9 %copy-start = (bf16[8192,256]{1,0:T(8,128)(2,1)S(1)}, bf16[8192,256]{1,0:T(8,128)(2,1)}, u32[]{:S(2)}) copy-start(bf16[8192,256]{1,0:T(8,128)(2,1)} %shard_map.113) | copy-start | bytes 12582916
  45.5 2.7 %collective-permute-start.6 = (bf16[2,2048,128]{2,1,0:T(8,128)(2,1)S(1)}, bf16[2,2048,128]{2,1,0:T(8,128)(2,1)S(1)}, u32[]{:S(2)}, u32[]{:S(2)}) collective-permute-start(bf16[2,2048,128]{2,1,0:T(8,128)(2,1)S(1)} %fusion), channel_id=1, source_target_pairs={{0,1},{1,0},{2,3},{3,2},{4,5},{5,4},{6,7},{7,6},{8,9},{9,8},{10,11... | collective-permute-start | bytes 3145736 | tf_op jit(solution)/shard_map/ppermute | solution.py:122
  45.7 2.8 %copy-start.1 = (bf16[8192,256]{1,0:T(8,128)(2,1)S(1)}, bf16[8192,256]{1,0:T(8,128)(2,1)}, u32[]{:S(2)}) copy-start(bf16[8192,256]{1,0:T(8,128)(2,1)} %shard_map.113) | copy-start | bytes 12582916
  49.3 14.3 %collective-permute-start.7 = (bf16[1,2048,128]{2,1,0:T(8,128)(2,1)S(1)}, bf16[1,2048,128]{2,1,0:T(8,128)(2,1)S(1)}, u32[]{:S(2)}, u32[]{:S(2)}) collective-permute-start(bf16[1,2048,128]{2,1,0:T(8,128)(2,1)S(1)} %dynamic-slice_convert_fusion), channel_id=1, source_target_pairs={{0,2},{1,3},{2,0},{3,1},{4,6},{5,7},{6,4},{7,5},{8,10},{9,11},{10,... | collective-permute-start | bytes 1572872 | tf_op jit(solution)/shard_map/ppermute | solution.py:130

commit v15 on v14

--- a/solution.py
+++ b/solution.py
@@ -134,9 +134,11 @@
     return current.reshape(block, -1).astype(jnp.bfloat16)
 
 
-def attention_kernel(query_ref, grad_ref, kv_ref, mask_ref, query_out, own_out, sent_out):
+def attention_kernel(
+    query_ref, grad_ref, key_ref, value_ref, mask_ref, query_out, own_out, sent_out
+):
     inv_root = HD ** (-0.5)
-    kv_cols = kv_ref.shape[1] // 2
+    kv_cols = key_ref.shape[1]
     kv_heads = kv_cols // HD
     rows = query_ref.shape[0]
     group_size = query_ref.shape[1] // kv_cols
@@ -147,8 +149,8 @@
     across = (((1,), (1,)), ((), ()))
     down = (((0,), (0,)), ((), ()))
     for kv_head in range(kv_heads):
-        key_head = kv_ref[:, kv_head * HD : (kv_head + 1) * HD]
-        value_head = kv_ref[:, kv_cols + kv_head * HD : kv_cols + (kv_head + 1) * HD]
+        key_head = key_ref[:, kv_head * HD : (kv_head + 1) * HD]
+        value_head = value_ref[:, kv_head * HD : (kv_head + 1) * HD]
         base = kv_head * group_size * HD
         query_stack = jnp.concatenate(
             [query_ref[:, base + m * HD : base + (m + 1) * HD] for m in range(group_size)], axis=0
@@ -192,17 +194,18 @@
         sent_out[:, value_cols] = value_sum[rows:].astype(jnp.bfloat16)
 
 
-def attention_block(queries, out_grad, kv_rows, allowed, interpret=False):
+def attention_block(queries, out_grad, key_rows, value_rows, allowed, interpret=False):
     rows = queries.shape[0]
+    width = 2 * key_rows.shape[1]
     return pl.pallas_call(
         attention_kernel,
         out_shape=(
             jax.ShapeDtypeStruct(queries.shape, jnp.bfloat16),
-            jax.ShapeDtypeStruct((rows, kv_rows.shape[1]), jnp.float32),
-            jax.ShapeDtypeStruct((kv_rows.shape[0] - rows, kv_rows.shape[1]), jnp.bfloat16),
+            jax.ShapeDtypeStruct((rows, width), jnp.float32),
+            jax.ShapeDtypeStruct((key_rows.shape[0] - rows, width), jnp.bfloat16),
         ),
         interpret=interpret,
-    )(queries, out_grad, kv_rows, allowed.astype(jnp.int32))
+    )(queries, out_grad, key_rows, value_rows, allowed.astype(jnp.int32))
 
 
 def local(
@@ -221,9 +224,9 @@
     )
     own_flags = select_rows(mask_flags, own_blocks)
 
-    kv_rows, sources = gather_slots(
-        jnp.concatenate([key_states, value_states], axis=1), "ctx"
-    )
+    key_rows, sources = gather_slots(key_states, "ctx")
+    value_rows = gather_slots(value_states, "ctx")[0]
+    kv_rows = jnp.concatenate([key_rows, value_rows], axis=1)
     row_count = kv_rows.shape[0]
     blocks_here = rows_here // BLK
     key_blocks = lax.iota(jnp.int32, row_count // BLK)
@@ -295,7 +298,9 @@
             allowed = jnp.repeat(column_flags, BLK, axis=1)
         else:
             allowed = chunk(0)[2]
-        query_grad, own_part, sent_part = attention_block(queries, out_grad, kv_rows, allowed)
+        query_grad, own_part, sent_part = attention_block(
+            queries, out_grad, key_rows, value_rows, allowed
+        )
         kv_grad = scatter_parts(own_part, sent_part, "ctx")
     else:
         start_stats = (

time: 64.9 us -> 65.5 us (level)
  starting transfers between devices: 12.4 us -> 18.2 us
  waiting for transfers between devices: 21 us -> 15.3 us
  other arithmetic: 3.63 us -> 5.92 us
  local copies, waits for them, and re-layouts: 5.35 us -> 3.66 us
    ppermute x3 -> x6, waiting for transfers between devices: 7.1 us -> 0.67 us  [gather_slots(): lax.ppermute(block, axis, shifted_pairs(count, steps))]
    ppermute x3 -> x6, starting transfers between devices: 6.06 us -> 11.8 us  [gather_slots(): lax.ppermute(block, axis, shifted_pairs(count, steps))]
    concatenate x1 -> x2, other arithmetic: 0.83 us -> 3.12 us  [gather_slots(): return (jnp.concatenate(pieces, axis=0), sources)]
    concatenate x1 -> x0, local copies, waits for them, and re-layouts: 0.84 us -> none  [local(): jnp.concatenate([key_states, value_states], axis=1)]
    unnamed x11 -> x10, local copies, waits for them, and re-layouts: 1.5 us -> 0.65 us
    ppermute x3, waiting for transfers between devices: 1.02 us -> 1.73 us  [scatter_parts(): lax.ppermute(sent[(steps - 1) * rows:steps * rows], axis, shifted_pairs(c...]
  transfers between devices with their start and end apart: 8 -> 11, of which waited for: 4 -> 4; matrix products, arithmetic and copies ran while one was open for 9% -> 11% of each run, Pallas kernels for 13% -> 13%
where the time goes in v15:
time: 65.5 us; the launch traced here: 65.2 us
  starting transfers between devices  18.2 us (28%)
  waiting for transfers between devices  15.3 us (23%)
  Pallas kernels  15 us (23%)
  matrix products  6.33 us (10%)
  other arithmetic  5.92 us (9%)
  local copies, waits for them, and re-layouts  3.66 us (6%)
  between operations  0.8 us (1%)
    ppermute x1, waiting for transfers between devices, head_reduce(): lax.ppermute(sent.astype(jnp.bfloat16), 'head', [(i, i ^ 1 << level) for...  12.8 us
    ppermute x6, starting transfers between devices, gather_slots(): lax.ppermute(block, axis, shifted_pairs(count, steps))  11.8 us
    pallas_call x2, Pallas kernels, staged(): pl.pallas_call(copy_to_vmem, out_shape=jax.ShapeDtypeStruct(weights.shape...  8.33 us
    pallas_call x1, Pallas kernels, attention_block(): pl.pallas_call(attention_kernel, out_shape=(jax.ShapeDtypeStruct(queries....  6.67 us
    dot_general x2, matrix products, project(): jnp.einsum('arf,tf->art', lax.dynamic_index_in_dim(key_split, half, 1, ke...  4.88 us
    ppermute x3, starting transfers between devices, scatter_parts(): lax.ppermute(sent[(steps - 1) * rows:steps * rows], axis, shifted_pairs(c...  4.73 us
    concatenate x2, other arithmetic, gather_slots(): return (jnp.concatenate(pieces, axis=0), sources)  3.12 us
    ppermute x3, waiting for transfers between devices, scatter_parts(): lax.ppermute(sent[(steps - 1) * rows:steps * rows], axis, shifted_pairs(c...  1.73 us
  transfers between devices with their start and end apart: 11, of which 4 were waited for; matrix products, arithmetic and copies ran while one was open for 11% of the time, Pallas kernels for 13%

profile of v15, /device:TPU:0, one launch (start us, length us, event | category | flops | bytes accessed | tf_op | source)
XLA Modules:
  0.0 65.2 jit_solution(17350850754167136977)
XLA Ops:
  0.6 4.1 %collective-permute-start.1 = (bf16[128,256]{1,0:T(8,128)(2,1)}, bf16[128,256]{1,0:T(8,128)(2,1)S(1)}, u32[]{:S(2)}, u32[]{:S(2)}) collective-permute-start(bf16[128,256]{1,0:T(8,128)(2,1)} %param.9), channel_id=1, source_target_pairs={{0,8},{4,12},{8,0},{12,4},{1,9},{5,13},{9,1},{13,5},{2,10},{6,14},... | collective-permute-start | bytes 196616 | tf_op jit(solution)/shard_map/ppermute | solution.py:43
  4.7 1.6 %collective-permute-start = (bf16[128,256]{1,0:T(8,128)(2,1)}, bf16[128,256]{1,0:T(8,128)(2,1)S(1)}, u32[]{:S(2)}, u32[]{:S(2)}) collective-permute-start(bf16[128,256]{1,0:T(8,128)(2,1)} %param.9), channel_id=1, source_target_pairs={{0,4},{4,8},{8,12},{12,0},{1,5},{5,9},{9,13},{13,1},{2,6},{6,10},{... | collective-permute-start | bytes 196616 | tf_op jit(solution)/shard_map/ppermute | solution.py:43
  6.3 2.2 %collective-permute-start.2 = (bf16[128,256]{1,0:T(8,128)(2,1)}, bf16[128,256]{1,0:T(8,128)(2,1)S(1)}, u32[]{:S(2)}, u32[]{:S(2)}) collective-permute-start(bf16[128,256]{1,0:T(8,128)(2,1)} %param.9), channel_id=1, source_target_pairs={{0,12},{4,0},{8,4},{12,8},{1,13},{5,1},{9,5},{13,9},{2,14},{6,2},{... | collective-permute-start | bytes 196616 | tf_op jit(solution)/shard_map/ppermute | solution.py:43
  9.1 1.2 %dynamic_slice.19 = s32[1]{0:T(128)} dynamic-slice(s32[4]{0:T(128)} %param.13, s32[]{:T(128)S(6)} %select_n.53), dynamic_slice_sizes={1} | dynamic-slice | bytes 12 | tf_op jit(solution)/shard_map/dynamic_slice | solution.py:222
  10.4 0.6 compare_convert_fusion.1
  11.1 0.9 %multiply_reduce_fusion = (s32[4]{0:T(128)S(1)}, s32[4]{0:T(128)S(1)}) fusion(s32[4,4]{1,0:T(4,128)} %param.12, s32[4]{0:T(128)S(1)} %compare_convert_fusion.1, s32[4]{0:T(128)} %param.13, s32[4]{0:T(128)S(1)} %select_reduce_fusion.2), kind=kLoop, calls=%fused_computation.27 | loop fusion | flops 72 | bytes 144 | tf_op jit(solution)/shard_map/reduce_sum | solution.py:19
  12.2 3.3 %collective-permute-start.5 = (bf16[128,256]{1,0:T(8,128)(2,1)}, bf16[128,256]{1,0:T(8,128)(2,1)S(1)}, u32[]{:S(2)}, u32[]{:S(2)}) collective-permute-start(bf16[128,256]{1,0:T(8,128)(2,1)} %param.10), channel_id=1, source_target_pairs={{0,12},{4,0},{8,4},{12,8},{1,13},{5,1},{9,5},{13,9},{2,14},{6,2},{... | collective-permute-start | bytes 196616 | tf_op jit(solution)/shard_map/ppermute | solution.py:43
  15.5 1.6 %pad_maximum_fusion.key_ref = bf16[512,256]{1,0:T(8,128)(2,1)} fusion(bf16[128,256]{1,0:T(8,128)(2,1)S(1)} %collective-permute-done.2, bf16[128,256]{1,0:T(8,128)(2,1)S(1)} %collective-permute-done.1, bf16[128,256]{1,0:T(8,128)(2,1)S(1)} %collective-permute-done, bf16[128,256]{1,0:T(8,128)(2,1)} %param.9), kind=kLoop, calls=%fused_computation.17 | loop fusion | flops 1048576 | bytes 524288 | tf_op jit(solution)/shard_map/concatenate | solution.py:46
  17.1 0.7 %collective-permute-done.5 = bf16[128,256]{1,0:T(8,128)(2,1)S(1)} collective-permute-done((bf16[128,256]{1,0:T(8,128)(2,1)}, bf16[128,256]{1,0:T(8,128)(2,1)S(1)}, u32[]{:S(2)}, u32[]{:S(2)}) %collective-permute-start.5) | collective-permute-done | bytes 65568 | tf_op jit(solution)/shard_map/ppermute | solution.py:43
  17.8 1.6 %pad_maximum_fusion.1.value_ref = bf16[512,256]{1,0:T(8,128)(2,1)} fusion(bf16[128,256]{1,0:T(8,128)(2,1)S(1)} %collective-permute-done.5, bf16[128,256]{1,0:T(8,128)(2,1)S(1)} %collective-permute-done.4, bf16[128,256]{1,0:T(8,128)(2,1)S(1)} %collective-permute-done.3, bf16[128,256]{1,0:T(8,128)(2,1)} %param.10), kind=kLoop, calls=%fused_computation.18 | loop fusion | flops 1048576 | bytes 524288 | tf_op jit(solution)/shard_map/concatenate | solution.py:46
  19.3 0.6 broadcast_in_dim.2
  20.0 6.7 %shard_map.111 = (bf16[128,2048]{1,0:T(8,128)(2,1)}, f32[128,512]{1,0:T(8,128)}, bf16[384,512]{1,0:T(8,128)(2,1)}) custom-call(bf16[128,2048]{1,0:T(8,128)(2,1)} %query_ref.1, bf16[128,2048]{1,0:T(8,128)(2,1)} %grad_ref.1, bf16[512,256]{1,0:T(8,128)(2,1)} %pad_maximum_fusion.key_ref, bf16[512,256]{1,0:T(8,128)(2,1)} %pad_maximum_fusion.1.value_ref, ...), custom_call_target="tpu_custom_call" | custom-call | tf_op jit(solution)/shard_map/pallas_call | solution.py:200
  26.6 1.1 %fusion.23 = (bf16[128,512]{1,0:T(8,128)(2,1)S(1)}, bf16[128,512]{1,0:T(8,128)(2,1)S(1)}, bf16[128,512]{1,0:T(8,128)(2,1)S(1)}) fusion(bf16[384,512]{1,0:T(8,128)(2,1)} %get-tuple-element.9), kind=kLoop, calls=%fused_computation.41 | loop fusion | bytes 786432 | tf_op jit(solution)/shard_map/slice | solution.py:70
  27.7 4.1 %collective-permute-start.6 = (bf16[128,512]{1,0:T(8,128)(2,1)S(1)}, bf16[128,512]{1,0:T(8,128)(2,1)S(1)}, u32[]{:S(2)}, u32[]{:S(2)}) collective-permute-start(bf16[128,512]{1,0:T(8,128)(2,1)S(1)} %get-tuple-element.10), channel_id=1, source_target_pairs={{0,12},{4,0},{8,4},{12,8},{1,13},{5,1},{9,5},{13,9},{2,14},{6,2},{... | collective-permute-start | bytes 393224 | tf_op jit(solution)/shard_map/ppermute | solution.py:69
  32.4 4.1 %shard_map.112 = bf16[8192,256]{1,0:T(8,128)(2,1)} custom-call(bf16[8192,256]{1,0:T(8,128)(2,1)} %source.2), custom_call_target="tpu_custom_call" | custom-call | tf_op jit(solution)/shard_map/pallas_call | solution.py:80
  36.6 4.2 %shard_map.113 = bf16[8192,256]{1,0:T(8,128)(2,1)} custom-call(bf16[8192,256]{1,0:T(8,128)(2,1)} %source.3), custom_call_target="tpu_custom_call" | custom-call | tf_op jit(solution)/shard_map/pallas_call | solution.py:80
  40.8 1.7 %collective-permute-done.7 = bf16[128,512]{1,0:T(8,128)(2,1)S(1)} collective-permute-done((bf16[128,512]{1,0:T(8,128)(2,1)S(1)}, bf16[128,512]{1,0:T(8,128)(2,1)S(1)}, u32[]{:S(2)}, u32[]{:S(2)}) %collective-permute-start.7) | collective-permute-done | bytes 131104 | tf_op jit(solution)/shard_map/ppermute | solution.py:69
  42.6 2.4 %fusion.2 = f32[2,2048,128]{2,1,0:T(8,128)S(1)} fusion(bf16[2,2,2048,256]{3,2,1,0:T(8,128)(2,1)} %bitcast.30, s32[]{:T(128)S(6)} %select_n.56, bf16[128,256]{1,0:T(8,128)(2,1)S(1)} %get-tuple-element.14), kind=kOutput, calls=%fused_computation.4 | convolution fusion | flops 268435456 | bytes 4259844 | tf_op jit(solution)/shard_map/arf,tf->art/dot_general | solution.py:107
  45.5 0.7 %fusion = bf16[2,2048,128]{2,1,0:T(8,128)(2,1)S(1)} fusion(f32[2,2048,128]{2,1,0:T(8,128)S(1)} %fusion.2, bf16[2,2,2048,256]{3,2,1,0:T(8,128)(2,1)S(1)} %bitcast.32, s32[]{:T(128)S(6)} %select_n.56, bf16[128,256]{1,0:T(8,128)(2,1)S(1)} %get-tuple-element.13), kind=kOutput, calls=%fused_computation.2 | convolution fusion | flops 269484032 | bytes 5308420 | tf_op jit(solution)/shard_map/arf,tf->art/dot_general | solution.py:112
  46.3 2.4 %fusion.5 = f32[2,2048,128]{2,1,0:T(8,128)S(1)} fusion(bf16[2,2,2048,256]{3,2,1,0:T(8,128)(2,1)} %bitcast.31, s32[]{:T(128)S(6)} %select_n.55, bf16[128,256]{1,0:T(8,128)(2,1)S(1)} %get-tuple-element.14), kind=kOutput, calls=%fused_computation.7 | convolution fusion | flops 268435456 | bytes 4259844 | tf_op jit(solution)/shard_map/arf,tf->art/dot_general | solution.py:107
  49.1 0.7 %convert_add_fusion = f32[2,2048,128]{2,1,0:T(8,128)S(1)} fusion(bf16[2,2048,128]{2,1,0:T(8,128)(2,1)S(1)} %collective-permute-done.9, f32[2,2048,128]{2,1,0:T(8,128)S(1)} %fusion.5, bf16[2,2,2048,256]{3,2,1,0:T(8,128)(2,1)S(1)} %bitcast.33, s32[]{:T(128)S(6)} %select_n.55, bf16[128,256]{1,0:T(8,128)(2,1)S(1)} %get-tuple-element.13), kind=kOutput, calls=%fused_computation.9 | convolution fusion | flops 270008320 | bytes 7405572 | tf_op jit(solution)/shard_map/arf,tf->art/dot_general | solution.py:112
  50.0 1.6 %collective-permute-start.10 = (bf16[1,2048,128]{2,1,0:T(8,128)(2,1)S(1)}, bf16[1,2048,128]{2,1,0:T(8,128)(2,1)S(1)}, u32[]{:S(2)}, u32[]{:S(2)}) collective-permute-start(bf16[1,2048,128]{2,1,0:T(8,128)(2,1)S(1)} %dynamic-slice_convert_fusion), channel_id=1, source_target_pairs={{0,2},{1,3},{2,0},{3,1},{4,6},{5,7},{6,4},{7,5},{8,10},{9,11},{10,... | collective-permute-start | bytes 1572872 | tf_op jit(solution)/shard_map/ppermute | solution.py:130
  51.5 12.8 %collective-permute-done.10 = bf16[1,2048,128]{2,1,0:T(8,128)(2,1)S(1)} collective-permute-done((bf16[1,2048,128]{2,1,0:T(8,128)(2,1)S(1)}, bf16[1,2048,128]{2,1,0:T(8,128)(2,1)S(1)}, u32[]{:S(2)}, u32[]{:S(2)}) %collective-permute-start.10) | collective-permute-done | bytes 524320 | tf_op jit(solution)/shard_map/ppermute | solution.py:130
  64.3 0.9 %fusion.13 = bf16[2048,128]{1,0:T(8,128)(2,1)} fusion(bf16[1,2048,128]{2,1,0:T(8,128)(2,1)S(1)} %collective-permute-done.10, f32[2,2048,128]{2,1,0:T(8,128)S(1)} %convert_add_fusion, s32[]{:T(128)S(6)} %select_n.59), kind=kLoop, calls=%fused_computation.16 | loop fusion | flops 786432 | bytes 2097156 | tf_op jit(solution)/shard_map/convert_element_type | solution.py:134
  (30 shorter events, 2.5 us)
Async XLA Ops:
  0.6 11.6 %collective-permute-start.1 = (bf16[128,256]{1,0:T(8,128)(2,1)}, bf16[128,256]{1,0:T(8,128)(2,1)S(1)}, u32[]{:S(2)}, u32[]{:S(2)}) collective-permute-start(bf16[128,256]{1,0:T(8,128)(2,1)} %param.9), channel_id=1, source_target_pairs={{0,8},{4,12},{8,0},{12,4},{1,9},{5,13},{9,1},{13,5},{2,10},{6,14},... | collective-permute-start | bytes 196616 | tf_op jit(solution)/shard_map/ppermute | solution.py:43
  4.7 10.8 %collective-permute-start = (bf16[128,256]{1,0:T(8,128)(2,1)}, bf16[128,256]{1,0:T(8,128)(2,1)S(1)}, u32[]{:S(2)}, u32[]{:S(2)}) collective-permute-start(bf16[128,256]{1,0:T(8,128)(2,1)} %param.9), channel_id=1, source_target_pairs={{0,4},{4,8},{8,12},{12,0},{1,5},{5,9},{9,13},{13,1},{2,6},{6,10},{... | collective-permute-start | bytes 196616 | tf_op jit(solution)/shard_map/ppermute | solution.py:43
  6.3 9.2 %collective-permute-start.2 = (bf16[128,256]{1,0:T(8,128)(2,1)}, bf16[128,256]{1,0:T(8,128)(2,1)S(1)}, u32[]{:S(2)}, u32[]{:S(2)}) collective-permute-start(bf16[128,256]{1,0:T(8,128)(2,1)} %param.9), channel_id=1, source_target_pairs={{0,12},{4,0},{8,4},{12,8},{1,13},{5,1},{9,5},{13,9},{2,14},{6,2},{... | collective-permute-start | bytes 196616 | tf_op jit(solution)/shard_map/ppermute | solution.py:43
  8.6 8.5 %collective-permute-start.4 = (bf16[128,256]{1,0:T(8,128)(2,1)}, bf16[128,256]{1,0:T(8,128)(2,1)S(1)}, u32[]{:S(2)}, u32[]{:S(2)}) collective-permute-start(bf16[128,256]{1,0:T(8,128)(2,1)} %param.10), channel_id=1, source_target_pairs={{0,8},{4,12},{8,0},{12,4},{1,9},{5,13},{9,1},{13,5},{2,10},{6,14},... | collective-permute-start | bytes 196616 | tf_op jit(solution)/shard_map/ppermute | solution.py:43
  8.6 8.5 %collective-permute-start.3 = (bf16[128,256]{1,0:T(8,128)(2,1)}, bf16[128,256]{1,0:T(8,128)(2,1)S(1)}, u32[]{:S(2)}, u32[]{:S(2)}) collective-permute-start(bf16[128,256]{1,0:T(8,128)(2,1)} %param.10), channel_id=1, source_target_pairs={{0,4},{4,8},{8,12},{12,0},{1,5},{5,9},{9,13},{13,1},{2,6},{6,10},{... | collective-permute-start | bytes 196616 | tf_op jit(solution)/shard_map/ppermute | solution.py:43
  12.2 5.5 %collective-permute-start.5 = (bf16[128,256]{1,0:T(8,128)(2,1)}, bf16[128,256]{1,0:T(8,128)(2,1)S(1)}, u32[]{:S(2)}, u32[]{:S(2)}) collective-permute-start(bf16[128,256]{1,0:T(8,128)(2,1)} %param.10), channel_id=1, source_target_pairs={{0,12},{4,0},{8,4},{12,8},{1,13},{5,1},{9,5},{13,9},{2,14},{6,2},{... | collective-permute-start | bytes 196616 | tf_op jit(solution)/shard_map/ppermute | solution.py:43
  27.7 13.1 %collective-permute-start.6 = (bf16[128,512]{1,0:T(8,128)(2,1)S(1)}, bf16[128,512]{1,0:T(8,128)(2,1)S(1)}, u32[]{:S(2)}, u32[]{:S(2)}) collective-permute-start(bf16[128,512]{1,0:T(8,128)(2,1)S(1)} %get-tuple-element.10), channel_id=1, source_target_pairs={{0,12},{4,0},{8,4},{12,8},{1,13},{5,1},{9,5},{13,9},{2,14},{6,2},{... | collective-permute-start | bytes 393224 | tf_op jit(solution)/shard_map/ppermute | solution.py:69
  31.8 9.0 %collective-permute-start.8 = (bf16[128,512]{1,0:T(8,128)(2,1)S(1)}, bf16[128,512]{1,0:T(8,128)(2,1)S(1)}, u32[]{:S(2)}, u32[]{:S(2)}) collective-permute-start(bf16[128,512]{1,0:T(8,128)(2,1)S(1)} %get-tuple-element.11), channel_id=1, source_target_pairs={{0,4},{4,8},{8,12},{12,0},{1,5},{5,9},{9,13},{13,1},{2,6},{6,10},{... | collective-permute-start | bytes 393224 | tf_op jit(solution)/shard_map/ppermute | solution.py:69
  31.8 10.7 %collective-permute-start.7 = (bf16[128,512]{1,0:T(8,128)(2,1)S(1)}, bf16[128,512]{1,0:T(8,128)(2,1)S(1)}, u32[]{:S(2)}, u32[]{:S(2)}) collective-permute-start(bf16[128,512]{1,0:T(8,128)(2,1)S(1)} %get-tuple-element.12), channel_id=1, source_target_pairs={{0,8},{4,12},{8,0},{12,4},{1,9},{5,13},{9,1},{13,5},{2,10},{6,14},... | collective-permute-start | bytes 393224 | tf_op jit(solution)/shard_map/ppermute | solution.py:69
  36.6 5.9 %copy-start.4 = (f32[128,512]{1,0:T(8,128)S(1)}, f32[128,512]{1,0:T(8,128)}, u32[]{:S(2)}) copy-start(f32[128,512]{1,0:T(8,128)} %get-tuple-element.8) | copy-start | bytes 786436
  42.6 3.7 %copy-start.3 = (bf16[128,256]{1,0:T(8,128)(2,1)}, bf16[128,256]{1,0:T(8,128)(2,1)S(1)}, u32[]{:S(2)}) copy-start(bf16[128,256]{1,0:T(8,128)(2,1)S(1)} %get-tuple-element.14) | copy-start | bytes 196612
  42.6 6.3 %copy-start.2 = (bf16[128,256]{1,0:T(8,128)(2,1)}, bf16[128,256]{1,0:T(8,128)(2,1)S(1)}, u32[]{:S(2)}) copy-start(bf16[128,256]{1,0:T(8,128)(2,1)S(1)} %get-tuple-element.13) | copy-start | bytes 196612
  42.6 2.9 %copy-start = (bf16[8192,256]{1,0:T(8,128)(2,1)S(1)}, bf16[8192,256]{1,0:T(8,128)(2,1)}, u32[]{:S(2)}) copy-start(bf16[8192,256]{1,0:T(8,128)(2,1)} %shard_map.113) | copy-start | bytes 12582916
  46.2 2.7 %collective-permute-start.9 = (bf16[2,2048,128]{2,1,0:T(8,128)(2,1)S(1)}, bf16[2,2048,128]{2,1,0:T(8,128)(2,1)S(1)}, u32[]{:S(2)}, u32[]{:S(2)}) collective-permute-start(bf16[2,2048,128]{2,1,0:T(8,128)(2,1)S(1)} %fusion), channel_id=1, source_target_pairs={{0,1},{1,0},{2,3},{3,2},{4,5},{5,4},{6,7},{7,6},{8,9},{9,8},{10,11... | collective-permute-start | bytes 3145736 | tf_op jit(solution)/shard_map/ppermute | solution.py:122
  46.3 2.8 %copy-start.1 = (bf16[8192,256]{1,0:T(8,128)(2,1)S(1)}, bf16[8192,256]{1,0:T(8,128)(2,1)}, u32[]{:S(2)}) copy-start(bf16[8192,256]{1,0:T(8,128)(2,1)} %shard_map.113) | copy-start | bytes 12582916
  50.0 14.3 %collective-permute-start.10 = (bf16[1,2048,128]{2,1,0:T(8,128)(2,1)S(1)}, bf16[1,2048,128]{2,1,0:T(8,128)(2,1)S(1)}, u32[]{:S(2)}, u32[]{:S(2)}) collective-permute-start(bf16[1,2048,128]{2,1,0:T(8,128)(2,1)S(1)} %dynamic-slice_convert_fusion), channel_id=1, source_target_pairs={{0,2},{1,3},{2,0},{3,1},{4,6},{5,7},{6,4},{7,5},{8,10},{9,11},{10,... | collective-permute-start | bytes 1572872 | tf_op jit(solution)/shard_map/ppermute | solution.py:130

commit v16 on v12

--- a/solution.py
+++ b/solution.py
@@ -4,6 +4,7 @@
 import jax.numpy as jnp
 from jax import lax
 from jax.experimental import pallas as pl
+from jax.experimental.pallas import tpu as pltpu
 from jax.sharding import PartitionSpec as P
 
 HD = 128
@@ -71,6 +72,24 @@
     return total
 
 
+def copy_in_order(order_ref, source, target):
+    blocks = order_ref.shape[0]
+    rows = target.shape[0] // blocks
+    for i in range(blocks):
+        pltpu.sync_copy(
+            source.at[pl.ds(order_ref[i] * rows, rows)], target.at[pl.ds(i * rows, rows)]
+        )
+
+
+def staged(weights, order):
+    return pl.pallas_call(
+        copy_in_order,
+        out_shape=jax.ShapeDtypeStruct(weights.shape, weights.dtype),
+        in_specs=[pl.BlockSpec(memory_space=pltpu.SMEM), pl.BlockSpec(memory_space=pl.ANY)],
+        out_specs=pl.BlockSpec(memory_space=pl.ANY),
+    )(order, weights)
+
+
 def head_reduce(key_proj, value_proj, key_grad, value_grad):
     count = lax.axis_size("head")
     position = lax.axis_index("head")
@@ -84,25 +103,21 @@
             jnp.bfloat16
         )
     block = key_proj.shape[0] // count
-    key_split = key_proj.reshape(count // 2, 2, block, key_proj.shape[1])
-    value_split = value_proj.reshape(count // 2, 2, block, value_proj.shape[1])
-
-    def project(half):
+    own_bit = position % 2
+    upper = lax.iota(jnp.int32, count // 2) * 2
+    order = jnp.concatenate([upper + 1 - own_bit, upper + own_bit])
+    key_split = staged(key_proj, order).reshape(2, count // 2, block, key_proj.shape[1])
+    value_split = staged(value_proj, order).reshape(2, count // 2, block, value_proj.shape[1])
+
+    def project(part):
         return jnp.einsum(
-            "arf,tf->art",
-            lax.dynamic_index_in_dim(key_split, half, 1, keepdims=False),
-            key_grad,
-            preferred_element_type=jnp.float32,
+            "arf,tf->art", key_split[part], key_grad, preferred_element_type=jnp.float32
         ) + jnp.einsum(
-            "arf,tf->art",
-            lax.dynamic_index_in_dim(value_split, half, 1, keepdims=False),
-            value_grad,
-            preferred_element_type=jnp.float32,
-        )
-
-    own_bit = position % 2
-    sent = project(1 - own_bit)
-    kept = project(own_bit)
+            "arf,tf->art", value_split[part], value_grad, preferred_element_type=jnp.float32
+        )
+
+    sent = project(0)
+    kept = project(1)
     current = kept + lax.ppermute(
         sent.astype(jnp.bfloat16), "head", [(i, i ^ 1) for i in range(count)]
     ).astype(jnp.float32)

time: 65.8 us -> 327 us (4.97)
  Pallas kernels: 6.69 us -> 271 us
  local copies, waits for them, and re-layouts: 5.35 us -> 12.6 us
  waiting for transfers between devices: 29.3 us -> 23.3 us
    pallas_call x0 -> x2, Pallas kernels: none -> 264 us  [staged(): pl.pallas_call(copy_in_order, out_shape=jax.ShapeDtypeStruct(weights.shap...]
    ppermute x3, waiting for transfers between devices: 7.1 us -> 0.01 us  [gather_slots(): lax.ppermute(block, axis, shifted_pairs(count, steps))]
    slice x0 -> x2, local copies, waits for them, and re-layouts: none -> 6.95 us  [the longest x1 4.46 us: project(): value_split[part]]
  transfers between devices with their start and end apart: 8 -> 8, of which waited for: 6 -> 5; matrix products, arithmetic and copies ran while one was open for 8% -> 3% of each run, Pallas kernels for 0% -> 81%
where the time goes in v16:
time: 327 us
  Pallas kernels  271 us (83%)
  waiting for transfers between devices  23.3 us (7%)
  local copies, waits for them, and re-layouts  12.6 us (4%)
  starting transfers between devices  11.6 us (4%)
  matrix products  3.81 us (1%)
  other arithmetic  3.53 us (1%)
    pallas_call x2, Pallas kernels, staged(): pl.pallas_call(copy_in_order, out_shape=jax.ShapeDtypeStruct(weights.shap...  264 us
    ppermute x1, waiting for transfers between devices, head_reduce(): lax.ppermute(sent.astype(jnp.bfloat16), 'head', [(i, i ^ 1 << level) for...  12.5 us
    ppermute x3, waiting for transfers between devices, scatter_parts(): lax.ppermute(sent[(steps - 1) * rows:steps * rows], axis, shifted_pairs(c...  8.69 us
    pallas_call x1, Pallas kernels, attention_block(): pl.pallas_call(attention_kernel, out_shape=(jax.ShapeDtypeStruct(queries....  6.73 us
  transfers between devices with their start and end apart: 8, of which 5 were waited for; matrix products, arithmetic and copies ran while one was open for 3% of the time, Pallas kernels for 81%

profile of v16, /device:TPU:0, one launch (start us, length us, event | category | flops | bytes accessed | tf_op | source)
XLA Modules:
  0.0 326.8 jit_solution(892060591454761125)
XLA Ops:
  0.6 0.8 constant_dynamic-update-slice_fusion.1
  1.5 0.8 constant_dynamic-update-slice_fusion
  2.3 5.0 %collective-permute-start.2 = (bf16[128,512]{1,0:T(8,128)(2,1)S(1)}, bf16[128,512]{1,0:T(8,128)(2,1)S(1)}, u32[]{:S(2)}, u32[]{:S(2)}) collective-permute-start(bf16[128,512]{1,0:T(8,128)(2,1)S(1)} %constant_dynamic-update-slice_fusion), channel_id=1, source_target_pairs={{0,12},{4,0},{8,4},{12,8},{1,13},{5,1},{9,5},{13,9},{2,14},{6,2},{... | collective-permute-start | bytes 393224 | tf_op jit(solution)/shard_map/ppermute | solution.py:43
  7.4 1.0 collective-permute-start
  8.4 1.2 dynamic_slice.6
  11.0 132.1 %shard_map.113 = bf16[8192,256]{1,0:T(8,128)(2,1)} custom-call(s32[4]{0:T(128)} %pad_add_fusion.order_ref, bf16[8192,256]{1,0:T(8,128)(2,1)} %source.3), custom_call_target="tpu_custom_call" | custom-call | tf_op jit(solution)/shard_map/pallas_call | solution.py:85
  143.1 4.5 %fusion.12 = (bf16[4096,256]{1,0:T(8,128)(2,1)}, bf16[4096,256]{1,0:T(8,128)(2,1)}) fusion(bf16[8192,256]{1,0:T(8,128)(2,1)} %shard_map.113), kind=kLoop, calls=%fused_computation.34 | loop fusion | bytes 8388608 | tf_op jit(solution)/shard_map/slice | solution.py:116
  147.6 132.2 %shard_map.112 = bf16[8192,256]{1,0:T(8,128)(2,1)} custom-call(s32[4]{0:T(128)} %pad_add_fusion.order_ref, bf16[8192,256]{1,0:T(8,128)(2,1)} %source.2), custom_call_target="tpu_custom_call" | custom-call | tf_op jit(solution)/shard_map/pallas_call | solution.py:85
  280.2 0.8 pad_maximum_fusion.kv_ref
  281.7 6.7 %shard_map.111 = (bf16[128,2048]{1,0:T(8,128)(2,1)}, f32[128,512]{1,0:T(8,128)}, bf16[384,512]{1,0:T(8,128)(2,1)}) custom-call(bf16[128,2048]{1,0:T(8,128)(2,1)} %query_ref.1, bf16[128,2048]{1,0:T(8,128)(2,1)} %grad_ref.1, bf16[512,512]{1,0:T(8,128)(2,1)} %pad_maximum_fusion.kv_ref, s32[1,512]{1,0:T(1,128)} %bitcast.28), custom_call_target="tpu_custom_call" | custom-call | tf_op jit(solution)/shard_map/pallas_call | solution.py:196
  288.5 1.1 fusion.14
  289.5 2.9 collective-permute-start.3
  292.4 1.1 collective-permute-start.4
  293.5 2.5 fusion.13
  296.3 3.9 %collective-permute-done.5 = bf16[128,512]{1,0:T(8,128)(2,1)S(1)} collective-permute-done((bf16[128,512]{1,0:T(8,128)(2,1)S(1)}, bf16[128,512]{1,0:T(8,128)(2,1)S(1)}, u32[]{:S(2)}, u32[]{:S(2)}) %collective-permute-start.5) | collective-permute-done | bytes 131104 | tf_op jit(solution)/shard_map/ppermute | solution.py:69
  300.2 4.5 %collective-permute-done.4 = bf16[128,512]{1,0:T(8,128)(2,1)S(1)} collective-permute-done((bf16[128,512]{1,0:T(8,128)(2,1)S(1)}, bf16[128,512]{1,0:T(8,128)(2,1)S(1)}, u32[]{:S(2)}, u32[]{:S(2)}) %collective-permute-start.4) | collective-permute-done | bytes 131104 | tf_op jit(solution)/shard_map/ppermute | solution.py:69
  304.8 0.7 fusion.6
  305.5 0.9 copy-done.1
  306.5 1.7 fusion
  308.8 2.2 collective-permute-done.6
  311.0 0.7 convert_add_fusion
  311.8 1.6 collective-permute-start.7
  313.4 12.5 %collective-permute-done.7 = bf16[1,2048,128]{2,1,0:T(8,128)(2,1)S(1)} collective-permute-done((bf16[1,2048,128]{2,1,0:T(8,128)(2,1)S(1)}, bf16[1,2048,128]{2,1,0:T(8,128)(2,1)S(1)}, u32[]{:S(2)}, u32[]{:S(2)}) %collective-permute-start.7) | collective-permute-done | bytes 524320 | tf_op jit(solution)/shard_map/ppermute | solution.py:129
  325.9 0.9 fusion.1
  (33 shorter events, 3.6 us)
Async XLA Ops:
  2.3 277.9 %collective-permute-start.2 = (bf16[128,512]{1,0:T(8,128)(2,1)S(1)}, bf16[128,512]{1,0:T(8,128)(2,1)S(1)}, u32[]{:S(2)}, u32[]{:S(2)}) collective-permute-start(bf16[128,512]{1,0:T(8,128)(2,1)S(1)} %constant_dynamic-update-slice_fusion), channel_id=1, source_target_pairs={{0,12},{4,0},{8,4},{12,8},{1,13},{5,1},{9,5},{13,9},{2,14},{6,2},{... | collective-permute-start | bytes 393224 | tf_op jit(solution)/shard_map/ppermute | solution.py:43
  7.4 272.9 %collective-permute-start.1 = (bf16[128,512]{1,0:T(8,128)(2,1)S(1)}, bf16[128,512]{1,0:T(8,128)(2,1)S(1)}, u32[]{:S(2)}, u32[]{:S(2)}) collective-permute-start(bf16[128,512]{1,0:T(8,128)(2,1)S(1)} %constant_dynamic-update-slice_fusion), channel_id=1, source_target_pairs={{0,8},{4,12},{8,0},{12,4},{1,9},{5,13},{9,1},{13,5},{2,10},{6,14},... | collective-permute-start | bytes 393224 | tf_op jit(solution)/shard_map/ppermute | solution.py:43
  7.4 272.9 %collective-permute-start = (bf16[128,512]{1,0:T(8,128)(2,1)S(1)}, bf16[128,512]{1,0:T(8,128)(2,1)S(1)}, u32[]{:S(2)}, u32[]{:S(2)}) collective-permute-start(bf16[128,512]{1,0:T(8,128)(2,1)S(1)} %constant_dynamic-update-slice_fusion), channel_id=1, source_target_pairs={{0,4},{4,8},{8,12},{12,0},{1,5},{5,9},{9,13},{13,1},{2,6},{6,10},{... | collective-permute-start | bytes 393224 | tf_op jit(solution)/shard_map/ppermute | solution.py:43
  147.6 132.3 %copy-start.5 = (s32[4,4]{1,0:T(4,128)S(1)}, s32[4,4]{1,0:T(4,128)}, u32[]{:S(2)}) copy-start(s32[4,4]{1,0:T(4,128)} %param.12) | copy-start | bytes 196
  147.6 132.3 %copy-start.6 = (s32[4]{0:T(128)S(1)}, s32[4]{0:T(128)}, u32[]{:S(2)}) copy-start(s32[4]{0:T(128)} %param.13) | copy-start | bytes 52
  289.5 6.8 %collective-permute-start.3 = (bf16[128,512]{1,0:T(8,128)(2,1)S(1)}, bf16[128,512]{1,0:T(8,128)(2,1)S(1)}, u32[]{:S(2)}, u32[]{:S(2)}) collective-permute-start(bf16[128,512]{1,0:T(8,128)(2,1)S(1)} %get-tuple-element.14), channel_id=1, source_target_pairs={{0,12},{4,0},{8,4},{12,8},{1,13},{5,1},{9,5},{13,9},{2,14},{6,2},{... | collective-permute-start | bytes 393224 | tf_op jit(solution)/shard_map/ppermute | solution.py:69
  292.4 7.8 %collective-permute-start.5 = (bf16[128,512]{1,0:T(8,128)(2,1)S(1)}, bf16[128,512]{1,0:T(8,128)(2,1)S(1)}, u32[]{:S(2)}, u32[]{:S(2)}) collective-permute-start(bf16[128,512]{1,0:T(8,128)(2,1)S(1)} %get-tuple-element.15), channel_id=1, source_target_pairs={{0,4},{4,8},{8,12},{12,0},{1,5},{5,9},{9,13},{13,1},{2,6},{6,10},{... | collective-permute-start | bytes 393224 | tf_op jit(solution)/shard_map/ppermute | solution.py:69
  292.4 12.3 %copy-start.4 = (f32[128,512]{1,0:T(8,128)S(1)}, f32[128,512]{1,0:T(8,128)}, u32[]{:S(2)}) copy-start(f32[128,512]{1,0:T(8,128)} %get-tuple-element.8) | copy-start | bytes 786436
  292.4 12.3 %collective-permute-start.4 = (bf16[128,512]{1,0:T(8,128)(2,1)S(1)}, bf16[128,512]{1,0:T(8,128)(2,1)S(1)}, u32[]{:S(2)}, u32[]{:S(2)}) collective-permute-start(bf16[128,512]{1,0:T(8,128)(2,1)S(1)} %get-tuple-element.16), channel_id=1, source_target_pairs={{0,8},{4,12},{8,0},{12,4},{1,9},{5,13},{9,1},{13,5},{2,10},{6,14},... | collective-permute-start | bytes 393224 | tf_op jit(solution)/shard_map/ppermute | solution.py:69
  304.8 3.4 %copy-start.2 = (bf16[128,256]{1,0:T(8,128)(2,1)}, bf16[128,256]{1,0:T(8,128)(2,1)S(1)}, u32[]{:S(2)}) copy-start(bf16[128,256]{1,0:T(8,128)(2,1)S(1)} %get-tuple-element.18) | copy-start | bytes 196612
  304.8 6.2 %copy-start.3 = (bf16[128,256]{1,0:T(8,128)(2,1)}, bf16[128,256]{1,0:T(8,128)(2,1)S(1)}, u32[]{:S(2)}) copy-start(bf16[128,256]{1,0:T(8,128)(2,1)S(1)} %get-tuple-element.17) | copy-start | bytes 196612
  304.8 1.6 copy-start.1
  308.1 2.9 collective-permute-start.6
  308.1 2.9 copy-start
  311.8 14.0 %collective-permute-start.7 = (bf16[1,2048,128]{2,1,0:T(8,128)(2,1)S(1)}, bf16[1,2048,128]{2,1,0:T(8,128)(2,1)S(1)}, u32[]{:S(2)}, u32[]{:S(2)}) collective-permute-start(bf16[1,2048,128]{2,1,0:T(8,128)(2,1)S(1)} %dynamic-slice_convert_fusion), channel_id=1, source_target_pairs={{0,2},{1,3},{2,0},{3,1},{4,6},{5,7},{6,4},{7,5},{8,10},{9,11},{10,... | collective-permute-start | bytes 1572872 | tf_op jit(solution)/shard_map/ppermute | solution.py:129

commit v17 on v14

--- a/solution.py
+++ b/solution.py
@@ -67,7 +67,7 @@
     total = own
     for steps in range(1, count):
         total = total + lax.ppermute(
-            sent[(steps - 1) * rows : steps * rows], axis, shifted_pairs(count, -steps)
+            sent[steps - 1], axis, shifted_pairs(count, -steps)
         ).astype(jnp.float32)
     return total
 
@@ -134,7 +134,7 @@
     return current.reshape(block, -1).astype(jnp.bfloat16)
 
 
-def attention_kernel(query_ref, grad_ref, kv_ref, mask_ref, query_out, own_out, sent_out):
+def attention_kernel(query_ref, grad_ref, kv_ref, mask_ref, query_out, own_out, *sent_outs):
     inv_root = HD ** (-0.5)
     kv_cols = kv_ref.shape[1] // 2
     kv_heads = kv_cols // HD
@@ -188,8 +188,11 @@
         value_cols = slice(kv_cols + kv_head * HD, kv_cols + (kv_head + 1) * HD)
         own_out[:, key_cols] = key_sum[:rows]
         own_out[:, value_cols] = value_sum[:rows]
-        sent_out[:, key_cols] = key_sum[rows:].astype(jnp.bfloat16)
-        sent_out[:, value_cols] = value_sum[rows:].astype(jnp.bfloat16)
+        for slot, sent_out in enumerate(sent_outs, start=1):
+            sent_out[:, key_cols] = key_sum[slot * rows : (slot + 1) * rows].astype(jnp.bfloat16)
+            sent_out[:, value_cols] = value_sum[slot * rows : (slot + 1) * rows].astype(
+                jnp.bfloat16
+            )
 
 
 def attention_block(queries, out_grad, kv_rows, allowed, interpret=False):
@@ -199,7 +202,10 @@
         out_shape=(
             jax.ShapeDtypeStruct(queries.shape, jnp.bfloat16),
             jax.ShapeDtypeStruct((rows, kv_rows.shape[1]), jnp.float32),
-            jax.ShapeDtypeStruct((kv_rows.shape[0] - rows, kv_rows.shape[1]), jnp.bfloat16),
+        )
+        + tuple(
+            jax.ShapeDtypeStruct((rows, kv_rows.shape[1]), jnp.bfloat16)
+            for _ in range(kv_rows.shape[0] // rows - 1)
         ),
         interpret=interpret,
     )(queries, out_grad, kv_rows, allowed.astype(jnp.int32))
@@ -295,8 +301,8 @@
             allowed = jnp.repeat(column_flags, BLK, axis=1)
         else:
             allowed = chunk(0)[2]
-        query_grad, own_part, sent_part = attention_block(queries, out_grad, kv_rows, allowed)
-        kv_grad = scatter_parts(own_part, sent_part, "ctx")
+        query_grad, own_part, *sent_parts = attention_block(queries, out_grad, kv_rows, allowed)
+        kv_grad = scatter_parts(own_part, sent_parts, "ctx")
     else:
         start_stats = (
             jnp.full((kv_heads, group_size, rows_here), masked_score, jnp.float32),

time: 64.9 us -> 63.9 us (0.985)
  local copies, waits for them, and re-layouts: 5.35 us -> 4.29 us
    slice x1 -> x0, local copies, waits for them, and re-layouts: 1.06 us -> none  [scatter_parts(): sent[(steps - 1) * rows:steps * rows]]
where the time goes in v17:
time: 63.9 us; the launch traced here: 63.6 us
  waiting for transfers between devices  21.2 us (33%)
  Pallas kernels  15 us (23%)
  starting transfers between devices  12.3 us (19%)
  matrix products  6.33 us (10%)
  local copies, waits for them, and re-layouts  4.29 us (7%)
  other arithmetic  3.63 us (6%)
  between operations  0.8 us (1%)
    ppermute x1, waiting for transfers between devices, head_reduce(): lax.ppermute(sent.astype(jnp.bfloat16), 'head', [(i, i ^ 1 << level) for...  12.8 us
    pallas_call x2, Pallas kernels, staged(): pl.pallas_call(copy_to_vmem, out_shape=jax.ShapeDtypeStruct(weights.shape...  8.32 us
    ppermute x3, waiting for transfers between devices, gather_slots(): lax.ppermute(block, axis, shifted_pairs(count, steps))  7.1 us
    pallas_call x1, Pallas kernels, attention_block(): pl.pallas_call(attention_kernel, out_shape=(jax.ShapeDtypeStruct(queries....  6.66 us
    ppermute x3, starting transfers between devices, gather_slots(): lax.ppermute(block, axis, shifted_pairs(count, steps))  6.06 us
    dot_general x2, matrix products, project(): jnp.einsum('arf,tf->art', lax.dynamic_index_in_dim(key_split, half, 1, ke...  4.88 us
    ppermute x3, starting transfers between devices, scatter_parts(): lax.ppermute(sent[steps - 1], axis, shifted_pairs(count, -steps))  4.65 us
    ppermute x1, starting transfers between devices, head_reduce(): lax.ppermute(sent.astype(jnp.bfloat16), 'head', [(i, i ^ 1 << level) for...  1.55 us
  transfers between devices with their start and end apart: 8, of which 4 were waited for; matrix products, arithmetic and copies ran while one was open for 9% of the time, Pallas kernels for 13%

profile of v17, /device:TPU:0, one launch (start us, length us, event | category | flops | bytes accessed | tf_op | source)
XLA Modules:
  0.0 63.6 jit_solution(9682329428500604903)
XLA Ops:
  0.6 0.8 %constant_dynamic-update-slice_fusion.1 = bf16[128,512]{1,0:T(8,128)(2,1)S(1)} fusion(bf16[128,256]{1,0:T(8,128)(2,1)} %param.9), kind=kLoop, calls=%fused_computation.24 | loop fusion | bytes 131072
  1.5 0.8 %constant_dynamic-update-slice_fusion = bf16[128,512]{1,0:T(8,128)(2,1)S(1)} fusion(bf16[128,512]{1,0:T(8,128)(2,1)S(1)} %constant_dynamic-update-slice_fusion.1, bf16[128,256]{1,0:T(8,128)(2,1)} %param.10), kind=kLoop, calls=%fused_computation.23 | loop fusion | bytes 131072 | tf_op jit(solution)/shard_map/concatenate | solution.py:231
  2.3 5.0 %collective-permute-start.2 = (bf16[128,512]{1,0:T(8,128)(2,1)S(1)}, bf16[128,512]{1,0:T(8,128)(2,1)S(1)}, u32[]{:S(2)}, u32[]{:S(2)}) collective-permute-start(bf16[128,512]{1,0:T(8,128)(2,1)S(1)} %constant_dynamic-update-slice_fusion), channel_id=1, source_target_pairs={{0,12},{4,0},{8,4},{12,8},{1,13},{5,1},{9,5},{13,9},{2,14},{6,2},{... | collective-permute-start | bytes 393224 | tf_op jit(solution)/shard_map/ppermute | solution.py:43
  7.4 1.0 %collective-permute-start = (bf16[128,512]{1,0:T(8,128)(2,1)S(1)}, bf16[128,512]{1,0:T(8,128)(2,1)S(1)}, u32[]{:S(2)}, u32[]{:S(2)}) collective-permute-start(bf16[128,512]{1,0:T(8,128)(2,1)S(1)} %constant_dynamic-update-slice_fusion), channel_id=1, source_target_pairs={{0,4},{4,8},{8,12},{12,0},{1,5},{5,9},{9,13},{13,1},{2,6},{6,10},{... | collective-permute-start | bytes 393224 | tf_op jit(solution)/shard_map/ppermute | solution.py:43
  8.4 1.2 %dynamic_slice.19 = s32[1]{0:T(128)} dynamic-slice(s32[4]{0:T(128)} %param.13, s32[]{:T(128)S(6)} %select_n.53), dynamic_slice_sizes={1} | dynamic-slice | bytes 12 | tf_op jit(solution)/shard_map/dynamic_slice | solution.py:225
  9.6 0.6 %compare_convert_fusion.1 = s32[4]{0:T(128)S(1)} fusion(s32[]{:T(128)} %bitcast), kind=kLoop, calls=%fused_computation.35 | loop fusion | flops 8 | bytes 20 | tf_op jit(solution)/shard_map/convert_element_type | solution.py:18
  10.4 0.9 %multiply_reduce_fusion = (s32[4]{0:T(128)S(1)}, s32[4]{0:T(128)S(1)}) fusion(s32[4,4]{1,0:T(4,128)} %param.12, s32[4]{0:T(128)S(1)} %compare_convert_fusion.1, s32[4]{0:T(128)} %param.13, s32[4]{0:T(128)S(1)} %select_reduce_fusion.2), kind=kLoop, calls=%fused_computation.28 | loop fusion | flops 72 | bytes 144 | tf_op jit(solution)/shard_map/reduce_sum | solution.py:19
  11.5 7.1 %collective-permute-done.1 = bf16[128,512]{1,0:T(8,128)(2,1)S(1)} collective-permute-done((bf16[128,512]{1,0:T(8,128)(2,1)S(1)}, bf16[128,512]{1,0:T(8,128)(2,1)S(1)}, u32[]{:S(2)}, u32[]{:S(2)}) %collective-permute-start.1) | collective-permute-done | bytes 131104 | tf_op jit(solution)/shard_map/ppermute | solution.py:43
  18.6 0.8 %pad_maximum_fusion.kv_ref = bf16[512,512]{1,0:T(8,128)(2,1)} fusion(bf16[128,512]{1,0:T(8,128)(2,1)S(1)} %collective-permute-done.2, bf16[128,512]{1,0:T(8,128)(2,1)S(1)} %collective-permute-done.1, bf16[128,512]{1,0:T(8,128)(2,1)S(1)} %collective-permute-done, bf16[128,512]{1,0:T(8,128)(2,1)S(1)} %constant_dynamic-update-slice_fusion), kind=kLoop, calls=%fused_computation.17 | loop fusion | flops 2097152 | bytes 1048576 | tf_op jit(solution)/shard_map/concatenate | solution.py:46
  19.4 0.6 %broadcast_in_dim.2 = s32[4,128]{1,0:T(4,128)} broadcast(s32[4]{0:T(128)S(1)} %compare_convert_fusion), dimensions={0} | broadcast | bytes 2064 | tf_op jit(solution)/shard_map/broadcast_in_dim | solution.py:301
  20.1 6.7 %shard_map.111 = (bf16[128,2048]{1,0:T(8,128)(2,1)}, f32[128,512]{1,0:T(8,128)}, bf16[128,512]{1,0:T(8,128)(2,1)}, bf16[128,512]{1,0:T(8,128)(2,1)}, bf16[128,512]{1,0:T(8,128)(2,1)}) custom-call(bf16[128,2048]{1,0:T(8,128)(2,1)} %query_ref.1, bf16[128,2048]{1,0:T(8,128)(2,1)} %grad_ref.1, bf16[512,512]{1,0:T(8,128)(2,1)} %pad_maximum_fusion.kv_ref, ...), custom_call_target="tpu_custom_call" | custom-call | tf_op jit(solution)/shard_map/pallas_call | solution.py:200
  26.7 1.6 %collective-permute-start.3 = (bf16[128,512]{1,0:T(8,128)(2,1)}, bf16[128,512]{1,0:T(8,128)(2,1)S(1)}, u32[]{:S(2)}, u32[]{:S(2)}) collective-permute-start(bf16[128,512]{1,0:T(8,128)(2,1)} %get-tuple-element.11), channel_id=1, source_target_pairs={{0,12},{4,0},{8,4},{12,8},{1,13},{5,1},{9,5},{13,9},{2,14},{6,2},{... | collective-permute-start | bytes 393224 | tf_op jit(solution)/shard_map/ppermute | solution.py:69
  28.3 1.0 %collective-permute-start.4 = (bf16[128,512]{1,0:T(8,128)(2,1)}, bf16[128,512]{1,0:T(8,128)(2,1)S(1)}, u32[]{:S(2)}, u32[]{:S(2)}) collective-permute-start(bf16[128,512]{1,0:T(8,128)(2,1)} %get-tuple-element.12), channel_id=1, source_target_pairs={{0,8},{4,12},{8,0},{12,4},{1,9},{5,13},{9,1},{13,5},{2,10},{6,14},... | collective-permute-start | bytes 393224 | tf_op jit(solution)/shard_map/ppermute | solution.py:69
  29.3 2.0 %collective-permute-start.5 = (bf16[128,512]{1,0:T(8,128)(2,1)}, bf16[128,512]{1,0:T(8,128)(2,1)S(1)}, u32[]{:S(2)}, u32[]{:S(2)}) collective-permute-start(bf16[128,512]{1,0:T(8,128)(2,1)} %get-tuple-element.13), channel_id=1, source_target_pairs={{0,4},{4,8},{8,12},{12,0},{1,5},{5,9},{9,13},{13,1},{2,6},{6,10},{... | collective-permute-start | bytes 393224 | tf_op jit(solution)/shard_map/ppermute | solution.py:69
  31.4 4.1 %shard_map.112 = bf16[8192,256]{1,0:T(8,128)(2,1)} custom-call(bf16[8192,256]{1,0:T(8,128)(2,1)} %source.2), custom_call_target="tpu_custom_call" | custom-call | tf_op jit(solution)/shard_map/pallas_call | solution.py:80
  35.5 4.2 %shard_map.113 = bf16[8192,256]{1,0:T(8,128)(2,1)} custom-call(bf16[8192,256]{1,0:T(8,128)(2,1)} %source.3), custom_call_target="tpu_custom_call" | custom-call | tf_op jit(solution)/shard_map/pallas_call | solution.py:80
  39.7 1.2 %collective-permute-done.4 = bf16[128,512]{1,0:T(8,128)(2,1)S(1)} collective-permute-done((bf16[128,512]{1,0:T(8,128)(2,1)}, bf16[128,512]{1,0:T(8,128)(2,1)S(1)}, u32[]{:S(2)}, u32[]{:S(2)}) %collective-permute-start.4) | collective-permute-done | bytes 131104 | tf_op jit(solution)/shard_map/ppermute | solution.py:69
  41.0 2.4 %fusion.2 = f32[2,2048,128]{2,1,0:T(8,128)S(1)} fusion(bf16[2,2,2048,256]{3,2,1,0:T(8,128)(2,1)} %bitcast.30, s32[]{:T(128)S(6)} %select_n.56, bf16[128,256]{1,0:T(8,128)(2,1)S(1)} %get-tuple-element.15), kind=kOutput, calls=%fused_computation.4 | convolution fusion | flops 268435456 | bytes 4259844 | tf_op jit(solution)/shard_map/arf,tf->art/dot_general | solution.py:107
  43.9 0.7 %fusion = bf16[2,2048,128]{2,1,0:T(8,128)(2,1)S(1)} fusion(f32[2,2048,128]{2,1,0:T(8,128)S(1)} %fusion.2, bf16[2,2,2048,256]{3,2,1,0:T(8,128)(2,1)S(1)} %bitcast.32, s32[]{:T(128)S(6)} %select_n.56, bf16[128,256]{1,0:T(8,128)(2,1)S(1)} %get-tuple-element.14), kind=kOutput, calls=%fused_computation.2 | convolution fusion | flops 269484032 | bytes 5308420 | tf_op jit(solution)/shard_map/arf,tf->art/dot_general | solution.py:112
  44.7 2.4 %fusion.5 = f32[2,2048,128]{2,1,0:T(8,128)S(1)} fusion(bf16[2,2,2048,256]{3,2,1,0:T(8,128)(2,1)} %bitcast.31, s32[]{:T(128)S(6)} %select_n.55, bf16[128,256]{1,0:T(8,128)(2,1)S(1)} %get-tuple-element.15), kind=kOutput, calls=%fused_computation.7 | convolution fusion | flops 268435456 | bytes 4259844 | tf_op jit(solution)/shard_map/arf,tf->art/dot_general | solution.py:107
  47.5 0.7 %convert_add_fusion = f32[2,2048,128]{2,1,0:T(8,128)S(1)} fusion(bf16[2,2048,128]{2,1,0:T(8,128)(2,1)S(1)} %collective-permute-done.6, f32[2,2048,128]{2,1,0:T(8,128)S(1)} %fusion.5, bf16[2,2,2048,256]{3,2,1,0:T(8,128)(2,1)S(1)} %bitcast.33, s32[]{:T(128)S(6)} %select_n.55, bf16[128,256]{1,0:T(8,128)(2,1)S(1)} %get-tuple-element.14), kind=kOutput, calls=%fused_computation.9 | convolution fusion | flops 270008320 | bytes 7405572 | tf_op jit(solution)/shard_map/arf,tf->art/dot_general | solution.py:112
  48.3 1.6 %collective-permute-start.7 = (bf16[1,2048,128]{2,1,0:T(8,128)(2,1)S(1)}, bf16[1,2048,128]{2,1,0:T(8,128)(2,1)S(1)}, u32[]{:S(2)}, u32[]{:S(2)}) collective-permute-start(bf16[1,2048,128]{2,1,0:T(8,128)(2,1)S(1)} %dynamic-slice_convert_fusion), channel_id=1, source_target_pairs={{0,2},{1,3},{2,0},{3,1},{4,6},{5,7},{6,4},{7,5},{8,10},{9,11},{10,... | collective-permute-start | bytes 1572872 | tf_op jit(solution)/shard_map/ppermute | solution.py:130
  49.9 12.8 %collective-permute-done.7 = bf16[1,2048,128]{2,1,0:T(8,128)(2,1)S(1)} collective-permute-done((bf16[1,2048,128]{2,1,0:T(8,128)(2,1)S(1)}, bf16[1,2048,128]{2,1,0:T(8,128)(2,1)S(1)}, u32[]{:S(2)}, u32[]{:S(2)}) %collective-permute-start.7) | collective-permute-done | bytes 524320 | tf_op jit(solution)/shard_map/ppermute | solution.py:130
  62.7 0.9 %fusion.13 = bf16[2048,128]{1,0:T(8,128)(2,1)} fusion(bf16[1,2048,128]{2,1,0:T(8,128)(2,1)S(1)} %collective-permute-done.7, f32[2,2048,128]{2,1,0:T(8,128)S(1)} %convert_add_fusion, s32[]{:T(128)S(6)} %select_n.59), kind=kLoop, calls=%fused_computation.16 | loop fusion | flops 786432 | bytes 2097156 | tf_op jit(solution)/shard_map/convert_element_type | solution.py:134
  (24 shorter events, 1.3 us)
Async XLA Ops:
  2.3 9.2 %collective-permute-start.2 = (bf16[128,512]{1,0:T(8,128)(2,1)S(1)}, bf16[128,512]{1,0:T(8,128)(2,1)S(1)}, u32[]{:S(2)}, u32[]{:S(2)}) collective-permute-start(bf16[128,512]{1,0:T(8,128)(2,1)S(1)} %constant_dynamic-update-slice_fusion), channel_id=1, source_target_pairs={{0,12},{4,0},{8,4},{12,8},{1,13},{5,1},{9,5},{13,9},{2,14},{6,2},{... | collective-permute-start | bytes 393224 | tf_op jit(solution)/shard_map/ppermute | solution.py:43
  7.4 11.2 %collective-permute-start.1 = (bf16[128,512]{1,0:T(8,128)(2,1)S(1)}, bf16[128,512]{1,0:T(8,128)(2,1)S(1)}, u32[]{:S(2)}, u32[]{:S(2)}) collective-permute-start(bf16[128,512]{1,0:T(8,128)(2,1)S(1)} %constant_dynamic-update-slice_fusion), channel_id=1, source_target_pairs={{0,8},{4,12},{8,0},{12,4},{1,9},{5,13},{9,1},{13,5},{2,10},{6,14},... | collective-permute-start | bytes 393224 | tf_op jit(solution)/shard_map/ppermute | solution.py:43
  7.4 11.2 %collective-permute-start = (bf16[128,512]{1,0:T(8,128)(2,1)S(1)}, bf16[128,512]{1,0:T(8,128)(2,1)S(1)}, u32[]{:S(2)}, u32[]{:S(2)}) collective-permute-start(bf16[128,512]{1,0:T(8,128)(2,1)S(1)} %constant_dynamic-update-slice_fusion), channel_id=1, source_target_pairs={{0,4},{4,8},{8,12},{12,0},{1,5},{5,9},{9,13},{13,1},{2,6},{6,10},{... | collective-permute-start | bytes 393224 | tf_op jit(solution)/shard_map/ppermute | solution.py:43
  26.7 13.0 %collective-permute-start.3 = (bf16[128,512]{1,0:T(8,128)(2,1)}, bf16[128,512]{1,0:T(8,128)(2,1)S(1)}, u32[]{:S(2)}, u32[]{:S(2)}) collective-permute-start(bf16[128,512]{1,0:T(8,128)(2,1)} %get-tuple-element.11), channel_id=1, source_target_pairs={{0,12},{4,0},{8,4},{12,8},{1,13},{5,1},{9,5},{13,9},{2,14},{6,2},{... | collective-permute-start | bytes 393224 | tf_op jit(solution)/shard_map/ppermute | solution.py:69
  28.3 12.6 %collective-permute-start.4 = (bf16[128,512]{1,0:T(8,128)(2,1)}, bf16[128,512]{1,0:T(8,128)(2,1)S(1)}, u32[]{:S(2)}, u32[]{:S(2)}) collective-permute-start(bf16[128,512]{1,0:T(8,128)(2,1)} %get-tuple-element.12), channel_id=1, source_target_pairs={{0,8},{4,12},{8,0},{12,4},{1,9},{5,13},{9,1},{13,5},{2,10},{6,14},... | collective-permute-start | bytes 393224 | tf_op jit(solution)/shard_map/ppermute | solution.py:69
  29.3 11.5 %collective-permute-start.5 = (bf16[128,512]{1,0:T(8,128)(2,1)}, bf16[128,512]{1,0:T(8,128)(2,1)S(1)}, u32[]{:S(2)}, u32[]{:S(2)}) collective-permute-start(bf16[128,512]{1,0:T(8,128)(2,1)} %get-tuple-element.13), channel_id=1, source_target_pairs={{0,4},{4,8},{8,12},{12,0},{1,5},{5,9},{9,13},{13,1},{2,6},{6,10},{... | collective-permute-start | bytes 393224 | tf_op jit(solution)/shard_map/ppermute | solution.py:69
  35.5 5.4 %copy-start.4 = (f32[128,512]{1,0:T(8,128)S(1)}, f32[128,512]{1,0:T(8,128)}, u32[]{:S(2)}) copy-start(f32[128,512]{1,0:T(8,128)} %get-tuple-element.10) | copy-start | bytes 786436
  41.0 3.7 %copy-start.3 = (bf16[128,256]{1,0:T(8,128)(2,1)}, bf16[128,256]{1,0:T(8,128)(2,1)S(1)}, u32[]{:S(2)}) copy-start(bf16[128,256]{1,0:T(8,128)(2,1)S(1)} %get-tuple-element.15) | copy-start | bytes 196612
  41.0 6.3 %copy-start.2 = (bf16[128,256]{1,0:T(8,128)(2,1)}, bf16[128,256]{1,0:T(8,128)(2,1)S(1)}, u32[]{:S(2)}) copy-start(bf16[128,256]{1,0:T(8,128)(2,1)S(1)} %get-tuple-element.14) | copy-start | bytes 196612
  41.0 2.9 %copy-start = (bf16[8192,256]{1,0:T(8,128)(2,1)S(1)}, bf16[8192,256]{1,0:T(8,128)(2,1)}, u32[]{:S(2)}) copy-start(bf16[8192,256]{1,0:T(8,128)(2,1)} %shard_map.113) | copy-start | bytes 12582916
  44.6 2.7 %collective-permute-start.6 = (bf16[2,2048,128]{2,1,0:T(8,128)(2,1)S(1)}, bf16[2,2048,128]{2,1,0:T(8,128)(2,1)S(1)}, u32[]{:S(2)}, u32[]{:S(2)}) collective-permute-start(bf16[2,2048,128]{2,1,0:T(8,128)(2,1)S(1)} %fusion), channel_id=1, source_target_pairs={{0,1},{1,0},{2,3},{3,2},{4,5},{5,4},{6,7},{7,6},{8,9},{9,8},{10,11... | collective-permute-start | bytes 3145736 | tf_op jit(solution)/shard_map/ppermute | solution.py:122
  44.7 2.8 %copy-start.1 = (bf16[8192,256]{1,0:T(8,128)(2,1)S(1)}, bf16[8192,256]{1,0:T(8,128)(2,1)}, u32[]{:S(2)}) copy-start(bf16[8192,256]{1,0:T(8,128)(2,1)} %shard_map.113) | copy-start | bytes 12582916
  48.3 14.3 %collective-permute-start.7 = (bf16[1,2048,128]{2,1,0:T(8,128)(2,1)S(1)}, bf16[1,2048,128]{2,1,0:T(8,128)(2,1)S(1)}, u32[]{:S(2)}, u32[]{:S(2)}) collective-permute-start(bf16[1,2048,128]{2,1,0:T(8,128)(2,1)S(1)} %dynamic-slice_convert_fusion), channel_id=1, source_target_pairs={{0,2},{1,3},{2,0},{3,1},{4,6},{5,7},{6,4},{7,5},{8,10},{9,11},{10,... | collective-permute-start | bytes 1572872 | tf_op jit(solution)/shard_map/ppermute | solution.py:130

commit v18 on v17

--- a/solution.py
+++ b/solution.py
@@ -38,12 +38,12 @@
     position = lax.axis_index(axis)
     if count > 8:
         gathered = lax.all_gather(block, axis, axis=0, tiled=True)
-        return gathered, lax.iota(jnp.int32, count)
+        return [gathered], lax.iota(jnp.int32, count)
     pieces = [block] + [
         lax.ppermute(block, axis, shifted_pairs(count, steps)) for steps in range(1, count)
     ]
     sources = (position - lax.iota(jnp.int32, count)) % count
-    return jnp.concatenate(pieces, axis=0), sources
+    return pieces, sources
 
 
 def scatter_slots(slots, axis):
@@ -134,7 +134,11 @@
     return current.reshape(block, -1).astype(jnp.bfloat16)
 
 
-def attention_kernel(query_ref, grad_ref, kv_ref, mask_ref, query_out, own_out, *sent_outs):
+def attention_kernel(query_ref, grad_ref, mask_ref, *refs):
+    slot_count = (len(refs) - 1) // 2
+    kv_ref = jnp.concatenate([piece[...] for piece in refs[:slot_count]], axis=0)
+    query_out, own_out = refs[slot_count], refs[slot_count + 1]
+    sent_outs = refs[slot_count + 2 :]
     inv_root = HD ** (-0.5)
     kv_cols = kv_ref.shape[1] // 2
     kv_heads = kv_cols // HD
@@ -195,20 +199,20 @@
             )
 
 
-def attention_block(queries, out_grad, kv_rows, allowed, interpret=False):
+def attention_block(queries, out_grad, kv_pieces, allowed, interpret=False):
     rows = queries.shape[0]
+    width = kv_pieces[0].shape[1]
     return pl.pallas_call(
         attention_kernel,
         out_shape=(
             jax.ShapeDtypeStruct(queries.shape, jnp.bfloat16),
-            jax.ShapeDtypeStruct((rows, kv_rows.shape[1]), jnp.float32),
+            jax.ShapeDtypeStruct((rows, width), jnp.float32),
         )
         + tuple(
-            jax.ShapeDtypeStruct((rows, kv_rows.shape[1]), jnp.bfloat16)
-            for _ in range(kv_rows.shape[0] // rows - 1)
+            jax.ShapeDtypeStruct((rows, width), jnp.bfloat16) for _ in range(len(kv_pieces) - 1)
         ),
         interpret=interpret,
-    )(queries, out_grad, kv_rows, allowed.astype(jnp.int32))
+    )(queries, out_grad, allowed.astype(jnp.int32), *kv_pieces)
 
 
 def local(
@@ -227,9 +231,10 @@
     )
     own_flags = select_rows(mask_flags, own_blocks)
 
-    kv_rows, sources = gather_slots(
+    kv_pieces, sources = gather_slots(
         jnp.concatenate([key_states, value_states], axis=1), "ctx"
     )
+    kv_rows = jnp.concatenate(kv_pieces, axis=0)
     row_count = kv_rows.shape[0]
     blocks_here = rows_here // BLK
     key_blocks = lax.iota(jnp.int32, row_count // BLK)
@@ -301,7 +306,7 @@
             allowed = jnp.repeat(column_flags, BLK, axis=1)
         else:
             allowed = chunk(0)[2]
-        query_grad, own_part, *sent_parts = attention_block(queries, out_grad, kv_rows, allowed)
+        query_grad, own_part, *sent_parts = attention_block(queries, out_grad, kv_pieces, allowed)
         kv_grad = scatter_parts(own_part, sent_parts, "ctx")
     else:
         start_stats = (

time: 63.9 us -> 63.1 us (0.987)
  other arithmetic: 3.63 us -> 2.8 us
    concatenate x1 -> x0, other arithmetic: 0.83 us -> none  [gather_slots(): return (jnp.concatenate(pieces, axis=0), sources)]
    unnamed x11 -> x19, local copies, waits for them, and re-layouts: 1.5 us -> 1.53 us
where the time goes in v18:
time: 63.1 us; the launch traced here: 62.8 us
  waiting for transfers between devices  21.2 us (34%)
  Pallas kernels  15 us (24%)
  starting transfers between devices  12.3 us (19%)
  matrix products  6.33 us (10%)
  local copies, waits for them, and re-layouts  4.34 us (7%)
  other arithmetic  2.8 us (4%)
  between operations  0.81 us (1%)
    ppermute x1, waiting for transfers between devices, head_reduce(): lax.ppermute(sent.astype(jnp.bfloat16), 'head', [(i, i ^ 1 << level) for...  12.8 us
    pallas_call x2, Pallas kernels, staged(): pl.pallas_call(copy_to_vmem, out_shape=jax.ShapeDtypeStruct(weights.shape...  8.33 us
    ppermute x3, waiting for transfers between devices, gather_slots(): lax.ppermute(block, axis, shifted_pairs(count, steps))  7.09 us
    pallas_call x1, Pallas kernels, attention_block(): pl.pallas_call(attention_kernel, out_shape=(jax.ShapeDtypeStruct(queries....  6.66 us
    ppermute x3, starting transfers between devices, gather_slots(): lax.ppermute(block, axis, shifted_pairs(count, steps))  6.06 us
    dot_general x2, matrix products, project(): jnp.einsum('arf,tf->art', lax.dynamic_index_in_dim(key_split, half, 1, ke...  4.88 us
    ppermute x3, starting transfers between devices, scatter_parts(): lax.ppermute(sent[steps - 1], axis, shifted_pairs(count, -steps))  4.63 us
    ppermute x1, starting transfers between devices, head_reduce(): lax.ppermute(sent.astype(jnp.bfloat16), 'head', [(i, i ^ 1 << level) for...  1.56 us
  transfers between devices with their start and end apart: 8, of which 4 were waited for; matrix products, arithmetic and copies ran while one was open for 9% of the time, Pallas kernels for 13%

profile of v18, /device:TPU:0, one launch (start us, length us, event | category | flops | bytes accessed | tf_op | source)
XLA Modules:
  0.0 62.8 jit_solution(11852287353001948527)
XLA Ops:
  0.6 0.8 %constant_dynamic-update-slice_fusion.1 = bf16[128,512]{1,0:T(8,128)(2,1)S(1)} fusion(bf16[128,256]{1,0:T(8,128)(2,1)} %param.9), kind=kLoop, calls=%fused_computation.23 | loop fusion | bytes 131072
  1.5 0.8 %constant_dynamic-update-slice_fusion.refs_0_ = bf16[128,512]{1,0:T(8,128)(2,1)S(1)} fusion(bf16[128,512]{1,0:T(8,128)(2,1)S(1)} %constant_dynamic-update-slice_fusion.1, bf16[128,256]{1,0:T(8,128)(2,1)} %param.10), kind=kLoop, calls=%fused_computation.22 | loop fusion | bytes 131072 | tf_op jit(solution)/shard_map/concatenate | solution.py:235
  2.3 5.0 %collective-permute-start.2 = (bf16[128,512]{1,0:T(8,128)(2,1)S(1)}, bf16[128,512]{1,0:T(8,128)(2,1)S(1)}, u32[]{:S(2)}, u32[]{:S(2)}) collective-permute-start(bf16[128,512]{1,0:T(8,128)(2,1)S(1)} %constant_dynamic-update-slice_fusion.refs_0_), channel_id=1, source_target_pairs={{0,12},{4,0},{8,4},{12,8},{1,13},{5,1},{9,5},{13,9},{2,14},{6,2},{... | collective-permute-start | bytes 393224 | tf_op jit(solution)/shard_map/ppermute | solution.py:43
  7.4 1.0 %collective-permute-start = (bf16[128,512]{1,0:T(8,128)(2,1)S(1)}, bf16[128,512]{1,0:T(8,128)(2,1)S(1)}, u32[]{:S(2)}, u32[]{:S(2)}) collective-permute-start(bf16[128,512]{1,0:T(8,128)(2,1)S(1)} %constant_dynamic-update-slice_fusion.refs_0_), channel_id=1, source_target_pairs={{0,4},{4,8},{8,12},{12,0},{1,5},{5,9},{9,13},{13,1},{2,6},{6,10},{... | collective-permute-start | bytes 393224 | tf_op jit(solution)/shard_map/ppermute | solution.py:43
  8.4 1.2 %dynamic_slice.19 = s32[1]{0:T(128)} dynamic-slice(s32[4]{0:T(128)} %param.13, s32[]{:T(128)S(6)} %select_n.53), dynamic_slice_sizes={1} | dynamic-slice | bytes 12 | tf_op jit(solution)/shard_map/dynamic_slice | solution.py:229
  9.6 0.6 %compare_convert_fusion.1 = s32[4]{0:T(128)S(1)} fusion(s32[]{:T(128)} %bitcast), kind=kLoop, calls=%fused_computation.34 | loop fusion | flops 8 | bytes 20 | tf_op jit(solution)/shard_map/convert_element_type | solution.py:18
  10.4 0.9 %multiply_reduce_fusion = (s32[4]{0:T(128)S(1)}, s32[4]{0:T(128)S(1)}) fusion(s32[4,4]{1,0:T(4,128)} %param.12, s32[4]{0:T(128)S(1)} %compare_convert_fusion.1, s32[4]{0:T(128)} %param.13, s32[4]{0:T(128)S(1)} %select_reduce_fusion.2), kind=kLoop, calls=%fused_computation.27 | loop fusion | flops 72 | bytes 144 | tf_op jit(solution)/shard_map/reduce_sum | solution.py:19
  11.5 7.1 %collective-permute-done.1.refs_2_ = bf16[128,512]{1,0:T(8,128)(2,1)S(1)} collective-permute-done((bf16[128,512]{1,0:T(8,128)(2,1)S(1)}, bf16[128,512]{1,0:T(8,128)(2,1)S(1)}, u32[]{:S(2)}, u32[]{:S(2)}) %collective-permute-start.1) | collective-permute-done | bytes 131104 | tf_op jit(solution)/shard_map/ppermute | solution.py:43
  18.6 0.7 %broadcast_in_dim.2 = s32[4,128]{1,0:T(4,128)} broadcast(s32[4]{0:T(128)S(1)} %compare_convert_fusion), dimensions={0} | broadcast | bytes 2064 | tf_op jit(solution)/shard_map/broadcast_in_dim | solution.py:306
  19.3 6.7 %shard_map.111 = (bf16[128,2048]{1,0:T(8,128)(2,1)}, f32[128,512]{1,0:T(8,128)}, bf16[128,512]{1,0:T(8,128)(2,1)}, bf16[128,512]{1,0:T(8,128)(2,1)}, bf16[128,512]{1,0:T(8,128)(2,1)}) custom-call(bf16[128,2048]{1,0:T(8,128)(2,1)} %query_ref.1, bf16[128,2048]{1,0:T(8,128)(2,1)} %grad_ref.1, s32[1,512]{1,0:T(1,128)} %bitcast.34, bf16[128,512]{1,0:T(8,128)(2,1)} %copy-done.4, ...), custom_call_target="tpu_custom_call" | custom-call | tf_op jit(solution)/shard_map/pallas_call | solution.py:205
  25.9 1.6 %collective-permute-start.3 = (bf16[128,512]{1,0:T(8,128)(2,1)}, bf16[128,512]{1,0:T(8,128)(2,1)S(1)}, u32[]{:S(2)}, u32[]{:S(2)}) collective-permute-start(bf16[128,512]{1,0:T(8,128)(2,1)} %get-tuple-element.11), channel_id=1, source_target_pairs={{0,12},{4,0},{8,4},{12,8},{1,13},{5,1},{9,5},{13,9},{2,14},{6,2},{... | collective-permute-start | bytes 393224 | tf_op jit(solution)/shard_map/ppermute | solution.py:69
  27.5 1.0 %collective-permute-start.4 = (bf16[128,512]{1,0:T(8,128)(2,1)}, bf16[128,512]{1,0:T(8,128)(2,1)S(1)}, u32[]{:S(2)}, u32[]{:S(2)}) collective-permute-start(bf16[128,512]{1,0:T(8,128)(2,1)} %get-tuple-element.12), channel_id=1, source_target_pairs={{0,8},{4,12},{8,0},{12,4},{1,9},{5,13},{9,1},{13,5},{2,10},{6,14},... | collective-permute-start | bytes 393224 | tf_op jit(solution)/shard_map/ppermute | solution.py:69
  28.5 2.0 %collective-permute-start.5 = (bf16[128,512]{1,0:T(8,128)(2,1)}, bf16[128,512]{1,0:T(8,128)(2,1)S(1)}, u32[]{:S(2)}, u32[]{:S(2)}) collective-permute-start(bf16[128,512]{1,0:T(8,128)(2,1)} %get-tuple-element.13), channel_id=1, source_target_pairs={{0,4},{4,8},{8,12},{12,0},{1,5},{5,9},{9,13},{13,1},{2,6},{6,10},{... | collective-permute-start | bytes 393224 | tf_op jit(solution)/shard_map/ppermute | solution.py:69
  30.6 4.1 %shard_map.112 = bf16[8192,256]{1,0:T(8,128)(2,1)} custom-call(bf16[8192,256]{1,0:T(8,128)(2,1)} %source.2), custom_call_target="tpu_custom_call" | custom-call | tf_op jit(solution)/shard_map/pallas_call | solution.py:80
  34.7 4.2 %shard_map.113 = bf16[8192,256]{1,0:T(8,128)(2,1)} custom-call(bf16[8192,256]{1,0:T(8,128)(2,1)} %source.3), custom_call_target="tpu_custom_call" | custom-call | tf_op jit(solution)/shard_map/pallas_call | solution.py:80
  38.9 1.2 %collective-permute-done.4 = bf16[128,512]{1,0:T(8,128)(2,1)S(1)} collective-permute-done((bf16[128,512]{1,0:T(8,128)(2,1)}, bf16[128,512]{1,0:T(8,128)(2,1)S(1)}, u32[]{:S(2)}, u32[]{:S(2)}) %collective-permute-start.4) | collective-permute-done | bytes 131104 | tf_op jit(solution)/shard_map/ppermute | solution.py:69
  40.2 2.4 %fusion.2 = f32[2,2048,128]{2,1,0:T(8,128)S(1)} fusion(bf16[2,2,2048,256]{3,2,1,0:T(8,128)(2,1)} %bitcast.30, s32[]{:T(128)S(6)} %select_n.56, bf16[128,256]{1,0:T(8,128)(2,1)S(1)} %get-tuple-element.15), kind=kOutput, calls=%fused_computation.4 | convolution fusion | flops 268435456 | bytes 4259844 | tf_op jit(solution)/shard_map/arf,tf->art/dot_general | solution.py:107
  42.7 0.4 copy-done
  43.1 0.7 %fusion = bf16[2,2048,128]{2,1,0:T(8,128)(2,1)S(1)} fusion(f32[2,2048,128]{2,1,0:T(8,128)S(1)} %fusion.2, bf16[2,2,2048,256]{3,2,1,0:T(8,128)(2,1)S(1)} %bitcast.32, s32[]{:T(128)S(6)} %select_n.56, bf16[128,256]{1,0:T(8,128)(2,1)S(1)} %get-tuple-element.14), kind=kOutput, calls=%fused_computation.2 | convolution fusion | flops 269484032 | bytes 5308420 | tf_op jit(solution)/shard_map/arf,tf->art/dot_general | solution.py:112
  43.9 2.4 %fusion.5 = f32[2,2048,128]{2,1,0:T(8,128)S(1)} fusion(bf16[2,2,2048,256]{3,2,1,0:T(8,128)(2,1)} %bitcast.31, s32[]{:T(128)S(6)} %select_n.55, bf16[128,256]{1,0:T(8,128)(2,1)S(1)} %get-tuple-element.15), kind=kOutput, calls=%fused_computation.7 | convolution fusion | flops 268435456 | bytes 4259844 | tf_op jit(solution)/shard_map/arf,tf->art/dot_general | solution.py:107
  46.7 0.7 %convert_add_fusion = f32[2,2048,128]{2,1,0:T(8,128)S(1)} fusion(bf16[2,2048,128]{2,1,0:T(8,128)(2,1)S(1)} %collective-permute-done.6, f32[2,2048,128]{2,1,0:T(8,128)S(1)} %fusion.5, bf16[2,2,2048,256]{3,2,1,0:T(8,128)(2,1)S(1)} %bitcast.33, s32[]{:T(128)S(6)} %select_n.55, bf16[128,256]{1,0:T(8,128)(2,1)S(1)} %get-tuple-element.14), kind=kOutput, calls=%fused_computation.9 | convolution fusion | flops 270008320 | bytes 7405572 | tf_op jit(solution)/shard_map/arf,tf->art/dot_general | solution.py:112
  47.5 1.6 %collective-permute-start.7 = (bf16[1,2048,128]{2,1,0:T(8,128)(2,1)S(1)}, bf16[1,2048,128]{2,1,0:T(8,128)(2,1)S(1)}, u32[]{:S(2)}, u32[]{:S(2)}) collective-permute-start(bf16[1,2048,128]{2,1,0:T(8,128)(2,1)S(1)} %dynamic-slice_convert_fusion), channel_id=1, source_target_pairs={{0,2},{1,3},{2,0},{3,1},{4,6},{5,7},{6,4},{7,5},{8,10},{9,11},{10,... | collective-permute-start | bytes 1572872 | tf_op jit(solution)/shard_map/ppermute | solution.py:130
  49.1 12.8 %collective-permute-done.7 = bf16[1,2048,128]{2,1,0:T(8,128)(2,1)S(1)} collective-permute-done((bf16[1,2048,128]{2,1,0:T(8,128)(2,1)S(1)}, bf16[1,2048,128]{2,1,0:T(8,128)(2,1)S(1)}, u32[]{:S(2)}, u32[]{:S(2)}) %collective-permute-start.7) | collective-permute-done | bytes 524320 | tf_op jit(solution)/shard_map/ppermute | solution.py:130
  61.9 0.9 %fusion.13 = bf16[2048,128]{1,0:T(8,128)(2,1)} fusion(bf16[1,2048,128]{2,1,0:T(8,128)(2,1)S(1)} %collective-permute-done.7, f32[2,2048,128]{2,1,0:T(8,128)S(1)} %convert_add_fusion, s32[]{:T(128)S(6)} %select_n.59), kind=kLoop, calls=%fused_computation.16 | loop fusion | flops 786432 | bytes 2097156 | tf_op jit(solution)/shard_map/convert_element_type | solution.py:134
  (31 shorter events, 1.0 us)
Async XLA Ops:
  2.3 16.9 %copy-start.4 = (bf16[128,512]{1,0:T(8,128)(2,1)}, bf16[128,512]{1,0:T(8,128)(2,1)S(1)}, u32[]{:S(2)}) copy-start(bf16[128,512]{1,0:T(8,128)(2,1)S(1)} %constant_dynamic-update-slice_fusion.refs_0_) | copy-start | bytes 393220
  2.3 9.2 %collective-permute-start.2 = (bf16[128,512]{1,0:T(8,128)(2,1)S(1)}, bf16[128,512]{1,0:T(8,128)(2,1)S(1)}, u32[]{:S(2)}, u32[]{:S(2)}) collective-permute-start(bf16[128,512]{1,0:T(8,128)(2,1)S(1)} %constant_dynamic-update-slice_fusion.refs_0_), channel_id=1, source_target_pairs={{0,12},{4,0},{8,4},{12,8},{1,13},{5,1},{9,5},{13,9},{2,14},{6,2},{... | collective-permute-start | bytes 393224 | tf_op jit(solution)/shard_map/ppermute | solution.py:43
  7.4 11.2 %collective-permute-start.1 = (bf16[128,512]{1,0:T(8,128)(2,1)S(1)}, bf16[128,512]{1,0:T(8,128)(2,1)S(1)}, u32[]{:S(2)}, u32[]{:S(2)}) collective-permute-start(bf16[128,512]{1,0:T(8,128)(2,1)S(1)} %constant_dynamic-update-slice_fusion.refs_0_), channel_id=1, source_target_pairs={{0,8},{4,12},{8,0},{12,4},{1,9},{5,13},{9,1},{13,5},{2,10},{6,14},... | collective-permute-start | bytes 393224 | tf_op jit(solution)/shard_map/ppermute | solution.py:43
  7.4 11.2 %collective-permute-start = (bf16[128,512]{1,0:T(8,128)(2,1)S(1)}, bf16[128,512]{1,0:T(8,128)(2,1)S(1)}, u32[]{:S(2)}, u32[]{:S(2)}) collective-permute-start(bf16[128,512]{1,0:T(8,128)(2,1)S(1)} %constant_dynamic-update-slice_fusion.refs_0_), channel_id=1, source_target_pairs={{0,4},{4,8},{8,12},{12,0},{1,5},{5,9},{9,13},{13,1},{2,6},{6,10},{... | collective-permute-start | bytes 393224 | tf_op jit(solution)/shard_map/ppermute | solution.py:43
  11.5 7.8 %copy-start.6 = (bf16[128,512]{1,0:T(8,128)(2,1)}, bf16[128,512]{1,0:T(8,128)(2,1)S(1)}, u32[]{:S(2)}) copy-start(bf16[128,512]{1,0:T(8,128)(2,1)S(1)} %collective-permute-done.2.refs_3_) | copy-start | bytes 393220
  18.6 0.7 %copy-start.7 = (bf16[128,512]{1,0:T(8,128)(2,1)}, bf16[128,512]{1,0:T(8,128)(2,1)S(1)}, u32[]{:S(2)}) copy-start(bf16[128,512]{1,0:T(8,128)(2,1)S(1)} %collective-permute-done.1.refs_2_) | copy-start | bytes 393220
  18.6 0.7 %copy-start.8 = (bf16[128,512]{1,0:T(8,128)(2,1)}, bf16[128,512]{1,0:T(8,128)(2,1)S(1)}, u32[]{:S(2)}) copy-start(bf16[128,512]{1,0:T(8,128)(2,1)S(1)} %collective-permute-done.refs_1_) | copy-start | bytes 393220
  25.9 13.0 %collective-permute-start.3 = (bf16[128,512]{1,0:T(8,128)(2,1)}, bf16[128,512]{1,0:T(8,128)(2,1)S(1)}, u32[]{:S(2)}, u32[]{:S(2)}) collective-permute-start(bf16[128,512]{1,0:T(8,128)(2,1)} %get-tuple-element.11), channel_id=1, source_target_pairs={{0,12},{4,0},{8,4},{12,8},{1,13},{5,1},{9,5},{13,9},{2,14},{6,2},{... | collective-permute-start | bytes 393224 | tf_op jit(solution)/shard_map/ppermute | solution.py:69
  27.5 12.5 %collective-permute-start.4 = (bf16[128,512]{1,0:T(8,128)(2,1)}, bf16[128,512]{1,0:T(8,128)(2,1)S(1)}, u32[]{:S(2)}, u32[]{:S(2)}) collective-permute-start(bf16[128,512]{1,0:T(8,128)(2,1)} %get-tuple-element.12), channel_id=1, source_target_pairs={{0,8},{4,12},{8,0},{12,4},{1,9},{5,13},{9,1},{13,5},{2,10},{6,14},... | collective-permute-start | bytes 393224 | tf_op jit(solution)/shard_map/ppermute | solution.py:69
  28.5 11.5 %collective-permute-start.5 = (bf16[128,512]{1,0:T(8,128)(2,1)}, bf16[128,512]{1,0:T(8,128)(2,1)S(1)}, u32[]{:S(2)}, u32[]{:S(2)}) collective-permute-start(bf16[128,512]{1,0:T(8,128)(2,1)} %get-tuple-element.13), channel_id=1, source_target_pairs={{0,4},{4,8},{8,12},{12,0},{1,5},{5,9},{9,13},{13,1},{2,6},{6,10},{... | collective-permute-start | bytes 393224 | tf_op jit(solution)/shard_map/ppermute | solution.py:69
  34.7 5.4 %copy-start.5 = (f32[128,512]{1,0:T(8,128)S(1)}, f32[128,512]{1,0:T(8,128)}, u32[]{:S(2)}) copy-start(f32[128,512]{1,0:T(8,128)} %get-tuple-element.10) | copy-start | bytes 786436
  40.2 3.7 %copy-start.3 = (bf16[128,256]{1,0:T(8,128)(2,1)}, bf16[128,256]{1,0:T(8,128)(2,1)S(1)}, u32[]{:S(2)}) copy-start(bf16[128,256]{1,0:T(8,128)(2,1)S(1)} %get-tuple-element.15) | copy-start | bytes 196612
  40.2 6.3 %copy-start.2 = (bf16[128,256]{1,0:T(8,128)(2,1)}, bf16[128,256]{1,0:T(8,128)(2,1)S(1)}, u32[]{:S(2)}) copy-start(bf16[128,256]{1,0:T(8,128)(2,1)S(1)} %get-tuple-element.14) | copy-start | bytes 196612
  40.2 2.9 %copy-start = (bf16[8192,256]{1,0:T(8,128)(2,1)S(1)}, bf16[8192,256]{1,0:T(8,128)(2,1)}, u32[]{:S(2)}) copy-start(bf16[8192,256]{1,0:T(8,128)(2,1)} %shard_map.113) | copy-start | bytes 12582916
  43.8 2.7 %collective-permute-start.6 = (bf16[2,2048,128]{2,1,0:T(8,128)(2,1)S(1)}, bf16[2,2048,128]{2,1,0:T(8,128)(2,1)S(1)}, u32[]{:S(2)}, u32[]{:S(2)}) collective-permute-start(bf16[2,2048,128]{2,1,0:T(8,128)(2,1)S(1)} %fusion), channel_id=1, source_target_pairs={{0,1},{1,0},{2,3},{3,2},{4,5},{5,4},{6,7},{7,6},{8,9},{9,8},{10,11... | collective-permute-start | bytes 3145736 | tf_op jit(solution)/shard_map/ppermute | solution.py:122
  43.9 2.8 %copy-start.1 = (bf16[8192,256]{1,0:T(8,128)(2,1)S(1)}, bf16[8192,256]{1,0:T(8,128)(2,1)}, u32[]{:S(2)}) copy-start(bf16[8192,256]{1,0:T(8,128)(2,1)} %shard_map.113) | copy-start | bytes 12582916
  47.5 14.3 %collective-permute-start.7 = (bf16[1,2048,128]{2,1,0:T(8,128)(2,1)S(1)}, bf16[1,2048,128]{2,1,0:T(8,128)(2,1)S(1)}, u32[]{:S(2)}, u32[]{:S(2)}) collective-permute-start(bf16[1,2048,128]{2,1,0:T(8,128)(2,1)S(1)} %dynamic-slice_convert_fusion), channel_id=1, source_target_pairs={{0,2},{1,3},{2,0},{3,1},{4,6},{5,7},{6,4},{7,5},{8,10},{9,11},{10,... | collective-permute-start | bytes 1572872 | tf_op jit(solution)/shard_map/ppermute | solution.py:130

commit v19 on v18

--- a/solution.py
+++ b/solution.py
@@ -145,7 +145,12 @@
     rows = query_ref.shape[0]
     group_size = query_ref.shape[1] // kv_cols
     if mask_ref.shape[0] == 1:
-        allowed = mask_ref[...] > 0
+        key_count = refs[0].shape[0] * slot_count
+        column_block = lax.broadcasted_iota(jnp.int32, (1, key_count), 1) // BLK
+        flags = jnp.zeros((1, key_count), jnp.int32)
+        for block in range(mask_ref.shape[1]):
+            flags = jnp.where(column_block == block, mask_ref[0, block], flags)
+        allowed = flags > 0
     else:
         allowed = jnp.concatenate([mask_ref[...]] * group_size, axis=0) > 0
     across = (((1,), (1,)), ((), ()))
@@ -202,8 +207,12 @@
 def attention_block(queries, out_grad, kv_pieces, allowed, interpret=False):
     rows = queries.shape[0]
     width = kv_pieces[0].shape[1]
+    small_mask = allowed.shape[0] == 1
+    mask_spec = pl.BlockSpec(memory_space=pltpu.SMEM if small_mask else pltpu.VMEM)
+    other_spec = pl.BlockSpec(memory_space=pltpu.VMEM)
     return pl.pallas_call(
         attention_kernel,
+        in_specs=[other_spec, other_spec, mask_spec] + [other_spec] * len(kv_pieces),
         out_shape=(
             jax.ShapeDtypeStruct(queries.shape, jnp.bfloat16),
             jax.ShapeDtypeStruct((rows, width), jnp.float32),
@@ -302,8 +311,7 @@
 
     if steps == 1 and lax.axis_size("ctx") <= 8:
         if rows_here == BLK:
-            column_flags = select_cols(own_flags, key_doc_blocks) > 0
-            allowed = jnp.repeat(column_flags, BLK, axis=1)
+            allowed = select_cols(own_flags, key_doc_blocks) > 0
         else:
             allowed = chunk(0)[2]
         query_grad, own_part, *sent_parts = attention_block(queries, out_grad, kv_pieces, allowed)

time: 63.1 us -> 63.1 us (level)
    unnamed x19, local copies, waits for them, and re-layouts: 1.53 us -> 2.77 us
    broadcast_in_dim x1 -> x0, local copies, waits for them, and re-layouts: 0.66 us -> none  [local(): allowed = jnp.repeat(column_flags, BLK, axis=1)]
  transfers between devices with their start and end apart: 8 -> 8, of which waited for: 4 -> 4; matrix products, arithmetic and copies ran while one was open for 9% -> 10% of each run, Pallas kernels for 13% -> 13%
where the time goes in v19:
time: 63.1 us; the launch traced here: 62.8 us
  waiting for transfers between devices  20.7 us (33%)
  Pallas kernels  15 us (24%)
  starting transfers between devices  11.7 us (19%)
  matrix products  6.33 us (10%)
  local copies, waits for them, and re-layouts  4.93 us (8%)
  other arithmetic  3.31 us (5%)
  between operations  0.81 us (1%)
    ppermute x1, waiting for transfers between devices, head_reduce(): lax.ppermute(sent.astype(jnp.bfloat16), 'head', [(i, i ^ 1 << level) for...  12.8 us
    pallas_call x2, Pallas kernels, staged(): pl.pallas_call(copy_to_vmem, out_shape=jax.ShapeDtypeStruct(weights.shape...  8.33 us
    pallas_call x1, Pallas kernels, attention_block(): pl.pallas_call(attention_kernel, in_specs=[other_spec, other_spec, mask_s...  6.65 us
    ppermute x3, waiting for transfers between devices, gather_slots(): lax.ppermute(block, axis, shifted_pairs(count, steps))  6.59 us
    ppermute x3, starting transfers between devices, gather_slots(): lax.ppermute(block, axis, shifted_pairs(count, steps))  6.06 us
    dot_general x2, matrix products, project(): jnp.einsum('arf,tf->art', lax.dynamic_index_in_dim(key_split, half, 1, ke...  4.88 us
    ppermute x3, starting transfers between devices, scatter_parts(): lax.ppermute(sent[steps - 1], axis, shifted_pairs(count, -steps))  4.03 us
    unnamed x19, local copies, waits for them, and re-layouts  2.77 us
  transfers between devices with their start and end apart: 8, of which 4 were waited for; matrix products, arithmetic and copies ran while one was open for 10% of the time, Pallas kernels for 13%

profile of v19, /device:TPU:0, one launch (start us, length us, event | category | flops | bytes accessed | tf_op | source)
XLA Modules:
  0.0 62.8 jit_solution(619648347250016047)
XLA Ops:
  0.6 0.8 %constant_dynamic-update-slice_fusion.1 = bf16[128,512]{1,0:T(8,128)(2,1)S(1)} fusion(bf16[128,256]{1,0:T(8,128)(2,1)} %param.9), kind=kLoop, calls=%fused_computation.23 | loop fusion | bytes 131072
  1.5 0.8 %constant_dynamic-update-slice_fusion.refs_0_ = bf16[128,512]{1,0:T(8,128)(2,1)S(1)} fusion(bf16[128,512]{1,0:T(8,128)(2,1)S(1)} %constant_dynamic-update-slice_fusion.1, bf16[128,256]{1,0:T(8,128)(2,1)} %param.10), kind=kLoop, calls=%fused_computation.22 | loop fusion | bytes 131072 | tf_op jit(solution)/shard_map/concatenate | solution.py:244
  2.3 5.0 %collective-permute-start.2 = (bf16[128,512]{1,0:T(8,128)(2,1)S(1)}, bf16[128,512]{1,0:T(8,128)(2,1)S(1)}, u32[]{:S(2)}, u32[]{:S(2)}) collective-permute-start(bf16[128,512]{1,0:T(8,128)(2,1)S(1)} %constant_dynamic-update-slice_fusion.refs_0_), channel_id=1, source_target_pairs={{0,12},{4,0},{8,4},{12,8},{1,13},{5,1},{9,5},{13,9},{2,14},{6,2},{... | collective-permute-start | bytes 393224 | tf_op jit(solution)/shard_map/ppermute | solution.py:43
  7.4 1.0 %collective-permute-start = (bf16[128,512]{1,0:T(8,128)(2,1)S(1)}, bf16[128,512]{1,0:T(8,128)(2,1)S(1)}, u32[]{:S(2)}, u32[]{:S(2)}) collective-permute-start(bf16[128,512]{1,0:T(8,128)(2,1)S(1)} %constant_dynamic-update-slice_fusion.refs_0_), channel_id=1, source_target_pairs={{0,4},{4,8},{8,12},{12,0},{1,5},{5,9},{9,13},{13,1},{2,6},{6,10},{... | collective-permute-start | bytes 393224 | tf_op jit(solution)/shard_map/ppermute | solution.py:43
  8.4 1.2 %dynamic_slice.19 = s32[1]{0:T(128)} dynamic-slice(s32[4]{0:T(128)} %param.13, s32[]{:T(128)S(6)} %select_n.53), dynamic_slice_sizes={1} | dynamic-slice | bytes 12 | tf_op jit(solution)/shard_map/dynamic_slice | solution.py:238
  9.6 0.6 %compare_convert_fusion.1 = s32[4]{0:T(128)S(1)} fusion(s32[]{:T(128)} %bitcast), kind=kLoop, calls=%fused_computation.34 | loop fusion | flops 8 | bytes 20 | tf_op jit(solution)/shard_map/convert_element_type | solution.py:18
  10.4 0.9 %multiply_reduce_fusion = (s32[4]{0:T(128)S(1)}, s32[4]{0:T(128)S(1)}) fusion(s32[4,4]{1,0:T(4,128)} %param.12, s32[4]{0:T(128)S(1)} %compare_convert_fusion.1, s32[4]{0:T(128)} %param.13, s32[4]{0:T(128)S(1)} %select_reduce_fusion.2), kind=kLoop, calls=%fused_computation.27 | loop fusion | flops 72 | bytes 144 | tf_op jit(solution)/shard_map/reduce_sum | solution.py:19
  11.5 0.5 fusion.22.mask_ref
  12.0 6.6 %collective-permute-done.1.refs_2_ = bf16[128,512]{1,0:T(8,128)(2,1)S(1)} collective-permute-done((bf16[128,512]{1,0:T(8,128)(2,1)S(1)}, bf16[128,512]{1,0:T(8,128)(2,1)S(1)}, u32[]{:S(2)}, u32[]{:S(2)}) %collective-permute-start.1) | collective-permute-done | bytes 131104 | tf_op jit(solution)/shard_map/ppermute | solution.py:43
  18.6 0.6 copy-done.7
  19.2 0.7 %copy-done.8 = bf16[128,512]{1,0:T(8,128)(2,1)} copy-done((bf16[128,512]{1,0:T(8,128)(2,1)}, bf16[128,512]{1,0:T(8,128)(2,1)S(1)}, u32[]{:S(2)}) %copy-start.8) | copy-done | bytes 131096
  19.9 6.7 %shard_map.111 = (bf16[128,2048]{1,0:T(8,128)(2,1)}, f32[128,512]{1,0:T(8,128)}, bf16[128,512]{1,0:T(8,128)(2,1)}, bf16[128,512]{1,0:T(8,128)(2,1)}, bf16[128,512]{1,0:T(8,128)(2,1)}) custom-call(bf16[128,2048]{1,0:T(8,128)(2,1)} %query_ref.1, bf16[128,2048]{1,0:T(8,128)(2,1)} %grad_ref.1, s32[1,4]{1,0:T(1,128)} %fusion.22.mask_ref, ...), custom_call_target="tpu_custom_call" | custom-call | tf_op jit(solution)/shard_map/pallas_call | solution.py:213
  26.5 1.6 %collective-permute-start.3 = (bf16[128,512]{1,0:T(8,128)(2,1)}, bf16[128,512]{1,0:T(8,128)(2,1)S(1)}, u32[]{:S(2)}, u32[]{:S(2)}) collective-permute-start(bf16[128,512]{1,0:T(8,128)(2,1)} %get-tuple-element.11), channel_id=1, source_target_pairs={{0,12},{4,0},{8,4},{12,8},{1,13},{5,1},{9,5},{13,9},{2,14},{6,2},{... | collective-permute-start | bytes 393224 | tf_op jit(solution)/shard_map/ppermute | solution.py:69
  28.6 2.0 %collective-permute-start.5 = (bf16[128,512]{1,0:T(8,128)(2,1)}, bf16[128,512]{1,0:T(8,128)(2,1)S(1)}, u32[]{:S(2)}, u32[]{:S(2)}) collective-permute-start(bf16[128,512]{1,0:T(8,128)(2,1)} %get-tuple-element.13), channel_id=1, source_target_pairs={{0,4},{4,8},{8,12},{12,0},{1,5},{5,9},{9,13},{13,1},{2,6},{6,10},{... | collective-permute-start | bytes 393224 | tf_op jit(solution)/shard_map/ppermute | solution.py:69
  30.6 4.1 %shard_map.112 = bf16[8192,256]{1,0:T(8,128)(2,1)} custom-call(bf16[8192,256]{1,0:T(8,128)(2,1)} %source.2), custom_call_target="tpu_custom_call" | custom-call | tf_op jit(solution)/shard_map/pallas_call | solution.py:80
  34.7 4.2 %shard_map.113 = bf16[8192,256]{1,0:T(8,128)(2,1)} custom-call(bf16[8192,256]{1,0:T(8,128)(2,1)} %source.3), custom_call_target="tpu_custom_call" | custom-call | tf_op jit(solution)/shard_map/pallas_call | solution.py:80
  38.9 1.2 %collective-permute-done.4 = bf16[128,512]{1,0:T(8,128)(2,1)S(1)} collective-permute-done((bf16[128,512]{1,0:T(8,128)(2,1)}, bf16[128,512]{1,0:T(8,128)(2,1)S(1)}, u32[]{:S(2)}, u32[]{:S(2)}) %collective-permute-start.4) | collective-permute-done | bytes 131104 | tf_op jit(solution)/shard_map/ppermute | solution.py:69
  40.2 2.4 %fusion.2 = f32[2,2048,128]{2,1,0:T(8,128)S(1)} fusion(bf16[2,2,2048,256]{3,2,1,0:T(8,128)(2,1)} %bitcast.31, s32[]{:T(128)S(6)} %select_n.56, bf16[128,256]{1,0:T(8,128)(2,1)S(1)} %get-tuple-element.15), kind=kOutput, calls=%fused_computation.4 | convolution fusion | flops 268435456 | bytes 4259844 | tf_op jit(solution)/shard_map/arf,tf->art/dot_general | solution.py:107
  43.0 0.7 %fusion = bf16[2,2048,128]{2,1,0:T(8,128)(2,1)S(1)} fusion(f32[2,2048,128]{2,1,0:T(8,128)S(1)} %fusion.2, bf16[2,2,2048,256]{3,2,1,0:T(8,128)(2,1)S(1)} %bitcast.33, s32[]{:T(128)S(6)} %select_n.56, bf16[128,256]{1,0:T(8,128)(2,1)S(1)} %get-tuple-element.14), kind=kOutput, calls=%fused_computation.2 | convolution fusion | flops 269484032 | bytes 5308420 | tf_op jit(solution)/shard_map/arf,tf->art/dot_general | solution.py:112
  43.9 2.4 %fusion.5 = f32[2,2048,128]{2,1,0:T(8,128)S(1)} fusion(bf16[2,2,2048,256]{3,2,1,0:T(8,128)(2,1)} %bitcast.32, s32[]{:T(128)S(6)} %select_n.55, bf16[128,256]{1,0:T(8,128)(2,1)S(1)} %get-tuple-element.15), kind=kOutput, calls=%fused_computation.7 | convolution fusion | flops 268435456 | bytes 4259844 | tf_op jit(solution)/shard_map/arf,tf->art/dot_general | solution.py:107
  46.7 0.7 %convert_add_fusion = f32[2,2048,128]{2,1,0:T(8,128)S(1)} fusion(bf16[2,2048,128]{2,1,0:T(8,128)(2,1)S(1)} %collective-permute-done.6, f32[2,2048,128]{2,1,0:T(8,128)S(1)} %fusion.5, bf16[2,2,2048,256]{3,2,1,0:T(8,128)(2,1)S(1)} %bitcast.34, s32[]{:T(128)S(6)} %select_n.55, bf16[128,256]{1,0:T(8,128)(2,1)S(1)} %get-tuple-element.14), kind=kOutput, calls=%fused_computation.9 | convolution fusion | flops 270008320 | bytes 7405572 | tf_op jit(solution)/shard_map/arf,tf->art/dot_general | solution.py:112
  47.5 1.6 %collective-permute-start.7 = (bf16[1,2048,128]{2,1,0:T(8,128)(2,1)S(1)}, bf16[1,2048,128]{2,1,0:T(8,128)(2,1)S(1)}, u32[]{:S(2)}, u32[]{:S(2)}) collective-permute-start(bf16[1,2048,128]{2,1,0:T(8,128)(2,1)S(1)} %dynamic-slice_convert_fusion), channel_id=1, source_target_pairs={{0,2},{1,3},{2,0},{3,1},{4,6},{5,7},{6,4},{7,5},{8,10},{9,11},{10,... | collective-permute-start | bytes 1572872 | tf_op jit(solution)/shard_map/ppermute | solution.py:130
  49.1 12.8 %collective-permute-done.7 = bf16[1,2048,128]{2,1,0:T(8,128)(2,1)S(1)} collective-permute-done((bf16[1,2048,128]{2,1,0:T(8,128)(2,1)S(1)}, bf16[1,2048,128]{2,1,0:T(8,128)(2,1)S(1)}, u32[]{:S(2)}, u32[]{:S(2)}) %collective-permute-start.7) | collective-permute-done | bytes 524320 | tf_op jit(solution)/shard_map/ppermute | solution.py:130
  61.9 0.9 %fusion.13 = bf16[2048,128]{1,0:T(8,128)(2,1)} fusion(bf16[1,2048,128]{2,1,0:T(8,128)(2,1)S(1)} %collective-permute-done.7, f32[2,2048,128]{2,1,0:T(8,128)S(1)} %convert_add_fusion, s32[]{:T(128)S(6)} %select_n.59), kind=kLoop, calls=%fused_computation.16 | loop fusion | flops 786432 | bytes 2097156 | tf_op jit(solution)/shard_map/convert_element_type | solution.py:134
  (30 shorter events, 1.8 us)
Async XLA Ops:
  2.3 16.3 %copy-start.4 = (bf16[128,512]{1,0:T(8,128)(2,1)}, bf16[128,512]{1,0:T(8,128)(2,1)S(1)}, u32[]{:S(2)}) copy-start(bf16[128,512]{1,0:T(8,128)(2,1)S(1)} %constant_dynamic-update-slice_fusion.refs_0_) | copy-start | bytes 393220
  2.3 9.7 %collective-permute-start.2 = (bf16[128,512]{1,0:T(8,128)(2,1)S(1)}, bf16[128,512]{1,0:T(8,128)(2,1)S(1)}, u32[]{:S(2)}, u32[]{:S(2)}) collective-permute-start(bf16[128,512]{1,0:T(8,128)(2,1)S(1)} %constant_dynamic-update-slice_fusion.refs_0_), channel_id=1, source_target_pairs={{0,12},{4,0},{8,4},{12,8},{1,13},{5,1},{9,5},{13,9},{2,14},{6,2},{... | collective-permute-start | bytes 393224 | tf_op jit(solution)/shard_map/ppermute | solution.py:43
  7.4 11.2 %collective-permute-start.1 = (bf16[128,512]{1,0:T(8,128)(2,1)S(1)}, bf16[128,512]{1,0:T(8,128)(2,1)S(1)}, u32[]{:S(2)}, u32[]{:S(2)}) collective-permute-start(bf16[128,512]{1,0:T(8,128)(2,1)S(1)} %constant_dynamic-update-slice_fusion.refs_0_), channel_id=1, source_target_pairs={{0,8},{4,12},{8,0},{12,4},{1,9},{5,13},{9,1},{13,5},{2,10},{6,14},... | collective-permute-start | bytes 393224 | tf_op jit(solution)/shard_map/ppermute | solution.py:43
  7.4 11.2 %collective-permute-start = (bf16[128,512]{1,0:T(8,128)(2,1)S(1)}, bf16[128,512]{1,0:T(8,128)(2,1)S(1)}, u32[]{:S(2)}, u32[]{:S(2)}) collective-permute-start(bf16[128,512]{1,0:T(8,128)(2,1)S(1)} %constant_dynamic-update-slice_fusion.refs_0_), channel_id=1, source_target_pairs={{0,4},{4,8},{8,12},{12,0},{1,5},{5,9},{9,13},{13,1},{2,6},{6,10},{... | collective-permute-start | bytes 393224 | tf_op jit(solution)/shard_map/ppermute | solution.py:43
  12.0 6.6 %copy-start.6 = (bf16[128,512]{1,0:T(8,128)(2,1)}, bf16[128,512]{1,0:T(8,128)(2,1)S(1)}, u32[]{:S(2)}) copy-start(bf16[128,512]{1,0:T(8,128)(2,1)S(1)} %collective-permute-done.2.refs_3_) | copy-start | bytes 393220
  18.6 0.6 %copy-start.7 = (bf16[128,512]{1,0:T(8,128)(2,1)}, bf16[128,512]{1,0:T(8,128)(2,1)S(1)}, u32[]{:S(2)}) copy-start(bf16[128,512]{1,0:T(8,128)(2,1)S(1)} %collective-permute-done.1.refs_2_) | copy-start | bytes 393220
  19.2 0.7 %copy-start.8 = (bf16[128,512]{1,0:T(8,128)(2,1)}, bf16[128,512]{1,0:T(8,128)(2,1)S(1)}, u32[]{:S(2)}) copy-start(bf16[128,512]{1,0:T(8,128)(2,1)S(1)} %collective-permute-done.refs_1_) | copy-start | bytes 393220
  26.5 12.4 %collective-permute-start.3 = (bf16[128,512]{1,0:T(8,128)(2,1)}, bf16[128,512]{1,0:T(8,128)(2,1)S(1)}, u32[]{:S(2)}, u32[]{:S(2)}) collective-permute-start(bf16[128,512]{1,0:T(8,128)(2,1)} %get-tuple-element.11), channel_id=1, source_target_pairs={{0,12},{4,0},{8,4},{12,8},{1,13},{5,1},{9,5},{13,9},{2,14},{6,2},{... | collective-permute-start | bytes 393224 | tf_op jit(solution)/shard_map/ppermute | solution.py:69
  28.1 11.9 %collective-permute-start.4 = (bf16[128,512]{1,0:T(8,128)(2,1)}, bf16[128,512]{1,0:T(8,128)(2,1)S(1)}, u32[]{:S(2)}, u32[]{:S(2)}) collective-permute-start(bf16[128,512]{1,0:T(8,128)(2,1)} %get-tuple-element.12), channel_id=1, source_target_pairs={{0,8},{4,12},{8,0},{12,4},{1,9},{5,13},{9,1},{13,5},{2,10},{6,14},... | collective-permute-start | bytes 393224 | tf_op jit(solution)/shard_map/ppermute | solution.py:69
  28.6 11.5 %collective-permute-start.5 = (bf16[128,512]{1,0:T(8,128)(2,1)}, bf16[128,512]{1,0:T(8,128)(2,1)S(1)}, u32[]{:S(2)}, u32[]{:S(2)}) collective-permute-start(bf16[128,512]{1,0:T(8,128)(2,1)} %get-tuple-element.13), channel_id=1, source_target_pairs={{0,4},{4,8},{8,12},{12,0},{1,5},{5,9},{9,13},{13,1},{2,6},{6,10},{... | collective-permute-start | bytes 393224 | tf_op jit(solution)/shard_map/ppermute | solution.py:69
  34.7 5.4 %copy-start.5 = (f32[128,512]{1,0:T(8,128)S(1)}, f32[128,512]{1,0:T(8,128)}, u32[]{:S(2)}) copy-start(f32[128,512]{1,0:T(8,128)} %get-tuple-element.10) | copy-start | bytes 786436
  40.2 3.7 %copy-start.3 = (bf16[128,256]{1,0:T(8,128)(2,1)}, bf16[128,256]{1,0:T(8,128)(2,1)S(1)}, u32[]{:S(2)}) copy-start(bf16[128,256]{1,0:T(8,128)(2,1)S(1)} %get-tuple-element.15) | copy-start | bytes 196612
  40.2 6.3 %copy-start.2 = (bf16[128,256]{1,0:T(8,128)(2,1)}, bf16[128,256]{1,0:T(8,128)(2,1)S(1)}, u32[]{:S(2)}) copy-start(bf16[128,256]{1,0:T(8,128)(2,1)S(1)} %get-tuple-element.14) | copy-start | bytes 196612
  40.2 2.9 %copy-start = (bf16[8192,256]{1,0:T(8,128)(2,1)S(1)}, bf16[8192,256]{1,0:T(8,128)(2,1)}, u32[]{:S(2)}) copy-start(bf16[8192,256]{1,0:T(8,128)(2,1)} %shard_map.113) | copy-start | bytes 12582916
  43.8 2.7 %collective-permute-start.6 = (bf16[2,2048,128]{2,1,0:T(8,128)(2,1)S(1)}, bf16[2,2048,128]{2,1,0:T(8,128)(2,1)S(1)}, u32[]{:S(2)}, u32[]{:S(2)}) collective-permute-start(bf16[2,2048,128]{2,1,0:T(8,128)(2,1)S(1)} %fusion), channel_id=1, source_target_pairs={{0,1},{1,0},{2,3},{3,2},{4,5},{5,4},{6,7},{7,6},{8,9},{9,8},{10,11... | collective-permute-start | bytes 3145736 | tf_op jit(solution)/shard_map/ppermute | solution.py:122
  43.9 2.8 %copy-start.1 = (bf16[8192,256]{1,0:T(8,128)(2,1)S(1)}, bf16[8192,256]{1,0:T(8,128)(2,1)}, u32[]{:S(2)}) copy-start(bf16[8192,256]{1,0:T(8,128)(2,1)} %shard_map.113) | copy-start | bytes 12582916
  47.5 14.3 %collective-permute-start.7 = (bf16[1,2048,128]{2,1,0:T(8,128)(2,1)S(1)}, bf16[1,2048,128]{2,1,0:T(8,128)(2,1)S(1)}, u32[]{:S(2)}, u32[]{:S(2)}) collective-permute-start(bf16[1,2048,128]{2,1,0:T(8,128)(2,1)S(1)} %dynamic-slice_convert_fusion), channel_id=1, source_target_pairs={{0,2},{1,3},{2,0},{3,1},{4,6},{5,7},{6,4},{7,5},{8,10},{9,11},{10,... | collective-permute-start | bytes 1572872 | tf_op jit(solution)/shard_map/ppermute | solution.py:130

commit v20 on v18

--- a/solution.py
+++ b/solution.py
@@ -98,8 +98,6 @@
             jnp.bfloat16
         )
     block = key_proj.shape[0] // count
-    key_proj = staged(key_proj)
-    value_proj = staged(value_proj)
     key_split = key_proj.reshape(count // 2, 2, block, key_proj.shape[1])
     value_split = value_proj.reshape(count // 2, 2, block, value_proj.shape[1])
 

time: 63.1 us -> 64 us (1.014)
  Pallas kernels: 15 us -> 6.67 us
  waiting for transfers between devices: 21.2 us -> 29.5 us
  other arithmetic: 2.8 us -> 3.75 us
    ppermute x3, waiting for transfers between devices: 1.17 us -> 9.51 us  [scatter_parts(): lax.ppermute(sent[steps - 1], axis, shifted_pairs(count, -steps))]
    pallas_call x2 -> x0, Pallas kernels: 8.33 us -> none  [staged(): pl.pallas_call(copy_to_vmem, out_shape=jax.ShapeDtypeStruct(weights.shape...]
    another operation x1, other arithmetic: 0.06 us -> 1.01 us
    unnamed x19 -> x17, local copies, waits for them, and re-layouts: 1.53 us -> 1.54 us
  transfers between devices with their start and end apart: 8 -> 8, of which waited for: 4 -> 5; matrix products, arithmetic and copies ran while one was open for 9% -> 9% of each run, Pallas kernels for 13% -> 0%
where the time goes in v20:
time: 64 us; the launch traced here: 63.7 us
  waiting for transfers between devices  29.5 us (46%)
  starting transfers between devices  12.3 us (19%)
  Pallas kernels  6.67 us (10%)
  matrix products  6.32 us (10%)
  local copies, waits for them, and re-layouts  4.35 us (7%)
  other arithmetic  3.75 us (6%)
  between operations  0.81 us (1%)
    ppermute x1, waiting for transfers between devices, head_reduce(): lax.ppermute(sent.astype(jnp.bfloat16), 'head', [(i, i ^ 1 << level) for...  12.8 us
    ppermute x3, waiting for transfers between devices, scatter_parts(): lax.ppermute(sent[steps - 1], axis, shifted_pairs(count, -steps))  9.51 us
    ppermute x3, waiting for transfers between devices, gather_slots(): lax.ppermute(block, axis, shifted_pairs(count, steps))  7.09 us
    pallas_call x1, Pallas kernels, attention_block(): pl.pallas_call(attention_kernel, out_shape=(jax.ShapeDtypeStruct(queries....  6.67 us
    ppermute x3, starting transfers between devices, gather_slots(): lax.ppermute(block, axis, shifted_pairs(count, steps))  6.06 us
    dot_general x2, matrix products, project(): jnp.einsum('arf,tf->art', lax.dynamic_index_in_dim(key_split, half, 1, ke...  4.87 us
    ppermute x3, starting transfers between devices, scatter_parts(): lax.ppermute(sent[steps - 1], axis, shifted_pairs(count, -steps))  4.63 us
    ppermute x1, starting transfers between devices, head_reduce(): lax.ppermute(sent.astype(jnp.bfloat16), 'head', [(i, i ^ 1 << level) for...  1.56 us
  transfers between devices with their start and end apart: 8, of which 5 were waited for; matrix products, arithmetic and copies ran while one was open for 9% of the time, Pallas kernels for 0%

profile of v20, /device:TPU:0, one launch (start us, length us, event | category | flops | bytes accessed | tf_op | source)
XLA Modules:
  0.0 63.7 jit_solution(3880306517282745123)
XLA Ops:
  0.6 0.8 %constant_dynamic-update-slice_fusion.1 = bf16[128,512]{1,0:T(8,128)(2,1)S(1)} fusion(bf16[128,256]{1,0:T(8,128)(2,1)} %param.9), kind=kLoop, calls=%fused_computation.23 | loop fusion | bytes 131072
  1.5 0.8 %constant_dynamic-update-slice_fusion.refs_0_ = bf16[128,512]{1,0:T(8,128)(2,1)S(1)} fusion(bf16[128,512]{1,0:T(8,128)(2,1)S(1)} %constant_dynamic-update-slice_fusion.1, bf16[128,256]{1,0:T(8,128)(2,1)} %param.10), kind=kLoop, calls=%fused_computation.22 | loop fusion | bytes 131072 | tf_op jit(solution)/shard_map/concatenate | solution.py:233
  2.3 5.0 %collective-permute-start.2 = (bf16[128,512]{1,0:T(8,128)(2,1)S(1)}, bf16[128,512]{1,0:T(8,128)(2,1)S(1)}, u32[]{:S(2)}, u32[]{:S(2)}) collective-permute-start(bf16[128,512]{1,0:T(8,128)(2,1)S(1)} %constant_dynamic-update-slice_fusion.refs_0_), channel_id=1, source_target_pairs={{0,12},{4,0},{8,4},{12,8},{1,13},{5,1},{9,5},{13,9},{2,14},{6,2},{... | collective-permute-start | bytes 393224 | tf_op jit(solution)/shard_map/ppermute | solution.py:43
  7.4 1.0 %collective-permute-start = (bf16[128,512]{1,0:T(8,128)(2,1)S(1)}, bf16[128,512]{1,0:T(8,128)(2,1)S(1)}, u32[]{:S(2)}, u32[]{:S(2)}) collective-permute-start(bf16[128,512]{1,0:T(8,128)(2,1)S(1)} %constant_dynamic-update-slice_fusion.refs_0_), channel_id=1, source_target_pairs={{0,4},{4,8},{8,12},{12,0},{1,5},{5,9},{9,13},{13,1},{2,6},{6,10},{... | collective-permute-start | bytes 393224 | tf_op jit(solution)/shard_map/ppermute | solution.py:43
  8.4 1.2 %dynamic_slice.19 = s32[1]{0:T(128)} dynamic-slice(s32[4]{0:T(128)} %param.13, s32[]{:T(128)S(6)} %select_n.53), dynamic_slice_sizes={1} | dynamic-slice | bytes 12 | tf_op jit(solution)/shard_map/dynamic_slice | solution.py:227
  9.6 0.6 %compare_convert_fusion.1 = s32[4]{0:T(128)S(1)} fusion(s32[]{:T(128)} %bitcast), kind=kLoop, calls=%fused_computation.34 | loop fusion | flops 8 | bytes 20 | tf_op jit(solution)/shard_map/convert_element_type | solution.py:18
  10.4 0.9 %multiply_reduce_fusion = (s32[4]{0:T(128)S(1)}, s32[4]{0:T(128)S(1)}) fusion(s32[4,4]{1,0:T(4,128)} %param.12, s32[4]{0:T(128)S(1)} %compare_convert_fusion.1, s32[4]{0:T(128)} %param.13, s32[4]{0:T(128)S(1)} %select_reduce_fusion.2), kind=kLoop, calls=%fused_computation.27 | loop fusion | flops 72 | bytes 144 | tf_op jit(solution)/shard_map/reduce_sum | solution.py:19
  11.5 7.1 %collective-permute-done.1.refs_2_ = bf16[128,512]{1,0:T(8,128)(2,1)S(1)} collective-permute-done((bf16[128,512]{1,0:T(8,128)(2,1)S(1)}, bf16[128,512]{1,0:T(8,128)(2,1)S(1)}, u32[]{:S(2)}, u32[]{:S(2)}) %collective-permute-start.1) | collective-permute-done | bytes 131104 | tf_op jit(solution)/shard_map/ppermute | solution.py:43
  18.6 0.7 %broadcast_in_dim.2 = s32[4,128]{1,0:T(4,128)} broadcast(s32[4]{0:T(128)S(1)} %compare_convert_fusion), dimensions={0} | broadcast | bytes 2064 | tf_op jit(solution)/shard_map/broadcast_in_dim | solution.py:304
  19.3 6.7 %shard_map.111 = (bf16[128,2048]{1,0:T(8,128)(2,1)}, f32[128,512]{1,0:T(8,128)}, bf16[128,512]{1,0:T(8,128)(2,1)}, bf16[128,512]{1,0:T(8,128)(2,1)}, bf16[128,512]{1,0:T(8,128)(2,1)}) custom-call(bf16[128,2048]{1,0:T(8,128)(2,1)} %query_ref.1, bf16[128,2048]{1,0:T(8,128)(2,1)} %grad_ref.1, s32[1,512]{1,0:T(1,128)} %bitcast.42, bf16[128,512]{1,0:T(8,128)(2,1)} %copy-done.4, ...), custom_call_target="tpu_custom_call" | custom-call | tf_op jit(solution)/shard_map/pallas_call | solution.py:203
  25.9 1.6 %collective-permute-start.3 = (bf16[128,512]{1,0:T(8,128)(2,1)}, bf16[128,512]{1,0:T(8,128)(2,1)S(1)}, u32[]{:S(2)}, u32[]{:S(2)}) collective-permute-start(bf16[128,512]{1,0:T(8,128)(2,1)} %get-tuple-element.11), channel_id=1, source_target_pairs={{0,12},{4,0},{8,4},{12,8},{1,13},{5,1},{9,5},{13,9},{2,14},{6,2},{... | collective-permute-start | bytes 393224 | tf_op jit(solution)/shard_map/ppermute | solution.py:69
  27.5 1.0 %collective-permute-start.4 = (bf16[128,512]{1,0:T(8,128)(2,1)}, bf16[128,512]{1,0:T(8,128)(2,1)S(1)}, u32[]{:S(2)}, u32[]{:S(2)}) collective-permute-start(bf16[128,512]{1,0:T(8,128)(2,1)} %get-tuple-element.12), channel_id=1, source_target_pairs={{0,8},{4,12},{8,0},{12,4},{1,9},{5,13},{9,1},{13,5},{2,10},{6,14},... | collective-permute-start | bytes 393224 | tf_op jit(solution)/shard_map/ppermute | solution.py:69
  28.5 2.0 %collective-permute-start.5 = (bf16[128,512]{1,0:T(8,128)(2,1)}, bf16[128,512]{1,0:T(8,128)(2,1)S(1)}, u32[]{:S(2)}, u32[]{:S(2)}) collective-permute-start(bf16[128,512]{1,0:T(8,128)(2,1)} %get-tuple-element.13), channel_id=1, source_target_pairs={{0,4},{4,8},{8,12},{12,0},{1,5},{5,9},{9,13},{13,1},{2,6},{6,10},{... | collective-permute-start | bytes 393224 | tf_op jit(solution)/shard_map/ppermute | solution.py:69
  30.6 1.2 %collective-permute-done.3 = bf16[128,512]{1,0:T(8,128)(2,1)S(1)} collective-permute-done((bf16[128,512]{1,0:T(8,128)(2,1)}, bf16[128,512]{1,0:T(8,128)(2,1)S(1)}, u32[]{:S(2)}, u32[]{:S(2)}) %collective-permute-start.3) | collective-permute-done | bytes 131104 | tf_op jit(solution)/shard_map/ppermute | solution.py:69
  31.8 8.3 %collective-permute-done.4 = bf16[128,512]{1,0:T(8,128)(2,1)S(1)} collective-permute-done((bf16[128,512]{1,0:T(8,128)(2,1)}, bf16[128,512]{1,0:T(8,128)(2,1)S(1)}, u32[]{:S(2)}, u32[]{:S(2)}) %collective-permute-start.4) | collective-permute-done | bytes 131104 | tf_op jit(solution)/shard_map/ppermute | solution.py:69
  40.1 1.0 %add_convert_fusion.1 = bf16[128,512]{1,0:T(8,128)(2,1)S(1)} fusion(bf16[128,512]{1,0:T(8,128)(2,1)S(1)} %collective-permute-done.5, bf16[128,512]{1,0:T(8,128)(2,1)S(1)} %collective-permute-done.4, f32[128,512]{1,0:T(8,128)} %get-tuple-element.10, bf16[128,512]{1,0:T(8,128)(2,1)S(1)} %collective-permute-done.3), kind=kLoop, calls=%fused_computation.17 | loop fusion | flops 458752 | bytes 786432 | tf_op jit(solution)/shard_map/convert.1
  41.2 2.4 %fusion.2 = f32[2,2048,128]{2,1,0:T(8,128)S(1)} fusion(bf16[2,2,2048,256]{3,2,1,0:T(8,128)(2,1)} %bitcast.38, s32[]{:T(128)S(6)} %select_n.56, bf16[128,256]{1,0:T(8,128)(2,1)S(1)} %get-tuple-element.15), kind=kOutput, calls=%fused_computation.4 | convolution fusion | flops 268435456 | bytes 4259844 | tf_op jit(solution)/shard_map/arf,tf->art/dot_general | solution.py:105
  43.6 0.4 copy-done
  44.0 0.7 %fusion = bf16[2,2048,128]{2,1,0:T(8,128)(2,1)S(1)} fusion(f32[2,2048,128]{2,1,0:T(8,128)S(1)} %fusion.2, bf16[2,2,2048,256]{3,2,1,0:T(8,128)(2,1)S(1)} %bitcast.40, s32[]{:T(128)S(6)} %select_n.56, bf16[128,256]{1,0:T(8,128)(2,1)S(1)} %get-tuple-element.14), kind=kOutput, calls=%fused_computation.2 | convolution fusion | flops 269484032 | bytes 5308420 | tf_op jit(solution)/shard_map/arf,tf->art/dot_general | solution.py:110
  44.9 2.4 %fusion.5 = f32[2,2048,128]{2,1,0:T(8,128)S(1)} fusion(bf16[2,2,2048,256]{3,2,1,0:T(8,128)(2,1)} %bitcast.39, s32[]{:T(128)S(6)} %select_n.55, bf16[128,256]{1,0:T(8,128)(2,1)S(1)} %get-tuple-element.15), kind=kOutput, calls=%fused_computation.7 | convolution fusion | flops 268435456 | bytes 4259844 | tf_op jit(solution)/shard_map/arf,tf->art/dot_general | solution.py:105
  47.7 0.7 %convert_add_fusion = f32[2,2048,128]{2,1,0:T(8,128)S(1)} fusion(bf16[2,2048,128]{2,1,0:T(8,128)(2,1)S(1)} %collective-permute-done.6, f32[2,2048,128]{2,1,0:T(8,128)S(1)} %fusion.5, bf16[2,2,2048,256]{3,2,1,0:T(8,128)(2,1)S(1)} %bitcast.41, s32[]{:T(128)S(6)} %select_n.55, bf16[128,256]{1,0:T(8,128)(2,1)S(1)} %get-tuple-element.14), kind=kOutput, calls=%fused_computation.9 | convolution fusion | flops 270008320 | bytes 7405572 | tf_op jit(solution)/shard_map/arf,tf->art/dot_general | solution.py:110
  48.5 1.6 %collective-permute-start.7 = (bf16[1,2048,128]{2,1,0:T(8,128)(2,1)S(1)}, bf16[1,2048,128]{2,1,0:T(8,128)(2,1)S(1)}, u32[]{:S(2)}, u32[]{:S(2)}) collective-permute-start(bf16[1,2048,128]{2,1,0:T(8,128)(2,1)S(1)} %dynamic-slice_convert_fusion), channel_id=1, source_target_pairs={{0,2},{1,3},{2,0},{3,1},{4,6},{5,7},{6,4},{7,5},{8,10},{9,11},{10,... | collective-permute-start | bytes 1572872 | tf_op jit(solution)/shard_map/ppermute | solution.py:128
  50.0 12.8 %collective-permute-done.7 = bf16[1,2048,128]{2,1,0:T(8,128)(2,1)S(1)} collective-permute-done((bf16[1,2048,128]{2,1,0:T(8,128)(2,1)S(1)}, bf16[1,2048,128]{2,1,0:T(8,128)(2,1)S(1)}, u32[]{:S(2)}, u32[]{:S(2)}) %collective-permute-start.7) | collective-permute-done | bytes 524320 | tf_op jit(solution)/shard_map/ppermute | solution.py:128
  62.8 0.9 %fusion.13 = bf16[2048,128]{1,0:T(8,128)(2,1)} fusion(bf16[1,2048,128]{2,1,0:T(8,128)(2,1)S(1)} %collective-permute-done.7, f32[2,2048,128]{2,1,0:T(8,128)S(1)} %convert_add_fusion, s32[]{:T(128)S(6)} %select_n.59), kind=kLoop, calls=%fused_computation.16 | loop fusion | flops 786432 | bytes 2097156 | tf_op jit(solution)/shard_map/convert_element_type | solution.py:132
  (27 shorter events, 0.9 us)
Async XLA Ops:
  2.3 16.9 %copy-start.4 = (bf16[128,512]{1,0:T(8,128)(2,1)}, bf16[128,512]{1,0:T(8,128)(2,1)S(1)}, u32[]{:S(2)}) copy-start(bf16[128,512]{1,0:T(8,128)(2,1)S(1)} %constant_dynamic-update-slice_fusion.refs_0_) | copy-start | bytes 393220
  2.3 9.2 %collective-permute-start.2 = (bf16[128,512]{1,0:T(8,128)(2,1)S(1)}, bf16[128,512]{1,0:T(8,128)(2,1)S(1)}, u32[]{:S(2)}, u32[]{:S(2)}) collective-permute-start(bf16[128,512]{1,0:T(8,128)(2,1)S(1)} %constant_dynamic-update-slice_fusion.refs_0_), channel_id=1, source_target_pairs={{0,12},{4,0},{8,4},{12,8},{1,13},{5,1},{9,5},{13,9},{2,14},{6,2},{... | collective-permute-start | bytes 393224 | tf_op jit(solution)/shard_map/ppermute | solution.py:43
  7.4 11.2 %collective-permute-start.1 = (bf16[128,512]{1,0:T(8,128)(2,1)S(1)}, bf16[128,512]{1,0:T(8,128)(2,1)S(1)}, u32[]{:S(2)}, u32[]{:S(2)}) collective-permute-start(bf16[128,512]{1,0:T(8,128)(2,1)S(1)} %constant_dynamic-update-slice_fusion.refs_0_), channel_id=1, source_target_pairs={{0,8},{4,12},{8,0},{12,4},{1,9},{5,13},{9,1},{13,5},{2,10},{6,14},... | collective-permute-start | bytes 393224 | tf_op jit(solution)/shard_map/ppermute | solution.py:43
  7.4 11.2 %collective-permute-start = (bf16[128,512]{1,0:T(8,128)(2,1)S(1)}, bf16[128,512]{1,0:T(8,128)(2,1)S(1)}, u32[]{:S(2)}, u32[]{:S(2)}) collective-permute-start(bf16[128,512]{1,0:T(8,128)(2,1)S(1)} %constant_dynamic-update-slice_fusion.refs_0_), channel_id=1, source_target_pairs={{0,4},{4,8},{8,12},{12,0},{1,5},{5,9},{9,13},{13,1},{2,6},{6,10},{... | collective-permute-start | bytes 393224 | tf_op jit(solution)/shard_map/ppermute | solution.py:43
  11.5 7.8 %copy-start.5 = (bf16[128,512]{1,0:T(8,128)(2,1)}, bf16[128,512]{1,0:T(8,128)(2,1)S(1)}, u32[]{:S(2)}) copy-start(bf16[128,512]{1,0:T(8,128)(2,1)S(1)} %collective-permute-done.2.refs_3_) | copy-start | bytes 393220
  18.6 0.7 %copy-start.6 = (bf16[128,512]{1,0:T(8,128)(2,1)}, bf16[128,512]{1,0:T(8,128)(2,1)S(1)}, u32[]{:S(2)}) copy-start(bf16[128,512]{1,0:T(8,128)(2,1)S(1)} %collective-permute-done.1.refs_2_) | copy-start | bytes 393220
  18.6 0.7 %copy-start.7 = (bf16[128,512]{1,0:T(8,128)(2,1)}, bf16[128,512]{1,0:T(8,128)(2,1)S(1)}, u32[]{:S(2)}) copy-start(bf16[128,512]{1,0:T(8,128)(2,1)S(1)} %collective-permute-done.refs_1_) | copy-start | bytes 393220
  25.9 5.9 %collective-permute-start.3 = (bf16[128,512]{1,0:T(8,128)(2,1)}, bf16[128,512]{1,0:T(8,128)(2,1)S(1)}, u32[]{:S(2)}, u32[]{:S(2)}) collective-permute-start(bf16[128,512]{1,0:T(8,128)(2,1)} %get-tuple-element.11), channel_id=1, source_target_pairs={{0,12},{4,0},{8,4},{12,8},{1,13},{5,1},{9,5},{13,9},{2,14},{6,2},{... | collective-permute-start | bytes 393224 | tf_op jit(solution)/shard_map/ppermute | solution.py:69
  27.5 12.5 %collective-permute-start.4 = (bf16[128,512]{1,0:T(8,128)(2,1)}, bf16[128,512]{1,0:T(8,128)(2,1)S(1)}, u32[]{:S(2)}, u32[]{:S(2)}) collective-permute-start(bf16[128,512]{1,0:T(8,128)(2,1)} %get-tuple-element.12), channel_id=1, source_target_pairs={{0,8},{4,12},{8,0},{12,4},{1,9},{5,13},{9,1},{13,5},{2,10},{6,14},... | collective-permute-start | bytes 393224 | tf_op jit(solution)/shard_map/ppermute | solution.py:69
  28.5 11.5 %collective-permute-start.5 = (bf16[128,512]{1,0:T(8,128)(2,1)}, bf16[128,512]{1,0:T(8,128)(2,1)S(1)}, u32[]{:S(2)}, u32[]{:S(2)}) collective-permute-start(bf16[128,512]{1,0:T(8,128)(2,1)} %get-tuple-element.13), channel_id=1, source_target_pairs={{0,4},{4,8},{8,12},{12,0},{1,5},{5,9},{9,13},{13,1},{2,6},{6,10},{... | collective-permute-start | bytes 393224 | tf_op jit(solution)/shard_map/ppermute | solution.py:69
  41.1 3.7 %copy-start.3 = (bf16[128,256]{1,0:T(8,128)(2,1)}, bf16[128,256]{1,0:T(8,128)(2,1)S(1)}, u32[]{:S(2)}) copy-start(bf16[128,256]{1,0:T(8,128)(2,1)S(1)} %get-tuple-element.15) | copy-start | bytes 196612
  41.1 6.3 %copy-start.2 = (bf16[128,256]{1,0:T(8,128)(2,1)}, bf16[128,256]{1,0:T(8,128)(2,1)S(1)}, u32[]{:S(2)}) copy-start(bf16[128,256]{1,0:T(8,128)(2,1)S(1)} %get-tuple-element.14) | copy-start | bytes 196612
  41.1 2.9 %copy-start = (bf16[8192,256]{1,0:T(8,128)(2,1)S(1)}, bf16[8192,256]{1,0:T(8,128)(2,1)}, u32[]{:S(2)}) copy-start(bf16[8192,256]{1,0:T(8,128)(2,1)} %param.15) | copy-start | bytes 12582916
  44.7 2.7 %collective-permute-start.6 = (bf16[2,2048,128]{2,1,0:T(8,128)(2,1)S(1)}, bf16[2,2048,128]{2,1,0:T(8,128)(2,1)S(1)}, u32[]{:S(2)}, u32[]{:S(2)}) collective-permute-start(bf16[2,2048,128]{2,1,0:T(8,128)(2,1)S(1)} %fusion), channel_id=1, source_target_pairs={{0,1},{1,0},{2,3},{3,2},{4,5},{5,4},{6,7},{7,6},{8,9},{9,8},{10,11... | collective-permute-start | bytes 3145736 | tf_op jit(solution)/shard_map/ppermute | solution.py:120
  44.8 2.8 %copy-start.1 = (bf16[8192,256]{1,0:T(8,128)(2,1)S(1)}, bf16[8192,256]{1,0:T(8,128)(2,1)}, u32[]{:S(2)}) copy-start(bf16[8192,256]{1,0:T(8,128)(2,1)} %param.15) | copy-start | bytes 12582916
  48.5 14.3 %collective-permute-start.7 = (bf16[1,2048,128]{2,1,0:T(8,128)(2,1)S(1)}, bf16[1,2048,128]{2,1,0:T(8,128)(2,1)S(1)}, u32[]{:S(2)}, u32[]{:S(2)}) collective-permute-start(bf16[1,2048,128]{2,1,0:T(8,128)(2,1)S(1)} %dynamic-slice_convert_fusion), channel_id=1, source_target_pairs={{0,2},{1,3},{2,0},{3,1},{4,6},{5,7},{6,4},{7,5},{8,10},{9,11},{10,... | collective-permute-start | bytes 1572872 | tf_op jit(solution)/shard_map/ppermute | solution.py:128
